TPU v7x, 128 devices: a whole 4x4x4 slice. The times are simulated.
128 devices in a mesh: face: 2 (over core), elem: 64 (over y, z, x).
Axes of the slice: x: 4, y: 4, z: 4, core: 2. Of those that a mesh axis runs over, the one named last changes fastest.
Arguments:
- state: float32 [432, 32, 8192], P(None, 'face', 'elem'), may hold values from -6 to 6
- speed_x: float32 [432], replicated, may hold values from -0.25 to 0.25
- speed_y: float32 [432], replicated, may hold values from -0.25 to 0.25
- w_in: bfloat16 [512, 432], replicated, may hold values from -0.3125 to 0.3125
- b_in: float32 [512], replicated, may hold values from -1.8 to 1.8
- w_mid: bfloat16 [512, 512], replicated, may hold values from -0.25 to 0.25
- b_mid: float32 [512], replicated, may hold values from -1.8 to 1.8
- w_top: bfloat16 [512, 512], replicated, may hold values from -0.25 to 0.25
- b_top: float32 [512], replicated, may hold values from -1.8 to 1.8
- w_out: bfloat16 [360, 512], replicated, may hold values from -0.25 to 0.25
- b_out: float32 [360], replicated, may hold values from -1.8 to 1.8
- span_of: int32 [2, 64, 2048, 1], P('face', 'elem'), may hold values from 0 to 127; in each aligned block of 2048 rows (0 to 2047, 2048 to 4095, ..., all dimensions but the last counted through in order) at most 32 rows name the same one
Outputs:
- final_state: float32 [432, 32, 8192], P(None, 'face', 'elem')
- tendencies: bfloat16 [360, 32, 8192], P(None, 'face', 'elem')
- span_heating: float32 [128], P(('face', 'elem'))
Inputs may be any that keep to these rules, and one draw needn't show every extreme that they name: `span_of`: among the columns of one device, no span is named more than 32 times, a bound that some block reaches; every span is named by some column.
All inputs are finite; a program needn't handle non-finite values.
Results may differ from a plain program's by a relative error of at most 0.0095.
Values may be sent and summed in bfloat16 or wider, within the bound.
No kernel may reach another device: no remote copies, remote signals or barrier semaphores. Data moves between devices by JAX's collectives and lax.ppermute only.
A program may use at most 128 MiB of HBM per device.

v0:
```python
import functools
import math

import jax
import jax.numpy as jnp
import numpy as np
from jax import lax
from jax.experimental import pallas as pl
from jax.experimental.pallas import tpu as pltpu
from jax.sharding import PartitionSpec as P

NP = 4
LEV = 72
CHUNK = 48
FOLD = CHUNK // 2


def gll_matrix():
    inner_node = 1.0 / math.sqrt(5.0)
    gll_nodes = np.array([-1.0, -inner_node, inner_node, 1.0])
    weights = np.array(
        [
            1.0
            / np.prod([gll_nodes[outer] - gll_nodes[other] for other in range(4) if other != outer])
            for outer in range(4)
        ]
    )
    matrix = np.zeros((4, 4))
    for outer in range(4):
        for inner in range(4):
            if inner != outer:
                matrix[outer, inner] = (
                    weights[inner] / weights[outer] / (gll_nodes[outer] - gll_nodes[inner])
                )
    for outer in range(4):
        matrix[outer, outer] = -np.sum(matrix[outer])
    return matrix.astype(np.float32)


TABLE = gll_matrix()


def lanes(shape):
    return lax.broadcasted_iota(jnp.int32, shape, len(shape) - 1)


def roll(x, shift):
    shift = shift % x.shape[-1]
    return x if shift == 0 else pltpu.roll(x, shift, x.ndim - 1)


def raw_slabs(slabs, sx, sy, ahi, alo):
    rows = slabs[0].shape[0]
    stacked = jnp.concatenate(slabs, axis=0)
    hi = stacked.astype(jnp.bfloat16)
    lo = (stacked - hi.astype(jnp.float32)).astype(jnp.bfloat16)
    along_x = (
        jnp.dot(hi, ahi, preferred_element_type=jnp.float32)
        + jnp.dot(hi, alo, preferred_element_type=jnp.float32)
        + jnp.dot(lo, ahi, preferred_element_type=jnp.float32)
    )
    out = []
    for y, _ in enumerate(slabs):
        base = (y // NP) * NP
        j = y % NP
        along_y = float(TABLE[j, 0]) * slabs[base]
        for i in range(1, NP):
            along_y = along_y + float(TABLE[j, i]) * slabs[base + i]
        dx = along_x[y * rows : (y + 1) * rows]
        out.append(-(sx * dx + sy * along_y))
    return out


def pack_edges(tend):
    rows, width = tend[0].shape
    lane = lanes((rows, width))
    acc = jnp.zeros((rows, width), jnp.float32)
    for y, t in enumerate(tend):
        acc = jnp.where(lane == 2 * y, roll(t, 2 * y), acc)
        acc = jnp.where(lane == 2 * y + 1, roll(t, 2 * y + 2), acc)
    half = rows // 2
    lane_h = lanes((half, width))
    return jnp.where(lane_h < 32, acc[:half], roll(acc[half:], 32))


def unpack_edges(block):
    return jnp.concatenate([block, roll(block, 96)], axis=0)


def stiff_x(t, right_edges, left_edges, y):
    rows, width = t.shape
    lane = lanes((rows, width))
    right = jnp.where(lane == width - 1, roll(right_edges, width - 1 - 2 * y), roll(t, width - 1))
    left = jnp.where(lane == 0, roll(left_edges, width - 1 - 2 * y), roll(t, 1))
    place = lane % NP
    return jnp.where(
        place == NP - 1, 0.5 * (t + right), jnp.where(place == 0, 0.5 * (left + t), t)
    )


def section_kernel(*refs, first, combo, edges):
    refs = list(refs)
    v0_ref = None if combo is None or combo[0] is None else refs.pop(0)
    sp_ref = refs.pop(0)
    sx_ref, sy_ref, ahi_ref, alo_ref = refs[:4]
    refs = refs[4:]
    if not first:
        exr_ref, exl_ref, dr_ref, dl_ref, eyn_ref = refs[:5]
        refs = refs[5:]
    rows = CHUNK
    height = 16
    sx = sx_ref[...]
    sy = sy_ref[...]
    ahi = ahi_ref[...]
    alo = alo_ref[...]
    slabs = [sp_ref[pl.ds(y, rows, stride=height), :] for y in range(height)]
    tend = raw_slabs(slabs, sx, sy, ahi, alo)
    if first:
        ex_ref, ey_ref = refs
        ex_ref[...] = pack_edges(tend)
        ey_ref[0] = tend[0]
        ey_ref[1] = tend[height - 1]
        return
    exr = unpack_edges(exr_ref[...])
    exl = unpack_edges(exl_ref[...])
    dr = unpack_edges(dr_ref[...])
    dl = unpack_edges(dl_ref[...])
    tx = [stiff_x(t, exr, exl, y) for y, t in enumerate(tend)]
    down = stiff_x(eyn_ref[0], dr, dl, 0)
    up = stiff_x(eyn_ref[1], dr, dl, height - 1)
    ext = [up] + tx + [down]
    new = []
    for y in range(height):
        cur = ext[y + 1]
        if y % NP == NP - 1:
            op = 0.5 * (cur + ext[y + 2])
        elif y % NP == 0:
            op = 0.5 * (ext[y] + cur)
        else:
            op = cur
        inner = slabs[y] + op
        if combo[0] is None:
            val = inner
        else:
            v0 = v0_ref[pl.ds(y, rows, stride=height), :]
            if combo[0] == "third":
                val = v0 / 3.0 + 2.0 / 3.0 * inner
            else:
                val = combo[0] * v0 + combo[1] * inner
        new.append(val)
    out_ref = refs[0]
    for y in range(height):
        out_ref[pl.ds(y, rows, stride=height), :] = new[y]
    if edges:
        ex_ref, ey_ref = refs[1:3]
        tend = raw_slabs(new, sx, sy, ahi, alo)
        ex_ref[...] = pack_edges(tend)
        ey_ref[0] = tend[0]
        ey_ref[1] = tend[height - 1]


def run_section(field_rows, v0, sx, sy, ahi, alo, halos, *, first, combo, edges):
    total, width = field_rows.shape
    feats = sx.shape[0]
    steps = feats // CHUNK
    big = pl.BlockSpec((CHUNK * 16, width), lambda i: (i, 0))
    small = pl.BlockSpec((CHUNK, width), lambda i: (i, 0))
    const = pl.BlockSpec((width, width), lambda i: (0, 0))
    edge = pl.BlockSpec((FOLD, width), lambda i: (i, 0))
    rowsb = pl.BlockSpec((2, CHUNK, width), lambda i: (0, i, 0))
    args, specs = [], []
    if combo is not None and combo[0] is not None:
        args.append(v0)
        specs.append(big)
    args += [field_rows, sx, sy, ahi, alo]
    specs += [big, small, small, const, const]
    if not first:
        args += list(halos)
        specs += [edge, edge, edge, edge, rowsb]
    out_shape, out_specs = [], []
    ex_shape = jax.ShapeDtypeStruct((feats // 2, width), jnp.float32)
    ey_shape = jax.ShapeDtypeStruct((2, feats, width), jnp.float32)
    if first:
        out_shape = [ex_shape, ey_shape]
        out_specs = [edge, rowsb]
    else:
        out_shape = [jax.ShapeDtypeStruct((total, width), jnp.float32)]
        out_specs = [big]
        if edges:
            out_shape += [ex_shape, ey_shape]
            out_specs += [edge, rowsb]
    kernel = functools.partial(section_kernel, first=first, combo=combo, edges=edges)
    return pl.pallas_call(
        kernel,
        grid=(steps,),
        in_specs=specs,
        out_specs=out_specs,
        out_shape=out_shape,
        compiler_params=pltpu.CompilerParams(vmem_limit_bytes=48 * 1024 * 1024),
    )(*args)


def exchange(ex, ey):
    n_face = lax.axis_size("face")
    n_elem = lax.axis_size("elem")
    assert n_face == 2
    from_right = [(j, (j - 1) % n_elem) for j in range(n_elem)]
    from_left = [(j, (j + 1) % n_elem) for j in range(n_elem)]
    exr = lax.ppermute(ex, "elem", from_right)
    exl = lax.ppermute(ex, "elem", from_left)
    eyn = lax.ppermute(ey, "face", [(0, 1), (1, 0)])
    diag_r, diag_l = [], []
    for f in range(n_face):
        for j in range(n_elem):
            src = f * n_elem + j
            diag_r.append((src, (1 - f) * n_elem + (j - 1) % n_elem))
            diag_l.append((src, (1 - f) * n_elem + (j + 1) % n_elem))
    dr = lax.ppermute(ex, ("face", "elem"), diag_r)
    dl = lax.ppermute(ex, ("face", "elem"), diag_l)
    return (exr, exl, dr, dl, eyn)


def column_model(inputs, w_in, b_in, w_mid, b_mid, w_top, b_top, w_out, b_out):
    hidden = jax.nn.silu(
        jnp.dot(w_in, inputs, preferred_element_type=jnp.float32) + b_in[:, None]
    ).astype(jnp.bfloat16)
    hidden = jax.nn.silu(
        jnp.dot(w_mid, hidden, preferred_element_type=jnp.float32) + b_mid[:, None]
    ).astype(jnp.bfloat16)
    hidden = jax.nn.silu(
        jnp.dot(w_top, hidden, preferred_element_type=jnp.float32) + b_top[:, None]
    ).astype(jnp.bfloat16)
    outputs = jnp.dot(w_out, hidden, preferred_element_type=jnp.float32) + b_out[:, None]
    heating = jnp.sum(outputs[:LEV], axis=0)
    return (outputs.astype(jnp.bfloat16), heating)


def local(state, speed_x, speed_y, w_in, b_in, w_mid, b_mid, w_top, b_top, w_out, b_out, span_of):
    feats, height, breadth = state.shape
    across = np.kron(np.eye(breadth // NP, dtype=np.float32), TABLE.T)
    ahi_np = across.astype(jnp.bfloat16)
    alo_np = (across - ahi_np.astype(np.float32)).astype(jnp.bfloat16)
    ahi = jnp.asarray(ahi_np)
    alo = jnp.asarray(alo_np)
    sx = jnp.broadcast_to(speed_x[:, None], (feats, breadth))
    sy = jnp.broadcast_to(speed_y[:, None], (feats, breadth))
    v0 = state.reshape(feats * height, breadth)
    ex, ey = run_section(v0, None, sx, sy, ahi, alo, None, first=True, combo=None, edges=True)
    field = v0
    combos = [(None, None), (0.75, 0.25), ("third", None)]
    for k, combo in enumerate(combos):
        halos = exchange(ex, ey)
        outs = run_section(
            field, v0, sx, sy, ahi, alo, halos, first=False, combo=combo, edges=k < 2
        )
        if k < 2:
            field, ex, ey = outs
        else:
            (field,) = outs
    final_state = field.reshape(feats, height, breadth)
    column_count = height * breadth
    inputs = final_state.reshape(feats, column_count).astype(jnp.bfloat16)
    target = span_of.reshape(column_count)
    devices = lax.axis_size("face") * lax.axis_size("elem")
    span_ids = jnp.arange(devices, dtype=jnp.int32)
    weights = (w_in, b_in, w_mid, b_mid, w_top, b_top, w_out, b_out)
    tend_cols, heating = column_model(inputs, *weights)
    member = (target[:, None] == span_ids[None, :]).astype(jnp.float32)
    partial_sums = jnp.sum(member * heating[:, None], axis=0)
    received = lax.all_to_all(
        partial_sums.reshape(devices, 1), ("face", "elem"), 0, 1, tiled=True
    )
    span_heating = jnp.sum(received, axis=1) / column_count
    tendencies = tend_cols.reshape(-1, height, breadth)
    return (final_state, tendencies, span_heating)


def solution(mesh):
    return jax.shard_map(
        local,
        mesh=mesh,
        in_specs=(
            P(None, "face", "elem"),
            P(),
            P(),
            P(),
            P(),
            P(),
            P(),
            P(),
            P(),
            P(),
            P(),
            P("face", "elem", None, None),
        ),
        out_specs=(P(None, "face", "elem"), P(None, "face", "elem"), P(("face", "elem"))),
        check_vma=False,
    )
```

profile of v0, /device:TPU:1, one launch (start us, length us, event | category | flops | bytes accessed | tf_op | source)
XLA Modules:
  0.0 147.6 jit_solution(6381292801551431538)
XLA Ops:
  2.3 2.0 %copy-done.1 = f32[432,16,128]{2,1,0:T(8,128)S(1)} copy-done((f32[432,16,128]{2,1,0:T(8,128)S(1)}, f32[432,16,128]{2,1,0:T(8,128)}, u32[]{:S(2)}) %copy-start.1) | copy-done | bytes 3538968
  5.9 5.0 %shard_map.157 = (f32[216,128]{1,0:T(8,128)S(1)}, f32[2,432,128]{2,1,0:T(8,128)S(1)}) custom-call(f32[6912,128]{1,0:T(8,128)S(1)} %bitcast.61, f32[432,128]{1,0:T(8,128)S(1)} %broadcast_in_dim.4.refs_1_.refs_2_, f32[432,128]{1,0:T(8,128)S(1)} %broadcast_in_dim.5.refs_2_.refs_3_, bf16[128,128]{1,0:T(8,128)(2,1)S(1)} %copy-done.7, bf16[128,128]{1,0:T(8,128)(2,1)S(1)} %copy-done.5), custom_call_target="tpu_custom_call" | custom-call | tf_op jit(solution)/shard_map/pallas_call | solution.py:193
  13.6 7.3 %collective-permute-start.2 = (f32[216,128]{1,0:T(8,128)S(1)}, f32[216,128]{1,0:T(8,128)S(1)}, u32[]{:S(2)}, u32[]{:S(2)}) collective-permute-start(f32[216,128]{1,0:T(8,128)S(1)} %get-tuple-element.11), channel_id=1, source_target_pairs={{0,127},{1,64},{2,65},{3,66},{4,67},{5,68},{6,69},{7,70},{8,71},{9... | collective-permute-start | bytes 331784 | tf_op jit(solution)/shard_map/ppermute | solution.py:218
  20.9 6.9 %collective-permute-start = (f32[216,128]{1,0:T(8,128)S(1)}, f32[216,128]{1,0:T(8,128)S(1)}, u32[]{:S(2)}, u32[]{:S(2)}) collective-permute-start(f32[216,128]{1,0:T(8,128)S(1)} %get-tuple-element.11), channel_id=1, source_target_pairs={{0,63},{1,0},{2,1},{3,2},{4,3},{5,4},{6,5},{7,6},{8,7},{9,8},{10,9... | collective-permute-start | bytes 331784 | tf_op jit(solution)/shard_map/ppermute | solution.py:209
  27.8 2.8 %collective-permute-done.1.refs_6_ = f32[216,128]{1,0:T(8,128)S(1)} collective-permute-done((f32[216,128]{1,0:T(8,128)S(1)}, f32[216,128]{1,0:T(8,128)S(1)}, u32[]{:S(2)}, u32[]{:S(2)}) %collective-permute-start.1) | collective-permute-done | bytes 110624 | tf_op jit(solution)/shard_map/ppermute | solution.py:210
  30.6 12.8 %shard_map.158 = (f32[6912,128]{1,0:T(8,128)S(1)}, f32[216,128]{1,0:T(8,128)S(1)}, f32[2,432,128]{2,1,0:T(8,128)S(1)}) custom-call(f32[6912,128]{1,0:T(8,128)} %bitcast.59, f32[432,128]{1,0:T(8,128)S(1)} %broadcast_in_dim.4.refs_1_.refs_2_, f32[432,128]{1,0:T(8,128)S(1)} %broadcast_in_dim.5.refs_2_.refs_3_, bf16[128,128]{1,0:T(8,128)(2,1)S(1)} %copy-done.8, ...), custom_call_target="tpu_custom_call" | custom-call | tf_op jit(solution)/shard_map/pallas_call | solution.py:193
  43.4 1.8 %copy-done.4 = f32[6912,128]{1,0:T(8,128)} copy-done((f32[6912,128]{1,0:T(8,128)}, f32[6912,128]{1,0:T(8,128)S(1)}, u32[]{:S(2)}) %copy-start.4) | copy-done | bytes 3538968
  46.4 7.2 %collective-permute-start.7 = (f32[216,128]{1,0:T(8,128)S(1)}, f32[216,128]{1,0:T(8,128)S(1)}, u32[]{:S(2)}, u32[]{:S(2)}) collective-permute-start(f32[216,128]{1,0:T(8,128)S(1)} %get-tuple-element.14), channel_id=1, source_target_pairs={{0,127},{1,64},{2,65},{3,66},{4,67},{5,68},{6,69},{7,70},{8,71},{9... | collective-permute-start | bytes 331784 | tf_op jit(solution)/shard_map/ppermute | solution.py:218
  53.6 6.9 %collective-permute-start.5 = (f32[216,128]{1,0:T(8,128)S(1)}, f32[216,128]{1,0:T(8,128)S(1)}, u32[]{:S(2)}, u32[]{:S(2)}) collective-permute-start(f32[216,128]{1,0:T(8,128)S(1)} %get-tuple-element.14), channel_id=1, source_target_pairs={{0,63},{1,0},{2,1},{3,2},{4,3},{5,4},{6,5},{7,6},{8,7},{9,8},{10,9... | collective-permute-start | bytes 331784 | tf_op jit(solution)/shard_map/ppermute | solution.py:209
  60.5 3.0 %collective-permute-done.6.refs_7_ = f32[216,128]{1,0:T(8,128)S(1)} collective-permute-done((f32[216,128]{1,0:T(8,128)S(1)}, f32[216,128]{1,0:T(8,128)S(1)}, u32[]{:S(2)}, u32[]{:S(2)}) %collective-permute-start.6) | collective-permute-done | bytes 110624 | tf_op jit(solution)/shard_map/ppermute | solution.py:210
  63.5 13.5 %shard_map.159 = (f32[6912,128]{1,0:T(8,128)S(1)}, f32[216,128]{1,0:T(8,128)S(1)}, f32[2,432,128]{2,1,0:T(8,128)S(1)}) custom-call(f32[6912,128]{1,0:T(8,128)} %bitcast.60, f32[6912,128]{1,0:T(8,128)} %copy-done.4, f32[432,128]{1,0:T(8,128)S(1)} %broadcast_in_dim.4.refs_1_.refs_2_, f32[432,128]{1,0:T(8,128)S(1)} %broadcast_in_dim.5.refs_2_.refs_3_, ...), custom_call_target="tpu_custom_call" | custom-call | tf_op jit(solution)/shard_map/pallas_call | solution.py:193
  77.1 1.7 %copy-done.3 = f32[6912,128]{1,0:T(8,128)} copy-done((f32[6912,128]{1,0:T(8,128)}, f32[6912,128]{1,0:T(8,128)S(1)}, u32[]{:S(2)}) %copy-start.3) | copy-done | bytes 3538968
  79.8 7.2 %collective-permute-start.12 = (f32[216,128]{1,0:T(8,128)S(1)}, f32[216,128]{1,0:T(8,128)S(1)}, u32[]{:S(2)}, u32[]{:S(2)}) collective-permute-start(f32[216,128]{1,0:T(8,128)S(1)} %get-tuple-element.17), channel_id=1, source_target_pairs={{0,127},{1,64},{2,65},{3,66},{4,67},{5,68},{6,69},{7,70},{8,71},{9... | collective-permute-start | bytes 331784 | tf_op jit(solution)/shard_map/ppermute | solution.py:218
  87.0 6.9 %collective-permute-start.10 = (f32[216,128]{1,0:T(8,128)S(1)}, f32[216,128]{1,0:T(8,128)S(1)}, u32[]{:S(2)}, u32[]{:S(2)}) collective-permute-start(f32[216,128]{1,0:T(8,128)S(1)} %get-tuple-element.17), channel_id=1, source_target_pairs={{0,63},{1,0},{2,1},{3,2},{4,3},{5,4},{6,5},{7,6},{8,7},{9,8},{10,9... | collective-permute-start | bytes 331784 | tf_op jit(solution)/shard_map/ppermute | solution.py:209
  93.9 3.0 %collective-permute-done.11.refs_7_ = f32[216,128]{1,0:T(8,128)S(1)} collective-permute-done((f32[216,128]{1,0:T(8,128)S(1)}, f32[216,128]{1,0:T(8,128)S(1)}, u32[]{:S(2)}, u32[]{:S(2)}) %collective-permute-start.11) | collective-permute-done | bytes 110624 | tf_op jit(solution)/shard_map/ppermute | solution.py:210
  96.9 10.4 %shard_map.160 = f32[6912,128]{1,0:T(8,128)} custom-call(f32[6912,128]{1,0:T(8,128)S(1)} %bitcast.62, f32[6912,128]{1,0:T(8,128)} %copy-done.3, f32[432,128]{1,0:T(8,128)S(1)} %broadcast_in_dim.4.refs_1_.refs_2_, f32[432,128]{1,0:T(8,128)S(1)} %broadcast_in_dim.5.refs_2_.refs_3_, bf16[128,128]{1,0:T(8,128)(2,1)S(1)} %copy-done.8, ...), custom_call_target="tpu_custom_call" | custom-call | tf_op jit(solution)/shard_map/pallas_call | solution.py:193
  107.4 2.2 %convert_element_type.19 = bf16[6912,128]{1,0:T(8,128)(2,1)S(1)} convert(f32[6912,128]{1,0:T(8,128)} %shard_map.160) | non-fusion elementwise | flops 884736 | bytes 5308416 | tf_op jit(solution)/shard_map/convert_element_type | solution.py:262
  109.6 2.2 %convert_element_type.20 = bf16[432,2048]{1,0:T(8,128)(2,1)} reshape(bf16[6912,128]{1,0:T(8,128)(2,1)S(1)} %convert_element_type.19) | data formatting | bytes 3538944 | tf_op jit(solution)/shard_map/convert_element_type | solution.py:262
  111.8 6.3 %fusion.10 = bf16[512,2048]{0,1:T(8,128)(2,1)} fusion(bf16[512,512]{1,0:T(8,128)(2,1)S(1)} %copy-done, f32[512]{0:T(512)S(1)} %copy-done.13, bf16[432,2048]{1,0:T(8,128)(2,1)} %convert_element_type.20, bf16[512,432]{0,1:T(8,128)(2,1)S(1)} %copy-done.11, f32[512]{0:T(512)S(1)} %copy-done.14), kind=kOutput, calls=%fused_computation.16 | convolution fusion | flops 1992294400 | bytes 4837376 | tf_op jit(solution)/shard_map/dot_general | solution.py:228
  118.2 5.9 %add_bitcast_fusion = f32[360,2048]{1,0:T(8,128)} fusion(bf16[360,512]{1,0:T(8,128)(2,1)S(1)} %copy-done.12, f32[360]{0:T(512)S(1)} %copy-done.15, bf16[512,2048]{0,1:T(8,128)(2,1)} %fusion.10, bf16[512,512]{1,0:T(8,128)(2,1)S(1)} %copy-done.10, f32[512]{0:T(512)S(1)} %copy-done.16), kind=kOutput, calls=%fused_computation.18 | convolution fusion | flops 1835745280 | bytes 5942688 | tf_op jit(solution)/shard_map/dot_general | solution.py:233
  126.6 9.0 %all-to-all-start = ((f32[128,1,1]{2,1,0:T(1,128)}), f32[128,1,1]{2,1,0:T(1,128)S(1)}, u32[]{:S(2)}, u32[]{:S(2)}) async-start(f32[128,1,1]{2,1,0:T(1,128)} %copy.18), calls=%async_computation | async-start | bytes 131072 | tf_op jit(solution)/shard_map/all_to_all | solution.py:270
  135.6 2.1 %convert_bitcast_fusion = bf16[45,8,16,128]{3,1,2,0:T(8,128)(2,1)S(1)} fusion(f32[360,2048]{1,0:T(8,128)} %add_bitcast_fusion), kind=kLoop, calls=%fused_computation.19 | loop fusion | flops 737280 | bytes 4423680
  137.7 1.5 %copy.19 = bf16[45,8,16,128]{3,2,1,0:T(8,128)(2,1)} copy(bf16[45,8,16,128]{3,1,2,0:T(8,128)(2,1)S(1)} %convert_bitcast_fusion) | data formatting | bytes 2949120
  139.2 5.9 %all-to-all-done = f32[128,1,1]{2,1,0:T(1,128)S(1)} async-done(((f32[128,1,1]{2,1,0:T(1,128)}), f32[128,1,1]{2,1,0:T(1,128)S(1)}, u32[]{:S(2)}, u32[]{:S(2)}) %all-to-all-start) | async-done | bytes 544 | tf_op jit(solution)/shard_map/all_to_all | solution.py:270
  (58 shorter events, 11.5 us)
Async XLA Ops:
  0.6 111.1 %copy-start = (bf16[512,512]{1,0:T(8,128)(2,1)S(1)}, bf16[512,512]{1,0:T(8,128)(2,1)}, u32[]{:S(2)}) copy-start(bf16[512,512]{1,0:T(8,128)(2,1)} %param.19) | copy-start | bytes 1572868
  0.6 29.9 %copy-start.6 = (bf16[128,128]{1,0:T(8,128)(2,1)S(1)}, bf16[128,128]{1,0:T(8,128)(2,1)}, u32[]{:S(2)}) copy-start(bf16[128,128]{1,0:T(8,128)(2,1)} %constant.17.clone.refs_4_.refs_5_) | copy-start | bytes 98308
  0.7 29.9 %copy-start.8 = (bf16[128,128]{1,0:T(8,128)(2,1)S(1)}, bf16[128,128]{1,0:T(8,128)(2,1)}, u32[]{:S(2)}) copy-start(bf16[128,128]{1,0:T(8,128)(2,1)} %constant.16.clone.refs_3_.refs_4_) | copy-start | bytes 98308
  10.8 19.7 %collective-permute-start.4 = (f32[2,432,128]{2,1,0:T(8,128)S(1)}, f32[2,432,128]{2,1,0:T(8,128)S(1)}, u32[]{:S(2)}, u32[]{:S(2)}) collective-permute-start(f32[2,432,128]{2,1,0:T(8,128)S(1)} %get-tuple-element.12), channel_id=1, source_target_pairs={{0,64},{64,0},{1,65},{65,1},{2,66},{66,2},{3,67},{67,3},{4,68},{68... | collective-permute-start | bytes 1327112 | tf_op jit(solution)/shard_map/ppermute | solution.py:211
  12.3 15.5 %collective-permute-start.3 = (f32[216,128]{1,0:T(8,128)S(1)}, f32[216,128]{1,0:T(8,128)S(1)}, u32[]{:S(2)}, u32[]{:S(2)}) collective-permute-start(f32[216,128]{1,0:T(8,128)S(1)} %get-tuple-element.11), channel_id=1, source_target_pairs={{0,65},{1,66},{2,67},{3,68},{4,69},{5,70},{6,71},{7,72},{8,73},{9,... | collective-permute-start | bytes 331784 | tf_op jit(solution)/shard_map/ppermute | solution.py:219
  13.6 14.2 %collective-permute-start.2 = (f32[216,128]{1,0:T(8,128)S(1)}, f32[216,128]{1,0:T(8,128)S(1)}, u32[]{:S(2)}, u32[]{:S(2)}) collective-permute-start(f32[216,128]{1,0:T(8,128)S(1)} %get-tuple-element.11), channel_id=1, source_target_pairs={{0,127},{1,64},{2,65},{3,66},{4,67},{5,68},{6,69},{7,70},{8,71},{9... | collective-permute-start | bytes 331784 | tf_op jit(solution)/shard_map/ppermute | solution.py:218
  20.9 9.7 %collective-permute-start.1 = (f32[216,128]{1,0:T(8,128)S(1)}, f32[216,128]{1,0:T(8,128)S(1)}, u32[]{:S(2)}, u32[]{:S(2)}) collective-permute-start(f32[216,128]{1,0:T(8,128)S(1)} %get-tuple-element.11), channel_id=1, source_target_pairs={{0,1},{1,2},{2,3},{3,4},{4,5},{5,6},{6,7},{7,8},{8,9},{9,10},{10,1... | collective-permute-start | bytes 331784 | tf_op jit(solution)/shard_map/ppermute | solution.py:210
  20.9 9.7 %collective-permute-start = (f32[216,128]{1,0:T(8,128)S(1)}, f32[216,128]{1,0:T(8,128)S(1)}, u32[]{:S(2)}, u32[]{:S(2)}) collective-permute-start(f32[216,128]{1,0:T(8,128)S(1)} %get-tuple-element.11), channel_id=1, source_target_pairs={{0,63},{1,0},{2,1},{3,2},{4,3},{5,4},{6,5},{7,6},{8,7},{9,8},{10,9... | collective-permute-start | bytes 331784 | tf_op jit(solution)/shard_map/ppermute | solution.py:209
  45.2 18.3 %collective-permute-start.9 = (f32[2,432,128]{2,1,0:T(8,128)S(1)}, f32[2,432,128]{2,1,0:T(8,128)S(1)}, u32[]{:S(2)}, u32[]{:S(2)}) collective-permute-start(f32[2,432,128]{2,1,0:T(8,128)S(1)} %get-tuple-element.15), channel_id=1, source_target_pairs={{0,64},{64,0},{1,65},{65,1},{2,66},{66,2},{3,67},{67,3},{4,68},{68... | collective-permute-start | bytes 1327112 | tf_op jit(solution)/shard_map/ppermute | solution.py:211
  46.4 14.1 %collective-permute-start.8 = (f32[216,128]{1,0:T(8,128)S(1)}, f32[216,128]{1,0:T(8,128)S(1)}, u32[]{:S(2)}, u32[]{:S(2)}) collective-permute-start(f32[216,128]{1,0:T(8,128)S(1)} %get-tuple-element.14), channel_id=1, source_target_pairs={{0,65},{1,66},{2,67},{3,68},{4,69},{5,70},{6,71},{7,72},{8,73},{9,... | collective-permute-start | bytes 331784 | tf_op jit(solution)/shard_map/ppermute | solution.py:219
  46.4 14.1 %collective-permute-start.7 = (f32[216,128]{1,0:T(8,128)S(1)}, f32[216,128]{1,0:T(8,128)S(1)}, u32[]{:S(2)}, u32[]{:S(2)}) collective-permute-start(f32[216,128]{1,0:T(8,128)S(1)} %get-tuple-element.14), channel_id=1, source_target_pairs={{0,127},{1,64},{2,65},{3,66},{4,67},{5,68},{6,69},{7,70},{8,71},{9... | collective-permute-start | bytes 331784 | tf_op jit(solution)/shard_map/ppermute | solution.py:218
  53.6 9.9 %collective-permute-start.6 = (f32[216,128]{1,0:T(8,128)S(1)}, f32[216,128]{1,0:T(8,128)S(1)}, u32[]{:S(2)}, u32[]{:S(2)}) collective-permute-start(f32[216,128]{1,0:T(8,128)S(1)} %get-tuple-element.14), channel_id=1, source_target_pairs={{0,1},{1,2},{2,3},{3,4},{4,5},{5,6},{6,7},{7,8},{8,9},{9,10},{10,1... | collective-permute-start | bytes 331784 | tf_op jit(solution)/shard_map/ppermute | solution.py:210
  53.6 9.9 %collective-permute-start.5 = (f32[216,128]{1,0:T(8,128)S(1)}, f32[216,128]{1,0:T(8,128)S(1)}, u32[]{:S(2)}, u32[]{:S(2)}) collective-permute-start(f32[216,128]{1,0:T(8,128)S(1)} %get-tuple-element.14), channel_id=1, source_target_pairs={{0,63},{1,0},{2,1},{3,2},{4,3},{5,4},{6,5},{7,6},{8,7},{9,8},{10,9... | collective-permute-start | bytes 331784 | tf_op jit(solution)/shard_map/ppermute | solution.py:209
  63.5 33.4 %copy-start.2 = (f32[432,16,128]{2,1,0:T(8,128)S(1)}, f32[432,16,128]{2,1,0:T(8,128)}, u32[]{:S(2)}) copy-start(f32[432,16,128]{2,1,0:T(8,128)} %param.14) | copy-start | bytes 10616836
  78.8 18.1 %collective-permute-start.14 = (f32[2,432,128]{2,1,0:T(8,128)S(1)}, f32[2,432,128]{2,1,0:T(8,128)S(1)}, u32[]{:S(2)}, u32[]{:S(2)}) collective-permute-start(f32[2,432,128]{2,1,0:T(8,128)S(1)} %get-tuple-element.18), channel_id=1, source_target_pairs={{0,64},{64,0},{1,65},{65,1},{2,66},{66,2},{3,67},{67,3},{4,68},{68... | collective-permute-start | bytes 1327112 | tf_op jit(solution)/shard_map/ppermute | solution.py:211
  79.8 14.1 %collective-permute-start.13 = (f32[216,128]{1,0:T(8,128)S(1)}, f32[216,128]{1,0:T(8,128)S(1)}, u32[]{:S(2)}, u32[]{:S(2)}) collective-permute-start(f32[216,128]{1,0:T(8,128)S(1)} %get-tuple-element.17), channel_id=1, source_target_pairs={{0,65},{1,66},{2,67},{3,68},{4,69},{5,70},{6,71},{7,72},{8,73},{9,... | collective-permute-start | bytes 331784 | tf_op jit(solution)/shard_map/ppermute | solution.py:219
  79.8 14.1 %collective-permute-start.12 = (f32[216,128]{1,0:T(8,128)S(1)}, f32[216,128]{1,0:T(8,128)S(1)}, u32[]{:S(2)}, u32[]{:S(2)}) collective-permute-start(f32[216,128]{1,0:T(8,128)S(1)} %get-tuple-element.17), channel_id=1, source_target_pairs={{0,127},{1,64},{2,65},{3,66},{4,67},{5,68},{6,69},{7,70},{8,71},{9... | collective-permute-start | bytes 331784 | tf_op jit(solution)/shard_map/ppermute | solution.py:218
  87.0 9.9 %collective-permute-start.11 = (f32[216,128]{1,0:T(8,128)S(1)}, f32[216,128]{1,0:T(8,128)S(1)}, u32[]{:S(2)}, u32[]{:S(2)}) collective-permute-start(f32[216,128]{1,0:T(8,128)S(1)} %get-tuple-element.17), channel_id=1, source_target_pairs={{0,1},{1,2},{2,3},{3,4},{4,5},{5,6},{6,7},{7,8},{8,9},{9,10},{10,1... | collective-permute-start | bytes 331784 | tf_op jit(solution)/shard_map/ppermute | solution.py:210
  87.0 9.9 %collective-permute-start.10 = (f32[216,128]{1,0:T(8,128)S(1)}, f32[216,128]{1,0:T(8,128)S(1)}, u32[]{:S(2)}, u32[]{:S(2)}) collective-permute-start(f32[216,128]{1,0:T(8,128)S(1)} %get-tuple-element.17), channel_id=1, source_target_pairs={{0,63},{1,0},{2,1},{3,2},{4,3},{5,4},{6,5},{7,6},{8,7},{9,8},{10,9... | collective-permute-start | bytes 331784 | tf_op jit(solution)/shard_map/ppermute | solution.py:209
  111.8 6.3 %copy-start.10 = (bf16[512,512]{1,0:T(8,128)(2,1)S(1)}, bf16[512,512]{1,0:T(8,128)(2,1)}, u32[]{:S(2)}) copy-start(bf16[512,512]{1,0:T(8,128)(2,1)} %param.21) | copy-start | bytes 1572868
  111.8 6.3 %copy-start.12 = (bf16[360,512]{1,0:T(8,128)(2,1)S(1)}, bf16[360,512]{1,0:T(8,128)(2,1)}, u32[]{:S(2)}) copy-start(bf16[360,512]{1,0:T(8,128)(2,1)} %param.23) | copy-start | bytes 1105924
  111.8 6.3 %copy-start.15 = (f32[360]{0:T(512)S(1)}, f32[360]{0:T(512)}, u32[]{:S(2)}) copy-start(f32[360]{0:T(512)} %param.24) | copy-start | bytes 4324
  118.1 7.0 %copy-start.9 = (s32[1,1,2048,1]{2,3,1,0:T(1,128)S(1)}, s32[1,1,2048,1]{2,3,1,0:T(1,128)}, u32[]{:S(2)}) copy-start(s32[1,1,2048,1]{2,3,1,0:T(1,128)} %param.25) | copy-start | bytes 24580
  126.6 18.5 %all-to-all-start = ((f32[128,1,1]{2,1,0:T(1,128)}), f32[128,1,1]{2,1,0:T(1,128)S(1)}, u32[]{:S(2)}, u32[]{:S(2)}) async-start(f32[128,1,1]{2,1,0:T(1,128)} %copy.18), calls=%async_computation | async-start | bytes 131072 | tf_op jit(solution)/shard_map/all_to_all | solution.py:270
  (9 other events, 26.6 us)
where the time goes:
time: 148 us
  starting transfers between devices  56.2 us (38%)
  Pallas kernels  41.8 us (28%)
  waiting for transfers between devices  14.9 us (10%)
  local copies, waits for them, and re-layouts  13.1 us (9%)
  matrix products  12.2 us (8%)
  other arithmetic  6.84 us (5%)
  between operations  2.62 us (2%)
    pallas_call x4, Pallas kernels, run_section(): pl.pallas_call(kernel, grid=(steps,), in_specs=specs, out_specs=out_specs...  41.8 us
    ppermute x3, starting transfers between devices, exchange(): dr = lax.ppermute(ex, ('face', 'elem'), diag_r)  21.6 us
    ppermute x3, starting transfers between devices, exchange(): exr = lax.ppermute(ex, 'elem', from_right)  20.7 us
    all_to_all x1, starting transfers between devices, local(): lax.all_to_all(partial_sums.reshape(devices, 1), ('face', 'elem'), 0, 1,...  8.99 us
    ppermute x3, waiting for transfers between devices, exchange(): exl = lax.ppermute(ex, 'elem', from_left)  8.87 us
    unnamed x35, local copies, waits for them, and re-layouts  8.58 us
    dot_general x1, matrix products, column_model(): jnp.dot(w_mid, hidden, preferred_element_type=jnp.float32) + b_mid[:, None]  6.29 us
    all_to_all x1, waiting for transfers between devices, local(): lax.all_to_all(partial_sums.reshape(devices, 1), ('face', 'elem'), 0, 1,...  5.95 us
  transfers between devices with their start and end apart: 16, of which 4 were waited for; matrix products, arithmetic and copies ran while one was open for 2% of the time, Pallas kernels for 0%

commit v1 on v0

--- a/solution.py
+++ b/solution.py
@@ -12,6 +12,7 @@
 NP = 4
 LEV = 72
 CHUNK = 48
+PARTS = 3
 FOLD = CHUNK // 2
 
 
@@ -159,33 +160,34 @@
         ey_ref[1] = tend[height - 1]
 
 
-def run_section(field_rows, v0, sx, sy, ahi, alo, halos, *, first, combo, edges):
-    total, width = field_rows.shape
-    feats = sx.shape[0]
-    steps = feats // CHUNK
-    big = pl.BlockSpec((CHUNK * 16, width), lambda i: (i, 0))
-    small = pl.BlockSpec((CHUNK, width), lambda i: (i, 0))
+def run_section(field, field_at, v0, sx, sy, ahi, alo, halos, *, at, steps, first, combo, edges):
+    width = field.shape[1]
+    feats = steps * CHUNK
+
+    def big(o):
+        return pl.BlockSpec((CHUNK * 16, width), lambda i: (i + o, 0))
+
+    small = pl.BlockSpec((CHUNK, width), lambda i: (i + at, 0))
     const = pl.BlockSpec((width, width), lambda i: (0, 0))
     edge = pl.BlockSpec((FOLD, width), lambda i: (i, 0))
     rowsb = pl.BlockSpec((2, CHUNK, width), lambda i: (0, i, 0))
     args, specs = [], []
     if combo is not None and combo[0] is not None:
         args.append(v0)
-        specs.append(big)
-    args += [field_rows, sx, sy, ahi, alo]
-    specs += [big, small, small, const, const]
+        specs.append(big(at))
+    args += [field, sx, sy, ahi, alo]
+    specs += [big(field_at), small, small, const, const]
     if not first:
         args += list(halos)
         specs += [edge, edge, edge, edge, rowsb]
-    out_shape, out_specs = [], []
     ex_shape = jax.ShapeDtypeStruct((feats // 2, width), jnp.float32)
     ey_shape = jax.ShapeDtypeStruct((2, feats, width), jnp.float32)
     if first:
         out_shape = [ex_shape, ey_shape]
         out_specs = [edge, rowsb]
     else:
-        out_shape = [jax.ShapeDtypeStruct((total, width), jnp.float32)]
-        out_specs = [big]
+        out_shape = [jax.ShapeDtypeStruct((feats * 16, width), jnp.float32)]
+        out_specs = [big(0)]
         if edges:
             out_shape += [ex_shape, ey_shape]
             out_specs += [edge, rowsb]
@@ -245,18 +247,29 @@
     sx = jnp.broadcast_to(speed_x[:, None], (feats, breadth))
     sy = jnp.broadcast_to(speed_y[:, None], (feats, breadth))
     v0 = state.reshape(feats * height, breadth)
-    ex, ey = run_section(v0, None, sx, sy, ahi, alo, None, first=True, combo=None, edges=True)
-    field = v0
+    steps = feats // CHUNK // PARTS
     combos = [(None, None), (0.75, 0.25), ("third", None)]
+    fields, edges = [], []
+    for part in range(PARTS):
+        at = part * steps
+        edges.append(
+            run_section(v0, at, None, sx, sy, ahi, alo, None, at=at, steps=steps, first=True,
+                        combo=None, edges=True)
+        )
+        fields.append((v0, at))
     for k, combo in enumerate(combos):
-        halos = exchange(ex, ey)
-        outs = run_section(
-            field, v0, sx, sy, ahi, alo, halos, first=False, combo=combo, edges=k < 2
-        )
-        if k < 2:
-            field, ex, ey = outs
-        else:
-            (field,) = outs
+        for part in range(PARTS):
+            at = part * steps
+            halos = exchange(*edges[part])
+            field, field_at = fields[part]
+            outs = run_section(
+                field, field_at, v0, sx, sy, ahi, alo, halos, at=at, steps=steps, first=False,
+                combo=combo, edges=k < 2,
+            )
+            fields[part] = (outs[0], 0)
+            if k < 2:
+                edges[part] = outs[1:]
+    field = jnp.concatenate([f for f, _ in fields], axis=0)
     final_state = field.reshape(feats, height, breadth)
     column_count = height * breadth
     inputs = final_state.reshape(feats, column_count).astype(jnp.bfloat16)

time: 148 us -> 224 us (1.51)
  starting transfers between devices: 56.2 us -> 137 us
  local copies, waits for them, and re-layouts: 13.1 us -> 9.59 us
  other arithmetic: 6.84 us -> 3.92 us
    ppermute x3 -> x9, starting transfers between devices: 21.6 us -> 61.3 us  [exchange(): dr = lax.ppermute(ex, ('face', 'elem'), diag_r)]
    ppermute x3 -> x9, starting transfers between devices: 20.7 us -> 60.1 us  [exchange(): exr = lax.ppermute(ex, 'elem', from_right)]
    ppermute x3 -> x9, waiting for transfers between devices: 8.87 us -> 2.67 us  [exchange(): exl = lax.ppermute(ex, 'elem', from_left)]
    all_to_all x1, starting transfers between devices: 8.99 us -> 3.9 us  [local(): lax.all_to_all(partial_sums.reshape(devices, 1), ('face', 'elem'), 0, 1,...]
    ppermute x3 -> x9, waiting for transfers between devices: 0.01 us -> 4.6 us  [exchange(): dl = lax.ppermute(ex, ('face', 'elem'), diag_l)]
    unnamed x35 -> x25, local copies, waits for them, and re-layouts: 8.58 us -> 5.05 us
    ppermute x3 -> x9, starting transfers between devices: 1.3 us -> 3.86 us  [exchange(): dl = lax.ppermute(ex, ('face', 'elem'), diag_l)]
    ppermute x3 -> x9, starting transfers between devices: 3.62 us -> 6.07 us  [exchange(): eyn = lax.ppermute(ey, 'face', [(0, 1), (1, 0)])]
  transfers between devices with their start and end apart: 16 -> 46, of which waited for: 4 -> 11; matrix products, arithmetic and copies ran while one was open for 2% -> 1% of each run, Pallas kernels for 0% -> 17%
where the time goes in v1:
time: 224 us
  starting transfers between devices  137 us (61%)
  Pallas kernels  43.1 us (19%)
  waiting for transfers between devices  16.3 us (7%)
  matrix products  10.7 us (5%)
  local copies, waits for them, and re-layouts  9.59 us (4%)
  other arithmetic  3.92 us (2%)
  between operations  2.76 us (1%)
    ppermute x9, starting transfers between devices, exchange(): dr = lax.ppermute(ex, ('face', 'elem'), diag_r)  61.3 us
    ppermute x9, starting transfers between devices, exchange(): exr = lax.ppermute(ex, 'elem', from_right)  60.1 us
    pallas_call x12, Pallas kernels, run_section(): pl.pallas_call(kernel, grid=(steps,), in_specs=specs, out_specs=out_specs...  43.1 us
    all_to_all x1, waiting for transfers between devices, local(): lax.all_to_all(partial_sums.reshape(devices, 1), ('face', 'elem'), 0, 1,...  7.96 us
    dot_general x1, matrix products, column_model(): jnp.dot(w_mid, hidden, preferred_element_type=jnp.float32) + b_mid[:, None]  6.22 us
    ppermute x9, starting transfers between devices, exchange(): eyn = lax.ppermute(ey, 'face', [(0, 1), (1, 0)])  6.07 us
    unnamed x25, local copies, waits for them, and re-layouts  5.05 us
    ppermute x9, waiting for transfers between devices, exchange(): dl = lax.ppermute(ex, ('face', 'elem'), diag_l)  4.6 us
  transfers between devices with their start and end apart: 46, of which 11 were waited for; matrix products, arithmetic and copies ran while one was open for 1% of the time, Pallas kernels for 17%

profile of v1, /device:TPU:1, one launch (start us, length us, event | category | flops | bytes accessed | tf_op | source)
XLA Modules:
  0.0 223.7 jit_solution(17977687552834871432)
XLA Ops:
  15.1 5.7 %collective-permute-start.17 = (f32[72,128]{1,0:T(8,128)S(1)}, f32[72,128]{1,0:T(8,128)S(1)}, u32[]{:S(2)}, u32[]{:S(2)}) collective-permute-start(f32[72,128]{1,0:T(8,128)S(1)} %get-tuple-element.35), channel_id=1, source_target_pairs={{0,127},{1,64},{2,65},{3,66},{4,67},{5,68},{6,69},{7,70},{8,71},{9... | collective-permute-start | bytes 110600 | tf_op jit(solution)/shard_map/ppermute | solution.py:220
  21.3 6.9 %collective-permute-start.15 = (f32[72,128]{1,0:T(8,128)S(1)}, f32[72,128]{1,0:T(8,128)S(1)}, u32[]{:S(2)}, u32[]{:S(2)}) collective-permute-start(f32[72,128]{1,0:T(8,128)S(1)} %get-tuple-element.35), channel_id=1, source_target_pairs={{0,63},{1,0},{2,1},{3,2},{4,3},{5,4},{6,5},{7,6},{8,7},{9,8},{10,9... | collective-permute-start | bytes 110600 | tf_op jit(solution)/shard_map/ppermute | solution.py:211
  29.6 8.3 %collective-permute-start.2 = (f32[72,128]{1,0:T(8,128)S(1)}, f32[72,128]{1,0:T(8,128)S(1)}, u32[]{:S(2)}, u32[]{:S(2)}) collective-permute-start(f32[72,128]{1,0:T(8,128)S(1)} %get-tuple-element.27), channel_id=1, source_target_pairs={{0,127},{1,64},{2,65},{3,66},{4,67},{5,68},{6,69},{7,70},{8,71},{9... | collective-permute-start | bytes 110600 | tf_op jit(solution)/shard_map/ppermute | solution.py:220
  38.9 7.6 %collective-permute-start = (f32[72,128]{1,0:T(8,128)S(1)}, f32[72,128]{1,0:T(8,128)S(1)}, u32[]{:S(2)}, u32[]{:S(2)}) collective-permute-start(f32[72,128]{1,0:T(8,128)S(1)} %get-tuple-element.27), channel_id=1, source_target_pairs={{0,63},{1,0},{2,1},{3,2},{4,3},{5,4},{6,5},{7,6},{8,7},{9,8},{10,9... | collective-permute-start | bytes 110600 | tf_op jit(solution)/shard_map/ppermute | solution.py:211
  50.3 4.9 %collective-permute-start.30 = (f32[72,128]{1,0:T(8,128)S(1)}, f32[72,128]{1,0:T(8,128)S(1)}, u32[]{:S(2)}, u32[]{:S(2)}) collective-permute-start(f32[72,128]{1,0:T(8,128)S(1)} %get-tuple-element.43), channel_id=1, source_target_pairs={{0,63},{1,0},{2,1},{3,2},{4,3},{5,4},{6,5},{7,6},{8,7},{9,8},{10,9... | collective-permute-start | bytes 110600 | tf_op jit(solution)/shard_map/ppermute | solution.py:211
  59.2 4.0 %shard_map.162 = (f32[2304,128]{1,0:T(8,128)S(1)}, f32[72,128]{1,0:T(8,128)S(1)}, f32[2,144,128]{2,1,0:T(8,128)S(1)}) custom-call(f32[6912,128]{1,0:T(8,128)S(1)} %bitcast.69, f32[432,128]{1,0:T(8,128)S(1)} %broadcast_in_dim.4.refs_1_.refs_2_, f32[432,128]{1,0:T(8,128)S(1)} %broadcast_in_dim.5.refs_2_.refs_3_, bf16[128,128]{1,0:T(8,128)(2,1)S(1)} %copy-done.4, ...), custom_call_target="tpu_custom_call" | custom-call | tf_op jit(solution)/shard_map/pallas_call | solution.py:195
  64.8 7.1 %collective-permute-start.7 = (f32[72,128]{1,0:T(8,128)S(1)}, f32[72,128]{1,0:T(8,128)S(1)}, u32[]{:S(2)}, u32[]{:S(2)}) collective-permute-start(f32[72,128]{1,0:T(8,128)S(1)} %get-tuple-element.30), channel_id=1, source_target_pairs={{0,127},{1,64},{2,65},{3,66},{4,67},{5,68},{6,69},{7,70},{8,71},{9... | collective-permute-start | bytes 110600 | tf_op jit(solution)/shard_map/ppermute | solution.py:220
  71.9 6.9 %collective-permute-start.5 = (f32[72,128]{1,0:T(8,128)S(1)}, f32[72,128]{1,0:T(8,128)S(1)}, u32[]{:S(2)}, u32[]{:S(2)}) collective-permute-start(f32[72,128]{1,0:T(8,128)S(1)} %get-tuple-element.30), channel_id=1, source_target_pairs={{0,63},{1,0},{2,1},{3,2},{4,3},{5,4},{6,5},{7,6},{8,7},{9,8},{10,9... | collective-permute-start | bytes 110600 | tf_op jit(solution)/shard_map/ppermute | solution.py:211
  83.9 7.1 %collective-permute-start.22 = (f32[72,128]{1,0:T(8,128)S(1)}, f32[72,128]{1,0:T(8,128)S(1)}, u32[]{:S(2)}, u32[]{:S(2)}) collective-permute-start(f32[72,128]{1,0:T(8,128)S(1)} %get-tuple-element.38), channel_id=1, source_target_pairs={{0,127},{1,64},{2,65},{3,66},{4,67},{5,68},{6,69},{7,70},{8,71},{9... | collective-permute-start | bytes 110600 | tf_op jit(solution)/shard_map/ppermute | solution.py:220
  92.1 7.6 %collective-permute-start.20 = (f32[72,128]{1,0:T(8,128)S(1)}, f32[72,128]{1,0:T(8,128)S(1)}, u32[]{:S(2)}, u32[]{:S(2)}) collective-permute-start(f32[72,128]{1,0:T(8,128)S(1)} %get-tuple-element.38), channel_id=1, source_target_pairs={{0,63},{1,0},{2,1},{3,2},{4,3},{5,4},{6,5},{7,6},{8,7},{9,8},{10,9... | collective-permute-start | bytes 110600 | tf_op jit(solution)/shard_map/ppermute | solution.py:211
  100.7 8.6 %collective-permute-start.37 = (f32[72,128]{1,0:T(8,128)S(1)}, f32[72,128]{1,0:T(8,128)S(1)}, u32[]{:S(2)}, u32[]{:S(2)}) collective-permute-start(f32[72,128]{1,0:T(8,128)S(1)} %get-tuple-element.46), channel_id=1, source_target_pairs={{0,127},{1,64},{2,65},{3,66},{4,67},{5,68},{6,69},{7,70},{8,71},{9... | collective-permute-start | bytes 110600 | tf_op jit(solution)/shard_map/ppermute | solution.py:220
  109.3 6.9 %collective-permute-start.35 = (f32[72,128]{1,0:T(8,128)S(1)}, f32[72,128]{1,0:T(8,128)S(1)}, u32[]{:S(2)}, u32[]{:S(2)}) collective-permute-start(f32[72,128]{1,0:T(8,128)S(1)} %get-tuple-element.46), channel_id=1, source_target_pairs={{0,63},{1,0},{2,1},{3,2},{4,3},{5,4},{6,5},{7,6},{8,7},{9,8},{10,9... | collective-permute-start | bytes 110600 | tf_op jit(solution)/shard_map/ppermute | solution.py:211
  116.2 5.1 %shard_map.159 = (f32[2304,128]{1,0:T(8,128)S(1)}, f32[72,128]{1,0:T(8,128)S(1)}, f32[2,144,128]{2,1,0:T(8,128)S(1)}) custom-call(f32[6912,128]{1,0:T(8,128)} %bitcast.59, f32[2304,128]{1,0:T(8,128)S(1)} %get-tuple-element.29.refs_1_, f32[432,128]{1,0:T(8,128)S(1)} %broadcast_in_dim.4.refs_1_.refs_2_, f32[432,128]{1,0:T(8,128)S(1)} %broadcast_in_dim.5.refs_2_.refs_3_, ...), custom_call_target="tpu_custom_call" | custom-call | tf_op jit(solution)/shard_map/pallas_call | solution.py:195
  121.3 5.1 %shard_map.163 = (f32[2304,128]{1,0:T(8,128)S(1)}, f32[72,128]{1,0:T(8,128)S(1)}, f32[2,144,128]{2,1,0:T(8,128)S(1)}) custom-call(f32[6912,128]{1,0:T(8,128)} %bitcast.60, f32[2304,128]{1,0:T(8,128)S(1)} %get-tuple-element.37.refs_1_, f32[432,128]{1,0:T(8,128)S(1)} %broadcast_in_dim.4.refs_1_.refs_2_, f32[432,128]{1,0:T(8,128)S(1)} %broadcast_in_dim.5.refs_2_.refs_3_, ...), custom_call_target="tpu_custom_call" | custom-call | tf_op jit(solution)/shard_map/pallas_call | solution.py:195
  126.6 7.2 %collective-permute-start.12 = (f32[72,128]{1,0:T(8,128)S(1)}, f32[72,128]{1,0:T(8,128)S(1)}, u32[]{:S(2)}, u32[]{:S(2)}) collective-permute-start(f32[72,128]{1,0:T(8,128)S(1)} %get-tuple-element.33), channel_id=1, source_target_pairs={{0,127},{1,64},{2,65},{3,66},{4,67},{5,68},{6,69},{7,70},{8,71},{9... | collective-permute-start | bytes 110600 | tf_op jit(solution)/shard_map/ppermute | solution.py:220
  135.7 5.5 %collective-permute-start.10 = (f32[72,128]{1,0:T(8,128)S(1)}, f32[72,128]{1,0:T(8,128)S(1)}, u32[]{:S(2)}, u32[]{:S(2)}) collective-permute-start(f32[72,128]{1,0:T(8,128)S(1)} %get-tuple-element.33), channel_id=1, source_target_pairs={{0,63},{1,0},{2,1},{3,2},{4,3},{5,4},{6,5},{7,6},{8,7},{9,8},{10,9... | collective-permute-start | bytes 110600 | tf_op jit(solution)/shard_map/ppermute | solution.py:211
  141.3 5.1 %shard_map.167 = (f32[2304,128]{1,0:T(8,128)S(1)}, f32[72,128]{1,0:T(8,128)S(1)}, f32[2,144,128]{2,1,0:T(8,128)S(1)}) custom-call(f32[6912,128]{1,0:T(8,128)} %bitcast.61, f32[2304,128]{1,0:T(8,128)S(1)} %get-tuple-element.45.refs_1_, f32[432,128]{1,0:T(8,128)S(1)} %broadcast_in_dim.4.refs_1_.refs_2_, f32[432,128]{1,0:T(8,128)S(1)} %broadcast_in_dim.5.refs_2_.refs_3_, ...), custom_call_target="tpu_custom_call" | custom-call | tf_op jit(solution)/shard_map/pallas_call | solution.py:195
  147.4 7.2 %collective-permute-start.27 = (f32[72,128]{1,0:T(8,128)S(1)}, f32[72,128]{1,0:T(8,128)S(1)}, u32[]{:S(2)}, u32[]{:S(2)}) collective-permute-start(f32[72,128]{1,0:T(8,128)S(1)} %get-tuple-element.41), channel_id=1, source_target_pairs={{0,127},{1,64},{2,65},{3,66},{4,67},{5,68},{6,69},{7,70},{8,71},{9... | collective-permute-start | bytes 110600 | tf_op jit(solution)/shard_map/ppermute | solution.py:220
  156.3 7.0 %collective-permute-start.25 = (f32[72,128]{1,0:T(8,128)S(1)}, f32[72,128]{1,0:T(8,128)S(1)}, u32[]{:S(2)}, u32[]{:S(2)}) collective-permute-start(f32[72,128]{1,0:T(8,128)S(1)} %get-tuple-element.41), channel_id=1, source_target_pairs={{0,63},{1,0},{2,1},{3,2},{4,3},{5,4},{6,5},{7,6},{8,7},{9,8},{10,9... | collective-permute-start | bytes 110600 | tf_op jit(solution)/shard_map/ppermute | solution.py:211
  164.5 8.4 %collective-permute-start.42 = (f32[72,128]{1,0:T(8,128)S(1)}, f32[72,128]{1,0:T(8,128)S(1)}, u32[]{:S(2)}, u32[]{:S(2)}) collective-permute-start(f32[72,128]{1,0:T(8,128)S(1)} %get-tuple-element.49), channel_id=1, source_target_pairs={{0,127},{1,64},{2,65},{3,66},{4,67},{5,68},{6,69},{7,70},{8,71},{9... | collective-permute-start | bytes 110600 | tf_op jit(solution)/shard_map/ppermute | solution.py:220
  173.0 6.9 %collective-permute-start.40 = (f32[72,128]{1,0:T(8,128)S(1)}, f32[72,128]{1,0:T(8,128)S(1)}, u32[]{:S(2)}, u32[]{:S(2)}) collective-permute-start(f32[72,128]{1,0:T(8,128)S(1)} %get-tuple-element.49), channel_id=1, source_target_pairs={{0,63},{1,0},{2,1},{3,2},{4,3},{5,4},{6,5},{7,6},{8,7},{9,8},{10,9... | collective-permute-start | bytes 110600 | tf_op jit(solution)/shard_map/ppermute | solution.py:211
  195.4 6.2 %fusion.10 = bf16[512,2048]{0,1:T(8,128)(2,1)} fusion(bf16[512,512]{1,0:T(8,128)(2,1)S(1)} %copy-done, f32[512]{0:T(512)S(1)} %copy-done.8, bf16[432,2048]{1,0:T(8,128)(2,1)} %convert_element_type.20, bf16[512,432]{0,1:T(8,128)(2,1)S(1)} %copy-done.7, f32[512]{0:T(512)S(1)} %copy-done.9), kind=kOutput, calls=%fused_computation.16 | convolution fusion | flops 1992294400 | bytes 4837376 | tf_op jit(solution)/shard_map/dot_general | solution.py:230
  201.6 4.5 %add_bitcast_fusion = f32[360,2048]{1,0:T(8,128)S(1)} fusion(bf16[360,512]{1,0:T(8,128)(2,1)} %param.23, f32[360]{0:T(512)S(1)} %copy-done.10, bf16[512,2048]{0,1:T(8,128)(2,1)} %fusion.10, bf16[512,512]{1,0:T(8,128)(2,1)} %param.21, f32[512]{0:T(512)S(1)} %copy-done.11), kind=kOutput, calls=%fused_computation.19 | convolution fusion | flops 1835745280 | bytes 5942688 | tf_op jit(solution)/shard_map/dot_general | solution.py:235
  213.2 8.0 %all-to-all-done = f32[128,1,1]{2,1,0:T(1,128)S(1)} async-done(((f32[128,1,1]{2,1,0:T(1,128)}), f32[128,1,1]{2,1,0:T(1,128)S(1)}, u32[]{:S(2)}, u32[]{:S(2)}) %all-to-all-start) | async-done | bytes 544 | tf_op jit(solution)/shard_map/all_to_all | solution.py:283
  (117 shorter events, 63.3 us)
Async XLA Ops:
  7.5 13.8 %collective-permute-start.33 = (f32[72,128]{1,0:T(8,128)S(1)}, f32[72,128]{1,0:T(8,128)S(1)}, u32[]{:S(2)}, u32[]{:S(2)}) collective-permute-start(f32[72,128]{1,0:T(8,128)S(1)} %get-tuple-element.43), channel_id=1, source_target_pairs={{0,65},{1,66},{2,67},{3,68},{4,69},{5,70},{6,71},{7,72},{8,73},{9,... | collective-permute-start | bytes 110600 | tf_op jit(solution)/shard_map/ppermute | solution.py:221
  14.4 36.0 %collective-permute-start.4 = (f32[2,144,128]{2,1,0:T(8,128)S(1)}, f32[2,144,128]{2,1,0:T(8,128)S(1)}, u32[]{:S(2)}, u32[]{:S(2)}) collective-permute-start(f32[2,144,128]{2,1,0:T(8,128)S(1)} %get-tuple-element.28), channel_id=1, source_target_pairs={{0,64},{64,0},{1,65},{65,1},{2,66},{66,2},{3,67},{67,3},{4,68},{68... | collective-permute-start | bytes 442376 | tf_op jit(solution)/shard_map/ppermute | solution.py:213
  20.9 38.3 %collective-permute-start.19 = (f32[2,144,128]{2,1,0:T(8,128)S(1)}, f32[2,144,128]{2,1,0:T(8,128)S(1)}, u32[]{:S(2)}, u32[]{:S(2)}) collective-permute-start(f32[2,144,128]{2,1,0:T(8,128)S(1)} %get-tuple-element.36), channel_id=1, source_target_pairs={{0,64},{64,0},{1,65},{65,1},{2,66},{66,2},{3,67},{67,3},{4,68},{68... | collective-permute-start | bytes 442376 | tf_op jit(solution)/shard_map/ppermute | solution.py:213
  28.2 43.7 %collective-permute-start.34 = (f32[2,144,128]{2,1,0:T(8,128)S(1)}, f32[2,144,128]{2,1,0:T(8,128)S(1)}, u32[]{:S(2)}, u32[]{:S(2)}) collective-permute-start(f32[2,144,128]{2,1,0:T(8,128)S(1)} %get-tuple-element.44), channel_id=1, source_target_pairs={{0,64},{64,0},{1,65},{65,1},{2,66},{66,2},{3,67},{67,3},{4,68},{68... | collective-permute-start | bytes 442376 | tf_op jit(solution)/shard_map/ppermute | solution.py:213
  46.6 16.6 %collective-permute-start.32 = (f32[72,128]{1,0:T(8,128)S(1)}, f32[72,128]{1,0:T(8,128)S(1)}, u32[]{:S(2)}, u32[]{:S(2)}) collective-permute-start(f32[72,128]{1,0:T(8,128)S(1)} %get-tuple-element.43), channel_id=1, source_target_pairs={{0,127},{1,64},{2,65},{3,66},{4,67},{5,68},{6,69},{7,70},{8,71},{9... | collective-permute-start | bytes 110600 | tf_op jit(solution)/shard_map/ppermute | solution.py:220
  48.3 16.4 %collective-permute-start.31 = (f32[72,128]{1,0:T(8,128)S(1)}, f32[72,128]{1,0:T(8,128)S(1)}, u32[]{:S(2)}, u32[]{:S(2)}) collective-permute-start(f32[72,128]{1,0:T(8,128)S(1)} %get-tuple-element.43), channel_id=1, source_target_pairs={{0,1},{1,2},{2,3},{3,4},{4,5},{5,6},{6,7},{7,8},{8,9},{9,10},{10,1... | collective-permute-start | bytes 110600 | tf_op jit(solution)/shard_map/ppermute | solution.py:212
  50.3 14.4 %collective-permute-start.30 = (f32[72,128]{1,0:T(8,128)S(1)}, f32[72,128]{1,0:T(8,128)S(1)}, u32[]{:S(2)}, u32[]{:S(2)}) collective-permute-start(f32[72,128]{1,0:T(8,128)S(1)} %get-tuple-element.43), channel_id=1, source_target_pairs={{0,63},{1,0},{2,1},{3,2},{4,3},{5,4},{6,5},{7,6},{8,7},{9,8},{10,9... | collective-permute-start | bytes 110600 | tf_op jit(solution)/shard_map/ppermute | solution.py:211
  63.2 46.1 %collective-permute-start.9 = (f32[2,144,128]{2,1,0:T(8,128)S(1)}, f32[2,144,128]{2,1,0:T(8,128)S(1)}, u32[]{:S(2)}, u32[]{:S(2)}) collective-permute-start(f32[2,144,128]{2,1,0:T(8,128)S(1)} %get-tuple-element.31), channel_id=1, source_target_pairs={{0,64},{64,0},{1,65},{65,1},{2,66},{66,2},{3,67},{67,3},{4,68},{68... | collective-permute-start | bytes 442376 | tf_op jit(solution)/shard_map/ppermute | solution.py:213
  64.7 44.7 %collective-permute-start.24 = (f32[2,144,128]{2,1,0:T(8,128)S(1)}, f32[2,144,128]{2,1,0:T(8,128)S(1)}, u32[]{:S(2)}, u32[]{:S(2)}) collective-permute-start(f32[2,144,128]{2,1,0:T(8,128)S(1)} %get-tuple-element.39), channel_id=1, source_target_pairs={{0,64},{64,0},{1,65},{65,1},{2,66},{66,2},{3,67},{67,3},{4,68},{68... | collective-permute-start | bytes 442376 | tf_op jit(solution)/shard_map/ppermute | solution.py:213
  64.8 18.0 %collective-permute-start.7 = (f32[72,128]{1,0:T(8,128)S(1)}, f32[72,128]{1,0:T(8,128)S(1)}, u32[]{:S(2)}, u32[]{:S(2)}) collective-permute-start(f32[72,128]{1,0:T(8,128)S(1)} %get-tuple-element.30), channel_id=1, source_target_pairs={{0,127},{1,64},{2,65},{3,66},{4,67},{5,68},{6,69},{7,70},{8,71},{9... | collective-permute-start | bytes 110600 | tf_op jit(solution)/shard_map/ppermute | solution.py:220
  82.9 51.5 %collective-permute-start.39 = (f32[2,144,128]{2,1,0:T(8,128)S(1)}, f32[2,144,128]{2,1,0:T(8,128)S(1)}, u32[]{:S(2)}, u32[]{:S(2)}) collective-permute-start(f32[2,144,128]{2,1,0:T(8,128)S(1)} %get-tuple-element.47), channel_id=1, source_target_pairs={{0,64},{64,0},{1,65},{65,1},{2,66},{66,2},{3,67},{67,3},{4,68},{68... | collective-permute-start | bytes 442376 | tf_op jit(solution)/shard_map/ppermute | solution.py:213
  100.3 26.2 %collective-permute-start.38 = (f32[72,128]{1,0:T(8,128)S(1)}, f32[72,128]{1,0:T(8,128)S(1)}, u32[]{:S(2)}, u32[]{:S(2)}) collective-permute-start(f32[72,128]{1,0:T(8,128)S(1)} %get-tuple-element.46), channel_id=1, source_target_pairs={{0,65},{1,66},{2,67},{3,68},{4,69},{5,70},{6,71},{7,72},{8,73},{9,... | collective-permute-start | bytes 110600 | tf_op jit(solution)/shard_map/ppermute | solution.py:221
  100.7 25.9 %collective-permute-start.37 = (f32[72,128]{1,0:T(8,128)S(1)}, f32[72,128]{1,0:T(8,128)S(1)}, u32[]{:S(2)}, u32[]{:S(2)}) collective-permute-start(f32[72,128]{1,0:T(8,128)S(1)} %get-tuple-element.46), channel_id=1, source_target_pairs={{0,127},{1,64},{2,65},{3,66},{4,67},{5,68},{6,69},{7,70},{8,71},{9... | collective-permute-start | bytes 110600 | tf_op jit(solution)/shard_map/ppermute | solution.py:220
  109.3 24.4 %collective-permute-start.36 = (f32[72,128]{1,0:T(8,128)S(1)}, f32[72,128]{1,0:T(8,128)S(1)}, u32[]{:S(2)}, u32[]{:S(2)}) collective-permute-start(f32[72,128]{1,0:T(8,128)S(1)} %get-tuple-element.46), channel_id=1, source_target_pairs={{0,1},{1,2},{2,3},{3,4},{4,5},{5,6},{6,7},{7,8},{8,9},{9,10},{10,1... | collective-permute-start | bytes 110600 | tf_op jit(solution)/shard_map/ppermute | solution.py:212
  109.3 24.9 %collective-permute-start.35 = (f32[72,128]{1,0:T(8,128)S(1)}, f32[72,128]{1,0:T(8,128)S(1)}, u32[]{:S(2)}, u32[]{:S(2)}) collective-permute-start(f32[72,128]{1,0:T(8,128)S(1)} %get-tuple-element.46), channel_id=1, source_target_pairs={{0,63},{1,0},{2,1},{3,2},{4,3},{5,4},{6,5},{7,6},{8,7},{9,8},{10,9... | collective-permute-start | bytes 110600 | tf_op jit(solution)/shard_map/ppermute | solution.py:211
  126.6 19.8 %collective-permute-start.12 = (f32[72,128]{1,0:T(8,128)S(1)}, f32[72,128]{1,0:T(8,128)S(1)}, u32[]{:S(2)}, u32[]{:S(2)}) collective-permute-start(f32[72,128]{1,0:T(8,128)S(1)} %get-tuple-element.33), channel_id=1, source_target_pairs={{0,127},{1,64},{2,65},{3,66},{4,67},{5,68},{6,69},{7,70},{8,71},{9... | collective-permute-start | bytes 110600 | tf_op jit(solution)/shard_map/ppermute | solution.py:220
  133.8 39.2 %collective-permute-start.14 = (f32[2,144,128]{2,1,0:T(8,128)S(1)}, f32[2,144,128]{2,1,0:T(8,128)S(1)}, u32[]{:S(2)}, u32[]{:S(2)}) collective-permute-start(f32[2,144,128]{2,1,0:T(8,128)S(1)} %get-tuple-element.34), channel_id=1, source_target_pairs={{0,64},{64,0},{1,65},{65,1},{2,66},{66,2},{3,67},{67,3},{4,68},{68... | collective-permute-start | bytes 442376 | tf_op jit(solution)/shard_map/ppermute | solution.py:213
  134.3 38.7 %collective-permute-start.29 = (f32[2,144,128]{2,1,0:T(8,128)S(1)}, f32[2,144,128]{2,1,0:T(8,128)S(1)}, u32[]{:S(2)}, u32[]{:S(2)}) collective-permute-start(f32[2,144,128]{2,1,0:T(8,128)S(1)} %get-tuple-element.42), channel_id=1, source_target_pairs={{0,64},{64,0},{1,65},{65,1},{2,66},{66,2},{3,67},{67,3},{4,68},{68... | collective-permute-start | bytes 442376 | tf_op jit(solution)/shard_map/ppermute | solution.py:213
  146.4 40.9 %collective-permute-start.44 = (f32[2,144,128]{2,1,0:T(8,128)S(1)}, f32[2,144,128]{2,1,0:T(8,128)S(1)}, u32[]{:S(2)}, u32[]{:S(2)}) collective-permute-start(f32[2,144,128]{2,1,0:T(8,128)S(1)} %get-tuple-element.50), channel_id=1, source_target_pairs={{0,64},{64,0},{1,65},{65,1},{2,66},{66,2},{3,67},{67,3},{4,68},{68... | collective-permute-start | bytes 442376 | tf_op jit(solution)/shard_map/ppermute | solution.py:213
  164.5 22.7 %collective-permute-start.43 = (f32[72,128]{1,0:T(8,128)S(1)}, f32[72,128]{1,0:T(8,128)S(1)}, u32[]{:S(2)}, u32[]{:S(2)}) collective-permute-start(f32[72,128]{1,0:T(8,128)S(1)} %get-tuple-element.49), channel_id=1, source_target_pairs={{0,65},{1,66},{2,67},{3,68},{4,69},{5,70},{6,71},{7,72},{8,73},{9,... | collective-permute-start | bytes 110600 | tf_op jit(solution)/shard_map/ppermute | solution.py:221
  164.5 22.7 %collective-permute-start.42 = (f32[72,128]{1,0:T(8,128)S(1)}, f32[72,128]{1,0:T(8,128)S(1)}, u32[]{:S(2)}, u32[]{:S(2)}) collective-permute-start(f32[72,128]{1,0:T(8,128)S(1)} %get-tuple-element.49), channel_id=1, source_target_pairs={{0,127},{1,64},{2,65},{3,66},{4,67},{5,68},{6,69},{7,70},{8,71},{9... | collective-permute-start | bytes 110600 | tf_op jit(solution)/shard_map/ppermute | solution.py:220
  172.9 14.3 %collective-permute-start.41 = (f32[72,128]{1,0:T(8,128)S(1)}, f32[72,128]{1,0:T(8,128)S(1)}, u32[]{:S(2)}, u32[]{:S(2)}) collective-permute-start(f32[72,128]{1,0:T(8,128)S(1)} %get-tuple-element.49), channel_id=1, source_target_pairs={{0,1},{1,2},{2,3},{3,4},{4,5},{5,6},{6,7},{7,8},{8,9},{9,10},{10,1... | collective-permute-start | bytes 110600 | tf_op jit(solution)/shard_map/ppermute | solution.py:212
  173.0 14.3 %collective-permute-start.40 = (f32[72,128]{1,0:T(8,128)S(1)}, f32[72,128]{1,0:T(8,128)S(1)}, u32[]{:S(2)}, u32[]{:S(2)}) collective-permute-start(f32[72,128]{1,0:T(8,128)S(1)} %get-tuple-element.49), channel_id=1, source_target_pairs={{0,63},{1,0},{2,1},{3,2},{4,3},{5,4},{6,5},{7,6},{8,7},{9,8},{10,9... | collective-permute-start | bytes 110600 | tf_op jit(solution)/shard_map/ppermute | solution.py:211
  207.6 13.6 %all-to-all-start = ((f32[128,1,1]{2,1,0:T(1,128)}), f32[128,1,1]{2,1,0:T(1,128)S(1)}, u32[]{:S(2)}, u32[]{:S(2)}) async-start(f32[128,1,1]{2,1,0:T(1,128)} %copy.18), calls=%async_computation | async-start | bytes 131072 | tf_op jit(solution)/shard_map/all_to_all | solution.py:283
  (34 other events, 541.5 us)

commit v2 on v0

--- a/solution.py
+++ b/solution.py
@@ -235,6 +235,50 @@
     return (outputs.astype(jnp.bfloat16), heating)
 
 
+def mlp_kernel(fin_ref, w_in_ref, b_in_ref, w_mid_ref, b_mid_ref, w_top_ref, b_top_ref,
+               w_out_ref, b_out_ref, tend_ref, heat_ref, scratch):
+    feats = w_in_ref.shape[1]
+    outs = w_out_ref.shape[0]
+    height = heat_ref.shape[0]
+    width = heat_ref.shape[1]
+
+    def layer(w_ref, b_ref, x):
+        a = jnp.dot(w_ref[...], x, preferred_element_type=jnp.float32) + b_ref[...]
+        return (a / (1.0 + jnp.exp(-a))).astype(jnp.bfloat16)
+
+    for pair in range(height // 2):
+        y = 2 * pair
+        x = jnp.concatenate(
+            [fin_ref[pl.ds(y, feats, stride=height), :], fin_ref[pl.ds(y + 1, feats, stride=height), :]],
+            axis=1,
+        ).astype(jnp.bfloat16)
+        h = layer(w_in_ref, b_in_ref, x)
+        h = layer(w_mid_ref, b_mid_ref, h)
+        h = layer(w_top_ref, b_top_ref, h)
+        out = jnp.dot(w_out_ref[...], h, preferred_element_type=jnp.float32) + b_out_ref[...]
+        heat = jnp.sum(out[:LEV], axis=0, keepdims=True)
+        heat_ref[y : y + 1, :] = heat[:, :width]
+        heat_ref[y + 1 : y + 2, :] = heat[:, width:]
+        scratch[pl.ds(y, outs, stride=height), :] = out[:, :width]
+        scratch[pl.ds(y + 1, outs, stride=height), :] = out[:, width:]
+    tend_ref[...] = scratch[...].astype(jnp.bfloat16)
+
+
+def run_mlp(fin, height, w_in, b_in, w_mid, b_mid, w_top, b_top, w_out, b_out):
+    width = fin.shape[1]
+    outs = w_out.shape[0]
+    col = lambda b: b.reshape(-1, 1)
+    return pl.pallas_call(
+        mlp_kernel,
+        out_shape=[
+            jax.ShapeDtypeStruct((outs * height, width), jnp.bfloat16),
+            jax.ShapeDtypeStruct((height, width), jnp.float32),
+        ],
+        scratch_shapes=[pltpu.VMEM((outs * height, width), jnp.float32)],
+        compiler_params=pltpu.CompilerParams(vmem_limit_bytes=48 * 1024 * 1024),
+    )(fin, w_in, col(b_in), w_mid, col(b_mid), w_top, col(b_top), w_out, col(b_out))
+
+
 def local(state, speed_x, speed_y, w_in, b_in, w_mid, b_mid, w_top, b_top, w_out, b_out, span_of):
     feats, height, breadth = state.shape
     across = np.kron(np.eye(breadth // NP, dtype=np.float32), TABLE.T)
@@ -259,19 +303,18 @@
             (field,) = outs
     final_state = field.reshape(feats, height, breadth)
     column_count = height * breadth
-    inputs = final_state.reshape(feats, column_count).astype(jnp.bfloat16)
     target = span_of.reshape(column_count)
     devices = lax.axis_size("face") * lax.axis_size("elem")
     span_ids = jnp.arange(devices, dtype=jnp.int32)
-    weights = (w_in, b_in, w_mid, b_mid, w_top, b_top, w_out, b_out)
-    tend_cols, heating = column_model(inputs, *weights)
+    tend_rows, heat_rows = run_mlp(field, height, w_in, b_in, w_mid, b_mid, w_top, b_top, w_out, b_out)
+    heating = heat_rows.reshape(column_count)
     member = (target[:, None] == span_ids[None, :]).astype(jnp.float32)
     partial_sums = jnp.sum(member * heating[:, None], axis=0)
     received = lax.all_to_all(
         partial_sums.reshape(devices, 1), ("face", "elem"), 0, 1, tiled=True
     )
     span_heating = jnp.sum(received, axis=1) / column_count
-    tendencies = tend_cols.reshape(-1, height, breadth)
+    tendencies = tend_rows.reshape(-1, height, breadth)
     return (final_state, tendencies, span_heating)
 
 

time: 148 us -> 150 us (1.014)
  starting transfers between devices: 56.2 us -> 34.2 us
  Pallas kernels: 41.8 us -> 56.5 us
  blocking collectives: 0 us -> 12.3 us
  matrix products: 12.2 us -> 0 us
  waiting for transfers between devices: 14.9 us -> 25.4 us
  other arithmetic: 6.84 us -> 1.43 us
  local copies, waits for them, and re-layouts: 13.1 us -> 17 us
    ppermute x3, waiting for transfers between devices: 0.01 us -> 19.7 us  [exchange(): dl = lax.ppermute(ex, ('face', 'elem'), diag_l)]
    pallas_call x0 -> x1, Pallas kernels: none -> 13.7 us  [run_mlp(): pl.pallas_call(mlp_kernel, out_shape=[jax.ShapeDtypeStruct((outs * height...]
    all_to_all x0 -> x1, blocking collectives: none -> 12.3 us  [local(): lax.all_to_all(partial_sums.reshape(devices, 1), ('face', 'elem'), 0, 1,...]
    dot_general x2 -> x0, matrix products: 12.2 us -> none  [the longest x1 6.29 us: column_model(): jnp.dot(w_mid, hidden, preferred_element_type=jnp.float32) + b_mid[:, None]]
    ppermute x3, starting transfers between devices: 20.7 us -> 10.4 us  [exchange(): exr = lax.ppermute(ex, 'elem', from_right)]
    all_to_all x1 -> x0, starting transfers between devices: 8.99 us -> none  [local(): lax.all_to_all(partial_sums.reshape(devices, 1), ('face', 'elem'), 0, 1,...]
    all_to_all x1 -> x0, waiting for transfers between devices: 5.95 us -> none  [local(): lax.all_to_all(partial_sums.reshape(devices, 1), ('face', 'elem'), 0, 1,...]
    ppermute x3, waiting for transfers between devices: 8.87 us -> 4.45 us  [exchange(): exl = lax.ppermute(ex, 'elem', from_left)]
  transfers between devices with their start and end apart: 16 -> 15, of which waited for: 4 -> 7; matrix products, arithmetic and copies ran while one was open for 2% -> 3% of each run, Pallas kernels for 0% -> 0%
where the time goes in v2:
time: 150 us
  Pallas kernels  56.5 us (38%)
  starting transfers between devices  34.2 us (23%)
  waiting for transfers between devices  25.4 us (17%)
  local copies, waits for them, and re-layouts  17 us (11%)
  blocking collectives  12.3 us (8%)
  between operations  2.67 us (2%)
    pallas_call x4, Pallas kernels, run_section(): pl.pallas_call(kernel, grid=(steps,), in_specs=specs, out_specs=out_specs...  42.8 us
    ppermute x3, starting transfers between devices, exchange(): dr = lax.ppermute(ex, ('face', 'elem'), diag_r)  21.3 us
    ppermute x3, waiting for transfers between devices, exchange(): dl = lax.ppermute(ex, ('face', 'elem'), diag_l)  19.7 us
    pallas_call x1, Pallas kernels, run_mlp(): pl.pallas_call(mlp_kernel, out_shape=[jax.ShapeDtypeStruct((outs * height...  13.7 us
    unnamed x53, local copies, waits for them, and re-layouts  12.6 us
    all_to_all x1, blocking collectives, local(): lax.all_to_all(partial_sums.reshape(devices, 1), ('face', 'elem'), 0, 1,...  12.3 us
    ppermute x3, starting transfers between devices, exchange(): exr = lax.ppermute(ex, 'elem', from_right)  10.4 us
    ppermute x3, waiting for transfers between devices, exchange(): exl = lax.ppermute(ex, 'elem', from_left)  4.45 us
  transfers between devices with their start and end apart: 15, of which 7 were waited for; matrix products, arithmetic and copies ran while one was open for 3% of the time, Pallas kernels for 0%

profile of v2, /device:TPU:1, one launch (start us, length us, event | category | flops | bytes accessed | tf_op | source)
XLA Modules:
  0.0 149.5 jit_solution(14485047345875362635)
XLA Ops:
  2.3 2.1 %copy-done = f32[432,16,128]{2,1,0:T(8,128)S(1)} copy-done((f32[432,16,128]{2,1,0:T(8,128)S(1)}, f32[432,16,128]{2,1,0:T(8,128)}, u32[]{:S(2)}) %copy-start) | copy-done | bytes 3538968
  5.9 4.9 %shard_map.157 = (f32[216,128]{1,0:T(8,128)S(1)}, f32[2,432,128]{2,1,0:T(8,128)S(1)}) custom-call(f32[6912,128]{1,0:T(8,128)S(1)} %bitcast.12, f32[432,128]{1,0:T(8,128)S(1)} %broadcast_in_dim.4.refs_1_.refs_2_, f32[432,128]{1,0:T(8,128)S(1)} %broadcast_in_dim.5.refs_2_.refs_3_, bf16[128,128]{1,0:T(8,128)(2,1)S(1)} %copy-done.12, bf16[128,128]{1,0:T(8,128)(2,1)S(1)} %copy-done.15), custom_call_target="tpu_custom_call" | custom-call | tf_op jit(solution)/shard_map/pallas_call | solution.py:193
  10.8 1.5 collective-permute-start.4
  12.3 8.5 %collective-permute-start = (f32[216,128]{1,0:T(8,128)S(1)}, f32[216,128]{1,0:T(8,128)S(1)}, u32[]{:S(2)}, u32[]{:S(2)}) collective-permute-start(f32[216,128]{1,0:T(8,128)S(1)} %get-tuple-element.13), channel_id=1, source_target_pairs={{0,63},{1,0},{2,1},{3,2},{4,3},{5,4},{6,5},{7,6},{8,7},{9,8},{10,9... | collective-permute-start | bytes 331784 | tf_op jit(solution)/shard_map/ppermute | solution.py:209
  20.8 7.4 %collective-permute-start.2 = (f32[216,128]{1,0:T(8,128)S(1)}, f32[216,128]{1,0:T(8,128)S(1)}, u32[]{:S(2)}, u32[]{:S(2)}) collective-permute-start(f32[216,128]{1,0:T(8,128)S(1)} %get-tuple-element.13), channel_id=1, source_target_pairs={{0,127},{1,64},{2,65},{3,66},{4,67},{5,68},{6,69},{7,70},{8,71},{9... | collective-permute-start | bytes 331784 | tf_op jit(solution)/shard_map/ppermute | solution.py:218
  28.2 2.3 %collective-permute-done.1.refs_6_ = f32[216,128]{1,0:T(8,128)S(1)} collective-permute-done((f32[216,128]{1,0:T(8,128)S(1)}, f32[216,128]{1,0:T(8,128)S(1)}, u32[]{:S(2)}, u32[]{:S(2)}) %collective-permute-start.1) | collective-permute-done | bytes 110624 | tf_op jit(solution)/shard_map/ppermute | solution.py:210
  31.1 7.1 %collective-permute-done.3.refs_8_ = f32[216,128]{1,0:T(8,128)S(1)} collective-permute-done((f32[216,128]{1,0:T(8,128)S(1)}, f32[216,128]{1,0:T(8,128)S(1)}, u32[]{:S(2)}, u32[]{:S(2)}) %collective-permute-start.3) | collective-permute-done | bytes 110624 | tf_op jit(solution)/shard_map/ppermute | solution.py:219
  38.2 12.9 %shard_map.158 = (f32[6912,128]{1,0:T(8,128)S(1)}, f32[216,128]{1,0:T(8,128)S(1)}, f32[2,432,128]{2,1,0:T(8,128)S(1)}) custom-call(f32[6912,128]{1,0:T(8,128)} %bitcast.10, f32[432,128]{1,0:T(8,128)S(1)} %broadcast_in_dim.4.refs_1_.refs_2_, f32[432,128]{1,0:T(8,128)S(1)} %broadcast_in_dim.5.refs_2_.refs_3_, bf16[128,128]{1,0:T(8,128)(2,1)S(1)} %copy-done.13, ...), custom_call_target="tpu_custom_call" | custom-call | tf_op jit(solution)/shard_map/pallas_call | solution.py:193
  51.1 1.8 %copy-done.7 = f32[6912,128]{1,0:T(8,128)} copy-done((f32[6912,128]{1,0:T(8,128)}, f32[6912,128]{1,0:T(8,128)S(1)}, u32[]{:S(2)}) %copy-start.7) | copy-done | bytes 3538968
  52.9 0.9 collective-permute-start.5
  54.3 6.9 %collective-permute-start.7 = (f32[216,128]{1,0:T(8,128)S(1)}, f32[216,128]{1,0:T(8,128)S(1)}, u32[]{:S(2)}, u32[]{:S(2)}) collective-permute-start(f32[216,128]{1,0:T(8,128)S(1)} %get-tuple-element.16), channel_id=1, source_target_pairs={{0,127},{1,64},{2,65},{3,66},{4,67},{5,68},{6,69},{7,70},{8,71},{9... | collective-permute-start | bytes 331784 | tf_op jit(solution)/shard_map/ppermute | solution.py:218
  61.2 2.2 %collective-permute-done.6.refs_7_ = f32[216,128]{1,0:T(8,128)S(1)} collective-permute-done((f32[216,128]{1,0:T(8,128)S(1)}, f32[216,128]{1,0:T(8,128)S(1)}, u32[]{:S(2)}, u32[]{:S(2)}) %collective-permute-start.6) | collective-permute-done | bytes 110624 | tf_op jit(solution)/shard_map/ppermute | solution.py:210
  64.1 7.1 %collective-permute-done.8.refs_9_ = f32[216,128]{1,0:T(8,128)S(1)} collective-permute-done((f32[216,128]{1,0:T(8,128)S(1)}, f32[216,128]{1,0:T(8,128)S(1)}, u32[]{:S(2)}, u32[]{:S(2)}) %collective-permute-start.8) | collective-permute-done | bytes 110624 | tf_op jit(solution)/shard_map/ppermute | solution.py:219
  71.2 14.3 %shard_map.159 = (f32[6912,128]{1,0:T(8,128)S(1)}, f32[216,128]{1,0:T(8,128)}, f32[2,432,128]{2,1,0:T(8,128)}) custom-call(f32[6912,128]{1,0:T(8,128)} %bitcast.11, f32[6912,128]{1,0:T(8,128)} %copy-done.7, f32[432,128]{1,0:T(8,128)S(1)} %broadcast_in_dim.4.refs_1_.refs_2_, f32[432,128]{1,0:T(8,128)S(1)} %broadcast_in_dim.5.refs_2_.refs_3_, ...), custom_call_target="tpu_custom_call" | custom-call | tf_op jit(solution)/shard_map/pallas_call | solution.py:193
  85.5 1.7 %copy-done.6 = f32[6912,128]{1,0:T(8,128)} copy-done((f32[6912,128]{1,0:T(8,128)}, f32[6912,128]{1,0:T(8,128)S(1)}, u32[]{:S(2)}) %copy-start.6) | copy-done | bytes 3538968
  87.2 1.0 collective-permute-start.10
  88.7 7.0 %collective-permute-start.12 = (f32[216,128]{1,0:T(8,128)}, f32[216,128]{1,0:T(8,128)}, u32[]{:S(2)}, u32[]{:S(2)}) collective-permute-start(f32[216,128]{1,0:T(8,128)} %get-tuple-element.19), channel_id=1, source_target_pairs={{0,127},{1,64},{2,65},{3,66},{4,67},{5,68},{6,69},{7,70},{8,71},{9... | collective-permute-start | bytes 331784 | tf_op jit(solution)/shard_map/ppermute | solution.py:218
  95.7 2.0 %copy.29.w_in_ref = bf16[512,432]{1,0:T(8,128)(2,1)} copy(bf16[512,432]{0,1:T(8,128)(2,1)} %param.17) | data formatting | bytes 884736 | tf_op args[3]
  100.4 5.5 %collective-permute-done.13.refs_9_ = f32[216,128]{1,0:T(8,128)} collective-permute-done((f32[216,128]{1,0:T(8,128)}, f32[216,128]{1,0:T(8,128)}, u32[]{:S(2)}, u32[]{:S(2)}) %collective-permute-start.13) | collective-permute-done | bytes 110624 | tf_op jit(solution)/shard_map/ppermute | solution.py:219
  105.9 0.9 copy-done.3
  106.9 0.9 copy-done.5
  109.4 10.7 %shard_map.160.fin_ref = f32[6912,128]{1,0:T(8,128)} custom-call(f32[6912,128]{1,0:T(8,128)S(1)} %bitcast.13, f32[6912,128]{1,0:T(8,128)} %copy-done.6, f32[432,128]{1,0:T(8,128)S(1)} %copy-done.3, f32[432,128]{1,0:T(8,128)S(1)} %copy-done.5, bf16[128,128]{1,0:T(8,128)(2,1)S(1)} %copy-done.14, bf16[128,128]{1,0:T(8,128)(2,1)S(1)} %copy-done.17, ...), custom_call_target="tpu_custom_call" | custom-call | tf_op jit(solution)/shard_map/pallas_call | solution.py:193
  120.2 13.7 %shard_map.161 = (bf16[5760,128]{1,0:T(8,128)(2,1)}, f32[16,128]{1,0:T(8,128)S(1)}) custom-call(f32[6912,128]{1,0:T(8,128)} %shard_map.160.fin_ref, bf16[512,432]{1,0:T(8,128)(2,1)S(1)} %copy-done.8, f32[512,1]{1,0:T(8,128)S(1)} %copy-done.9, bf16[512,512]{1,0:T(8,128)(2,1)S(1)} %copy-done.18, f32[512,1]{1,0:T(8,128)S(1)} %copy-done.10, ...), custom_call_target="tpu_custom_call" | custom-call | tf_op jit(solution)/shard_map/pallas_call | solution.py:271
  134.7 12.3 %all_to_all.13 = f32[128,1,1]{2,1,0:T(1,128)S(1)} all-to-all(f32[128,1,1]{2,1,0:T(1,128)S(1)} %copy.34), channel_id=1, replica_groups=mesh['face'=2,'elem'=64] {'face','elem'}, dimensions={0} | all-to-all | bytes 1024 | tf_op jit(solution)/shard_map/all_to_all | solution.py:313
  (74 shorter events, 11.3 us)
Async XLA Ops:
  0.6 37.6 %copy-start.13 = (bf16[128,128]{1,0:T(8,128)(2,1)S(1)}, bf16[128,128]{1,0:T(8,128)(2,1)}, u32[]{:S(2)}) copy-start(bf16[128,128]{1,0:T(8,128)(2,1)} %constant.11.clone.refs_3_.refs_4_) | copy-start | bytes 98308
  0.6 37.6 %copy-start.16 = (bf16[128,128]{1,0:T(8,128)(2,1)S(1)}, bf16[128,128]{1,0:T(8,128)(2,1)}, u32[]{:S(2)}) copy-start(bf16[128,128]{1,0:T(8,128)(2,1)} %constant.12.clone.refs_4_.refs_5_) | copy-start | bytes 98308
  1.5 69.7 %copy-start.2 = (f32[432,128]{1,0:T(8,128)}, f32[432,128]{1,0:T(8,128)S(1)}, u32[]{:S(2)}) copy-start(f32[432,128]{1,0:T(8,128)S(1)} %broadcast_in_dim.4.refs_1_.refs_2_) | copy-start | bytes 663556
  2.3 68.9 %copy-start.4 = (f32[432,128]{1,0:T(8,128)}, f32[432,128]{1,0:T(8,128)S(1)}, u32[]{:S(2)}) copy-start(f32[432,128]{1,0:T(8,128)S(1)} %broadcast_in_dim.5.refs_2_.refs_3_) | copy-start | bytes 663556
  10.8 27.4 %collective-permute-start.4 = (f32[2,432,128]{2,1,0:T(8,128)S(1)}, f32[2,432,128]{2,1,0:T(8,128)S(1)}, u32[]{:S(2)}, u32[]{:S(2)}) collective-permute-start(f32[2,432,128]{2,1,0:T(8,128)S(1)} %get-tuple-element.14), channel_id=1, source_target_pairs={{0,64},{64,0},{1,65},{65,1},{2,66},{66,2},{3,67},{67,3},{4,68},{68... | collective-permute-start | bytes 1327112 | tf_op jit(solution)/shard_map/ppermute | solution.py:211
  12.3 15.9 %collective-permute-start = (f32[216,128]{1,0:T(8,128)S(1)}, f32[216,128]{1,0:T(8,128)S(1)}, u32[]{:S(2)}, u32[]{:S(2)}) collective-permute-start(f32[216,128]{1,0:T(8,128)S(1)} %get-tuple-element.13), channel_id=1, source_target_pairs={{0,63},{1,0},{2,1},{3,2},{4,3},{5,4},{6,5},{7,6},{8,7},{9,8},{10,9... | collective-permute-start | bytes 331784 | tf_op jit(solution)/shard_map/ppermute | solution.py:209
  20.8 9.7 %collective-permute-start.1 = (f32[216,128]{1,0:T(8,128)S(1)}, f32[216,128]{1,0:T(8,128)S(1)}, u32[]{:S(2)}, u32[]{:S(2)}) collective-permute-start(f32[216,128]{1,0:T(8,128)S(1)} %get-tuple-element.13), channel_id=1, source_target_pairs={{0,1},{1,2},{2,3},{3,4},{4,5},{5,6},{6,7},{7,8},{8,9},{9,10},{10,1... | collective-permute-start | bytes 331784 | tf_op jit(solution)/shard_map/ppermute | solution.py:210
  20.8 10.2 %collective-permute-start.2 = (f32[216,128]{1,0:T(8,128)S(1)}, f32[216,128]{1,0:T(8,128)S(1)}, u32[]{:S(2)}, u32[]{:S(2)}) collective-permute-start(f32[216,128]{1,0:T(8,128)S(1)} %get-tuple-element.13), channel_id=1, source_target_pairs={{0,127},{1,64},{2,65},{3,66},{4,67},{5,68},{6,69},{7,70},{8,71},{9... | collective-permute-start | bytes 331784 | tf_op jit(solution)/shard_map/ppermute | solution.py:218
  28.2 10.0 %collective-permute-start.3 = (f32[216,128]{1,0:T(8,128)S(1)}, f32[216,128]{1,0:T(8,128)S(1)}, u32[]{:S(2)}, u32[]{:S(2)}) collective-permute-start(f32[216,128]{1,0:T(8,128)S(1)} %get-tuple-element.13), channel_id=1, source_target_pairs={{0,65},{1,66},{2,67},{3,68},{4,69},{5,70},{6,71},{7,72},{8,73},{9,... | collective-permute-start | bytes 331784 | tf_op jit(solution)/shard_map/ppermute | solution.py:219
  52.9 18.3 %collective-permute-start.9 = (f32[2,432,128]{2,1,0:T(8,128)S(1)}, f32[2,432,128]{2,1,0:T(8,128)S(1)}, u32[]{:S(2)}, u32[]{:S(2)}) collective-permute-start(f32[2,432,128]{2,1,0:T(8,128)S(1)} %get-tuple-element.17), channel_id=1, source_target_pairs={{0,64},{64,0},{1,65},{65,1},{2,66},{66,2},{3,67},{67,3},{4,68},{68... | collective-permute-start | bytes 1327112 | tf_op jit(solution)/shard_map/ppermute | solution.py:211
  52.9 8.4 %collective-permute-start.5 = (f32[216,128]{1,0:T(8,128)S(1)}, f32[216,128]{1,0:T(8,128)S(1)}, u32[]{:S(2)}, u32[]{:S(2)}) collective-permute-start(f32[216,128]{1,0:T(8,128)S(1)} %get-tuple-element.16), channel_id=1, source_target_pairs={{0,63},{1,0},{2,1},{3,2},{4,3},{5,4},{6,5},{7,6},{8,7},{9,8},{10,9... | collective-permute-start | bytes 331784 | tf_op jit(solution)/shard_map/ppermute | solution.py:209
  53.8 9.7 %collective-permute-start.6 = (f32[216,128]{1,0:T(8,128)S(1)}, f32[216,128]{1,0:T(8,128)S(1)}, u32[]{:S(2)}, u32[]{:S(2)}) collective-permute-start(f32[216,128]{1,0:T(8,128)S(1)} %get-tuple-element.16), channel_id=1, source_target_pairs={{0,1},{1,2},{2,3},{3,4},{4,5},{5,6},{6,7},{7,8},{8,9},{9,10},{10,1... | collective-permute-start | bytes 331784 | tf_op jit(solution)/shard_map/ppermute | solution.py:210
  54.3 9.7 %collective-permute-start.7 = (f32[216,128]{1,0:T(8,128)S(1)}, f32[216,128]{1,0:T(8,128)S(1)}, u32[]{:S(2)}, u32[]{:S(2)}) collective-permute-start(f32[216,128]{1,0:T(8,128)S(1)} %get-tuple-element.16), channel_id=1, source_target_pairs={{0,127},{1,64},{2,65},{3,66},{4,67},{5,68},{6,69},{7,70},{8,71},{9... | collective-permute-start | bytes 331784 | tf_op jit(solution)/shard_map/ppermute | solution.py:218
  61.2 9.9 %collective-permute-start.8 = (f32[216,128]{1,0:T(8,128)S(1)}, f32[216,128]{1,0:T(8,128)S(1)}, u32[]{:S(2)}, u32[]{:S(2)}) collective-permute-start(f32[216,128]{1,0:T(8,128)S(1)} %get-tuple-element.16), channel_id=1, source_target_pairs={{0,65},{1,66},{2,67},{3,68},{4,69},{5,70},{6,71},{7,72},{8,73},{9,... | collective-permute-start | bytes 331784 | tf_op jit(solution)/shard_map/ppermute | solution.py:219
  71.2 26.5 %copy-start.22 = (f32[512]{0:T(512)S(1)}, f32[512]{0:T(512)}, u32[]{:S(2)}) copy-start(f32[512]{0:T(512)} %param.18) | copy-start | bytes 6148
  71.2 27.4 %copy-start.23 = (f32[512]{0:T(512)S(1)}, f32[512]{0:T(512)}, u32[]{:S(2)}) copy-start(f32[512]{0:T(512)} %param.20) | copy-start | bytes 6148
  71.2 28.2 %copy-start.24 = (f32[512]{0:T(512)S(1)}, f32[512]{0:T(512)}, u32[]{:S(2)}) copy-start(f32[512]{0:T(512)} %param.22) | copy-start | bytes 6148
  71.2 29.1 %copy-start.25 = (f32[360]{0:T(512)S(1)}, f32[360]{0:T(512)}, u32[]{:S(2)}) copy-start(f32[360]{0:T(512)} %param.24) | copy-start | bytes 4324
  71.2 34.7 %copy-start.1 = (f32[432,16,128]{2,1,0:T(8,128)S(1)}, f32[432,16,128]{2,1,0:T(8,128)}, u32[]{:S(2)}) copy-start(f32[432,16,128]{2,1,0:T(8,128)} %param.14) | copy-start | bytes 10616836
  87.2 18.7 %collective-permute-start.14 = (f32[2,432,128]{2,1,0:T(8,128)}, f32[2,432,128]{2,1,0:T(8,128)}, u32[]{:S(2)}, u32[]{:S(2)}) collective-permute-start(f32[2,432,128]{2,1,0:T(8,128)} %get-tuple-element.20), channel_id=1, source_target_pairs={{0,64},{64,0},{1,65},{65,1},{2,66},{66,2},{3,67},{67,3},{4,68},{68... | collective-permute-start | bytes 1327112 | tf_op jit(solution)/shard_map/ppermute | solution.py:211
  87.2 13.1 %collective-permute-start.10 = (f32[216,128]{1,0:T(8,128)}, f32[216,128]{1,0:T(8,128)}, u32[]{:S(2)}, u32[]{:S(2)}) collective-permute-start(f32[216,128]{1,0:T(8,128)} %get-tuple-element.19), channel_id=1, source_target_pairs={{0,63},{1,0},{2,1},{3,2},{4,3},{5,4},{6,5},{7,6},{8,7},{9,8},{10,9... | collective-permute-start | bytes 331784 | tf_op jit(solution)/shard_map/ppermute | solution.py:209
  88.2 12.2 %collective-permute-start.11 = (f32[216,128]{1,0:T(8,128)}, f32[216,128]{1,0:T(8,128)}, u32[]{:S(2)}, u32[]{:S(2)}) collective-permute-start(f32[216,128]{1,0:T(8,128)} %get-tuple-element.19), channel_id=1, source_target_pairs={{0,1},{1,2},{2,3},{3,4},{4,5},{5,6},{6,7},{7,8},{8,9},{9,10},{10,1... | collective-permute-start | bytes 331784 | tf_op jit(solution)/shard_map/ppermute | solution.py:210
  88.7 11.7 %collective-permute-start.12 = (f32[216,128]{1,0:T(8,128)}, f32[216,128]{1,0:T(8,128)}, u32[]{:S(2)}, u32[]{:S(2)}) collective-permute-start(f32[216,128]{1,0:T(8,128)} %get-tuple-element.19), channel_id=1, source_target_pairs={{0,127},{1,64},{2,65},{3,66},{4,67},{5,68},{6,69},{7,70},{8,71},{9... | collective-permute-start | bytes 331784 | tf_op jit(solution)/shard_map/ppermute | solution.py:218
  95.7 10.2 %collective-permute-start.13 = (f32[216,128]{1,0:T(8,128)}, f32[216,128]{1,0:T(8,128)}, u32[]{:S(2)}, u32[]{:S(2)}) collective-permute-start(f32[216,128]{1,0:T(8,128)} %get-tuple-element.19), channel_id=1, source_target_pairs={{0,65},{1,66},{2,67},{3,68},{4,69},{5,70},{6,71},{7,72},{8,73},{9,... | collective-permute-start | bytes 331784 | tf_op jit(solution)/shard_map/ppermute | solution.py:219
  (17 other events, 99.8 us)

commit v3 on v2

--- a/solution.py
+++ b/solution.py
@@ -244,7 +244,7 @@
 
     def layer(w_ref, b_ref, x):
         a = jnp.dot(w_ref[...], x, preferred_element_type=jnp.float32) + b_ref[...]
-        return (a / (1.0 + jnp.exp(-a))).astype(jnp.bfloat16)
+        return (a * (0.5 + 0.5 * jnp.tanh(0.5 * a))).astype(jnp.bfloat16)
 
     for pair in range(height // 2):
         y = 2 * pair

time: 150 us -> 150 us (level)
  no operation moved by 1% of the time
where the time goes in v3:
time: 150 us; the launch traced here: 149 us
  Pallas kernels  56.4 us (38%)
  starting transfers between devices  34.2 us (23%)
  waiting for transfers between devices  25.4 us (17%)
  local copies, waits for them, and re-layouts  17 us (11%)
  blocking collectives  12.3 us (8%)
  between operations  2.67 us (2%)
    pallas_call x4, Pallas kernels, run_section(): pl.pallas_call(kernel, grid=(steps,), in_specs=specs, out_specs=out_specs...  42.8 us
    ppermute x3, starting transfers between devices, exchange(): dr = lax.ppermute(ex, ('face', 'elem'), diag_r)  21.3 us
    ppermute x3, waiting for transfers between devices, exchange(): dl = lax.ppermute(ex, ('face', 'elem'), diag_l)  19.7 us
    pallas_call x1, Pallas kernels, run_mlp(): pl.pallas_call(mlp_kernel, out_shape=[jax.ShapeDtypeStruct((outs * height...  13.6 us
    unnamed x53, local copies, waits for them, and re-layouts  12.6 us
    all_to_all x1, blocking collectives, local(): lax.all_to_all(partial_sums.reshape(devices, 1), ('face', 'elem'), 0, 1,...  12.3 us
    ppermute x3, starting transfers between devices, exchange(): exr = lax.ppermute(ex, 'elem', from_right)  10.4 us
    ppermute x3, waiting for transfers between devices, exchange(): exl = lax.ppermute(ex, 'elem', from_left)  4.45 us
  transfers between devices with their start and end apart: 15, of which 7 were waited for; matrix products, arithmetic and copies ran while one was open for 3% of the time, Pallas kernels for 0%

profile of v3, /device:TPU:1, one launch (start us, length us, event | category | flops | bytes accessed | tf_op | source)
XLA Modules:
  0.0 149.4 jit_solution(3760843799678096578)
XLA Ops:
  2.3 2.1 %copy-done = f32[432,16,128]{2,1,0:T(8,128)S(1)} copy-done((f32[432,16,128]{2,1,0:T(8,128)S(1)}, f32[432,16,128]{2,1,0:T(8,128)}, u32[]{:S(2)}) %copy-start) | copy-done | bytes 3538968
  5.9 4.9 %shard_map.157 = (f32[216,128]{1,0:T(8,128)S(1)}, f32[2,432,128]{2,1,0:T(8,128)S(1)}) custom-call(f32[6912,128]{1,0:T(8,128)S(1)} %bitcast.12, f32[432,128]{1,0:T(8,128)S(1)} %broadcast_in_dim.4.refs_1_.refs_2_, f32[432,128]{1,0:T(8,128)S(1)} %broadcast_in_dim.5.refs_2_.refs_3_, bf16[128,128]{1,0:T(8,128)(2,1)S(1)} %copy-done.12, bf16[128,128]{1,0:T(8,128)(2,1)S(1)} %copy-done.15), custom_call_target="tpu_custom_call" | custom-call | tf_op jit(solution)/shard_map/pallas_call | solution.py:193
  10.8 1.5 collective-permute-start.4
  12.3 8.5 %collective-permute-start = (f32[216,128]{1,0:T(8,128)S(1)}, f32[216,128]{1,0:T(8,128)S(1)}, u32[]{:S(2)}, u32[]{:S(2)}) collective-permute-start(f32[216,128]{1,0:T(8,128)S(1)} %get-tuple-element.13), channel_id=1, source_target_pairs={{0,63},{1,0},{2,1},{3,2},{4,3},{5,4},{6,5},{7,6},{8,7},{9,8},{10,9... | collective-permute-start | bytes 331784 | tf_op jit(solution)/shard_map/ppermute | solution.py:209
  20.8 7.4 %collective-permute-start.2 = (f32[216,128]{1,0:T(8,128)S(1)}, f32[216,128]{1,0:T(8,128)S(1)}, u32[]{:S(2)}, u32[]{:S(2)}) collective-permute-start(f32[216,128]{1,0:T(8,128)S(1)} %get-tuple-element.13), channel_id=1, source_target_pairs={{0,127},{1,64},{2,65},{3,66},{4,67},{5,68},{6,69},{7,70},{8,71},{9... | collective-permute-start | bytes 331784 | tf_op jit(solution)/shard_map/ppermute | solution.py:218
  28.2 2.3 %collective-permute-done.1.refs_6_ = f32[216,128]{1,0:T(8,128)S(1)} collective-permute-done((f32[216,128]{1,0:T(8,128)S(1)}, f32[216,128]{1,0:T(8,128)S(1)}, u32[]{:S(2)}, u32[]{:S(2)}) %collective-permute-start.1) | collective-permute-done | bytes 110624 | tf_op jit(solution)/shard_map/ppermute | solution.py:210
  31.1 7.1 %collective-permute-done.3.refs_8_ = f32[216,128]{1,0:T(8,128)S(1)} collective-permute-done((f32[216,128]{1,0:T(8,128)S(1)}, f32[216,128]{1,0:T(8,128)S(1)}, u32[]{:S(2)}, u32[]{:S(2)}) %collective-permute-start.3) | collective-permute-done | bytes 110624 | tf_op jit(solution)/shard_map/ppermute | solution.py:219
  38.2 12.9 %shard_map.158 = (f32[6912,128]{1,0:T(8,128)S(1)}, f32[216,128]{1,0:T(8,128)S(1)}, f32[2,432,128]{2,1,0:T(8,128)S(1)}) custom-call(f32[6912,128]{1,0:T(8,128)} %bitcast.10, f32[432,128]{1,0:T(8,128)S(1)} %broadcast_in_dim.4.refs_1_.refs_2_, f32[432,128]{1,0:T(8,128)S(1)} %broadcast_in_dim.5.refs_2_.refs_3_, bf16[128,128]{1,0:T(8,128)(2,1)S(1)} %copy-done.13, ...), custom_call_target="tpu_custom_call" | custom-call | tf_op jit(solution)/shard_map/pallas_call | solution.py:193
  51.1 1.8 %copy-done.7 = f32[6912,128]{1,0:T(8,128)} copy-done((f32[6912,128]{1,0:T(8,128)}, f32[6912,128]{1,0:T(8,128)S(1)}, u32[]{:S(2)}) %copy-start.7) | copy-done | bytes 3538968
  52.9 0.9 collective-permute-start.5
  54.3 6.9 %collective-permute-start.7 = (f32[216,128]{1,0:T(8,128)S(1)}, f32[216,128]{1,0:T(8,128)S(1)}, u32[]{:S(2)}, u32[]{:S(2)}) collective-permute-start(f32[216,128]{1,0:T(8,128)S(1)} %get-tuple-element.16), channel_id=1, source_target_pairs={{0,127},{1,64},{2,65},{3,66},{4,67},{5,68},{6,69},{7,70},{8,71},{9... | collective-permute-start | bytes 331784 | tf_op jit(solution)/shard_map/ppermute | solution.py:218
  61.2 2.2 %collective-permute-done.6.refs_7_ = f32[216,128]{1,0:T(8,128)S(1)} collective-permute-done((f32[216,128]{1,0:T(8,128)S(1)}, f32[216,128]{1,0:T(8,128)S(1)}, u32[]{:S(2)}, u32[]{:S(2)}) %collective-permute-start.6) | collective-permute-done | bytes 110624 | tf_op jit(solution)/shard_map/ppermute | solution.py:210
  64.1 7.1 %collective-permute-done.8.refs_9_ = f32[216,128]{1,0:T(8,128)S(1)} collective-permute-done((f32[216,128]{1,0:T(8,128)S(1)}, f32[216,128]{1,0:T(8,128)S(1)}, u32[]{:S(2)}, u32[]{:S(2)}) %collective-permute-start.8) | collective-permute-done | bytes 110624 | tf_op jit(solution)/shard_map/ppermute | solution.py:219
  71.2 14.3 %shard_map.159 = (f32[6912,128]{1,0:T(8,128)S(1)}, f32[216,128]{1,0:T(8,128)}, f32[2,432,128]{2,1,0:T(8,128)}) custom-call(f32[6912,128]{1,0:T(8,128)} %bitcast.11, f32[6912,128]{1,0:T(8,128)} %copy-done.7, f32[432,128]{1,0:T(8,128)S(1)} %broadcast_in_dim.4.refs_1_.refs_2_, f32[432,128]{1,0:T(8,128)S(1)} %broadcast_in_dim.5.refs_2_.refs_3_, ...), custom_call_target="tpu_custom_call" | custom-call | tf_op jit(solution)/shard_map/pallas_call | solution.py:193
  85.5 1.7 %copy-done.6 = f32[6912,128]{1,0:T(8,128)} copy-done((f32[6912,128]{1,0:T(8,128)}, f32[6912,128]{1,0:T(8,128)S(1)}, u32[]{:S(2)}) %copy-start.6) | copy-done | bytes 3538968
  87.2 1.0 collective-permute-start.10
  88.7 7.0 %collective-permute-start.12 = (f32[216,128]{1,0:T(8,128)}, f32[216,128]{1,0:T(8,128)}, u32[]{:S(2)}, u32[]{:S(2)}) collective-permute-start(f32[216,128]{1,0:T(8,128)} %get-tuple-element.19), channel_id=1, source_target_pairs={{0,127},{1,64},{2,65},{3,66},{4,67},{5,68},{6,69},{7,70},{8,71},{9... | collective-permute-start | bytes 331784 | tf_op jit(solution)/shard_map/ppermute | solution.py:218
  95.7 2.0 %copy.29.w_in_ref = bf16[512,432]{1,0:T(8,128)(2,1)} copy(bf16[512,432]{0,1:T(8,128)(2,1)} %param.17) | data formatting | bytes 884736 | tf_op args[3]
  100.4 5.5 %collective-permute-done.13.refs_9_ = f32[216,128]{1,0:T(8,128)} collective-permute-done((f32[216,128]{1,0:T(8,128)}, f32[216,128]{1,0:T(8,128)}, u32[]{:S(2)}, u32[]{:S(2)}) %collective-permute-start.13) | collective-permute-done | bytes 110624 | tf_op jit(solution)/shard_map/ppermute | solution.py:219
  105.9 0.9 copy-done.3
  106.9 0.9 copy-done.5
  109.4 10.7 %shard_map.160.fin_ref = f32[6912,128]{1,0:T(8,128)} custom-call(f32[6912,128]{1,0:T(8,128)S(1)} %bitcast.13, f32[6912,128]{1,0:T(8,128)} %copy-done.6, f32[432,128]{1,0:T(8,128)S(1)} %copy-done.3, f32[432,128]{1,0:T(8,128)S(1)} %copy-done.5, bf16[128,128]{1,0:T(8,128)(2,1)S(1)} %copy-done.14, bf16[128,128]{1,0:T(8,128)(2,1)S(1)} %copy-done.17, ...), custom_call_target="tpu_custom_call" | custom-call | tf_op jit(solution)/shard_map/pallas_call | solution.py:193
  120.2 13.6 %shard_map.161 = (bf16[5760,128]{1,0:T(8,128)(2,1)}, f32[16,128]{1,0:T(8,128)S(1)}) custom-call(f32[6912,128]{1,0:T(8,128)} %shard_map.160.fin_ref, bf16[512,432]{1,0:T(8,128)(2,1)S(1)} %copy-done.8, f32[512,1]{1,0:T(8,128)S(1)} %copy-done.9, bf16[512,512]{1,0:T(8,128)(2,1)S(1)} %copy-done.18, f32[512,1]{1,0:T(8,128)S(1)} %copy-done.10, ...), custom_call_target="tpu_custom_call" | custom-call | tf_op jit(solution)/shard_map/pallas_call | solution.py:271
  134.5 12.3 %all_to_all.13 = f32[128,1,1]{2,1,0:T(1,128)S(1)} all-to-all(f32[128,1,1]{2,1,0:T(1,128)S(1)} %copy.34), channel_id=1, replica_groups=mesh['face'=2,'elem'=64] {'face','elem'}, dimensions={0} | all-to-all | bytes 1024 | tf_op jit(solution)/shard_map/all_to_all | solution.py:313
  (74 shorter events, 11.3 us)
Async XLA Ops:
  0.6 37.6 %copy-start.13 = (bf16[128,128]{1,0:T(8,128)(2,1)S(1)}, bf16[128,128]{1,0:T(8,128)(2,1)}, u32[]{:S(2)}) copy-start(bf16[128,128]{1,0:T(8,128)(2,1)} %constant.11.clone.refs_3_.refs_4_) | copy-start | bytes 98308
  0.6 37.6 %copy-start.16 = (bf16[128,128]{1,0:T(8,128)(2,1)S(1)}, bf16[128,128]{1,0:T(8,128)(2,1)}, u32[]{:S(2)}) copy-start(bf16[128,128]{1,0:T(8,128)(2,1)} %constant.12.clone.refs_4_.refs_5_) | copy-start | bytes 98308
  1.5 69.7 %copy-start.2 = (f32[432,128]{1,0:T(8,128)}, f32[432,128]{1,0:T(8,128)S(1)}, u32[]{:S(2)}) copy-start(f32[432,128]{1,0:T(8,128)S(1)} %broadcast_in_dim.4.refs_1_.refs_2_) | copy-start | bytes 663556
  2.3 68.9 %copy-start.4 = (f32[432,128]{1,0:T(8,128)}, f32[432,128]{1,0:T(8,128)S(1)}, u32[]{:S(2)}) copy-start(f32[432,128]{1,0:T(8,128)S(1)} %broadcast_in_dim.5.refs_2_.refs_3_) | copy-start | bytes 663556
  10.8 27.4 %collective-permute-start.4 = (f32[2,432,128]{2,1,0:T(8,128)S(1)}, f32[2,432,128]{2,1,0:T(8,128)S(1)}, u32[]{:S(2)}, u32[]{:S(2)}) collective-permute-start(f32[2,432,128]{2,1,0:T(8,128)S(1)} %get-tuple-element.14), channel_id=1, source_target_pairs={{0,64},{64,0},{1,65},{65,1},{2,66},{66,2},{3,67},{67,3},{4,68},{68... | collective-permute-start | bytes 1327112 | tf_op jit(solution)/shard_map/ppermute | solution.py:211
  12.3 15.9 %collective-permute-start = (f32[216,128]{1,0:T(8,128)S(1)}, f32[216,128]{1,0:T(8,128)S(1)}, u32[]{:S(2)}, u32[]{:S(2)}) collective-permute-start(f32[216,128]{1,0:T(8,128)S(1)} %get-tuple-element.13), channel_id=1, source_target_pairs={{0,63},{1,0},{2,1},{3,2},{4,3},{5,4},{6,5},{7,6},{8,7},{9,8},{10,9... | collective-permute-start | bytes 331784 | tf_op jit(solution)/shard_map/ppermute | solution.py:209
  20.8 9.7 %collective-permute-start.1 = (f32[216,128]{1,0:T(8,128)S(1)}, f32[216,128]{1,0:T(8,128)S(1)}, u32[]{:S(2)}, u32[]{:S(2)}) collective-permute-start(f32[216,128]{1,0:T(8,128)S(1)} %get-tuple-element.13), channel_id=1, source_target_pairs={{0,1},{1,2},{2,3},{3,4},{4,5},{5,6},{6,7},{7,8},{8,9},{9,10},{10,1... | collective-permute-start | bytes 331784 | tf_op jit(solution)/shard_map/ppermute | solution.py:210
  20.8 10.2 %collective-permute-start.2 = (f32[216,128]{1,0:T(8,128)S(1)}, f32[216,128]{1,0:T(8,128)S(1)}, u32[]{:S(2)}, u32[]{:S(2)}) collective-permute-start(f32[216,128]{1,0:T(8,128)S(1)} %get-tuple-element.13), channel_id=1, source_target_pairs={{0,127},{1,64},{2,65},{3,66},{4,67},{5,68},{6,69},{7,70},{8,71},{9... | collective-permute-start | bytes 331784 | tf_op jit(solution)/shard_map/ppermute | solution.py:218
  28.2 10.0 %collective-permute-start.3 = (f32[216,128]{1,0:T(8,128)S(1)}, f32[216,128]{1,0:T(8,128)S(1)}, u32[]{:S(2)}, u32[]{:S(2)}) collective-permute-start(f32[216,128]{1,0:T(8,128)S(1)} %get-tuple-element.13), channel_id=1, source_target_pairs={{0,65},{1,66},{2,67},{3,68},{4,69},{5,70},{6,71},{7,72},{8,73},{9,... | collective-permute-start | bytes 331784 | tf_op jit(solution)/shard_map/ppermute | solution.py:219
  52.9 18.3 %collective-permute-start.9 = (f32[2,432,128]{2,1,0:T(8,128)S(1)}, f32[2,432,128]{2,1,0:T(8,128)S(1)}, u32[]{:S(2)}, u32[]{:S(2)}) collective-permute-start(f32[2,432,128]{2,1,0:T(8,128)S(1)} %get-tuple-element.17), channel_id=1, source_target_pairs={{0,64},{64,0},{1,65},{65,1},{2,66},{66,2},{3,67},{67,3},{4,68},{68... | collective-permute-start | bytes 1327112 | tf_op jit(solution)/shard_map/ppermute | solution.py:211
  52.9 8.4 %collective-permute-start.5 = (f32[216,128]{1,0:T(8,128)S(1)}, f32[216,128]{1,0:T(8,128)S(1)}, u32[]{:S(2)}, u32[]{:S(2)}) collective-permute-start(f32[216,128]{1,0:T(8,128)S(1)} %get-tuple-element.16), channel_id=1, source_target_pairs={{0,63},{1,0},{2,1},{3,2},{4,3},{5,4},{6,5},{7,6},{8,7},{9,8},{10,9... | collective-permute-start | bytes 331784 | tf_op jit(solution)/shard_map/ppermute | solution.py:209
  53.8 9.7 %collective-permute-start.6 = (f32[216,128]{1,0:T(8,128)S(1)}, f32[216,128]{1,0:T(8,128)S(1)}, u32[]{:S(2)}, u32[]{:S(2)}) collective-permute-start(f32[216,128]{1,0:T(8,128)S(1)} %get-tuple-element.16), channel_id=1, source_target_pairs={{0,1},{1,2},{2,3},{3,4},{4,5},{5,6},{6,7},{7,8},{8,9},{9,10},{10,1... | collective-permute-start | bytes 331784 | tf_op jit(solution)/shard_map/ppermute | solution.py:210
  54.3 9.7 %collective-permute-start.7 = (f32[216,128]{1,0:T(8,128)S(1)}, f32[216,128]{1,0:T(8,128)S(1)}, u32[]{:S(2)}, u32[]{:S(2)}) collective-permute-start(f32[216,128]{1,0:T(8,128)S(1)} %get-tuple-element.16), channel_id=1, source_target_pairs={{0,127},{1,64},{2,65},{3,66},{4,67},{5,68},{6,69},{7,70},{8,71},{9... | collective-permute-start | bytes 331784 | tf_op jit(solution)/shard_map/ppermute | solution.py:218
  61.2 9.9 %collective-permute-start.8 = (f32[216,128]{1,0:T(8,128)S(1)}, f32[216,128]{1,0:T(8,128)S(1)}, u32[]{:S(2)}, u32[]{:S(2)}) collective-permute-start(f32[216,128]{1,0:T(8,128)S(1)} %get-tuple-element.16), channel_id=1, source_target_pairs={{0,65},{1,66},{2,67},{3,68},{4,69},{5,70},{6,71},{7,72},{8,73},{9,... | collective-permute-start | bytes 331784 | tf_op jit(solution)/shard_map/ppermute | solution.py:219
  71.2 26.5 %copy-start.22 = (f32[512]{0:T(512)S(1)}, f32[512]{0:T(512)}, u32[]{:S(2)}) copy-start(f32[512]{0:T(512)} %param.18) | copy-start | bytes 6148
  71.2 27.4 %copy-start.23 = (f32[512]{0:T(512)S(1)}, f32[512]{0:T(512)}, u32[]{:S(2)}) copy-start(f32[512]{0:T(512)} %param.20) | copy-start | bytes 6148
  71.2 28.2 %copy-start.24 = (f32[512]{0:T(512)S(1)}, f32[512]{0:T(512)}, u32[]{:S(2)}) copy-start(f32[512]{0:T(512)} %param.22) | copy-start | bytes 6148
  71.2 29.1 %copy-start.25 = (f32[360]{0:T(512)S(1)}, f32[360]{0:T(512)}, u32[]{:S(2)}) copy-start(f32[360]{0:T(512)} %param.24) | copy-start | bytes 4324
  71.2 34.7 %copy-start.1 = (f32[432,16,128]{2,1,0:T(8,128)S(1)}, f32[432,16,128]{2,1,0:T(8,128)}, u32[]{:S(2)}) copy-start(f32[432,16,128]{2,1,0:T(8,128)} %param.14) | copy-start | bytes 10616836
  87.2 18.7 %collective-permute-start.14 = (f32[2,432,128]{2,1,0:T(8,128)}, f32[2,432,128]{2,1,0:T(8,128)}, u32[]{:S(2)}, u32[]{:S(2)}) collective-permute-start(f32[2,432,128]{2,1,0:T(8,128)} %get-tuple-element.20), channel_id=1, source_target_pairs={{0,64},{64,0},{1,65},{65,1},{2,66},{66,2},{3,67},{67,3},{4,68},{68... | collective-permute-start | bytes 1327112 | tf_op jit(solution)/shard_map/ppermute | solution.py:211
  87.2 13.1 %collective-permute-start.10 = (f32[216,128]{1,0:T(8,128)}, f32[216,128]{1,0:T(8,128)}, u32[]{:S(2)}, u32[]{:S(2)}) collective-permute-start(f32[216,128]{1,0:T(8,128)} %get-tuple-element.19), channel_id=1, source_target_pairs={{0,63},{1,0},{2,1},{3,2},{4,3},{5,4},{6,5},{7,6},{8,7},{9,8},{10,9... | collective-permute-start | bytes 331784 | tf_op jit(solution)/shard_map/ppermute | solution.py:209
  88.2 12.2 %collective-permute-start.11 = (f32[216,128]{1,0:T(8,128)}, f32[216,128]{1,0:T(8,128)}, u32[]{:S(2)}, u32[]{:S(2)}) collective-permute-start(f32[216,128]{1,0:T(8,128)} %get-tuple-element.19), channel_id=1, source_target_pairs={{0,1},{1,2},{2,3},{3,4},{4,5},{5,6},{6,7},{7,8},{8,9},{9,10},{10,1... | collective-permute-start | bytes 331784 | tf_op jit(solution)/shard_map/ppermute | solution.py:210
  88.7 11.7 %collective-permute-start.12 = (f32[216,128]{1,0:T(8,128)}, f32[216,128]{1,0:T(8,128)}, u32[]{:S(2)}, u32[]{:S(2)}) collective-permute-start(f32[216,128]{1,0:T(8,128)} %get-tuple-element.19), channel_id=1, source_target_pairs={{0,127},{1,64},{2,65},{3,66},{4,67},{5,68},{6,69},{7,70},{8,71},{9... | collective-permute-start | bytes 331784 | tf_op jit(solution)/shard_map/ppermute | solution.py:218
  95.7 10.2 %collective-permute-start.13 = (f32[216,128]{1,0:T(8,128)}, f32[216,128]{1,0:T(8,128)}, u32[]{:S(2)}, u32[]{:S(2)}) collective-permute-start(f32[216,128]{1,0:T(8,128)} %get-tuple-element.19), channel_id=1, source_target_pairs={{0,65},{1,66},{2,67},{3,68},{4,69},{5,70},{6,71},{7,72},{8,73},{9,... | collective-permute-start | bytes 331784 | tf_op jit(solution)/shard_map/ppermute | solution.py:219
  (17 other events, 99.7 us)

commit v4 on v3

--- a/solution.py
+++ b/solution.py
@@ -105,8 +105,8 @@
     sx_ref, sy_ref, ahi_ref, alo_ref = refs[:4]
     refs = refs[4:]
     if not first:
-        exr_ref, exl_ref, dr_ref, dl_ref, eyn_ref = refs[:5]
-        refs = refs[5:]
+        exr_ref, exl_ref, dr_ref, dl_ref, top_ref, bottom_ref = refs[:6]
+        refs = refs[6:]
     rows = CHUNK
     height = 16
     sx = sx_ref[...]
@@ -126,8 +126,8 @@
     dr = unpack_edges(dr_ref[...])
     dl = unpack_edges(dl_ref[...])
     tx = [stiff_x(t, exr, exl, y) for y, t in enumerate(tend)]
-    down = stiff_x(eyn_ref[0], dr, dl, 0)
-    up = stiff_x(eyn_ref[1], dr, dl, height - 1)
+    down = stiff_x(top_ref[...], dr, dl, 0)
+    up = stiff_x(bottom_ref[...], dr, dl, height - 1)
     ext = [up] + tx + [down]
     new = []
     for y in range(height):
@@ -175,8 +175,17 @@
     args += [field_rows, sx, sy, ahi, alo]
     specs += [big, small, small, const, const]
     if not first:
-        args += list(halos)
-        specs += [edge, edge, edge, edge, rowsb]
+        exr, exl, partner = halos
+        blocks = field_rows.shape[0] // (CHUNK * 16)
+        args += [exr, exl, partner, partner, partner, partner]
+        specs += [
+            edge,
+            edge,
+            pl.BlockSpec((FOLD, width), lambda i: (4 * blocks + i, 0)),
+            pl.BlockSpec((FOLD, width), lambda i: (5 * blocks + i, 0)),
+            pl.BlockSpec((CHUNK, width), lambda i: (i, 0)),
+            pl.BlockSpec((CHUNK, width), lambda i: (blocks + i, 0)),
+        ]
     out_shape, out_specs = [], []
     ex_shape = jax.ShapeDtypeStruct((feats // 2, width), jnp.float32)
     ey_shape = jax.ShapeDtypeStruct((2, feats, width), jnp.float32)
@@ -208,16 +217,10 @@
     from_left = [(j, (j + 1) % n_elem) for j in range(n_elem)]
     exr = lax.ppermute(ex, "elem", from_right)
     exl = lax.ppermute(ex, "elem", from_left)
-    eyn = lax.ppermute(ey, "face", [(0, 1), (1, 0)])
-    diag_r, diag_l = [], []
-    for f in range(n_face):
-        for j in range(n_elem):
-            src = f * n_elem + j
-            diag_r.append((src, (1 - f) * n_elem + (j - 1) % n_elem))
-            diag_l.append((src, (1 - f) * n_elem + (j + 1) % n_elem))
-    dr = lax.ppermute(ex, ("face", "elem"), diag_r)
-    dl = lax.ppermute(ex, ("face", "elem"), diag_l)
-    return (exr, exl, dr, dl, eyn)
+    feats = ey.shape[1]
+    bundle = jnp.concatenate([ey.reshape(2 * feats, ey.shape[2]), exr, exl], axis=0)
+    partner = lax.ppermute(bundle, "face", [(0, 1), (1, 0)])
+    return (exr, exl, partner)
 
 
 def column_model(inputs, w_in, b_in, w_mid, b_mid, w_top, b_top, w_out, b_out):

time: 150 us -> 140 us (0.933)
  starting transfers between devices: 34.2 us -> 17.3 us
  waiting for transfers between devices: 25.4 us -> 28.6 us
  local copies, waits for them, and re-layouts: 17 us -> 19.5 us
    ppermute x9 -> x3, starting transfers between devices: 22.7 us -> 5.06 us  [exchange(): partner = lax.ppermute(bundle, 'face', [(0, 1), (1, 0)])]
    ppermute x9 -> x3, waiting for transfers between devices: 20.9 us -> 3.48 us  [exchange(): partner = lax.ppermute(bundle, 'face', [(0, 1), (1, 0)])]
    ppermute x3, waiting for transfers between devices: 4.45 us -> 17.8 us  [exchange(): exl = lax.ppermute(ex, 'elem', from_left)]
    ppermute x3, waiting for transfers between devices: 0.01 us -> 7.3 us  [exchange(): exr = lax.ppermute(ex, 'elem', from_right)]
    unnamed x53 -> x61, local copies, waits for them, and re-layouts: 12.6 us -> 15 us
    ppermute x3, starting transfers between devices: 1.07 us -> 2.93 us  [exchange(): exl = lax.ppermute(ex, 'elem', from_left)]
  transfers between devices with their start and end apart: 15 -> 9, of which waited for: 7 -> 8; matrix products, arithmetic and copies ran while one was open for 3% -> 3% of each run, Pallas kernels for 0% -> 0%
where the time goes in v4:
time: 140 us; the launch traced here: 139 us
  Pallas kernels  55.9 us (40%)
  waiting for transfers between devices  28.6 us (20%)
  local copies, waits for them, and re-layouts  19.5 us (14%)
  starting transfers between devices  17.3 us (12%)
  blocking collectives  12.4 us (9%)
  between operations  2.67 us (2%)
  other arithmetic  2.41 us (2%)
    pallas_call x4, Pallas kernels, run_section(): pl.pallas_call(kernel, grid=(steps,), in_specs=specs, out_specs=out_specs...  42.3 us
    ppermute x3, waiting for transfers between devices, exchange(): exl = lax.ppermute(ex, 'elem', from_left)  17.8 us
    unnamed x61, local copies, waits for them, and re-layouts  15 us
    pallas_call x1, Pallas kernels, run_mlp(): pl.pallas_call(mlp_kernel, out_shape=[jax.ShapeDtypeStruct((outs * height...  13.6 us
    all_to_all x1, blocking collectives, local(): lax.all_to_all(partial_sums.reshape(devices, 1), ('face', 'elem'), 0, 1,...  12.4 us
    ppermute x3, starting transfers between devices, exchange(): exr = lax.ppermute(ex, 'elem', from_right)  9.29 us
    ppermute x3, waiting for transfers between devices, exchange(): exr = lax.ppermute(ex, 'elem', from_right)  7.3 us
    ppermute x3, starting transfers between devices, exchange(): partner = lax.ppermute(bundle, 'face', [(0, 1), (1, 0)])  5.06 us
  transfers between devices with their start and end apart: 9, of which 8 were waited for; matrix products, arithmetic and copies ran while one was open for 3% of the time, Pallas kernels for 0%

profile of v4, /device:TPU:1, one launch (start us, length us, event | category | flops | bytes accessed | tf_op | source)
XLA Modules:
  0.0 138.7 jit_solution(13939745768245395884)
XLA Ops:
  2.3 2.1 %copy-done = f32[432,16,128]{2,1,0:T(8,128)S(1)} copy-done((f32[432,16,128]{2,1,0:T(8,128)S(1)}, f32[432,16,128]{2,1,0:T(8,128)}, u32[]{:S(2)}) %copy-start) | copy-done | bytes 3538968
  5.9 4.9 %shard_map.157 = (f32[216,128]{1,0:T(8,128)S(1)}, f32[2,432,128]{2,1,0:T(8,128)S(1)}) custom-call(f32[6912,128]{1,0:T(8,128)S(1)} %bitcast.15, f32[432,128]{1,0:T(8,128)S(1)} %broadcast_in_dim.4.refs_1_.refs_2_, f32[432,128]{1,0:T(8,128)S(1)} %broadcast_in_dim.5.refs_2_.refs_3_, bf16[128,128]{1,0:T(8,128)(2,1)S(1)} %copy-done.12, bf16[128,128]{1,0:T(8,128)(2,1)S(1)} %copy-done.15), custom_call_target="tpu_custom_call" | custom-call | tf_op jit(solution)/shard_map/pallas_call | solution.py:202
  10.8 9.3 %collective-permute-start = (f32[216,128]{1,0:T(8,128)S(1)}, f32[216,128]{1,0:T(8,128)S(1)}, u32[]{:S(2)}, u32[]{:S(2)}) collective-permute-start(f32[216,128]{1,0:T(8,128)S(1)} %get-tuple-element.13), channel_id=1, source_target_pairs={{0,63},{1,0},{2,1},{3,2},{4,3},{5,4},{6,5},{7,6},{8,7},{9,8},{10,9... | collective-permute-start | bytes 331784 | tf_op jit(solution)/shard_map/ppermute | solution.py:218
  20.1 1.8 %collective-permute-done.refs_5_ = f32[216,128]{1,0:T(8,128)S(1)} collective-permute-done((f32[216,128]{1,0:T(8,128)S(1)}, f32[216,128]{1,0:T(8,128)S(1)}, u32[]{:S(2)}, u32[]{:S(2)}) %collective-permute-start) | collective-permute-done | bytes 110624 | tf_op jit(solution)/shard_map/ppermute | solution.py:218
  21.9 7.3 %collective-permute-done.1.refs_6_ = f32[216,128]{1,0:T(8,128)S(1)} collective-permute-done((f32[216,128]{1,0:T(8,128)S(1)}, f32[216,128]{1,0:T(8,128)S(1)}, u32[]{:S(2)}, u32[]{:S(2)}) %collective-permute-start.1) | collective-permute-done | bytes 110624 | tf_op jit(solution)/shard_map/ppermute | solution.py:219
  29.2 2.2 %collective-permute-start.2 = (f32[1296,128]{1,0:T(8,128)S(1)}, f32[1296,128]{1,0:T(8,128)S(1)}, u32[]{:S(2)}, u32[]{:S(2)}) collective-permute-start(f32[1296,128]{1,0:T(8,128)S(1)} %pad_maximum_fusion), channel_id=1, source_target_pairs={{0,64},{64,0},{1,65},{65,1},{2,66},{66,2},{3,67},{67,3},{4,68},{68... | collective-permute-start | bytes 1990664 | tf_op jit(solution)/shard_map/ppermute | solution.py:222
  31.4 1.7 %collective-permute-done.2.refs_7_.refs_8_.refs_9_.refs_10_ = f32[1296,128]{1,0:T(8,128)S(1)} collective-permute-done((f32[1296,128]{1,0:T(8,128)S(1)}, f32[1296,128]{1,0:T(8,128)S(1)}, u32[]{:S(2)}, u32[]{:S(2)}) %collective-permute-start.2) | collective-permute-done | bytes 663584 | tf_op jit(solution)/shard_map/ppermute | solution.py:222
  33.1 13.0 %shard_map.158 = (f32[6912,128]{1,0:T(8,128)S(1)}, f32[216,128]{1,0:T(8,128)S(1)}, f32[2,432,128]{2,1,0:T(8,128)S(1)}) custom-call(f32[6912,128]{1,0:T(8,128)} %bitcast.13, f32[432,128]{1,0:T(8,128)S(1)} %broadcast_in_dim.4.refs_1_.refs_2_, f32[432,128]{1,0:T(8,128)S(1)} %broadcast_in_dim.5.refs_2_.refs_3_, bf16[128,128]{1,0:T(8,128)(2,1)S(1)} %copy-done.13, ...), custom_call_target="tpu_custom_call" | custom-call | tf_op jit(solution)/shard_map/pallas_call | solution.py:202
  46.1 1.8 %copy-done.7 = f32[6912,128]{1,0:T(8,128)} copy-done((f32[6912,128]{1,0:T(8,128)}, f32[6912,128]{1,0:T(8,128)S(1)}, u32[]{:S(2)}) %copy-start.7) | copy-done | bytes 3538968
  47.9 1.5 %collective-permute-start.4 = (f32[216,128]{1,0:T(8,128)S(1)}, f32[216,128]{1,0:T(8,128)S(1)}, u32[]{:S(2)}, u32[]{:S(2)}) collective-permute-start(f32[216,128]{1,0:T(8,128)S(1)} %get-tuple-element.16), channel_id=1, source_target_pairs={{0,1},{1,2},{2,3},{3,4},{4,5},{5,6},{6,7},{7,8},{8,9},{9,10},{10,1... | collective-permute-start | bytes 331784 | tf_op jit(solution)/shard_map/ppermute | solution.py:219
  49.3 2.8 %collective-permute-done.3.refs_6_ = f32[216,128]{1,0:T(8,128)S(1)} collective-permute-done((f32[216,128]{1,0:T(8,128)S(1)}, f32[216,128]{1,0:T(8,128)S(1)}, u32[]{:S(2)}, u32[]{:S(2)}) %collective-permute-start.3) | collective-permute-done | bytes 110624 | tf_op jit(solution)/shard_map/ppermute | solution.py:218
  52.1 5.4 %collective-permute-done.4.refs_7_ = f32[216,128]{1,0:T(8,128)S(1)} collective-permute-done((f32[216,128]{1,0:T(8,128)S(1)}, f32[216,128]{1,0:T(8,128)S(1)}, u32[]{:S(2)}, u32[]{:S(2)}) %collective-permute-start.4) | collective-permute-done | bytes 110624 | tf_op jit(solution)/shard_map/ppermute | solution.py:219
  57.6 1.4 collective-permute-start.5
  58.9 1.7 %collective-permute-done.5.refs_8_.refs_9_.refs_10_.refs_11_ = f32[1296,128]{1,0:T(8,128)S(1)} collective-permute-done((f32[1296,128]{1,0:T(8,128)S(1)}, f32[1296,128]{1,0:T(8,128)S(1)}, u32[]{:S(2)}, u32[]{:S(2)}) %collective-permute-start.5) | collective-permute-done | bytes 663584 | tf_op jit(solution)/shard_map/ppermute | solution.py:222
  60.7 13.7 %shard_map.159 = (f32[6912,128]{1,0:T(8,128)S(1)}, f32[216,128]{1,0:T(8,128)S(1)}, f32[2,432,128]{2,1,0:T(8,128)S(1)}) custom-call(f32[6912,128]{1,0:T(8,128)} %bitcast.14, f32[6912,128]{1,0:T(8,128)} %copy-done.7, f32[432,128]{1,0:T(8,128)S(1)} %broadcast_in_dim.4.refs_1_.refs_2_, f32[432,128]{1,0:T(8,128)S(1)} %broadcast_in_dim.5.refs_2_.refs_3_, ...), custom_call_target="tpu_custom_call" | custom-call | tf_op jit(solution)/shard_map/pallas_call | solution.py:202
  74.4 1.7 %copy-done.6 = f32[6912,128]{1,0:T(8,128)} copy-done((f32[6912,128]{1,0:T(8,128)}, f32[6912,128]{1,0:T(8,128)S(1)}, u32[]{:S(2)}) %copy-start.6) | copy-done | bytes 3538968
  76.1 1.5 %collective-permute-start.7 = (f32[216,128]{1,0:T(8,128)S(1)}, f32[216,128]{1,0:T(8,128)S(1)}, u32[]{:S(2)}, u32[]{:S(2)}) collective-permute-start(f32[216,128]{1,0:T(8,128)S(1)} %get-tuple-element.19), channel_id=1, source_target_pairs={{0,1},{1,2},{2,3},{3,4},{4,5},{5,6},{6,7},{7,8},{8,9},{9,10},{10,1... | collective-permute-start | bytes 331784 | tf_op jit(solution)/shard_map/ppermute | solution.py:219
  77.6 2.8 %collective-permute-done.6.refs_6_ = f32[216,128]{1,0:T(8,128)S(1)} collective-permute-done((f32[216,128]{1,0:T(8,128)S(1)}, f32[216,128]{1,0:T(8,128)S(1)}, u32[]{:S(2)}, u32[]{:S(2)}) %collective-permute-start.6) | collective-permute-done | bytes 110624 | tf_op jit(solution)/shard_map/ppermute | solution.py:218
  80.3 5.2 %collective-permute-done.7.refs_7_ = f32[216,128]{1,0:T(8,128)S(1)} collective-permute-done((f32[216,128]{1,0:T(8,128)S(1)}, f32[216,128]{1,0:T(8,128)S(1)}, u32[]{:S(2)}, u32[]{:S(2)}) %collective-permute-start.7) | collective-permute-done | bytes 110624 | tf_op jit(solution)/shard_map/ppermute | solution.py:219
  87.0 1.5 %collective-permute-start.8 = (f32[1296,128]{1,0:T(8,128)}, f32[1296,128]{1,0:T(8,128)}, u32[]{:S(2)}, u32[]{:S(2)}) collective-permute-start(f32[1296,128]{1,0:T(8,128)} %pad_maximum_fusion.2), channel_id=1, source_target_pairs={{0,64},{64,0},{1,65},{65,1},{2,66},{66,2},{3,67},{67,3},{4,68},{68... | collective-permute-start | bytes 1990664 | tf_op jit(solution)/shard_map/ppermute | solution.py:222
  88.6 2.0 %copy.29.w_in_ref = bf16[512,432]{1,0:T(8,128)(2,1)} copy(bf16[512,432]{0,1:T(8,128)(2,1)} %param.17) | data formatting | bytes 884736 | tf_op args[3]
  98.5 10.8 %shard_map.160.fin_ref = f32[6912,128]{1,0:T(8,128)} custom-call(f32[6912,128]{1,0:T(8,128)S(1)} %bitcast.16, f32[6912,128]{1,0:T(8,128)} %copy-done.6, f32[432,128]{1,0:T(8,128)S(1)} %copy-done.3, f32[432,128]{1,0:T(8,128)S(1)} %copy-done.5, bf16[128,128]{1,0:T(8,128)(2,1)S(1)} %copy-done.14, bf16[128,128]{1,0:T(8,128)(2,1)S(1)} %copy-done.17, ...), custom_call_target="tpu_custom_call" | custom-call | tf_op jit(solution)/shard_map/pallas_call | solution.py:202
  109.4 13.6 %shard_map.161 = (bf16[5760,128]{1,0:T(8,128)(2,1)}, f32[16,128]{1,0:T(8,128)S(1)}) custom-call(f32[6912,128]{1,0:T(8,128)} %shard_map.160.fin_ref, bf16[512,432]{1,0:T(8,128)(2,1)S(1)} %copy-done.8, f32[512,1]{1,0:T(8,128)S(1)} %copy-done.9, bf16[512,512]{1,0:T(8,128)(2,1)S(1)} %copy-done.18, f32[512,1]{1,0:T(8,128)S(1)} %copy-done.10, ...), custom_call_target="tpu_custom_call" | custom-call | tf_op jit(solution)/shard_map/pallas_call | solution.py:274
  123.8 12.4 %all_to_all.13 = f32[128,1,1]{2,1,0:T(1,128)S(1)} all-to-all(f32[128,1,1]{2,1,0:T(1,128)S(1)} %copy.34), channel_id=1, replica_groups=mesh['face'=2,'elem'=64] {'face','elem'}, dimensions={0} | all-to-all | bytes 1024 | tf_op jit(solution)/shard_map/all_to_all | solution.py:316
  (73 shorter events, 14.3 us)
Async XLA Ops:
  0.6 32.5 %copy-start.13 = (bf16[128,128]{1,0:T(8,128)(2,1)S(1)}, bf16[128,128]{1,0:T(8,128)(2,1)}, u32[]{:S(2)}) copy-start(bf16[128,128]{1,0:T(8,128)(2,1)} %constant.11.clone.refs_3_.refs_4_) | copy-start | bytes 98308
  0.6 32.5 %copy-start.16 = (bf16[128,128]{1,0:T(8,128)(2,1)S(1)}, bf16[128,128]{1,0:T(8,128)(2,1)}, u32[]{:S(2)}) copy-start(bf16[128,128]{1,0:T(8,128)(2,1)} %constant.12.clone.refs_4_.refs_5_) | copy-start | bytes 98308
  1.5 59.2 %copy-start.2 = (f32[432,128]{1,0:T(8,128)}, f32[432,128]{1,0:T(8,128)S(1)}, u32[]{:S(2)}) copy-start(f32[432,128]{1,0:T(8,128)S(1)} %broadcast_in_dim.4.refs_1_.refs_2_) | copy-start | bytes 663556
  2.3 58.4 %copy-start.4 = (f32[432,128]{1,0:T(8,128)}, f32[432,128]{1,0:T(8,128)S(1)}, u32[]{:S(2)}) copy-start(f32[432,128]{1,0:T(8,128)S(1)} %broadcast_in_dim.5.refs_2_.refs_3_) | copy-start | bytes 663556
  10.8 11.0 %collective-permute-start = (f32[216,128]{1,0:T(8,128)S(1)}, f32[216,128]{1,0:T(8,128)S(1)}, u32[]{:S(2)}, u32[]{:S(2)}) collective-permute-start(f32[216,128]{1,0:T(8,128)S(1)} %get-tuple-element.13), channel_id=1, source_target_pairs={{0,63},{1,0},{2,1},{3,2},{4,3},{5,4},{6,5},{7,6},{8,7},{9,8},{10,9... | collective-permute-start | bytes 331784 | tf_op jit(solution)/shard_map/ppermute | solution.py:218
  20.1 9.0 %collective-permute-start.1 = (f32[216,128]{1,0:T(8,128)S(1)}, f32[216,128]{1,0:T(8,128)S(1)}, u32[]{:S(2)}, u32[]{:S(2)}) collective-permute-start(f32[216,128]{1,0:T(8,128)S(1)} %get-tuple-element.13), channel_id=1, source_target_pairs={{0,1},{1,2},{2,3},{3,4},{4,5},{5,6},{6,7},{7,8},{8,9},{9,10},{10,1... | collective-permute-start | bytes 331784 | tf_op jit(solution)/shard_map/ppermute | solution.py:219
  29.2 3.9 %collective-permute-start.2 = (f32[1296,128]{1,0:T(8,128)S(1)}, f32[1296,128]{1,0:T(8,128)S(1)}, u32[]{:S(2)}, u32[]{:S(2)}) collective-permute-start(f32[1296,128]{1,0:T(8,128)S(1)} %pad_maximum_fusion), channel_id=1, source_target_pairs={{0,64},{64,0},{1,65},{65,1},{2,66},{66,2},{3,67},{67,3},{4,68},{68... | collective-permute-start | bytes 1990664 | tf_op jit(solution)/shard_map/ppermute | solution.py:222
  47.9 4.2 %collective-permute-start.3 = (f32[216,128]{1,0:T(8,128)S(1)}, f32[216,128]{1,0:T(8,128)S(1)}, u32[]{:S(2)}, u32[]{:S(2)}) collective-permute-start(f32[216,128]{1,0:T(8,128)S(1)} %get-tuple-element.16), channel_id=1, source_target_pairs={{0,63},{1,0},{2,1},{3,2},{4,3},{5,4},{6,5},{7,6},{8,7},{9,8},{10,9... | collective-permute-start | bytes 331784 | tf_op jit(solution)/shard_map/ppermute | solution.py:218
  47.9 9.6 %collective-permute-start.4 = (f32[216,128]{1,0:T(8,128)S(1)}, f32[216,128]{1,0:T(8,128)S(1)}, u32[]{:S(2)}, u32[]{:S(2)}) collective-permute-start(f32[216,128]{1,0:T(8,128)S(1)} %get-tuple-element.16), channel_id=1, source_target_pairs={{0,1},{1,2},{2,3},{3,4},{4,5},{5,6},{6,7},{7,8},{8,9},{9,10},{10,1... | collective-permute-start | bytes 331784 | tf_op jit(solution)/shard_map/ppermute | solution.py:219
  57.6 3.1 %collective-permute-start.5 = (f32[1296,128]{1,0:T(8,128)S(1)}, f32[1296,128]{1,0:T(8,128)S(1)}, u32[]{:S(2)}, u32[]{:S(2)}) collective-permute-start(f32[1296,128]{1,0:T(8,128)S(1)} %pad_maximum_fusion.1), channel_id=1, source_target_pairs={{0,64},{64,0},{1,65},{65,1},{2,66},{66,2},{3,67},{67,3},{4,68},{68... | collective-permute-start | bytes 1990664 | tf_op jit(solution)/shard_map/ppermute | solution.py:222
  60.7 29.9 %copy-start.26 = (f32[512]{0:T(512)S(1)}, f32[512]{0:T(512)}, u32[]{:S(2)}) copy-start(f32[512]{0:T(512)} %param.18) | copy-start | bytes 6148
  60.7 30.8 %copy-start.27 = (f32[512]{0:T(512)S(1)}, f32[512]{0:T(512)}, u32[]{:S(2)}) copy-start(f32[512]{0:T(512)} %param.20) | copy-start | bytes 6148
  60.7 31.6 %copy-start.28 = (f32[512]{0:T(512)S(1)}, f32[512]{0:T(512)}, u32[]{:S(2)}) copy-start(f32[512]{0:T(512)} %param.22) | copy-start | bytes 6148
  60.7 32.5 %copy-start.29 = (f32[360]{0:T(512)S(1)}, f32[360]{0:T(512)}, u32[]{:S(2)}) copy-start(f32[360]{0:T(512)} %param.24) | copy-start | bytes 4324
  60.7 32.6 %copy-start.1 = (f32[432,16,128]{2,1,0:T(8,128)S(1)}, f32[432,16,128]{2,1,0:T(8,128)}, u32[]{:S(2)}) copy-start(f32[432,16,128]{2,1,0:T(8,128)} %param.14) | copy-start | bytes 10616836
  76.1 4.2 %collective-permute-start.6 = (f32[216,128]{1,0:T(8,128)S(1)}, f32[216,128]{1,0:T(8,128)S(1)}, u32[]{:S(2)}, u32[]{:S(2)}) collective-permute-start(f32[216,128]{1,0:T(8,128)S(1)} %get-tuple-element.19), channel_id=1, source_target_pairs={{0,63},{1,0},{2,1},{3,2},{4,3},{5,4},{6,5},{7,6},{8,7},{9,8},{10,9... | collective-permute-start | bytes 331784 | tf_op jit(solution)/shard_map/ppermute | solution.py:218
  76.1 9.4 %collective-permute-start.7 = (f32[216,128]{1,0:T(8,128)S(1)}, f32[216,128]{1,0:T(8,128)S(1)}, u32[]{:S(2)}, u32[]{:S(2)}) collective-permute-start(f32[216,128]{1,0:T(8,128)S(1)} %get-tuple-element.19), channel_id=1, source_target_pairs={{0,1},{1,2},{2,3},{3,4},{4,5},{5,6},{6,7},{7,8},{8,9},{9,10},{10,1... | collective-permute-start | bytes 331784 | tf_op jit(solution)/shard_map/ppermute | solution.py:219
  87.0 6.2 %collective-permute-start.8 = (f32[1296,128]{1,0:T(8,128)}, f32[1296,128]{1,0:T(8,128)}, u32[]{:S(2)}, u32[]{:S(2)}) collective-permute-start(f32[1296,128]{1,0:T(8,128)} %pad_maximum_fusion.2), channel_id=1, source_target_pairs={{0,64},{64,0},{1,65},{65,1},{2,66},{66,2},{3,67},{67,3},{4,68},{68... | collective-permute-start | bytes 1990664 | tf_op jit(solution)/shard_map/ppermute | solution.py:222
  98.5 10.8 %copy-start.10 = (f32[512,1]{1,0:T(8,128)S(1)}, f32[512,1]{1,0:T(8,128)}, u32[]{:S(2)}) copy-start(f32[512,1]{1,0:T(8,128)} %copy.31.b_mid_ref) | copy-start | bytes 6148
  98.5 10.8 %copy-start.11 = (f32[512,1]{1,0:T(8,128)S(1)}, f32[512,1]{1,0:T(8,128)}, u32[]{:S(2)}) copy-start(f32[512,1]{1,0:T(8,128)} %copy.32.b_top_ref) | copy-start | bytes 6148
  98.5 10.8 %copy-start.18 = (bf16[512,512]{1,0:T(8,128)(2,1)S(1)}, bf16[512,512]{1,0:T(8,128)(2,1)}, u32[]{:S(2)}) copy-start(bf16[512,512]{1,0:T(8,128)(2,1)} %w_mid_ref.1) | copy-start | bytes 1572868
  98.5 10.8 %copy-start.19 = (bf16[512,512]{1,0:T(8,128)(2,1)S(1)}, bf16[512,512]{1,0:T(8,128)(2,1)}, u32[]{:S(2)}) copy-start(bf16[512,512]{1,0:T(8,128)(2,1)} %w_top_ref.1) | copy-start | bytes 1572868
  98.5 10.8 %copy-start.24 = (bf16[360,512]{1,0:T(8,128)(2,1)S(1)}, bf16[360,512]{1,0:T(8,128)(2,1)}, u32[]{:S(2)}) copy-start(bf16[360,512]{1,0:T(8,128)(2,1)} %w_out_ref.1) | copy-start | bytes 1105924
  109.4 13.6 %copy-start.25 = (s32[1,1,2048,1]{2,3,1,0:T(1,128)S(1)}, s32[1,1,2048,1]{2,3,1,0:T(1,128)}, u32[]{:S(2)}) copy-start(s32[1,1,2048,1]{2,3,1,0:T(1,128)} %param.25) | copy-start | bytes 24580
  (15 other events, 35.5 us)

commit v5 on v4

--- a/solution.py
+++ b/solution.py
@@ -238,16 +238,20 @@
     return (outputs.astype(jnp.bfloat16), heating)
 
 
-def mlp_kernel(fin_ref, w_in_ref, b_in_ref, w_mid_ref, b_mid_ref, w_top_ref, b_top_ref,
-               w_out_ref, b_out_ref, tend_ref, heat_ref, scratch):
-    feats = w_in_ref.shape[1]
+def mlp_kernel(fin_ref, w_in_ref, w_mid_ref, w_top_ref, w_out_ref, b_ref, tend_ref, heat_ref, scratch):
+    feats = w_in_ref.shape[0]
     outs = w_out_ref.shape[0]
     height = heat_ref.shape[0]
     width = heat_ref.shape[1]
 
-    def layer(w_ref, b_ref, x):
-        a = jnp.dot(w_ref[...], x, preferred_element_type=jnp.float32) + b_ref[...]
+    def act(a):
         return (a * (0.5 + 0.5 * jnp.tanh(0.5 * a))).astype(jnp.bfloat16)
+
+    hid = w_mid_ref.shape[0]
+    b_in = b_ref[0:hid]
+    b_mid = b_ref[hid : 2 * hid]
+    b_top = b_ref[2 * hid : 3 * hid]
+    b_out = b_ref[3 * hid : 3 * hid + outs]
 
     for pair in range(height // 2):
         y = 2 * pair
@@ -255,10 +259,15 @@
             [fin_ref[pl.ds(y, feats, stride=height), :], fin_ref[pl.ds(y + 1, feats, stride=height), :]],
             axis=1,
         ).astype(jnp.bfloat16)
-        h = layer(w_in_ref, b_in_ref, x)
-        h = layer(w_mid_ref, b_mid_ref, h)
-        h = layer(w_top_ref, b_top_ref, h)
-        out = jnp.dot(w_out_ref[...], h, preferred_element_type=jnp.float32) + b_out_ref[...]
+        h = act(
+            lax.dot_general(
+                w_in_ref[...], x, (((0,), (0,)), ((), ())), preferred_element_type=jnp.float32
+            )
+            + b_in
+        )
+        h = act(jnp.dot(w_mid_ref[...], h, preferred_element_type=jnp.float32) + b_mid)
+        h = act(jnp.dot(w_top_ref[...], h, preferred_element_type=jnp.float32) + b_top)
+        out = jnp.dot(w_out_ref[...], h, preferred_element_type=jnp.float32) + b_out
         heat = jnp.sum(out[:LEV], axis=0, keepdims=True)
         heat_ref[y : y + 1, :] = heat[:, :width]
         heat_ref[y + 1 : y + 2, :] = heat[:, width:]
@@ -270,7 +279,7 @@
 def run_mlp(fin, height, w_in, b_in, w_mid, b_mid, w_top, b_top, w_out, b_out):
     width = fin.shape[1]
     outs = w_out.shape[0]
-    col = lambda b: b.reshape(-1, 1)
+    biases = jnp.concatenate([b_in, b_mid, b_top, b_out]).reshape(-1, 1)
     return pl.pallas_call(
         mlp_kernel,
         out_shape=[
@@ -279,7 +288,7 @@
         ],
         scratch_shapes=[pltpu.VMEM((outs * height, width), jnp.float32)],
         compiler_params=pltpu.CompilerParams(vmem_limit_bytes=48 * 1024 * 1024),
-    )(fin, w_in, col(b_in), w_mid, col(b_mid), w_top, col(b_top), w_out, col(b_out))
+    )(fin, w_in.T, w_mid, w_top, w_out, biases)
 
 
 def local(state, speed_x, speed_y, w_in, b_in, w_mid, b_mid, w_top, b_top, w_out, b_out, span_of):

time: 140 us -> 130 us (0.929)
  local copies, waits for them, and re-layouts: 19.5 us -> 9.12 us
    unnamed x61 -> x34, local copies, waits for them, and re-layouts: 15 us -> 7.11 us
    reshape x4 -> x1, local copies, waits for them, and re-layouts: 2.69 us -> 0.3 us  [run_mlp(): biases = jnp.concatenate([b_in, b_mid, b_top, b_out]).reshape(-1, 1)]
  transfers between devices with their start and end apart: 9 -> 9, of which waited for: 8 -> 9; matrix products, arithmetic and copies ran while one was open for 3% -> 0% of each run, Pallas kernels for 0% -> 0%
where the time goes in v5:
time: 130 us; the launch traced here: 129 us
  Pallas kernels  55.7 us (43%)
  waiting for transfers between devices  30 us (23%)
  starting transfers between devices  17.5 us (13%)
  blocking collectives  12.8 us (10%)
  local copies, waits for them, and re-layouts  9.12 us (7%)
  between operations  2.58 us (2%)
  other arithmetic  1.57 us (1%)
    pallas_call x4, Pallas kernels, run_section(): pl.pallas_call(kernel, grid=(steps,), in_specs=specs, out_specs=out_specs...  42.2 us
    ppermute x3, waiting for transfers between devices, exchange(): exl = lax.ppermute(ex, 'elem', from_left)  17.8 us
    pallas_call x1, Pallas kernels, run_mlp(): pl.pallas_call(mlp_kernel, out_shape=[jax.ShapeDtypeStruct((outs * height...  13.5 us
    all_to_all x1, blocking collectives, local(): lax.all_to_all(partial_sums.reshape(devices, 1), ('face', 'elem'), 0, 1,...  12.8 us
    ppermute x3, starting transfers between devices, exchange(): exr = lax.ppermute(ex, 'elem', from_right)  9.29 us
    ppermute x3, waiting for transfers between devices, exchange(): exr = lax.ppermute(ex, 'elem', from_right)  7.3 us
    unnamed x34, local copies, waits for them, and re-layouts  7.11 us
    ppermute x3, starting transfers between devices, exchange(): partner = lax.ppermute(bundle, 'face', [(0, 1), (1, 0)])  5.32 us
  transfers between devices with their start and end apart: 9, of which 9 were waited for; matrix products, arithmetic and copies ran while one was open for 0% of the time, Pallas kernels for 0%

profile of v5, /device:TPU:1, one launch (start us, length us, event | category | flops | bytes accessed | tf_op | source)
XLA Modules:
  0.0 129.3 jit_solution(12426814430466070108)
XLA Ops:
  2.2 2.0 %copy-done = f32[432,16,128]{2,1,0:T(8,128)S(1)} copy-done((f32[432,16,128]{2,1,0:T(8,128)S(1)}, f32[432,16,128]{2,1,0:T(8,128)}, u32[]{:S(2)}) %copy-start) | copy-done | bytes 3538968
  5.8 4.9 %shard_map.157 = (f32[216,128]{1,0:T(8,128)S(1)}, f32[2,432,128]{2,1,0:T(8,128)S(1)}) custom-call(f32[6912,128]{1,0:T(8,128)S(1)} %bitcast.13, f32[432,128]{1,0:T(8,128)S(1)} %broadcast_in_dim.4.refs_1_.refs_2_, f32[432,128]{1,0:T(8,128)S(1)} %broadcast_in_dim.5.refs_2_.refs_3_, bf16[128,128]{1,0:T(8,128)(2,1)S(1)} %copy-done.4, bf16[128,128]{1,0:T(8,128)(2,1)S(1)} %copy-done.6), custom_call_target="tpu_custom_call" | custom-call | tf_op jit(solution)/shard_map/pallas_call | solution.py:202
  10.7 9.3 %collective-permute-start = (f32[216,128]{1,0:T(8,128)S(1)}, f32[216,128]{1,0:T(8,128)S(1)}, u32[]{:S(2)}, u32[]{:S(2)}) collective-permute-start(f32[216,128]{1,0:T(8,128)S(1)} %get-tuple-element.13), channel_id=1, source_target_pairs={{0,63},{1,0},{2,1},{3,2},{4,3},{5,4},{6,5},{7,6},{8,7},{9,8},{10,9... | collective-permute-start | bytes 331784 | tf_op jit(solution)/shard_map/ppermute | solution.py:218
  20.0 1.8 %collective-permute-done.refs_5_ = f32[216,128]{1,0:T(8,128)S(1)} collective-permute-done((f32[216,128]{1,0:T(8,128)S(1)}, f32[216,128]{1,0:T(8,128)S(1)}, u32[]{:S(2)}, u32[]{:S(2)}) %collective-permute-start) | collective-permute-done | bytes 110624 | tf_op jit(solution)/shard_map/ppermute | solution.py:218
  21.7 7.3 %collective-permute-done.1.refs_6_ = f32[216,128]{1,0:T(8,128)S(1)} collective-permute-done((f32[216,128]{1,0:T(8,128)S(1)}, f32[216,128]{1,0:T(8,128)S(1)}, u32[]{:S(2)}, u32[]{:S(2)}) %collective-permute-start.1) | collective-permute-done | bytes 110624 | tf_op jit(solution)/shard_map/ppermute | solution.py:219
  29.1 2.2 %collective-permute-start.2 = (f32[1296,128]{1,0:T(8,128)S(1)}, f32[1296,128]{1,0:T(8,128)S(1)}, u32[]{:S(2)}, u32[]{:S(2)}) collective-permute-start(f32[1296,128]{1,0:T(8,128)S(1)} %pad_maximum_fusion), channel_id=1, source_target_pairs={{0,64},{64,0},{1,65},{65,1},{2,66},{66,2},{3,67},{67,3},{4,68},{68... | collective-permute-start | bytes 1990664 | tf_op jit(solution)/shard_map/ppermute | solution.py:222
  31.2 1.7 %collective-permute-done.2.refs_7_.refs_8_.refs_9_.refs_10_ = f32[1296,128]{1,0:T(8,128)S(1)} collective-permute-done((f32[1296,128]{1,0:T(8,128)S(1)}, f32[1296,128]{1,0:T(8,128)S(1)}, u32[]{:S(2)}, u32[]{:S(2)}) %collective-permute-start.2) | collective-permute-done | bytes 663584 | tf_op jit(solution)/shard_map/ppermute | solution.py:222
  33.0 12.9 %shard_map.158 = (f32[6912,128]{1,0:T(8,128)S(1)}, f32[216,128]{1,0:T(8,128)S(1)}, f32[2,432,128]{2,1,0:T(8,128)S(1)}) custom-call(f32[6912,128]{1,0:T(8,128)} %bitcast.11, f32[432,128]{1,0:T(8,128)S(1)} %broadcast_in_dim.4.refs_1_.refs_2_, f32[432,128]{1,0:T(8,128)S(1)} %broadcast_in_dim.5.refs_2_.refs_3_, bf16[128,128]{1,0:T(8,128)(2,1)S(1)} %copy-done.4, ...), custom_call_target="tpu_custom_call" | custom-call | tf_op jit(solution)/shard_map/pallas_call | solution.py:202
  45.9 1.8 %copy-done.3 = f32[6912,128]{1,0:T(8,128)} copy-done((f32[6912,128]{1,0:T(8,128)}, f32[6912,128]{1,0:T(8,128)S(1)}, u32[]{:S(2)}) %copy-start.3) | copy-done | bytes 3538968
  47.7 1.5 %collective-permute-start.4 = (f32[216,128]{1,0:T(8,128)S(1)}, f32[216,128]{1,0:T(8,128)S(1)}, u32[]{:S(2)}, u32[]{:S(2)}) collective-permute-start(f32[216,128]{1,0:T(8,128)S(1)} %get-tuple-element.16), channel_id=1, source_target_pairs={{0,1},{1,2},{2,3},{3,4},{4,5},{5,6},{6,7},{7,8},{8,9},{9,10},{10,1... | collective-permute-start | bytes 331784 | tf_op jit(solution)/shard_map/ppermute | solution.py:219
  49.1 2.8 %collective-permute-done.3.refs_6_ = f32[216,128]{1,0:T(8,128)S(1)} collective-permute-done((f32[216,128]{1,0:T(8,128)S(1)}, f32[216,128]{1,0:T(8,128)S(1)}, u32[]{:S(2)}, u32[]{:S(2)}) %collective-permute-start.3) | collective-permute-done | bytes 110624 | tf_op jit(solution)/shard_map/ppermute | solution.py:218
  51.9 5.4 %collective-permute-done.4.refs_7_ = f32[216,128]{1,0:T(8,128)S(1)} collective-permute-done((f32[216,128]{1,0:T(8,128)S(1)}, f32[216,128]{1,0:T(8,128)S(1)}, u32[]{:S(2)}, u32[]{:S(2)}) %collective-permute-start.4) | collective-permute-done | bytes 110624 | tf_op jit(solution)/shard_map/ppermute | solution.py:219
  57.3 1.4 %collective-permute-start.5 = (f32[1296,128]{1,0:T(8,128)S(1)}, f32[1296,128]{1,0:T(8,128)S(1)}, u32[]{:S(2)}, u32[]{:S(2)}) collective-permute-start(f32[1296,128]{1,0:T(8,128)S(1)} %pad_maximum_fusion.1), channel_id=1, source_target_pairs={{0,64},{64,0},{1,65},{65,1},{2,66},{66,2},{3,67},{67,3},{4,68},{68... | collective-permute-start | bytes 1990664 | tf_op jit(solution)/shard_map/ppermute | solution.py:222
  58.7 1.7 %collective-permute-done.5.refs_8_.refs_9_.refs_10_.refs_11_ = f32[1296,128]{1,0:T(8,128)S(1)} collective-permute-done((f32[1296,128]{1,0:T(8,128)S(1)}, f32[1296,128]{1,0:T(8,128)S(1)}, u32[]{:S(2)}, u32[]{:S(2)}) %collective-permute-start.5) | collective-permute-done | bytes 663584 | tf_op jit(solution)/shard_map/ppermute | solution.py:222
  60.5 13.6 %shard_map.159 = (f32[6912,128]{1,0:T(8,128)S(1)}, f32[216,128]{1,0:T(8,128)S(1)}, f32[2,432,128]{2,1,0:T(8,128)S(1)}) custom-call(f32[6912,128]{1,0:T(8,128)} %bitcast.12, f32[6912,128]{1,0:T(8,128)} %copy-done.3, f32[432,128]{1,0:T(8,128)S(1)} %broadcast_in_dim.4.refs_1_.refs_2_, f32[432,128]{1,0:T(8,128)S(1)} %broadcast_in_dim.5.refs_2_.refs_3_, ...), custom_call_target="tpu_custom_call" | custom-call | tf_op jit(solution)/shard_map/pallas_call | solution.py:202
  74.1 1.7 %copy-done.2 = f32[6912,128]{1,0:T(8,128)} copy-done((f32[6912,128]{1,0:T(8,128)}, f32[6912,128]{1,0:T(8,128)S(1)}, u32[]{:S(2)}) %copy-start.2) | copy-done | bytes 3538968
  75.9 1.5 %collective-permute-start.7 = (f32[216,128]{1,0:T(8,128)S(1)}, f32[216,128]{1,0:T(8,128)S(1)}, u32[]{:S(2)}, u32[]{:S(2)}) collective-permute-start(f32[216,128]{1,0:T(8,128)S(1)} %get-tuple-element.19), channel_id=1, source_target_pairs={{0,1},{1,2},{2,3},{3,4},{4,5},{5,6},{6,7},{7,8},{8,9},{9,10},{10,1... | collective-permute-start | bytes 331784 | tf_op jit(solution)/shard_map/ppermute | solution.py:219
  77.3 2.8 %collective-permute-done.6.refs_6_ = f32[216,128]{1,0:T(8,128)S(1)} collective-permute-done((f32[216,128]{1,0:T(8,128)S(1)}, f32[216,128]{1,0:T(8,128)S(1)}, u32[]{:S(2)}, u32[]{:S(2)}) %collective-permute-start.6) | collective-permute-done | bytes 110624 | tf_op jit(solution)/shard_map/ppermute | solution.py:218
  80.1 5.2 %collective-permute-done.7.refs_7_ = f32[216,128]{1,0:T(8,128)S(1)} collective-permute-done((f32[216,128]{1,0:T(8,128)S(1)}, f32[216,128]{1,0:T(8,128)S(1)}, u32[]{:S(2)}, u32[]{:S(2)}) %collective-permute-start.7) | collective-permute-done | bytes 110624 | tf_op jit(solution)/shard_map/ppermute | solution.py:219
  85.3 1.8 %collective-permute-start.8 = (f32[1296,128]{1,0:T(8,128)S(1)}, f32[1296,128]{1,0:T(8,128)S(1)}, u32[]{:S(2)}, u32[]{:S(2)}) collective-permute-start(f32[1296,128]{1,0:T(8,128)S(1)} %pad_maximum_fusion.2), channel_id=1, source_target_pairs={{0,64},{64,0},{1,65},{65,1},{2,66},{66,2},{3,67},{67,3},{4,68},{68... | collective-permute-start | bytes 1990664 | tf_op jit(solution)/shard_map/ppermute | solution.py:222
  87.4 1.4 %collective-permute-done.8.refs_8_.refs_9_.refs_10_.refs_11_ = f32[1296,128]{1,0:T(8,128)S(1)} collective-permute-done((f32[1296,128]{1,0:T(8,128)S(1)}, f32[1296,128]{1,0:T(8,128)S(1)}, u32[]{:S(2)}, u32[]{:S(2)}) %collective-permute-start.8) | collective-permute-done | bytes 663584 | tf_op jit(solution)/shard_map/ppermute | solution.py:222
  88.8 10.8 %shard_map.160.fin_ref = f32[6912,128]{1,0:T(8,128)} custom-call(f32[6912,128]{1,0:T(8,128)S(1)} %bitcast.14, f32[6912,128]{1,0:T(8,128)} %copy-done.2, f32[432,128]{1,0:T(8,128)S(1)} %broadcast_in_dim.4.refs_1_.refs_2_, f32[432,128]{1,0:T(8,128)S(1)} %broadcast_in_dim.5.refs_2_.refs_3_, bf16[128,128]{1,0:T(8,128)(2,1)S(1)} %copy-done.5, ...), custom_call_target="tpu_custom_call" | custom-call | tf_op jit(solution)/shard_map/pallas_call | solution.py:202
  99.7 13.5 %shard_map.161 = (bf16[5760,128]{1,0:T(8,128)(2,1)}, f32[16,128]{1,0:T(8,128)S(1)}) custom-call(f32[6912,128]{1,0:T(8,128)} %shard_map.160.fin_ref, bf16[432,512]{1,0:T(8,128)(2,1)S(1)} %bitcast.18, bf16[512,512]{1,0:T(8,128)(2,1)S(1)} %copy-done.8, bf16[512,512]{1,0:T(8,128)(2,1)S(1)} %copy-done.9, bf16[360,512]{1,0:T(8,128)(2,1)S(1)} %copy-done.11, ...), custom_call_target="tpu_custom_call" | custom-call | tf_op jit(solution)/shard_map/pallas_call | solution.py:283
  114.0 12.8 %all_to_all.13 = f32[128,1,1]{2,1,0:T(1,128)S(1)} all-to-all(f32[128,1,1]{2,1,0:T(1,128)S(1)} %copy.21), channel_id=1, replica_groups=mesh['face'=2,'elem'=64] {'face','elem'}, dimensions={0} | all-to-all | bytes 1024 | tf_op jit(solution)/shard_map/all_to_all | solution.py:325
  (44 shorter events, 5.2 us)
Async XLA Ops:
  2.2 2.0 %copy-start = (f32[432,16,128]{2,1,0:T(8,128)S(1)}, f32[432,16,128]{2,1,0:T(8,128)}, u32[]{:S(2)}) copy-start(f32[432,16,128]{2,1,0:T(8,128)} %param.14) | copy-start | bytes 10616836
  10.7 11.0 %collective-permute-start = (f32[216,128]{1,0:T(8,128)S(1)}, f32[216,128]{1,0:T(8,128)S(1)}, u32[]{:S(2)}, u32[]{:S(2)}) collective-permute-start(f32[216,128]{1,0:T(8,128)S(1)} %get-tuple-element.13), channel_id=1, source_target_pairs={{0,63},{1,0},{2,1},{3,2},{4,3},{5,4},{6,5},{7,6},{8,7},{9,8},{10,9... | collective-permute-start | bytes 331784 | tf_op jit(solution)/shard_map/ppermute | solution.py:218
  20.0 9.0 %collective-permute-start.1 = (f32[216,128]{1,0:T(8,128)S(1)}, f32[216,128]{1,0:T(8,128)S(1)}, u32[]{:S(2)}, u32[]{:S(2)}) collective-permute-start(f32[216,128]{1,0:T(8,128)S(1)} %get-tuple-element.13), channel_id=1, source_target_pairs={{0,1},{1,2},{2,3},{3,4},{4,5},{5,6},{6,7},{7,8},{8,9},{9,10},{10,1... | collective-permute-start | bytes 331784 | tf_op jit(solution)/shard_map/ppermute | solution.py:219
  29.0 31.4 %copy-start.5 = (bf16[128,128]{1,0:T(8,128)(2,1)S(1)}, bf16[128,128]{1,0:T(8,128)(2,1)}, u32[]{:S(2)}) copy-start(bf16[128,128]{1,0:T(8,128)(2,1)} %constant.11.clone.refs_3_.refs_4_) | copy-start | bytes 98308
  29.1 31.4 %copy-start.7 = (bf16[128,128]{1,0:T(8,128)(2,1)S(1)}, bf16[128,128]{1,0:T(8,128)(2,1)}, u32[]{:S(2)}) copy-start(bf16[128,128]{1,0:T(8,128)(2,1)} %constant.12.clone.refs_4_.refs_5_) | copy-start | bytes 98308
  29.1 3.9 %collective-permute-start.2 = (f32[1296,128]{1,0:T(8,128)S(1)}, f32[1296,128]{1,0:T(8,128)S(1)}, u32[]{:S(2)}, u32[]{:S(2)}) collective-permute-start(f32[1296,128]{1,0:T(8,128)S(1)} %pad_maximum_fusion), channel_id=1, source_target_pairs={{0,64},{64,0},{1,65},{65,1},{2,66},{66,2},{3,67},{67,3},{4,68},{68... | collective-permute-start | bytes 1990664 | tf_op jit(solution)/shard_map/ppermute | solution.py:222
  45.9 1.8 %copy-start.3 = (f32[6912,128]{1,0:T(8,128)}, f32[6912,128]{1,0:T(8,128)S(1)}, u32[]{:S(2)}) copy-start(f32[6912,128]{1,0:T(8,128)S(1)} %get-tuple-element.15.refs_1_) | copy-start | bytes 10616836
  47.7 4.2 %collective-permute-start.3 = (f32[216,128]{1,0:T(8,128)S(1)}, f32[216,128]{1,0:T(8,128)S(1)}, u32[]{:S(2)}, u32[]{:S(2)}) collective-permute-start(f32[216,128]{1,0:T(8,128)S(1)} %get-tuple-element.16), channel_id=1, source_target_pairs={{0,63},{1,0},{2,1},{3,2},{4,3},{5,4},{6,5},{7,6},{8,7},{9,8},{10,9... | collective-permute-start | bytes 331784 | tf_op jit(solution)/shard_map/ppermute | solution.py:218
  47.7 9.6 %collective-permute-start.4 = (f32[216,128]{1,0:T(8,128)S(1)}, f32[216,128]{1,0:T(8,128)S(1)}, u32[]{:S(2)}, u32[]{:S(2)}) collective-permute-start(f32[216,128]{1,0:T(8,128)S(1)} %get-tuple-element.16), channel_id=1, source_target_pairs={{0,1},{1,2},{2,3},{3,4},{4,5},{5,6},{6,7},{7,8},{8,9},{9,10},{10,1... | collective-permute-start | bytes 331784 | tf_op jit(solution)/shard_map/ppermute | solution.py:219
  57.3 3.1 %collective-permute-start.5 = (f32[1296,128]{1,0:T(8,128)S(1)}, f32[1296,128]{1,0:T(8,128)S(1)}, u32[]{:S(2)}, u32[]{:S(2)}) collective-permute-start(f32[1296,128]{1,0:T(8,128)S(1)} %pad_maximum_fusion.1), channel_id=1, source_target_pairs={{0,64},{64,0},{1,65},{65,1},{2,66},{66,2},{3,67},{67,3},{4,68},{68... | collective-permute-start | bytes 1990664 | tf_op jit(solution)/shard_map/ppermute | solution.py:222
  60.4 26.6 %copy-start.13 = (f32[360]{0:T(512)S(1)}, f32[360]{0:T(512)}, u32[]{:S(2)}) copy-start(f32[360]{0:T(512)} %param.24) | copy-start | bytes 4324
  60.4 26.6 %copy-start.14 = (f32[512]{0:T(512)S(1)}, f32[512]{0:T(512)}, u32[]{:S(2)}) copy-start(f32[512]{0:T(512)} %param.22) | copy-start | bytes 6148
  60.4 26.6 %copy-start.15 = (f32[512]{0:T(512)S(1)}, f32[512]{0:T(512)}, u32[]{:S(2)}) copy-start(f32[512]{0:T(512)} %param.20) | copy-start | bytes 6148
  60.5 26.6 %copy-start.16 = (f32[512]{0:T(512)S(1)}, f32[512]{0:T(512)}, u32[]{:S(2)}) copy-start(f32[512]{0:T(512)} %param.18) | copy-start | bytes 6148
  60.5 28.3 %copy-start.1 = (f32[432,16,128]{2,1,0:T(8,128)S(1)}, f32[432,16,128]{2,1,0:T(8,128)}, u32[]{:S(2)}) copy-start(f32[432,16,128]{2,1,0:T(8,128)} %param.14) | copy-start | bytes 10616836
  74.1 1.8 %copy-start.2 = (f32[6912,128]{1,0:T(8,128)}, f32[6912,128]{1,0:T(8,128)S(1)}, u32[]{:S(2)}) copy-start(f32[6912,128]{1,0:T(8,128)S(1)} %get-tuple-element.18.refs_1_) | copy-start | bytes 10616836
  75.9 4.2 %collective-permute-start.6 = (f32[216,128]{1,0:T(8,128)S(1)}, f32[216,128]{1,0:T(8,128)S(1)}, u32[]{:S(2)}, u32[]{:S(2)}) collective-permute-start(f32[216,128]{1,0:T(8,128)S(1)} %get-tuple-element.19), channel_id=1, source_target_pairs={{0,63},{1,0},{2,1},{3,2},{4,3},{5,4},{6,5},{7,6},{8,7},{9,8},{10,9... | collective-permute-start | bytes 331784 | tf_op jit(solution)/shard_map/ppermute | solution.py:218
  75.9 9.4 %collective-permute-start.7 = (f32[216,128]{1,0:T(8,128)S(1)}, f32[216,128]{1,0:T(8,128)S(1)}, u32[]{:S(2)}, u32[]{:S(2)}) collective-permute-start(f32[216,128]{1,0:T(8,128)S(1)} %get-tuple-element.19), channel_id=1, source_target_pairs={{0,1},{1,2},{2,3},{3,4},{4,5},{5,6},{6,7},{7,8},{8,9},{9,10},{10,1... | collective-permute-start | bytes 331784 | tf_op jit(solution)/shard_map/ppermute | solution.py:219
  85.3 3.5 %collective-permute-start.8 = (f32[1296,128]{1,0:T(8,128)S(1)}, f32[1296,128]{1,0:T(8,128)S(1)}, u32[]{:S(2)}, u32[]{:S(2)}) collective-permute-start(f32[1296,128]{1,0:T(8,128)S(1)} %pad_maximum_fusion.2), channel_id=1, source_target_pairs={{0,64},{64,0},{1,65},{65,1},{2,66},{66,2},{3,67},{67,3},{4,68},{68... | collective-permute-start | bytes 1990664 | tf_op jit(solution)/shard_map/ppermute | solution.py:222
  88.8 10.8 %copy-start.8 = (bf16[512,512]{1,0:T(8,128)(2,1)S(1)}, bf16[512,512]{1,0:T(8,128)(2,1)}, u32[]{:S(2)}) copy-start(bf16[512,512]{1,0:T(8,128)(2,1)} %w_mid_ref.1) | copy-start | bytes 1572868
  88.8 10.8 %copy-start.9 = (bf16[512,512]{1,0:T(8,128)(2,1)S(1)}, bf16[512,512]{1,0:T(8,128)(2,1)}, u32[]{:S(2)}) copy-start(bf16[512,512]{1,0:T(8,128)(2,1)} %w_top_ref.1) | copy-start | bytes 1572868
  88.8 10.8 %copy-start.10 = (bf16[512,432]{0,1:T(8,128)(2,1)S(1)}, bf16[512,432]{0,1:T(8,128)(2,1)}, u32[]{:S(2)}) copy-start(bf16[512,432]{0,1:T(8,128)(2,1)} %param.17) | copy-start | bytes 1327108
  88.8 10.8 %copy-start.11 = (bf16[360,512]{1,0:T(8,128)(2,1)S(1)}, bf16[360,512]{1,0:T(8,128)(2,1)}, u32[]{:S(2)}) copy-start(bf16[360,512]{1,0:T(8,128)(2,1)} %w_out_ref.1) | copy-start | bytes 1105924
  99.6 13.6 %copy-start.12 = (s32[1,1,2048,1]{2,3,1,0:T(1,128)S(1)}, s32[1,1,2048,1]{2,3,1,0:T(1,128)}, u32[]{:S(2)}) copy-start(s32[1,1,2048,1]{2,3,1,0:T(1,128)} %param.25) | copy-start | bytes 24580
  (2 other events, 1.5 us)

commit v6 on v5

--- a/solution.py
+++ b/solution.py
@@ -205,7 +205,7 @@
         in_specs=specs,
         out_specs=out_specs,
         out_shape=out_shape,
-        compiler_params=pltpu.CompilerParams(vmem_limit_bytes=48 * 1024 * 1024),
+        compiler_params=pltpu.CompilerParams(vmem_limit_bytes=60 * 1024 * 1024),
     )(*args)
 
 
@@ -287,7 +287,7 @@
             jax.ShapeDtypeStruct((height, width), jnp.float32),
         ],
         scratch_shapes=[pltpu.VMEM((outs * height, width), jnp.float32)],
-        compiler_params=pltpu.CompilerParams(vmem_limit_bytes=48 * 1024 * 1024),
+        compiler_params=pltpu.CompilerParams(vmem_limit_bytes=60 * 1024 * 1024),
     )(fin, w_in.T, w_mid, w_top, w_out, biases)
 
 

time: 130 us -> 139 us (1.069)
  Pallas kernels: 55.7 us -> 63 us
  other arithmetic: 1.57 us -> 5.42 us
  local copies, waits for them, and re-layouts: 9.12 us -> 6.97 us
    pallas_call x4, Pallas kernels: 42.2 us -> 48.7 us  [run_section(): pl.pallas_call(kernel, grid=(steps,), in_specs=specs, out_specs=out_specs...]
    unnamed x34 -> x28, local copies, waits for them, and re-layouts: 7.11 us -> 2.54 us
    concatenate x3, other arithmetic: 0.13 us -> 3.29 us  [exchange(): jnp.concatenate([ey.reshape(2 * feats, ey.shape[2]), exr, exl], axis=0)]
  transfers between devices with their start and end apart: 9 -> 9, of which waited for: 9 -> 9; matrix products, arithmetic and copies ran while one was open for 0% -> 1% of each run, Pallas kernels for 0% -> 0%
where the time goes in v6:
time: 139 us; the launch traced here: 138 us
  Pallas kernels  63 us (45%)
  waiting for transfers between devices  29.9 us (22%)
  starting transfers between devices  17.4 us (13%)
  blocking collectives  12.8 us (9%)
  local copies, waits for them, and re-layouts  6.97 us (5%)
  other arithmetic  5.42 us (4%)
  between operations  2.49 us (2%)
    pallas_call x4, Pallas kernels, run_section(): pl.pallas_call(kernel, grid=(steps,), in_specs=specs, out_specs=out_specs...  48.7 us
    ppermute x3, waiting for transfers between devices, exchange(): exl = lax.ppermute(ex, 'elem', from_left)  18 us
    pallas_call x1, Pallas kernels, run_mlp(): pl.pallas_call(mlp_kernel, out_shape=[jax.ShapeDtypeStruct((outs * height...  14.3 us
    all_to_all x1, blocking collectives, local(): lax.all_to_all(partial_sums.reshape(devices, 1), ('face', 'elem'), 0, 1,...  12.8 us
    ppermute x3, starting transfers between devices, exchange(): exr = lax.ppermute(ex, 'elem', from_right)  9.36 us
    ppermute x3, waiting for transfers between devices, exchange(): exr = lax.ppermute(ex, 'elem', from_right)  8.04 us
    ppermute x3, starting transfers between devices, exchange(): partner = lax.ppermute(bundle, 'face', [(0, 1), (1, 0)])  5.17 us
    ppermute x3, waiting for transfers between devices, exchange(): partner = lax.ppermute(bundle, 'face', [(0, 1), (1, 0)])  3.89 us
  transfers between devices with their start and end apart: 9, of which 9 were waited for; matrix products, arithmetic and copies ran while one was open for 1% of the time, Pallas kernels for 0%

profile of v6, /device:TPU:1, one launch (start us, length us, event | category | flops | bytes accessed | tf_op | source)
XLA Modules:
  0.0 138.0 jit_solution(6727943225085365534)
XLA Ops:
  0.6 1.5 %broadcast_in_dim.4.refs_1_.refs_2_ = f32[432,128]{1,0:T(8,128)} broadcast(f32[432]{0:T(512)} %param.15), dimensions={0} | broadcast | bytes 222912 | tf_op jit(solution)/shard_map/broadcast_in_dim | solution.py:301
  2.1 1.5 %broadcast_in_dim.5.refs_2_.refs_3_ = f32[432,128]{1,0:T(8,128)} broadcast(f32[432]{0:T(512)} %param.16), dimensions={0} | broadcast | bytes 222912 | tf_op jit(solution)/shard_map/broadcast_in_dim | solution.py:302
  3.6 8.6 %shard_map.157 = (f32[216,128]{1,0:T(8,128)}, f32[2,432,128]{2,1,0:T(8,128)}) custom-call(f32[6912,128]{1,0:T(8,128)} %bitcast.11, f32[432,128]{1,0:T(8,128)} %broadcast_in_dim.4.refs_1_.refs_2_, f32[432,128]{1,0:T(8,128)} %broadcast_in_dim.5.refs_2_.refs_3_, bf16[128,128]{1,0:T(8,128)(2,1)} %constant.11.clone.refs_3_.refs_4_, ...), custom_call_target="tpu_custom_call" | custom-call | tf_op jit(solution)/shard_map/pallas_call | solution.py:202
  12.2 9.2 %collective-permute-start = (f32[216,128]{1,0:T(8,128)}, f32[216,128]{1,0:T(8,128)S(1)}, u32[]{:S(2)}, u32[]{:S(2)}) collective-permute-start(f32[216,128]{1,0:T(8,128)} %get-tuple-element.13), channel_id=1, source_target_pairs={{0,63},{1,0},{2,1},{3,2},{4,3},{5,4},{6,5},{7,6},{8,7},{9,8},{10,9... | collective-permute-start | bytes 331784 | tf_op jit(solution)/shard_map/ppermute | solution.py:218
  21.5 2.1 %collective-permute-done.refs_5_ = f32[216,128]{1,0:T(8,128)S(1)} collective-permute-done((f32[216,128]{1,0:T(8,128)}, f32[216,128]{1,0:T(8,128)S(1)}, u32[]{:S(2)}, u32[]{:S(2)}) %collective-permute-start) | collective-permute-done | bytes 110624 | tf_op jit(solution)/shard_map/ppermute | solution.py:218
  23.5 7.2 %collective-permute-done.1.refs_6_ = f32[216,128]{1,0:T(8,128)S(1)} collective-permute-done((f32[216,128]{1,0:T(8,128)}, f32[216,128]{1,0:T(8,128)S(1)}, u32[]{:S(2)}, u32[]{:S(2)}) %collective-permute-start.1) | collective-permute-done | bytes 110624 | tf_op jit(solution)/shard_map/ppermute | solution.py:219
  31.8 2.2 %collective-permute-start.2 = (f32[1296,128]{1,0:T(8,128)S(1)}, f32[1296,128]{1,0:T(8,128)S(1)}, u32[]{:S(2)}, u32[]{:S(2)}) collective-permute-start(f32[1296,128]{1,0:T(8,128)S(1)} %pad_maximum_fusion), channel_id=1, source_target_pairs={{0,64},{64,0},{1,65},{65,1},{2,66},{66,2},{3,67},{67,3},{4,68},{68... | collective-permute-start | bytes 1990664 | tf_op jit(solution)/shard_map/ppermute | solution.py:222
  34.0 1.7 %collective-permute-done.2.refs_7_.refs_8_.refs_9_.refs_10_ = f32[1296,128]{1,0:T(8,128)S(1)} collective-permute-done((f32[1296,128]{1,0:T(8,128)S(1)}, f32[1296,128]{1,0:T(8,128)S(1)}, u32[]{:S(2)}, u32[]{:S(2)}) %collective-permute-start.2) | collective-permute-done | bytes 663584 | tf_op jit(solution)/shard_map/ppermute | solution.py:222
  36.6 13.9 %shard_map.158 = (f32[6912,128]{1,0:T(8,128)}, f32[216,128]{1,0:T(8,128)}, f32[2,432,128]{2,1,0:T(8,128)}) custom-call(f32[6912,128]{1,0:T(8,128)} %bitcast.12, f32[432,128]{1,0:T(8,128)} %broadcast_in_dim.4.refs_1_.refs_2_, f32[432,128]{1,0:T(8,128)} %broadcast_in_dim.5.refs_2_.refs_3_, bf16[128,128]{1,0:T(8,128)(2,1)} %constant.11.clone.refs_3_.refs_4_, ...), custom_call_target="tpu_custom_call" | custom-call | tf_op jit(solution)/shard_map/pallas_call | solution.py:202
  50.6 1.5 %collective-permute-start.4 = (f32[216,128]{1,0:T(8,128)}, f32[216,128]{1,0:T(8,128)S(1)}, u32[]{:S(2)}, u32[]{:S(2)}) collective-permute-start(f32[216,128]{1,0:T(8,128)} %get-tuple-element.16), channel_id=1, source_target_pairs={{0,1},{1,2},{2,3},{3,4},{4,5},{5,6},{6,7},{7,8},{8,9},{9,10},{10,1... | collective-permute-start | bytes 331784 | tf_op jit(solution)/shard_map/ppermute | solution.py:219
  52.0 3.0 %collective-permute-done.3.refs_6_ = f32[216,128]{1,0:T(8,128)S(1)} collective-permute-done((f32[216,128]{1,0:T(8,128)}, f32[216,128]{1,0:T(8,128)S(1)}, u32[]{:S(2)}, u32[]{:S(2)}) %collective-permute-start.3) | collective-permute-done | bytes 110624 | tf_op jit(solution)/shard_map/ppermute | solution.py:218
  55.0 5.5 %collective-permute-done.4.refs_7_ = f32[216,128]{1,0:T(8,128)S(1)} collective-permute-done((f32[216,128]{1,0:T(8,128)}, f32[216,128]{1,0:T(8,128)S(1)}, u32[]{:S(2)}, u32[]{:S(2)}) %collective-permute-start.4) | collective-permute-done | bytes 110624 | tf_op jit(solution)/shard_map/ppermute | solution.py:219
  61.6 1.3 collective-permute-start.5
  63.0 1.7 %collective-permute-done.5.refs_8_.refs_9_.refs_10_.refs_11_ = f32[1296,128]{1,0:T(8,128)S(1)} collective-permute-done((f32[1296,128]{1,0:T(8,128)S(1)}, f32[1296,128]{1,0:T(8,128)S(1)}, u32[]{:S(2)}, u32[]{:S(2)}) %collective-permute-start.5) | collective-permute-done | bytes 663584 | tf_op jit(solution)/shard_map/ppermute | solution.py:222
  65.5 14.8 %shard_map.159 = (f32[6912,128]{1,0:T(8,128)}, f32[216,128]{1,0:T(8,128)}, f32[2,432,128]{2,1,0:T(8,128)}) custom-call(f32[6912,128]{1,0:T(8,128)} %bitcast.13, f32[6912,128]{1,0:T(8,128)} %get-tuple-element.15.refs_1_, f32[432,128]{1,0:T(8,128)} %broadcast_in_dim.4.refs_1_.refs_2_, f32[432,128]{1,0:T(8,128)} %broadcast_in_dim.5.refs_2_.refs_3_, ...), custom_call_target="tpu_custom_call" | custom-call | tf_op jit(solution)/shard_map/pallas_call | solution.py:202
  80.4 1.5 %collective-permute-start.7 = (f32[216,128]{1,0:T(8,128)}, f32[216,128]{1,0:T(8,128)S(1)}, u32[]{:S(2)}, u32[]{:S(2)}) collective-permute-start(f32[216,128]{1,0:T(8,128)} %get-tuple-element.19), channel_id=1, source_target_pairs={{0,1},{1,2},{2,3},{3,4},{4,5},{5,6},{6,7},{7,8},{8,9},{9,10},{10,1... | collective-permute-start | bytes 331784 | tf_op jit(solution)/shard_map/ppermute | solution.py:219
  81.8 3.0 %collective-permute-done.6.refs_6_ = f32[216,128]{1,0:T(8,128)S(1)} collective-permute-done((f32[216,128]{1,0:T(8,128)}, f32[216,128]{1,0:T(8,128)S(1)}, u32[]{:S(2)}, u32[]{:S(2)}) %collective-permute-start.6) | collective-permute-done | bytes 110624 | tf_op jit(solution)/shard_map/ppermute | solution.py:218
  84.8 5.3 %collective-permute-done.7.refs_7_ = f32[216,128]{1,0:T(8,128)S(1)} collective-permute-done((f32[216,128]{1,0:T(8,128)}, f32[216,128]{1,0:T(8,128)S(1)}, u32[]{:S(2)}, u32[]{:S(2)}) %collective-permute-start.7) | collective-permute-done | bytes 110624 | tf_op jit(solution)/shard_map/ppermute | solution.py:219
  91.3 1.7 %collective-permute-start.8 = (f32[1296,128]{1,0:T(8,128)S(1)}, f32[1296,128]{1,0:T(8,128)S(1)}, u32[]{:S(2)}, u32[]{:S(2)}) collective-permute-start(f32[1296,128]{1,0:T(8,128)S(1)} %pad_maximum_fusion.2), channel_id=1, source_target_pairs={{0,64},{64,0},{1,65},{65,1},{2,66},{66,2},{3,67},{67,3},{4,68},{68... | collective-permute-start | bytes 1990664 | tf_op jit(solution)/shard_map/ppermute | solution.py:222
  93.0 1.3 reshape.48.b_ref
  95.5 11.4 %shard_map.160.fin_ref = f32[6912,128]{1,0:T(8,128)} custom-call(f32[6912,128]{1,0:T(8,128)} %bitcast.14, f32[6912,128]{1,0:T(8,128)} %get-tuple-element.18.refs_1_, f32[432,128]{1,0:T(8,128)} %broadcast_in_dim.4.refs_1_.refs_2_, f32[432,128]{1,0:T(8,128)} %broadcast_in_dim.5.refs_2_.refs_3_, bf16[128,128]{1,0:T(8,128)(2,1)} %constant.11.clone.refs_3_.refs_4_, ...), custom_call_target="tpu_custom_call" | custom-call | tf_op jit(solution)/shard_map/pallas_call | solution.py:202
  106.9 14.3 %shard_map.161 = (bf16[5760,128]{1,0:T(8,128)(2,1)}, f32[16,128]{1,0:T(8,128)}) custom-call(f32[6912,128]{1,0:T(8,128)} %shard_map.160.fin_ref, bf16[432,512]{1,0:T(8,128)(2,1)} %bitcast.19, bf16[512,512]{1,0:T(8,128)(2,1)} %w_mid_ref.1, bf16[512,512]{1,0:T(8,128)(2,1)} %w_top_ref.1, bf16[360,512]{1,0:T(8,128)(2,1)} %w_out_ref.1, f32[1896,1]{1,0:T(8,128)} %reshape.48.b_ref), custom_call_target="tpu_custom_call" | custom-call | tf_op jit(solution)/shard_map/pallas_call | solution.py:283
  121.2 1.4 %select_reduce_fusion = f32[128]{0:T(128)S(1)} fusion(f32[2048]{0:T(1024)} %bitcast.21, s32[2048]{0:T(1024)S(1)} %bitcast.20), kind=kLoop, calls=%fused_computation | loop fusion | flops 786304 | bytes 16896 | tf_op jit(solution)/shard_map/reduce_sum | solution.py:324
  122.7 12.8 %all_to_all.13 = f32[128,1,1]{2,1,0:T(1,128)S(1)} all-to-all(f32[128,1,1]{2,1,0:T(1,128)S(1)} %copy.21), channel_id=1, replica_groups=mesh['face'=2,'elem'=64] {'face','elem'}, dimensions={0} | all-to-all | bytes 1024 | tf_op jit(solution)/shard_map/all_to_all | solution.py:325
  (38 shorter events, 7.3 us)
Async XLA Ops:
  12.2 11.3 %collective-permute-start = (f32[216,128]{1,0:T(8,128)}, f32[216,128]{1,0:T(8,128)S(1)}, u32[]{:S(2)}, u32[]{:S(2)}) collective-permute-start(f32[216,128]{1,0:T(8,128)} %get-tuple-element.13), channel_id=1, source_target_pairs={{0,63},{1,0},{2,1},{3,2},{4,3},{5,4},{6,5},{7,6},{8,7},{9,8},{10,9... | collective-permute-start | bytes 331784 | tf_op jit(solution)/shard_map/ppermute | solution.py:218
  21.5 9.2 %collective-permute-start.1 = (f32[216,128]{1,0:T(8,128)}, f32[216,128]{1,0:T(8,128)S(1)}, u32[]{:S(2)}, u32[]{:S(2)}) collective-permute-start(f32[216,128]{1,0:T(8,128)} %get-tuple-element.13), channel_id=1, source_target_pairs={{0,1},{1,2},{2,3},{3,4},{4,5},{5,6},{6,7},{7,8},{8,9},{9,10},{10,1... | collective-permute-start | bytes 331784 | tf_op jit(solution)/shard_map/ppermute | solution.py:219
  23.5 12.2 %copy-start.7 = (f32[216,128]{1,0:T(8,128)}, f32[216,128]{1,0:T(8,128)S(1)}, u32[]{:S(2)}) copy-start(f32[216,128]{1,0:T(8,128)S(1)} %collective-permute-done.refs_5_) | copy-start | bytes 331780
  30.7 5.0 %copy-start.8 = (f32[216,128]{1,0:T(8,128)}, f32[216,128]{1,0:T(8,128)S(1)}, u32[]{:S(2)}) copy-start(f32[216,128]{1,0:T(8,128)S(1)} %collective-permute-done.1.refs_6_) | copy-start | bytes 331780
  31.8 3.9 %collective-permute-start.2 = (f32[1296,128]{1,0:T(8,128)S(1)}, f32[1296,128]{1,0:T(8,128)S(1)}, u32[]{:S(2)}, u32[]{:S(2)}) collective-permute-start(f32[1296,128]{1,0:T(8,128)S(1)} %pad_maximum_fusion), channel_id=1, source_target_pairs={{0,64},{64,0},{1,65},{65,1},{2,66},{66,2},{3,67},{67,3},{4,68},{68... | collective-permute-start | bytes 1990664 | tf_op jit(solution)/shard_map/ppermute | solution.py:222
  35.7 0.8 copy-start.2
  50.5 4.5 %collective-permute-start.3 = (f32[216,128]{1,0:T(8,128)}, f32[216,128]{1,0:T(8,128)S(1)}, u32[]{:S(2)}, u32[]{:S(2)}) collective-permute-start(f32[216,128]{1,0:T(8,128)} %get-tuple-element.16), channel_id=1, source_target_pairs={{0,63},{1,0},{2,1},{3,2},{4,3},{5,4},{6,5},{7,6},{8,7},{9,8},{10,9... | collective-permute-start | bytes 331784 | tf_op jit(solution)/shard_map/ppermute | solution.py:218
  50.6 9.9 %collective-permute-start.4 = (f32[216,128]{1,0:T(8,128)}, f32[216,128]{1,0:T(8,128)S(1)}, u32[]{:S(2)}, u32[]{:S(2)}) collective-permute-start(f32[216,128]{1,0:T(8,128)} %get-tuple-element.16), channel_id=1, source_target_pairs={{0,1},{1,2},{2,3},{3,4},{4,5},{5,6},{6,7},{7,8},{8,9},{9,10},{10,1... | collective-permute-start | bytes 331784 | tf_op jit(solution)/shard_map/ppermute | solution.py:219
  55.0 9.7 %copy-start.5 = (f32[216,128]{1,0:T(8,128)}, f32[216,128]{1,0:T(8,128)S(1)}, u32[]{:S(2)}) copy-start(f32[216,128]{1,0:T(8,128)S(1)} %collective-permute-done.3.refs_6_) | copy-start | bytes 331780
  60.5 4.2 %copy-start.6 = (f32[216,128]{1,0:T(8,128)}, f32[216,128]{1,0:T(8,128)S(1)}, u32[]{:S(2)}) copy-start(f32[216,128]{1,0:T(8,128)S(1)} %collective-permute-done.4.refs_7_) | copy-start | bytes 331780
  61.6 3.1 %collective-permute-start.5 = (f32[1296,128]{1,0:T(8,128)S(1)}, f32[1296,128]{1,0:T(8,128)S(1)}, u32[]{:S(2)}, u32[]{:S(2)}) collective-permute-start(f32[1296,128]{1,0:T(8,128)S(1)} %pad_maximum_fusion.1), channel_id=1, source_target_pairs={{0,64},{64,0},{1,65},{65,1},{2,66},{66,2},{3,67},{67,3},{4,68},{68... | collective-permute-start | bytes 1990664 | tf_op jit(solution)/shard_map/ppermute | solution.py:222
  64.7 0.8 copy-start.1
  65.5 27.4 %copy-start.10 = (f32[360]{0:T(512)S(1)}, f32[360]{0:T(512)}, u32[]{:S(2)}) copy-start(f32[360]{0:T(512)} %param.24) | copy-start | bytes 4324
  65.5 27.4 %copy-start.11 = (f32[512]{0:T(512)S(1)}, f32[512]{0:T(512)}, u32[]{:S(2)}) copy-start(f32[512]{0:T(512)} %param.22) | copy-start | bytes 6148
  65.5 27.4 %copy-start.12 = (f32[512]{0:T(512)S(1)}, f32[512]{0:T(512)}, u32[]{:S(2)}) copy-start(f32[512]{0:T(512)} %param.20) | copy-start | bytes 6148
  65.5 27.4 %copy-start.13 = (f32[512]{0:T(512)S(1)}, f32[512]{0:T(512)}, u32[]{:S(2)}) copy-start(f32[512]{0:T(512)} %param.18) | copy-start | bytes 6148
  80.3 4.5 %collective-permute-start.6 = (f32[216,128]{1,0:T(8,128)}, f32[216,128]{1,0:T(8,128)S(1)}, u32[]{:S(2)}, u32[]{:S(2)}) collective-permute-start(f32[216,128]{1,0:T(8,128)} %get-tuple-element.19), channel_id=1, source_target_pairs={{0,63},{1,0},{2,1},{3,2},{4,3},{5,4},{6,5},{7,6},{8,7},{9,8},{10,9... | collective-permute-start | bytes 331784 | tf_op jit(solution)/shard_map/ppermute | solution.py:218
  80.4 9.8 %collective-permute-start.7 = (f32[216,128]{1,0:T(8,128)}, f32[216,128]{1,0:T(8,128)S(1)}, u32[]{:S(2)}, u32[]{:S(2)}) collective-permute-start(f32[216,128]{1,0:T(8,128)} %get-tuple-element.19), channel_id=1, source_target_pairs={{0,1},{1,2},{2,3},{3,4},{4,5},{5,6},{6,7},{7,8},{8,9},{9,10},{10,1... | collective-permute-start | bytes 331784 | tf_op jit(solution)/shard_map/ppermute | solution.py:219
  84.8 9.8 %copy-start.3 = (f32[216,128]{1,0:T(8,128)}, f32[216,128]{1,0:T(8,128)S(1)}, u32[]{:S(2)}) copy-start(f32[216,128]{1,0:T(8,128)S(1)} %collective-permute-done.6.refs_6_) | copy-start | bytes 331780
  90.2 4.5 %copy-start.4 = (f32[216,128]{1,0:T(8,128)}, f32[216,128]{1,0:T(8,128)S(1)}, u32[]{:S(2)}) copy-start(f32[216,128]{1,0:T(8,128)S(1)} %collective-permute-done.7.refs_7_) | copy-start | bytes 331780
  91.3 3.4 %collective-permute-start.8 = (f32[1296,128]{1,0:T(8,128)S(1)}, f32[1296,128]{1,0:T(8,128)S(1)}, u32[]{:S(2)}, u32[]{:S(2)}) collective-permute-start(f32[1296,128]{1,0:T(8,128)S(1)} %pad_maximum_fusion.2), channel_id=1, source_target_pairs={{0,64},{64,0},{1,65},{65,1},{2,66},{66,2},{3,67},{67,3},{4,68},{68... | collective-permute-start | bytes 1990664 | tf_op jit(solution)/shard_map/ppermute | solution.py:222
  94.7 0.8 copy-start
  106.9 14.3 %copy-start.9 = (s32[1,1,2048,1]{2,3,1,0:T(1,128)S(1)}, s32[1,1,2048,1]{2,3,1,0:T(1,128)}, u32[]{:S(2)}) copy-start(s32[1,1,2048,1]{2,3,1,0:T(1,128)} %param.25) | copy-start | bytes 24580

commit v7 on v6

--- a/solution.py
+++ b/solution.py
@@ -205,7 +205,7 @@
         in_specs=specs,
         out_specs=out_specs,
         out_shape=out_shape,
-        compiler_params=pltpu.CompilerParams(vmem_limit_bytes=60 * 1024 * 1024),
+        compiler_params=pltpu.CompilerParams(vmem_limit_bytes=16 * 1024 * 1024),
     )(*args)
 
 
@@ -287,7 +287,7 @@
             jax.ShapeDtypeStruct((height, width), jnp.float32),
         ],
         scratch_shapes=[pltpu.VMEM((outs * height, width), jnp.float32)],
-        compiler_params=pltpu.CompilerParams(vmem_limit_bytes=60 * 1024 * 1024),
+        compiler_params=pltpu.CompilerParams(vmem_limit_bytes=16 * 1024 * 1024),
     )(fin, w_in.T, w_mid, w_top, w_out, biases)
 
 

time: 139 us -> 122 us (0.88)
  Pallas kernels: 63 us -> 48.9 us
  other arithmetic: 5.42 us -> 1.57 us
    pallas_call x4, Pallas kernels: 48.7 us -> 37.3 us  [run_section(): pl.pallas_call(kernel, grid=(steps,), in_specs=specs, out_specs=out_specs...]
    concatenate x3, other arithmetic: 3.29 us -> 0.13 us  [exchange(): jnp.concatenate([ey.reshape(2 * feats, ey.shape[2]), exr, exl], axis=0)]
    unnamed x28 -> x26, local copies, waits for them, and re-layouts: 2.54 us -> 5.54 us
    pallas_call x1, Pallas kernels: 14.3 us -> 11.5 us  [run_mlp(): pl.pallas_call(mlp_kernel, out_shape=[jax.ShapeDtypeStruct((outs * height...]
  transfers between devices with their start and end apart: 9 -> 9, of which waited for: 9 -> 9; matrix products, arithmetic and copies ran while one was open for 1% -> 0% of each run, Pallas kernels for 0% -> 0%
where the time goes in v7:
time: 122 us; the launch traced here: 121 us
  Pallas kernels  48.9 us (40%)
  waiting for transfers between devices  30.3 us (25%)
  starting transfers between devices  17.4 us (14%)
  blocking collectives  12.8 us (10%)
  local copies, waits for them, and re-layouts  7.55 us (6%)
  between operations  2.52 us (2%)
  other arithmetic  1.57 us (1%)
    pallas_call x4, Pallas kernels, run_section(): pl.pallas_call(kernel, grid=(steps,), in_specs=specs, out_specs=out_specs...  37.3 us
    ppermute x3, waiting for transfers between devices, exchange(): exl = lax.ppermute(ex, 'elem', from_left)  18.2 us
    all_to_all x1, blocking collectives, local(): lax.all_to_all(partial_sums.reshape(devices, 1), ('face', 'elem'), 0, 1,...  12.8 us
    pallas_call x1, Pallas kernels, run_mlp(): pl.pallas_call(mlp_kernel, out_shape=[jax.ShapeDtypeStruct((outs * height...  11.5 us
    ppermute x3, starting transfers between devices, exchange(): exr = lax.ppermute(ex, 'elem', from_right)  9.41 us
    ppermute x3, waiting for transfers between devices, exchange(): exr = lax.ppermute(ex, 'elem', from_right)  7.3 us
    unnamed x26, local copies, waits for them, and re-layouts  5.54 us
    ppermute x3, starting transfers between devices, exchange(): partner = lax.ppermute(bundle, 'face', [(0, 1), (1, 0)])  5.12 us
  transfers between devices with their start and end apart: 9, of which 9 were waited for; matrix products, arithmetic and copies ran while one was open for 0% of the time, Pallas kernels for 0%

profile of v7, /device:TPU:1, one launch (start us, length us, event | category | flops | bytes accessed | tf_op | source)
XLA Modules:
  0.0 121.1 jit_solution(1262841889202020309)
XLA Ops:
  1.4 0.8 broadcast_in_dim.5.refs_2_.refs_3_
  2.2 2.0 %copy-done = f32[432,16,128]{2,1,0:T(8,128)S(1)} copy-done((f32[432,16,128]{2,1,0:T(8,128)S(1)}, f32[432,16,128]{2,1,0:T(8,128)}, u32[]{:S(2)}) %copy-start) | copy-done | bytes 3538968
  5.8 4.9 %shard_map.157 = (f32[216,128]{1,0:T(8,128)S(1)}, f32[2,432,128]{2,1,0:T(8,128)S(1)}) custom-call(f32[6912,128]{1,0:T(8,128)S(1)} %bitcast.11, f32[432,128]{1,0:T(8,128)S(1)} %broadcast_in_dim.4.refs_1_.refs_2_, f32[432,128]{1,0:T(8,128)S(1)} %broadcast_in_dim.5.refs_2_.refs_3_, bf16[128,128]{1,0:T(8,128)(2,1)S(1)} %copy-done.2, bf16[128,128]{1,0:T(8,128)(2,1)S(1)} %copy-done.3), custom_call_target="tpu_custom_call" | custom-call | tf_op jit(solution)/shard_map/pallas_call | solution.py:202
  10.7 9.3 %collective-permute-start = (f32[216,128]{1,0:T(8,128)S(1)}, f32[216,128]{1,0:T(8,128)S(1)}, u32[]{:S(2)}, u32[]{:S(2)}) collective-permute-start(f32[216,128]{1,0:T(8,128)S(1)} %get-tuple-element.13), channel_id=1, source_target_pairs={{0,63},{1,0},{2,1},{3,2},{4,3},{5,4},{6,5},{7,6},{8,7},{9,8},{10,9... | collective-permute-start | bytes 331784 | tf_op jit(solution)/shard_map/ppermute | solution.py:218
  20.0 1.8 %collective-permute-done.refs_5_ = f32[216,128]{1,0:T(8,128)S(1)} collective-permute-done((f32[216,128]{1,0:T(8,128)S(1)}, f32[216,128]{1,0:T(8,128)S(1)}, u32[]{:S(2)}, u32[]{:S(2)}) %collective-permute-start) | collective-permute-done | bytes 110624 | tf_op jit(solution)/shard_map/ppermute | solution.py:218
  21.7 7.3 %collective-permute-done.1.refs_6_ = f32[216,128]{1,0:T(8,128)S(1)} collective-permute-done((f32[216,128]{1,0:T(8,128)S(1)}, f32[216,128]{1,0:T(8,128)S(1)}, u32[]{:S(2)}, u32[]{:S(2)}) %collective-permute-start.1) | collective-permute-done | bytes 110624 | tf_op jit(solution)/shard_map/ppermute | solution.py:219
  29.0 2.2 %collective-permute-start.2 = (f32[1296,128]{1,0:T(8,128)S(1)}, f32[1296,128]{1,0:T(8,128)S(1)}, u32[]{:S(2)}, u32[]{:S(2)}) collective-permute-start(f32[1296,128]{1,0:T(8,128)S(1)} %pad_maximum_fusion), channel_id=1, source_target_pairs={{0,64},{64,0},{1,65},{65,1},{2,66},{66,2},{3,67},{67,3},{4,68},{68... | collective-permute-start | bytes 1990664 | tf_op jit(solution)/shard_map/ppermute | solution.py:222
  31.2 1.7 %collective-permute-done.2.refs_7_.refs_8_.refs_9_.refs_10_ = f32[1296,128]{1,0:T(8,128)S(1)} collective-permute-done((f32[1296,128]{1,0:T(8,128)S(1)}, f32[1296,128]{1,0:T(8,128)S(1)}, u32[]{:S(2)}, u32[]{:S(2)}) %collective-permute-start.2) | collective-permute-done | bytes 663584 | tf_op jit(solution)/shard_map/ppermute | solution.py:222
  33.0 11.8 %shard_map.158 = (f32[6912,128]{1,0:T(8,128)S(1)}, f32[216,128]{1,0:T(8,128)S(1)}, f32[2,432,128]{2,1,0:T(8,128)S(1)}) custom-call(f32[6912,128]{1,0:T(8,128)S(1)} %bitcast.12, f32[432,128]{1,0:T(8,128)S(1)} %broadcast_in_dim.4.refs_1_.refs_2_, f32[432,128]{1,0:T(8,128)S(1)} %broadcast_in_dim.5.refs_2_.refs_3_, bf16[128,128]{1,0:T(8,128)(2,1)S(1)} %copy-done.2, ...), custom_call_target="tpu_custom_call" | custom-call | tf_op jit(solution)/shard_map/pallas_call | solution.py:202
  44.8 1.5 %collective-permute-start.4 = (f32[216,128]{1,0:T(8,128)S(1)}, f32[216,128]{1,0:T(8,128)S(1)}, u32[]{:S(2)}, u32[]{:S(2)}) collective-permute-start(f32[216,128]{1,0:T(8,128)S(1)} %get-tuple-element.16), channel_id=1, source_target_pairs={{0,1},{1,2},{2,3},{3,4},{4,5},{5,6},{6,7},{7,8},{8,9},{9,10},{10,1... | collective-permute-start | bytes 331784 | tf_op jit(solution)/shard_map/ppermute | solution.py:219
  46.3 2.8 %collective-permute-done.3.refs_6_ = f32[216,128]{1,0:T(8,128)S(1)} collective-permute-done((f32[216,128]{1,0:T(8,128)S(1)}, f32[216,128]{1,0:T(8,128)S(1)}, u32[]{:S(2)}, u32[]{:S(2)}) %collective-permute-start.3) | collective-permute-done | bytes 110624 | tf_op jit(solution)/shard_map/ppermute | solution.py:218
  49.1 5.5 %collective-permute-done.4.refs_7_ = f32[216,128]{1,0:T(8,128)S(1)} collective-permute-done((f32[216,128]{1,0:T(8,128)S(1)}, f32[216,128]{1,0:T(8,128)S(1)}, u32[]{:S(2)}, u32[]{:S(2)}) %collective-permute-start.4) | collective-permute-done | bytes 110624 | tf_op jit(solution)/shard_map/ppermute | solution.py:219
  54.6 1.3 %collective-permute-start.5 = (f32[1296,128]{1,0:T(8,128)S(1)}, f32[1296,128]{1,0:T(8,128)S(1)}, u32[]{:S(2)}, u32[]{:S(2)}) collective-permute-start(f32[1296,128]{1,0:T(8,128)S(1)} %pad_maximum_fusion.1), channel_id=1, source_target_pairs={{0,64},{64,0},{1,65},{65,1},{2,66},{66,2},{3,67},{67,3},{4,68},{68... | collective-permute-start | bytes 1990664 | tf_op jit(solution)/shard_map/ppermute | solution.py:222
  55.9 1.7 %collective-permute-done.5.refs_8_.refs_9_.refs_10_.refs_11_ = f32[1296,128]{1,0:T(8,128)S(1)} collective-permute-done((f32[1296,128]{1,0:T(8,128)S(1)}, f32[1296,128]{1,0:T(8,128)S(1)}, u32[]{:S(2)}, u32[]{:S(2)}) %collective-permute-start.5) | collective-permute-done | bytes 663584 | tf_op jit(solution)/shard_map/ppermute | solution.py:222
  57.7 12.3 %shard_map.159 = (f32[6912,128]{1,0:T(8,128)S(1)}, f32[216,128]{1,0:T(8,128)S(1)}, f32[2,432,128]{2,1,0:T(8,128)S(1)}) custom-call(f32[6912,128]{1,0:T(8,128)S(1)} %bitcast.13, f32[6912,128]{1,0:T(8,128)S(1)} %get-tuple-element.15.refs_1_, f32[432,128]{1,0:T(8,128)S(1)} %broadcast_in_dim.4.refs_1_.refs_2_, f32[432,128]{1,0:T(8,128)S(1)} %broadcast_in_dim.5.refs_2_.refs_3_, ...), custom_call_target="tpu_custom_call" | custom-call | tf_op jit(solution)/shard_map/pallas_call | solution.py:202
  70.1 1.5 %collective-permute-start.7 = (f32[216,128]{1,0:T(8,128)S(1)}, f32[216,128]{1,0:T(8,128)S(1)}, u32[]{:S(2)}, u32[]{:S(2)}) collective-permute-start(f32[216,128]{1,0:T(8,128)S(1)} %get-tuple-element.19), channel_id=1, source_target_pairs={{0,1},{1,2},{2,3},{3,4},{4,5},{5,6},{6,7},{7,8},{8,9},{9,10},{10,1... | collective-permute-start | bytes 331784 | tf_op jit(solution)/shard_map/ppermute | solution.py:219
  71.6 2.8 %collective-permute-done.6.refs_6_ = f32[216,128]{1,0:T(8,128)S(1)} collective-permute-done((f32[216,128]{1,0:T(8,128)S(1)}, f32[216,128]{1,0:T(8,128)S(1)}, u32[]{:S(2)}, u32[]{:S(2)}) %collective-permute-start.6) | collective-permute-done | bytes 110624 | tf_op jit(solution)/shard_map/ppermute | solution.py:218
  74.3 5.4 %collective-permute-done.7.refs_7_ = f32[216,128]{1,0:T(8,128)S(1)} collective-permute-done((f32[216,128]{1,0:T(8,128)S(1)}, f32[216,128]{1,0:T(8,128)S(1)}, u32[]{:S(2)}, u32[]{:S(2)}) %collective-permute-start.7) | collective-permute-done | bytes 110624 | tf_op jit(solution)/shard_map/ppermute | solution.py:219
  79.8 1.6 %collective-permute-start.8 = (f32[1296,128]{1,0:T(8,128)S(1)}, f32[1296,128]{1,0:T(8,128)S(1)}, u32[]{:S(2)}, u32[]{:S(2)}) collective-permute-start(f32[1296,128]{1,0:T(8,128)S(1)} %pad_maximum_fusion.2), channel_id=1, source_target_pairs={{0,64},{64,0},{1,65},{65,1},{2,66},{66,2},{3,67},{67,3},{4,68},{68... | collective-permute-start | bytes 1990664 | tf_op jit(solution)/shard_map/ppermute | solution.py:222
  81.7 1.4 %collective-permute-done.8.refs_8_.refs_9_.refs_10_.refs_11_ = f32[1296,128]{1,0:T(8,128)S(1)} collective-permute-done((f32[1296,128]{1,0:T(8,128)S(1)}, f32[1296,128]{1,0:T(8,128)S(1)}, u32[]{:S(2)}, u32[]{:S(2)}) %collective-permute-start.8) | collective-permute-done | bytes 663584 | tf_op jit(solution)/shard_map/ppermute | solution.py:222
  83.1 8.2 %shard_map.160.fin_ref = f32[6912,128]{1,0:T(8,128)} custom-call(f32[6912,128]{1,0:T(8,128)S(1)} %bitcast.14, f32[6912,128]{1,0:T(8,128)S(1)} %get-tuple-element.18.refs_1_, f32[432,128]{1,0:T(8,128)S(1)} %broadcast_in_dim.4.refs_1_.refs_2_, f32[432,128]{1,0:T(8,128)S(1)} %broadcast_in_dim.5.refs_2_.refs_3_, bf16[128,128]{1,0:T(8,128)(2,1)S(1)} %copy-done.2, ...), custom_call_target="tpu_custom_call" | custom-call | tf_op jit(solution)/shard_map/pallas_call | solution.py:202
  91.4 2.0 %copy-done.1 = f32[6912,128]{1,0:T(8,128)S(1)} copy-done((f32[6912,128]{1,0:T(8,128)S(1)}, f32[6912,128]{1,0:T(8,128)}, u32[]{:S(2)}) %copy-start.1) | copy-done | bytes 3538968
  93.4 11.5 %shard_map.161 = (bf16[5760,128]{1,0:T(8,128)(2,1)}, f32[16,128]{1,0:T(8,128)S(1)}) custom-call(f32[6912,128]{1,0:T(8,128)S(1)} %copy-done.1, bf16[432,512]{1,0:T(8,128)(2,1)S(1)} %bitcast.19, bf16[512,512]{1,0:T(8,128)(2,1)S(1)} %copy-done.4, bf16[512,512]{1,0:T(8,128)(2,1)S(1)} %copy-done.5, bf16[360,512]{1,0:T(8,128)(2,1)S(1)} %copy-done.7, ...), custom_call_target="tpu_custom_call" | custom-call | tf_op jit(solution)/shard_map/pallas_call | solution.py:283
  105.8 12.8 %all_to_all.13 = f32[128,1,1]{2,1,0:T(1,128)S(1)} all-to-all(f32[128,1,1]{2,1,0:T(1,128)S(1)} %copy.21), channel_id=1, replica_groups=mesh['face'=2,'elem'=64] {'face','elem'}, dimensions={0} | all-to-all | bytes 1024 | tf_op jit(solution)/shard_map/all_to_all | solution.py:325
  (36 shorter events, 4.5 us)
Async XLA Ops:
  2.2 2.0 %copy-start = (f32[432,16,128]{2,1,0:T(8,128)S(1)}, f32[432,16,128]{2,1,0:T(8,128)}, u32[]{:S(2)}) copy-start(f32[432,16,128]{2,1,0:T(8,128)} %param.14) | copy-start | bytes 10616836
  4.2 0.8 copy-start.2
  5.0 0.8 copy-start.3
  10.7 11.0 %collective-permute-start = (f32[216,128]{1,0:T(8,128)S(1)}, f32[216,128]{1,0:T(8,128)S(1)}, u32[]{:S(2)}, u32[]{:S(2)}) collective-permute-start(f32[216,128]{1,0:T(8,128)S(1)} %get-tuple-element.13), channel_id=1, source_target_pairs={{0,63},{1,0},{2,1},{3,2},{4,3},{5,4},{6,5},{7,6},{8,7},{9,8},{10,9... | collective-permute-start | bytes 331784 | tf_op jit(solution)/shard_map/ppermute | solution.py:218
  20.0 9.0 %collective-permute-start.1 = (f32[216,128]{1,0:T(8,128)S(1)}, f32[216,128]{1,0:T(8,128)S(1)}, u32[]{:S(2)}, u32[]{:S(2)}) collective-permute-start(f32[216,128]{1,0:T(8,128)S(1)} %get-tuple-element.13), channel_id=1, source_target_pairs={{0,1},{1,2},{2,3},{3,4},{4,5},{5,6},{6,7},{7,8},{8,9},{9,10},{10,1... | collective-permute-start | bytes 331784 | tf_op jit(solution)/shard_map/ppermute | solution.py:219
  29.0 3.9 %collective-permute-start.2 = (f32[1296,128]{1,0:T(8,128)S(1)}, f32[1296,128]{1,0:T(8,128)S(1)}, u32[]{:S(2)}, u32[]{:S(2)}) collective-permute-start(f32[1296,128]{1,0:T(8,128)S(1)} %pad_maximum_fusion), channel_id=1, source_target_pairs={{0,64},{64,0},{1,65},{65,1},{2,66},{66,2},{3,67},{67,3},{4,68},{68... | collective-permute-start | bytes 1990664 | tf_op jit(solution)/shard_map/ppermute | solution.py:222
  44.8 4.3 %collective-permute-start.3 = (f32[216,128]{1,0:T(8,128)S(1)}, f32[216,128]{1,0:T(8,128)S(1)}, u32[]{:S(2)}, u32[]{:S(2)}) collective-permute-start(f32[216,128]{1,0:T(8,128)S(1)} %get-tuple-element.16), channel_id=1, source_target_pairs={{0,63},{1,0},{2,1},{3,2},{4,3},{5,4},{6,5},{7,6},{8,7},{9,8},{10,9... | collective-permute-start | bytes 331784 | tf_op jit(solution)/shard_map/ppermute | solution.py:218
  44.8 9.7 %collective-permute-start.4 = (f32[216,128]{1,0:T(8,128)S(1)}, f32[216,128]{1,0:T(8,128)S(1)}, u32[]{:S(2)}, u32[]{:S(2)}) collective-permute-start(f32[216,128]{1,0:T(8,128)S(1)} %get-tuple-element.16), channel_id=1, source_target_pairs={{0,1},{1,2},{2,3},{3,4},{4,5},{5,6},{6,7},{7,8},{8,9},{9,10},{10,1... | collective-permute-start | bytes 331784 | tf_op jit(solution)/shard_map/ppermute | solution.py:219
  54.6 3.0 %collective-permute-start.5 = (f32[1296,128]{1,0:T(8,128)S(1)}, f32[1296,128]{1,0:T(8,128)S(1)}, u32[]{:S(2)}, u32[]{:S(2)}) collective-permute-start(f32[1296,128]{1,0:T(8,128)S(1)} %pad_maximum_fusion.1), channel_id=1, source_target_pairs={{0,64},{64,0},{1,65},{65,1},{2,66},{66,2},{3,67},{67,3},{4,68},{68... | collective-permute-start | bytes 1990664 | tf_op jit(solution)/shard_map/ppermute | solution.py:222
  57.7 23.7 %copy-start.9 = (f32[360]{0:T(512)S(1)}, f32[360]{0:T(512)}, u32[]{:S(2)}) copy-start(f32[360]{0:T(512)} %param.24) | copy-start | bytes 4324
  57.7 23.7 %copy-start.10 = (f32[512]{0:T(512)S(1)}, f32[512]{0:T(512)}, u32[]{:S(2)}) copy-start(f32[512]{0:T(512)} %param.22) | copy-start | bytes 6148
  57.7 23.7 %copy-start.11 = (f32[512]{0:T(512)S(1)}, f32[512]{0:T(512)}, u32[]{:S(2)}) copy-start(f32[512]{0:T(512)} %param.20) | copy-start | bytes 6148
  57.7 23.7 %copy-start.12 = (f32[512]{0:T(512)S(1)}, f32[512]{0:T(512)}, u32[]{:S(2)}) copy-start(f32[512]{0:T(512)} %param.18) | copy-start | bytes 6148
  70.0 4.3 %collective-permute-start.6 = (f32[216,128]{1,0:T(8,128)S(1)}, f32[216,128]{1,0:T(8,128)S(1)}, u32[]{:S(2)}, u32[]{:S(2)}) collective-permute-start(f32[216,128]{1,0:T(8,128)S(1)} %get-tuple-element.19), channel_id=1, source_target_pairs={{0,63},{1,0},{2,1},{3,2},{4,3},{5,4},{6,5},{7,6},{8,7},{9,8},{10,9... | collective-permute-start | bytes 331784 | tf_op jit(solution)/shard_map/ppermute | solution.py:218
  70.1 9.6 %collective-permute-start.7 = (f32[216,128]{1,0:T(8,128)S(1)}, f32[216,128]{1,0:T(8,128)S(1)}, u32[]{:S(2)}, u32[]{:S(2)}) collective-permute-start(f32[216,128]{1,0:T(8,128)S(1)} %get-tuple-element.19), channel_id=1, source_target_pairs={{0,1},{1,2},{2,3},{3,4},{4,5},{5,6},{6,7},{7,8},{8,9},{9,10},{10,1... | collective-permute-start | bytes 331784 | tf_op jit(solution)/shard_map/ppermute | solution.py:219
  79.8 3.4 %collective-permute-start.8 = (f32[1296,128]{1,0:T(8,128)S(1)}, f32[1296,128]{1,0:T(8,128)S(1)}, u32[]{:S(2)}, u32[]{:S(2)}) collective-permute-start(f32[1296,128]{1,0:T(8,128)S(1)} %pad_maximum_fusion.2), channel_id=1, source_target_pairs={{0,64},{64,0},{1,65},{65,1},{2,66},{66,2},{3,67},{67,3},{4,68},{68... | collective-permute-start | bytes 1990664 | tf_op jit(solution)/shard_map/ppermute | solution.py:222
  83.1 8.3 %copy-start.4 = (bf16[512,512]{1,0:T(8,128)(2,1)S(1)}, bf16[512,512]{1,0:T(8,128)(2,1)}, u32[]{:S(2)}) copy-start(bf16[512,512]{1,0:T(8,128)(2,1)} %w_mid_ref.1) | copy-start | bytes 1572868
  83.1 8.3 %copy-start.5 = (bf16[512,512]{1,0:T(8,128)(2,1)S(1)}, bf16[512,512]{1,0:T(8,128)(2,1)}, u32[]{:S(2)}) copy-start(bf16[512,512]{1,0:T(8,128)(2,1)} %w_top_ref.1) | copy-start | bytes 1572868
  83.1 8.3 %copy-start.6 = (bf16[512,432]{0,1:T(8,128)(2,1)S(1)}, bf16[512,432]{0,1:T(8,128)(2,1)}, u32[]{:S(2)}) copy-start(bf16[512,432]{0,1:T(8,128)(2,1)} %param.17) | copy-start | bytes 1327108
  83.1 8.3 %copy-start.7 = (bf16[360,512]{1,0:T(8,128)(2,1)S(1)}, bf16[360,512]{1,0:T(8,128)(2,1)}, u32[]{:S(2)}) copy-start(bf16[360,512]{1,0:T(8,128)(2,1)} %w_out_ref.1) | copy-start | bytes 1105924
  91.4 2.0 %copy-start.1 = (f32[6912,128]{1,0:T(8,128)S(1)}, f32[6912,128]{1,0:T(8,128)}, u32[]{:S(2)}) copy-start(f32[6912,128]{1,0:T(8,128)} %shard_map.160.fin_ref) | copy-start | bytes 10616836
  93.4 11.5 %copy-start.8 = (s32[1,1,2048,1]{2,3,1,0:T(1,128)S(1)}, s32[1,1,2048,1]{2,3,1,0:T(1,128)}, u32[]{:S(2)}) copy-start(s32[1,1,2048,1]{2,3,1,0:T(1,128)} %param.25) | copy-start | bytes 24580

commit v8 on v7

--- a/solution.py
+++ b/solution.py
@@ -205,7 +205,7 @@
         in_specs=specs,
         out_specs=out_specs,
         out_shape=out_shape,
-        compiler_params=pltpu.CompilerParams(vmem_limit_bytes=16 * 1024 * 1024),
+        compiler_params=pltpu.CompilerParams(vmem_limit_bytes=8 * 1024 * 1024),
     )(*args)
 
 
@@ -287,7 +287,7 @@
             jax.ShapeDtypeStruct((height, width), jnp.float32),
         ],
         scratch_shapes=[pltpu.VMEM((outs * height, width), jnp.float32)],
-        compiler_params=pltpu.CompilerParams(vmem_limit_bytes=16 * 1024 * 1024),
+        compiler_params=pltpu.CompilerParams(vmem_limit_bytes=12 * 1024 * 1024),
     )(fin, w_in.T, w_mid, w_top, w_out, biases)
 
 

time: 122 us -> 123 us (level)
    unnamed x26 -> x32, local copies, waits for them, and re-layouts: 5.54 us -> 5.56 us
where the time goes in v8:
time: 123 us; the launch traced here: 122 us
  Pallas kernels  49.8 us (40%)
  waiting for transfers between devices  30.3 us (25%)
  starting transfers between devices  17.5 us (14%)
  blocking collectives  12.8 us (10%)
  local copies, waits for them, and re-layouts  7.58 us (6%)
  between operations  2.54 us (2%)
  other arithmetic  1.57 us (1%)
    pallas_call x4, Pallas kernels, run_section(): pl.pallas_call(kernel, grid=(steps,), in_specs=specs, out_specs=out_specs...  38.2 us
    ppermute x3, waiting for transfers between devices, exchange(): exl = lax.ppermute(ex, 'elem', from_left)  18.2 us
    all_to_all x1, blocking collectives, local(): lax.all_to_all(partial_sums.reshape(devices, 1), ('face', 'elem'), 0, 1,...  12.8 us
    pallas_call x1, Pallas kernels, run_mlp(): pl.pallas_call(mlp_kernel, out_shape=[jax.ShapeDtypeStruct((outs * height...  11.5 us
    ppermute x3, starting transfers between devices, exchange(): exr = lax.ppermute(ex, 'elem', from_right)  9.41 us
    ppermute x3, waiting for transfers between devices, exchange(): exr = lax.ppermute(ex, 'elem', from_right)  7.27 us
    unnamed x32, local copies, waits for them, and re-layouts  5.56 us
    ppermute x3, starting transfers between devices, exchange(): partner = lax.ppermute(bundle, 'face', [(0, 1), (1, 0)])  5.14 us
  transfers between devices with their start and end apart: 9, of which 9 were waited for; matrix products, arithmetic and copies ran while one was open for 0% of the time, Pallas kernels for 0%

profile of v8, /device:TPU:1, one launch (start us, length us, event | category | flops | bytes accessed | tf_op | source)
XLA Modules:
  0.0 122.1 jit_solution(639581544429490340)
XLA Ops:
  0.7 0.8 broadcast_in_dim.4.refs_1_.refs_2_
  2.3 2.0 %copy-done = f32[432,16,128]{2,1,0:T(8,128)S(1)} copy-done((f32[432,16,128]{2,1,0:T(8,128)S(1)}, f32[432,16,128]{2,1,0:T(8,128)}, u32[]{:S(2)}) %copy-start) | copy-done | bytes 3538968
  5.8 4.9 %shard_map.157 = (f32[216,128]{1,0:T(8,128)S(1)}, f32[2,432,128]{2,1,0:T(8,128)S(1)}) custom-call(f32[6912,128]{1,0:T(8,128)S(1)} %bitcast.11, f32[432,128]{1,0:T(8,128)S(1)} %broadcast_in_dim.4.refs_1_.refs_2_, f32[432,128]{1,0:T(8,128)S(1)} %broadcast_in_dim.5.refs_2_.refs_3_, bf16[128,128]{1,0:T(8,128)(2,1)S(1)} %copy-done.3, bf16[128,128]{1,0:T(8,128)(2,1)S(1)} %copy-done.5), custom_call_target="tpu_custom_call" | custom-call | tf_op jit(solution)/shard_map/pallas_call | solution.py:202
  10.7 9.3 %collective-permute-start = (f32[216,128]{1,0:T(8,128)S(1)}, f32[216,128]{1,0:T(8,128)S(1)}, u32[]{:S(2)}, u32[]{:S(2)}) collective-permute-start(f32[216,128]{1,0:T(8,128)S(1)} %get-tuple-element.13), channel_id=1, source_target_pairs={{0,63},{1,0},{2,1},{3,2},{4,3},{5,4},{6,5},{7,6},{8,7},{9,8},{10,9... | collective-permute-start | bytes 331784 | tf_op jit(solution)/shard_map/ppermute | solution.py:218
  20.0 1.8 %collective-permute-done.refs_5_ = f32[216,128]{1,0:T(8,128)S(1)} collective-permute-done((f32[216,128]{1,0:T(8,128)S(1)}, f32[216,128]{1,0:T(8,128)S(1)}, u32[]{:S(2)}, u32[]{:S(2)}) %collective-permute-start) | collective-permute-done | bytes 110624 | tf_op jit(solution)/shard_map/ppermute | solution.py:218
  21.8 7.3 %collective-permute-done.1.refs_6_ = f32[216,128]{1,0:T(8,128)S(1)} collective-permute-done((f32[216,128]{1,0:T(8,128)S(1)}, f32[216,128]{1,0:T(8,128)S(1)}, u32[]{:S(2)}, u32[]{:S(2)}) %collective-permute-start.1) | collective-permute-done | bytes 110624 | tf_op jit(solution)/shard_map/ppermute | solution.py:219
  29.1 2.2 %collective-permute-start.2 = (f32[1296,128]{1,0:T(8,128)S(1)}, f32[1296,128]{1,0:T(8,128)S(1)}, u32[]{:S(2)}, u32[]{:S(2)}) collective-permute-start(f32[1296,128]{1,0:T(8,128)S(1)} %pad_maximum_fusion), channel_id=1, source_target_pairs={{0,64},{64,0},{1,65},{65,1},{2,66},{66,2},{3,67},{67,3},{4,68},{68... | collective-permute-start | bytes 1990664 | tf_op jit(solution)/shard_map/ppermute | solution.py:222
  31.3 1.7 %collective-permute-done.2.refs_7_.refs_8_.refs_9_.refs_10_ = f32[1296,128]{1,0:T(8,128)S(1)} collective-permute-done((f32[1296,128]{1,0:T(8,128)S(1)}, f32[1296,128]{1,0:T(8,128)S(1)}, u32[]{:S(2)}, u32[]{:S(2)}) %collective-permute-start.2) | collective-permute-done | bytes 663584 | tf_op jit(solution)/shard_map/ppermute | solution.py:222
  33.0 11.8 %shard_map.158 = (f32[6912,128]{1,0:T(8,128)S(1)}, f32[216,128]{1,0:T(8,128)S(1)}, f32[2,432,128]{2,1,0:T(8,128)S(1)}) custom-call(f32[6912,128]{1,0:T(8,128)S(1)} %bitcast.12, f32[432,128]{1,0:T(8,128)S(1)} %broadcast_in_dim.4.refs_1_.refs_2_, f32[432,128]{1,0:T(8,128)S(1)} %broadcast_in_dim.5.refs_2_.refs_3_, bf16[128,128]{1,0:T(8,128)(2,1)S(1)} %copy-done.4, ...), custom_call_target="tpu_custom_call" | custom-call | tf_op jit(solution)/shard_map/pallas_call | solution.py:202
  44.9 1.5 %collective-permute-start.4 = (f32[216,128]{1,0:T(8,128)S(1)}, f32[216,128]{1,0:T(8,128)S(1)}, u32[]{:S(2)}, u32[]{:S(2)}) collective-permute-start(f32[216,128]{1,0:T(8,128)S(1)} %get-tuple-element.16), channel_id=1, source_target_pairs={{0,1},{1,2},{2,3},{3,4},{4,5},{5,6},{6,7},{7,8},{8,9},{9,10},{10,1... | collective-permute-start | bytes 331784 | tf_op jit(solution)/shard_map/ppermute | solution.py:219
  46.4 2.7 %collective-permute-done.3.refs_6_ = f32[216,128]{1,0:T(8,128)S(1)} collective-permute-done((f32[216,128]{1,0:T(8,128)S(1)}, f32[216,128]{1,0:T(8,128)S(1)}, u32[]{:S(2)}, u32[]{:S(2)}) %collective-permute-start.3) | collective-permute-done | bytes 110624 | tf_op jit(solution)/shard_map/ppermute | solution.py:218
  49.1 5.5 %collective-permute-done.4.refs_7_ = f32[216,128]{1,0:T(8,128)S(1)} collective-permute-done((f32[216,128]{1,0:T(8,128)S(1)}, f32[216,128]{1,0:T(8,128)S(1)}, u32[]{:S(2)}, u32[]{:S(2)}) %collective-permute-start.4) | collective-permute-done | bytes 110624 | tf_op jit(solution)/shard_map/ppermute | solution.py:219
  54.7 1.3 %collective-permute-start.5 = (f32[1296,128]{1,0:T(8,128)S(1)}, f32[1296,128]{1,0:T(8,128)S(1)}, u32[]{:S(2)}, u32[]{:S(2)}) collective-permute-start(f32[1296,128]{1,0:T(8,128)S(1)} %pad_maximum_fusion.1), channel_id=1, source_target_pairs={{0,64},{64,0},{1,65},{65,1},{2,66},{66,2},{3,67},{67,3},{4,68},{68... | collective-permute-start | bytes 1990664 | tf_op jit(solution)/shard_map/ppermute | solution.py:222
  56.0 1.7 %collective-permute-done.5.refs_8_.refs_9_.refs_10_.refs_11_ = f32[1296,128]{1,0:T(8,128)S(1)} collective-permute-done((f32[1296,128]{1,0:T(8,128)S(1)}, f32[1296,128]{1,0:T(8,128)S(1)}, u32[]{:S(2)}, u32[]{:S(2)}) %collective-permute-start.5) | collective-permute-done | bytes 663584 | tf_op jit(solution)/shard_map/ppermute | solution.py:222
  57.8 12.8 %shard_map.159 = (f32[6912,128]{1,0:T(8,128)S(1)}, f32[216,128]{1,0:T(8,128)S(1)}, f32[2,432,128]{2,1,0:T(8,128)S(1)}) custom-call(f32[6912,128]{1,0:T(8,128)S(1)} %bitcast.13, f32[6912,128]{1,0:T(8,128)S(1)} %get-tuple-element.15.refs_1_, f32[432,128]{1,0:T(8,128)S(1)} %broadcast_in_dim.4.refs_1_.refs_2_, f32[432,128]{1,0:T(8,128)S(1)} %broadcast_in_dim.5.refs_2_.refs_3_, ...), custom_call_target="tpu_custom_call" | custom-call | tf_op jit(solution)/shard_map/pallas_call | solution.py:202
  70.7 1.5 %collective-permute-start.7 = (f32[216,128]{1,0:T(8,128)S(1)}, f32[216,128]{1,0:T(8,128)S(1)}, u32[]{:S(2)}, u32[]{:S(2)}) collective-permute-start(f32[216,128]{1,0:T(8,128)S(1)} %get-tuple-element.19), channel_id=1, source_target_pairs={{0,1},{1,2},{2,3},{3,4},{4,5},{5,6},{6,7},{7,8},{8,9},{9,10},{10,1... | collective-permute-start | bytes 331784 | tf_op jit(solution)/shard_map/ppermute | solution.py:219
  72.1 2.8 %collective-permute-done.6.refs_6_ = f32[216,128]{1,0:T(8,128)S(1)} collective-permute-done((f32[216,128]{1,0:T(8,128)S(1)}, f32[216,128]{1,0:T(8,128)S(1)}, u32[]{:S(2)}, u32[]{:S(2)}) %collective-permute-start.6) | collective-permute-done | bytes 110624 | tf_op jit(solution)/shard_map/ppermute | solution.py:218
  74.9 5.4 %collective-permute-done.7.refs_7_ = f32[216,128]{1,0:T(8,128)S(1)} collective-permute-done((f32[216,128]{1,0:T(8,128)S(1)}, f32[216,128]{1,0:T(8,128)S(1)}, u32[]{:S(2)}, u32[]{:S(2)}) %collective-permute-start.7) | collective-permute-done | bytes 110624 | tf_op jit(solution)/shard_map/ppermute | solution.py:219
  80.3 1.6 %collective-permute-start.8 = (f32[1296,128]{1,0:T(8,128)S(1)}, f32[1296,128]{1,0:T(8,128)S(1)}, u32[]{:S(2)}, u32[]{:S(2)}) collective-permute-start(f32[1296,128]{1,0:T(8,128)S(1)} %pad_maximum_fusion.2), channel_id=1, source_target_pairs={{0,64},{64,0},{1,65},{65,1},{2,66},{66,2},{3,67},{67,3},{4,68},{68... | collective-permute-start | bytes 1990664 | tf_op jit(solution)/shard_map/ppermute | solution.py:222
  82.3 1.4 %collective-permute-done.8.refs_8_.refs_9_.refs_10_.refs_11_ = f32[1296,128]{1,0:T(8,128)S(1)} collective-permute-done((f32[1296,128]{1,0:T(8,128)S(1)}, f32[1296,128]{1,0:T(8,128)S(1)}, u32[]{:S(2)}, u32[]{:S(2)}) %collective-permute-start.8) | collective-permute-done | bytes 663584 | tf_op jit(solution)/shard_map/ppermute | solution.py:222
  83.7 8.6 %shard_map.160.fin_ref = f32[6912,128]{1,0:T(8,128)} custom-call(f32[6912,128]{1,0:T(8,128)S(1)} %bitcast.14, f32[6912,128]{1,0:T(8,128)S(1)} %get-tuple-element.18.refs_1_, f32[432,128]{1,0:T(8,128)S(1)} %broadcast_in_dim.4.refs_1_.refs_2_, f32[432,128]{1,0:T(8,128)S(1)} %broadcast_in_dim.5.refs_2_.refs_3_, bf16[128,128]{1,0:T(8,128)(2,1)S(1)} %copy-done.4, ...), custom_call_target="tpu_custom_call" | custom-call | tf_op jit(solution)/shard_map/pallas_call | solution.py:202
  92.4 2.0 %copy-done.2 = f32[6912,128]{1,0:T(8,128)S(1)} copy-done((f32[6912,128]{1,0:T(8,128)S(1)}, f32[6912,128]{1,0:T(8,128)}, u32[]{:S(2)}) %copy-start.2) | copy-done | bytes 3538968
  94.4 11.5 %shard_map.161 = (bf16[5760,128]{1,0:T(8,128)(2,1)}, f32[16,128]{1,0:T(8,128)S(1)}) custom-call(f32[6912,128]{1,0:T(8,128)S(1)} %copy-done.2, bf16[432,512]{1,0:T(8,128)(2,1)S(1)} %bitcast.19, bf16[512,512]{1,0:T(8,128)(2,1)S(1)} %copy-done.7, bf16[512,512]{1,0:T(8,128)(2,1)S(1)} %copy-done.8, bf16[360,512]{1,0:T(8,128)(2,1)S(1)} %copy-done.10, ...), custom_call_target="tpu_custom_call" | custom-call | tf_op jit(solution)/shard_map/pallas_call | solution.py:283
  106.7 12.8 %all_to_all.13 = f32[128,1,1]{2,1,0:T(1,128)S(1)} all-to-all(f32[128,1,1]{2,1,0:T(1,128)S(1)} %copy.21), channel_id=1, replica_groups=mesh['face'=2,'elem'=64] {'face','elem'}, dimensions={0} | all-to-all | bytes 1024 | tf_op jit(solution)/shard_map/all_to_all | solution.py:325
  (42 shorter events, 4.5 us)
Async XLA Ops:
  0.6 32.4 %copy-start.4 = (bf16[128,128]{1,0:T(8,128)(2,1)S(1)}, bf16[128,128]{1,0:T(8,128)(2,1)}, u32[]{:S(2)}) copy-start(bf16[128,128]{1,0:T(8,128)(2,1)} %constant.11.clone.refs_3_.refs_4_) | copy-start | bytes 98308
  0.6 32.4 %copy-start.6 = (bf16[128,128]{1,0:T(8,128)(2,1)S(1)}, bf16[128,128]{1,0:T(8,128)(2,1)}, u32[]{:S(2)}) copy-start(bf16[128,128]{1,0:T(8,128)(2,1)} %constant.12.clone.refs_4_.refs_5_) | copy-start | bytes 98308
  2.3 2.0 %copy-start = (f32[432,16,128]{2,1,0:T(8,128)S(1)}, f32[432,16,128]{2,1,0:T(8,128)}, u32[]{:S(2)}) copy-start(f32[432,16,128]{2,1,0:T(8,128)} %param.14) | copy-start | bytes 10616836
  5.0 0.8 copy-start.5
  5.8 27.2 %copy-start.1 = (f32[432,16,128]{2,1,0:T(8,128)S(1)}, f32[432,16,128]{2,1,0:T(8,128)}, u32[]{:S(2)}) copy-start(f32[432,16,128]{2,1,0:T(8,128)} %param.14) | copy-start | bytes 10616836
  10.7 11.0 %collective-permute-start = (f32[216,128]{1,0:T(8,128)S(1)}, f32[216,128]{1,0:T(8,128)S(1)}, u32[]{:S(2)}, u32[]{:S(2)}) collective-permute-start(f32[216,128]{1,0:T(8,128)S(1)} %get-tuple-element.13), channel_id=1, source_target_pairs={{0,63},{1,0},{2,1},{3,2},{4,3},{5,4},{6,5},{7,6},{8,7},{9,8},{10,9... | collective-permute-start | bytes 331784 | tf_op jit(solution)/shard_map/ppermute | solution.py:218
  20.0 9.0 %collective-permute-start.1 = (f32[216,128]{1,0:T(8,128)S(1)}, f32[216,128]{1,0:T(8,128)S(1)}, u32[]{:S(2)}, u32[]{:S(2)}) collective-permute-start(f32[216,128]{1,0:T(8,128)S(1)} %get-tuple-element.13), channel_id=1, source_target_pairs={{0,1},{1,2},{2,3},{3,4},{4,5},{5,6},{6,7},{7,8},{8,9},{9,10},{10,1... | collective-permute-start | bytes 331784 | tf_op jit(solution)/shard_map/ppermute | solution.py:219
  29.1 3.9 %collective-permute-start.2 = (f32[1296,128]{1,0:T(8,128)S(1)}, f32[1296,128]{1,0:T(8,128)S(1)}, u32[]{:S(2)}, u32[]{:S(2)}) collective-permute-start(f32[1296,128]{1,0:T(8,128)S(1)} %pad_maximum_fusion), channel_id=1, source_target_pairs={{0,64},{64,0},{1,65},{65,1},{2,66},{66,2},{3,67},{67,3},{4,68},{68... | collective-permute-start | bytes 1990664 | tf_op jit(solution)/shard_map/ppermute | solution.py:222
  44.8 4.3 %collective-permute-start.3 = (f32[216,128]{1,0:T(8,128)S(1)}, f32[216,128]{1,0:T(8,128)S(1)}, u32[]{:S(2)}, u32[]{:S(2)}) collective-permute-start(f32[216,128]{1,0:T(8,128)S(1)} %get-tuple-element.16), channel_id=1, source_target_pairs={{0,63},{1,0},{2,1},{3,2},{4,3},{5,4},{6,5},{7,6},{8,7},{9,8},{10,9... | collective-permute-start | bytes 331784 | tf_op jit(solution)/shard_map/ppermute | solution.py:218
  44.9 9.7 %collective-permute-start.4 = (f32[216,128]{1,0:T(8,128)S(1)}, f32[216,128]{1,0:T(8,128)S(1)}, u32[]{:S(2)}, u32[]{:S(2)}) collective-permute-start(f32[216,128]{1,0:T(8,128)S(1)} %get-tuple-element.16), channel_id=1, source_target_pairs={{0,1},{1,2},{2,3},{3,4},{4,5},{5,6},{6,7},{7,8},{8,9},{9,10},{10,1... | collective-permute-start | bytes 331784 | tf_op jit(solution)/shard_map/ppermute | solution.py:219
  54.7 3.1 %collective-permute-start.5 = (f32[1296,128]{1,0:T(8,128)S(1)}, f32[1296,128]{1,0:T(8,128)S(1)}, u32[]{:S(2)}, u32[]{:S(2)}) collective-permute-start(f32[1296,128]{1,0:T(8,128)S(1)} %pad_maximum_fusion.1), channel_id=1, source_target_pairs={{0,64},{64,0},{1,65},{65,1},{2,66},{66,2},{3,67},{67,3},{4,68},{68... | collective-permute-start | bytes 1990664 | tf_op jit(solution)/shard_map/ppermute | solution.py:222
  57.8 24.2 %copy-start.12 = (f32[360]{0:T(512)S(1)}, f32[360]{0:T(512)}, u32[]{:S(2)}) copy-start(f32[360]{0:T(512)} %param.24) | copy-start | bytes 4324
  57.8 24.2 %copy-start.13 = (f32[512]{0:T(512)S(1)}, f32[512]{0:T(512)}, u32[]{:S(2)}) copy-start(f32[512]{0:T(512)} %param.22) | copy-start | bytes 6148
  57.8 24.2 %copy-start.14 = (f32[512]{0:T(512)S(1)}, f32[512]{0:T(512)}, u32[]{:S(2)}) copy-start(f32[512]{0:T(512)} %param.20) | copy-start | bytes 6148
  57.8 24.2 %copy-start.15 = (f32[512]{0:T(512)S(1)}, f32[512]{0:T(512)}, u32[]{:S(2)}) copy-start(f32[512]{0:T(512)} %param.18) | copy-start | bytes 6148
  70.6 4.3 %collective-permute-start.6 = (f32[216,128]{1,0:T(8,128)S(1)}, f32[216,128]{1,0:T(8,128)S(1)}, u32[]{:S(2)}, u32[]{:S(2)}) collective-permute-start(f32[216,128]{1,0:T(8,128)S(1)} %get-tuple-element.19), channel_id=1, source_target_pairs={{0,63},{1,0},{2,1},{3,2},{4,3},{5,4},{6,5},{7,6},{8,7},{9,8},{10,9... | collective-permute-start | bytes 331784 | tf_op jit(solution)/shard_map/ppermute | solution.py:218
  70.7 9.6 %collective-permute-start.7 = (f32[216,128]{1,0:T(8,128)S(1)}, f32[216,128]{1,0:T(8,128)S(1)}, u32[]{:S(2)}, u32[]{:S(2)}) collective-permute-start(f32[216,128]{1,0:T(8,128)S(1)} %get-tuple-element.19), channel_id=1, source_target_pairs={{0,1},{1,2},{2,3},{3,4},{4,5},{5,6},{6,7},{7,8},{8,9},{9,10},{10,1... | collective-permute-start | bytes 331784 | tf_op jit(solution)/shard_map/ppermute | solution.py:219
  80.3 3.4 %collective-permute-start.8 = (f32[1296,128]{1,0:T(8,128)S(1)}, f32[1296,128]{1,0:T(8,128)S(1)}, u32[]{:S(2)}, u32[]{:S(2)}) collective-permute-start(f32[1296,128]{1,0:T(8,128)S(1)} %pad_maximum_fusion.2), channel_id=1, source_target_pairs={{0,64},{64,0},{1,65},{65,1},{2,66},{66,2},{3,67},{67,3},{4,68},{68... | collective-permute-start | bytes 1990664 | tf_op jit(solution)/shard_map/ppermute | solution.py:222
  83.7 8.7 %copy-start.7 = (bf16[512,512]{1,0:T(8,128)(2,1)S(1)}, bf16[512,512]{1,0:T(8,128)(2,1)}, u32[]{:S(2)}) copy-start(bf16[512,512]{1,0:T(8,128)(2,1)} %w_mid_ref.1) | copy-start | bytes 1572868
  83.7 8.7 %copy-start.8 = (bf16[512,512]{1,0:T(8,128)(2,1)S(1)}, bf16[512,512]{1,0:T(8,128)(2,1)}, u32[]{:S(2)}) copy-start(bf16[512,512]{1,0:T(8,128)(2,1)} %w_top_ref.1) | copy-start | bytes 1572868
  83.7 8.7 %copy-start.9 = (bf16[512,432]{0,1:T(8,128)(2,1)S(1)}, bf16[512,432]{0,1:T(8,128)(2,1)}, u32[]{:S(2)}) copy-start(bf16[512,432]{0,1:T(8,128)(2,1)} %param.17) | copy-start | bytes 1327108
  83.7 8.7 %copy-start.10 = (bf16[360,512]{1,0:T(8,128)(2,1)S(1)}, bf16[360,512]{1,0:T(8,128)(2,1)}, u32[]{:S(2)}) copy-start(bf16[360,512]{1,0:T(8,128)(2,1)} %w_out_ref.1) | copy-start | bytes 1105924
  92.4 2.0 %copy-start.2 = (f32[6912,128]{1,0:T(8,128)S(1)}, f32[6912,128]{1,0:T(8,128)}, u32[]{:S(2)}) copy-start(f32[6912,128]{1,0:T(8,128)} %shard_map.160.fin_ref) | copy-start | bytes 10616836
  94.4 11.6 %copy-start.11 = (s32[1,1,2048,1]{2,3,1,0:T(1,128)S(1)}, s32[1,1,2048,1]{2,3,1,0:T(1,128)}, u32[]{:S(2)}) copy-start(s32[1,1,2048,1]{2,3,1,0:T(1,128)} %param.25) | copy-start | bytes 24580
  (1 other events, 0.8 us)

commit v9 on v7

--- a/solution.py
+++ b/solution.py
@@ -159,21 +159,23 @@
         ey_ref[1] = tend[height - 1]
 
 
-def run_section(field_rows, v0, sx, sy, ahi, alo, halos, *, first, combo, edges):
+def run_section(field_rows, v0, speeds, mats, halos, *, first, combo, edges):
     total, width = field_rows.shape
-    feats = sx.shape[0]
+    feats = speeds.shape[0] // 2
     steps = feats // CHUNK
     big = pl.BlockSpec((CHUNK * 16, width), lambda i: (i, 0))
     small = pl.BlockSpec((CHUNK, width), lambda i: (i, 0))
+    small_y = pl.BlockSpec((CHUNK, width), lambda i: (i + steps, 0))
     const = pl.BlockSpec((width, width), lambda i: (0, 0))
+    const_lo = pl.BlockSpec((width, width), lambda i: (1, 0))
     edge = pl.BlockSpec((FOLD, width), lambda i: (i, 0))
     rowsb = pl.BlockSpec((2, CHUNK, width), lambda i: (0, i, 0))
     args, specs = [], []
     if combo is not None and combo[0] is not None:
         args.append(v0)
         specs.append(big)
-    args += [field_rows, sx, sy, ahi, alo]
-    specs += [big, small, small, const, const]
+    args += [field_rows, speeds, speeds, mats, mats]
+    specs += [big, small, small_y, const, const_lo]
     if not first:
         exr, exl, partner = halos
         blocks = field_rows.shape[0] // (CHUNK * 16)
@@ -296,18 +298,16 @@
     across = np.kron(np.eye(breadth // NP, dtype=np.float32), TABLE.T)
     ahi_np = across.astype(jnp.bfloat16)
     alo_np = (across - ahi_np.astype(np.float32)).astype(jnp.bfloat16)
-    ahi = jnp.asarray(ahi_np)
-    alo = jnp.asarray(alo_np)
-    sx = jnp.broadcast_to(speed_x[:, None], (feats, breadth))
-    sy = jnp.broadcast_to(speed_y[:, None], (feats, breadth))
+    mats = jnp.asarray(np.concatenate([ahi_np, alo_np], axis=0))
+    speeds = jnp.broadcast_to(jnp.concatenate([speed_x, speed_y])[:, None], (2 * feats, breadth))
     v0 = state.reshape(feats * height, breadth)
-    ex, ey = run_section(v0, None, sx, sy, ahi, alo, None, first=True, combo=None, edges=True)
+    ex, ey = run_section(v0, None, speeds, mats, None, first=True, combo=None, edges=True)
     field = v0
     combos = [(None, None), (0.75, 0.25), ("third", None)]
     for k, combo in enumerate(combos):
         halos = exchange(ex, ey)
         outs = run_section(
-            field, v0, sx, sy, ahi, alo, halos, first=False, combo=combo, edges=k < 2
+            field, v0, speeds, mats, halos, first=False, combo=combo, edges=k < 2
         )
         if k < 2:
             field, ex, ey = outs

time: 122 us -> 120 us (0.984)
  local copies, waits for them, and re-layouts: 7.55 us -> 5.46 us
    broadcast_in_dim x2 -> x1, local copies, waits for them, and re-layouts: 1.59 us -> 0.17 us  [local(): jnp.broadcast_to(jnp.concatenate([speed_x, speed_y])[:, None], (2 * feats...]
    unnamed x26 -> x24, local copies, waits for them, and re-layouts: 5.54 us -> 4.87 us
where the time goes in v9:
time: 120 us
  Pallas kernels  48.8 us (41%)
  waiting for transfers between devices  30.3 us (25%)
  starting transfers between devices  17.4 us (14%)
  blocking collectives  12.8 us (11%)
  local copies, waits for them, and re-layouts  5.46 us (5%)
  between operations  2.51 us (2%)
  other arithmetic  2.35 us (2%)
    pallas_call x4, Pallas kernels, run_section(): pl.pallas_call(kernel, grid=(steps,), in_specs=specs, out_specs=out_specs...  37.2 us
    ppermute x3, waiting for transfers between devices, exchange(): exl = lax.ppermute(ex, 'elem', from_left)  18.2 us
    all_to_all x1, blocking collectives, local(): lax.all_to_all(partial_sums.reshape(devices, 1), ('face', 'elem'), 0, 1,...  12.8 us
    pallas_call x1, Pallas kernels, run_mlp(): pl.pallas_call(mlp_kernel, out_shape=[jax.ShapeDtypeStruct((outs * height...  11.6 us
    ppermute x3, starting transfers between devices, exchange(): exr = lax.ppermute(ex, 'elem', from_right)  9.41 us
    ppermute x3, waiting for transfers between devices, exchange(): exr = lax.ppermute(ex, 'elem', from_right)  7.29 us
    ppermute x3, starting transfers between devices, exchange(): partner = lax.ppermute(bundle, 'face', [(0, 1), (1, 0)])  5.12 us
    unnamed x24, local copies, waits for them, and re-layouts  4.87 us
  transfers between devices with their start and end apart: 9, of which 9 were waited for; matrix products, arithmetic and copies ran while one was open for 0% of the time, Pallas kernels for 0%

profile of v9, /device:TPU:1, one launch (start us, length us, event | category | flops | bytes accessed | tf_op | source)
XLA Modules:
  0.0 119.7 jit_solution(18365302780602083128)
XLA Ops:
  1.6 2.0 %copy-done = f32[432,16,128]{2,1,0:T(8,128)S(1)} copy-done((f32[432,16,128]{2,1,0:T(8,128)S(1)}, f32[432,16,128]{2,1,0:T(8,128)}, u32[]{:S(2)}) %copy-start) | copy-done | bytes 3538968
  3.6 0.8 copy-done.2
  4.4 4.9 %shard_map.148 = (f32[216,128]{1,0:T(8,128)S(1)}, f32[2,432,128]{2,1,0:T(8,128)S(1)}) custom-call(f32[6912,128]{1,0:T(8,128)S(1)} %bitcast.11, f32[864,128]{1,0:T(8,128)S(1)} %broadcast_in_dim.2.refs_1_.refs_2_.refs_3_, f32[864,128]{1,0:T(8,128)S(1)} %broadcast_in_dim.2.refs_1_.refs_2_.refs_3_, bf16[256,128]{1,0:T(8,128)(2,1)S(1)} %copy-done.2, ...), custom_call_target="tpu_custom_call" | custom-call | tf_op jit(solution)/shard_map/pallas_call | solution.py:204
  9.4 9.3 %collective-permute-start = (f32[216,128]{1,0:T(8,128)S(1)}, f32[216,128]{1,0:T(8,128)S(1)}, u32[]{:S(2)}, u32[]{:S(2)}) collective-permute-start(f32[216,128]{1,0:T(8,128)S(1)} %get-tuple-element.13), channel_id=1, source_target_pairs={{0,63},{1,0},{2,1},{3,2},{4,3},{5,4},{6,5},{7,6},{8,7},{9,8},{10,9... | collective-permute-start | bytes 331784 | tf_op jit(solution)/shard_map/ppermute | solution.py:220
  18.6 1.8 %collective-permute-done.refs_5_ = f32[216,128]{1,0:T(8,128)S(1)} collective-permute-done((f32[216,128]{1,0:T(8,128)S(1)}, f32[216,128]{1,0:T(8,128)S(1)}, u32[]{:S(2)}, u32[]{:S(2)}) %collective-permute-start) | collective-permute-done | bytes 110624 | tf_op jit(solution)/shard_map/ppermute | solution.py:220
  20.4 7.3 %collective-permute-done.1.refs_6_ = f32[216,128]{1,0:T(8,128)S(1)} collective-permute-done((f32[216,128]{1,0:T(8,128)S(1)}, f32[216,128]{1,0:T(8,128)S(1)}, u32[]{:S(2)}, u32[]{:S(2)}) %collective-permute-start.1) | collective-permute-done | bytes 110624 | tf_op jit(solution)/shard_map/ppermute | solution.py:221
  27.7 2.2 %collective-permute-start.2 = (f32[1296,128]{1,0:T(8,128)S(1)}, f32[1296,128]{1,0:T(8,128)S(1)}, u32[]{:S(2)}, u32[]{:S(2)}) collective-permute-start(f32[1296,128]{1,0:T(8,128)S(1)} %pad_maximum_fusion), channel_id=1, source_target_pairs={{0,64},{64,0},{1,65},{65,1},{2,66},{66,2},{3,67},{67,3},{4,68},{68... | collective-permute-start | bytes 1990664 | tf_op jit(solution)/shard_map/ppermute | solution.py:224
  29.9 1.7 %collective-permute-done.2.refs_7_.refs_8_.refs_9_.refs_10_ = f32[1296,128]{1,0:T(8,128)S(1)} collective-permute-done((f32[1296,128]{1,0:T(8,128)S(1)}, f32[1296,128]{1,0:T(8,128)S(1)}, u32[]{:S(2)}, u32[]{:S(2)}) %collective-permute-start.2) | collective-permute-done | bytes 663584 | tf_op jit(solution)/shard_map/ppermute | solution.py:224
  31.6 11.8 %shard_map.149 = (f32[6912,128]{1,0:T(8,128)S(1)}, f32[216,128]{1,0:T(8,128)S(1)}, f32[2,432,128]{2,1,0:T(8,128)S(1)}) custom-call(f32[6912,128]{1,0:T(8,128)S(1)} %bitcast.12, f32[864,128]{1,0:T(8,128)S(1)} %broadcast_in_dim.2.refs_1_.refs_2_.refs_3_, f32[864,128]{1,0:T(8,128)S(1)} %broadcast_in_dim.2.refs_1_.refs_2_.refs_3_, ...), custom_call_target="tpu_custom_call" | custom-call | tf_op jit(solution)/shard_map/pallas_call | solution.py:204
  43.5 1.5 %collective-permute-start.4 = (f32[216,128]{1,0:T(8,128)S(1)}, f32[216,128]{1,0:T(8,128)S(1)}, u32[]{:S(2)}, u32[]{:S(2)}) collective-permute-start(f32[216,128]{1,0:T(8,128)S(1)} %get-tuple-element.16), channel_id=1, source_target_pairs={{0,1},{1,2},{2,3},{3,4},{4,5},{5,6},{6,7},{7,8},{8,9},{9,10},{10,1... | collective-permute-start | bytes 331784 | tf_op jit(solution)/shard_map/ppermute | solution.py:221
  45.0 2.8 %collective-permute-done.3.refs_6_ = f32[216,128]{1,0:T(8,128)S(1)} collective-permute-done((f32[216,128]{1,0:T(8,128)S(1)}, f32[216,128]{1,0:T(8,128)S(1)}, u32[]{:S(2)}, u32[]{:S(2)}) %collective-permute-start.3) | collective-permute-done | bytes 110624 | tf_op jit(solution)/shard_map/ppermute | solution.py:220
  47.8 5.5 %collective-permute-done.4.refs_7_ = f32[216,128]{1,0:T(8,128)S(1)} collective-permute-done((f32[216,128]{1,0:T(8,128)S(1)}, f32[216,128]{1,0:T(8,128)S(1)}, u32[]{:S(2)}, u32[]{:S(2)}) %collective-permute-start.4) | collective-permute-done | bytes 110624 | tf_op jit(solution)/shard_map/ppermute | solution.py:221
  53.3 1.3 %collective-permute-start.5 = (f32[1296,128]{1,0:T(8,128)S(1)}, f32[1296,128]{1,0:T(8,128)S(1)}, u32[]{:S(2)}, u32[]{:S(2)}) collective-permute-start(f32[1296,128]{1,0:T(8,128)S(1)} %pad_maximum_fusion.1), channel_id=1, source_target_pairs={{0,64},{64,0},{1,65},{65,1},{2,66},{66,2},{3,67},{67,3},{4,68},{68... | collective-permute-start | bytes 1990664 | tf_op jit(solution)/shard_map/ppermute | solution.py:224
  54.6 1.7 %collective-permute-done.5.refs_8_.refs_9_.refs_10_.refs_11_ = f32[1296,128]{1,0:T(8,128)S(1)} collective-permute-done((f32[1296,128]{1,0:T(8,128)S(1)}, f32[1296,128]{1,0:T(8,128)S(1)}, u32[]{:S(2)}, u32[]{:S(2)}) %collective-permute-start.5) | collective-permute-done | bytes 663584 | tf_op jit(solution)/shard_map/ppermute | solution.py:224
  56.4 12.3 %shard_map.150 = (f32[6912,128]{1,0:T(8,128)S(1)}, f32[216,128]{1,0:T(8,128)S(1)}, f32[2,432,128]{2,1,0:T(8,128)S(1)}) custom-call(f32[6912,128]{1,0:T(8,128)S(1)} %bitcast.13, f32[6912,128]{1,0:T(8,128)S(1)} %get-tuple-element.15.refs_1_, f32[864,128]{1,0:T(8,128)S(1)} %broadcast_in_dim.2.refs_1_.refs_2_.refs_3_, ...), custom_call_target="tpu_custom_call" | custom-call | tf_op jit(solution)/shard_map/pallas_call | solution.py:204
  68.7 1.5 %collective-permute-start.7 = (f32[216,128]{1,0:T(8,128)S(1)}, f32[216,128]{1,0:T(8,128)S(1)}, u32[]{:S(2)}, u32[]{:S(2)}) collective-permute-start(f32[216,128]{1,0:T(8,128)S(1)} %get-tuple-element.19), channel_id=1, source_target_pairs={{0,1},{1,2},{2,3},{3,4},{4,5},{5,6},{6,7},{7,8},{8,9},{9,10},{10,1... | collective-permute-start | bytes 331784 | tf_op jit(solution)/shard_map/ppermute | solution.py:221
  70.2 2.8 %collective-permute-done.6.refs_6_ = f32[216,128]{1,0:T(8,128)S(1)} collective-permute-done((f32[216,128]{1,0:T(8,128)S(1)}, f32[216,128]{1,0:T(8,128)S(1)}, u32[]{:S(2)}, u32[]{:S(2)}) %collective-permute-start.6) | collective-permute-done | bytes 110624 | tf_op jit(solution)/shard_map/ppermute | solution.py:220
  73.0 5.4 %collective-permute-done.7.refs_7_ = f32[216,128]{1,0:T(8,128)S(1)} collective-permute-done((f32[216,128]{1,0:T(8,128)S(1)}, f32[216,128]{1,0:T(8,128)S(1)}, u32[]{:S(2)}, u32[]{:S(2)}) %collective-permute-start.7) | collective-permute-done | bytes 110624 | tf_op jit(solution)/shard_map/ppermute | solution.py:221
  78.4 1.6 %collective-permute-start.8 = (f32[1296,128]{1,0:T(8,128)S(1)}, f32[1296,128]{1,0:T(8,128)S(1)}, u32[]{:S(2)}, u32[]{:S(2)}) collective-permute-start(f32[1296,128]{1,0:T(8,128)S(1)} %pad_maximum_fusion.2), channel_id=1, source_target_pairs={{0,64},{64,0},{1,65},{65,1},{2,66},{66,2},{3,67},{67,3},{4,68},{68... | collective-permute-start | bytes 1990664 | tf_op jit(solution)/shard_map/ppermute | solution.py:224
  80.4 1.4 %collective-permute-done.8.refs_8_.refs_9_.refs_10_.refs_11_ = f32[1296,128]{1,0:T(8,128)S(1)} collective-permute-done((f32[1296,128]{1,0:T(8,128)S(1)}, f32[1296,128]{1,0:T(8,128)S(1)}, u32[]{:S(2)}, u32[]{:S(2)}) %collective-permute-start.8) | collective-permute-done | bytes 663584 | tf_op jit(solution)/shard_map/ppermute | solution.py:224
  81.8 8.2 %shard_map.151.fin_ref = f32[6912,128]{1,0:T(8,128)} custom-call(f32[6912,128]{1,0:T(8,128)S(1)} %bitcast.14, f32[6912,128]{1,0:T(8,128)S(1)} %get-tuple-element.18.refs_1_, f32[864,128]{1,0:T(8,128)S(1)} %broadcast_in_dim.2.refs_1_.refs_2_.refs_3_, f32[864,128]{1,0:T(8,128)S(1)} %broadcast_in_dim.2.refs_1_.refs_2_.refs_3_, bf16[256,128]{1,0:T(8,128)(2,1)S(1)} %copy-done.2, ...), custom_call_target="tpu_custom_call" | custom-call | tf_op jit(solution)/shard_map/pallas_call | solution.py:204
  90.0 2.0 %copy-done.1 = f32[6912,128]{1,0:T(8,128)S(1)} copy-done((f32[6912,128]{1,0:T(8,128)S(1)}, f32[6912,128]{1,0:T(8,128)}, u32[]{:S(2)}) %copy-start.1) | copy-done | bytes 3538968
  92.0 11.6 %shard_map.152 = (bf16[5760,128]{1,0:T(8,128)(2,1)}, f32[16,128]{1,0:T(8,128)S(1)}) custom-call(f32[6912,128]{1,0:T(8,128)S(1)} %copy-done.1, bf16[432,512]{1,0:T(8,128)(2,1)S(1)} %bitcast.19, bf16[512,512]{1,0:T(8,128)(2,1)S(1)} %copy-done.3, bf16[512,512]{1,0:T(8,128)(2,1)S(1)} %copy-done.4, bf16[360,512]{1,0:T(8,128)(2,1)S(1)} %copy-done.6, ...), custom_call_target="tpu_custom_call" | custom-call | tf_op jit(solution)/shard_map/pallas_call | solution.py:285
  104.4 12.8 %all_to_all.13 = f32[128,1,1]{2,1,0:T(1,128)S(1)} all-to-all(f32[128,1,1]{2,1,0:T(1,128)S(1)} %copy.20), channel_id=1, replica_groups=mesh['face'=2,'elem'=64] {'face','elem'}, dimensions={0} | all-to-all | bytes 1024 | tf_op jit(solution)/shard_map/all_to_all | solution.py:325
  (34 shorter events, 3.1 us)
Async XLA Ops:
  1.6 2.0 %copy-start = (f32[432,16,128]{2,1,0:T(8,128)S(1)}, f32[432,16,128]{2,1,0:T(8,128)}, u32[]{:S(2)}) copy-start(f32[432,16,128]{2,1,0:T(8,128)} %param.13) | copy-start | bytes 10616836
  3.6 0.8 copy-start.2
  9.4 11.0 %collective-permute-start = (f32[216,128]{1,0:T(8,128)S(1)}, f32[216,128]{1,0:T(8,128)S(1)}, u32[]{:S(2)}, u32[]{:S(2)}) collective-permute-start(f32[216,128]{1,0:T(8,128)S(1)} %get-tuple-element.13), channel_id=1, source_target_pairs={{0,63},{1,0},{2,1},{3,2},{4,3},{5,4},{6,5},{7,6},{8,7},{9,8},{10,9... | collective-permute-start | bytes 331784 | tf_op jit(solution)/shard_map/ppermute | solution.py:220
  18.6 9.0 %collective-permute-start.1 = (f32[216,128]{1,0:T(8,128)S(1)}, f32[216,128]{1,0:T(8,128)S(1)}, u32[]{:S(2)}, u32[]{:S(2)}) collective-permute-start(f32[216,128]{1,0:T(8,128)S(1)} %get-tuple-element.13), channel_id=1, source_target_pairs={{0,1},{1,2},{2,3},{3,4},{4,5},{5,6},{6,7},{7,8},{8,9},{9,10},{10,1... | collective-permute-start | bytes 331784 | tf_op jit(solution)/shard_map/ppermute | solution.py:221
  27.7 3.9 %collective-permute-start.2 = (f32[1296,128]{1,0:T(8,128)S(1)}, f32[1296,128]{1,0:T(8,128)S(1)}, u32[]{:S(2)}, u32[]{:S(2)}) collective-permute-start(f32[1296,128]{1,0:T(8,128)S(1)} %pad_maximum_fusion), channel_id=1, source_target_pairs={{0,64},{64,0},{1,65},{65,1},{2,66},{66,2},{3,67},{67,3},{4,68},{68... | collective-permute-start | bytes 1990664 | tf_op jit(solution)/shard_map/ppermute | solution.py:224
  43.5 4.3 %collective-permute-start.3 = (f32[216,128]{1,0:T(8,128)S(1)}, f32[216,128]{1,0:T(8,128)S(1)}, u32[]{:S(2)}, u32[]{:S(2)}) collective-permute-start(f32[216,128]{1,0:T(8,128)S(1)} %get-tuple-element.16), channel_id=1, source_target_pairs={{0,63},{1,0},{2,1},{3,2},{4,3},{5,4},{6,5},{7,6},{8,7},{9,8},{10,9... | collective-permute-start | bytes 331784 | tf_op jit(solution)/shard_map/ppermute | solution.py:220
  43.5 9.7 %collective-permute-start.4 = (f32[216,128]{1,0:T(8,128)S(1)}, f32[216,128]{1,0:T(8,128)S(1)}, u32[]{:S(2)}, u32[]{:S(2)}) collective-permute-start(f32[216,128]{1,0:T(8,128)S(1)} %get-tuple-element.16), channel_id=1, source_target_pairs={{0,1},{1,2},{2,3},{3,4},{4,5},{5,6},{6,7},{7,8},{8,9},{9,10},{10,1... | collective-permute-start | bytes 331784 | tf_op jit(solution)/shard_map/ppermute | solution.py:221
  53.3 3.0 %collective-permute-start.5 = (f32[1296,128]{1,0:T(8,128)S(1)}, f32[1296,128]{1,0:T(8,128)S(1)}, u32[]{:S(2)}, u32[]{:S(2)}) collective-permute-start(f32[1296,128]{1,0:T(8,128)S(1)} %pad_maximum_fusion.1), channel_id=1, source_target_pairs={{0,64},{64,0},{1,65},{65,1},{2,66},{66,2},{3,67},{67,3},{4,68},{68... | collective-permute-start | bytes 1990664 | tf_op jit(solution)/shard_map/ppermute | solution.py:224
  56.4 23.6 %copy-start.8 = (f32[360]{0:T(512)S(1)}, f32[360]{0:T(512)}, u32[]{:S(2)}) copy-start(f32[360]{0:T(512)} %param.23) | copy-start | bytes 4324
  56.4 23.6 %copy-start.9 = (f32[512]{0:T(512)S(1)}, f32[512]{0:T(512)}, u32[]{:S(2)}) copy-start(f32[512]{0:T(512)} %param.21) | copy-start | bytes 6148
  56.4 23.6 %copy-start.10 = (f32[512]{0:T(512)S(1)}, f32[512]{0:T(512)}, u32[]{:S(2)}) copy-start(f32[512]{0:T(512)} %param.19) | copy-start | bytes 6148
  56.4 23.6 %copy-start.11 = (f32[512]{0:T(512)S(1)}, f32[512]{0:T(512)}, u32[]{:S(2)}) copy-start(f32[512]{0:T(512)} %param.17) | copy-start | bytes 6148
  68.7 4.3 %collective-permute-start.6 = (f32[216,128]{1,0:T(8,128)S(1)}, f32[216,128]{1,0:T(8,128)S(1)}, u32[]{:S(2)}, u32[]{:S(2)}) collective-permute-start(f32[216,128]{1,0:T(8,128)S(1)} %get-tuple-element.19), channel_id=1, source_target_pairs={{0,63},{1,0},{2,1},{3,2},{4,3},{5,4},{6,5},{7,6},{8,7},{9,8},{10,9... | collective-permute-start | bytes 331784 | tf_op jit(solution)/shard_map/ppermute | solution.py:220
  68.7 9.6 %collective-permute-start.7 = (f32[216,128]{1,0:T(8,128)S(1)}, f32[216,128]{1,0:T(8,128)S(1)}, u32[]{:S(2)}, u32[]{:S(2)}) collective-permute-start(f32[216,128]{1,0:T(8,128)S(1)} %get-tuple-element.19), channel_id=1, source_target_pairs={{0,1},{1,2},{2,3},{3,4},{4,5},{5,6},{6,7},{7,8},{8,9},{9,10},{10,1... | collective-permute-start | bytes 331784 | tf_op jit(solution)/shard_map/ppermute | solution.py:221
  78.4 3.4 %collective-permute-start.8 = (f32[1296,128]{1,0:T(8,128)S(1)}, f32[1296,128]{1,0:T(8,128)S(1)}, u32[]{:S(2)}, u32[]{:S(2)}) collective-permute-start(f32[1296,128]{1,0:T(8,128)S(1)} %pad_maximum_fusion.2), channel_id=1, source_target_pairs={{0,64},{64,0},{1,65},{65,1},{2,66},{66,2},{3,67},{67,3},{4,68},{68... | collective-permute-start | bytes 1990664 | tf_op jit(solution)/shard_map/ppermute | solution.py:224
  81.8 8.2 %copy-start.3 = (bf16[512,512]{1,0:T(8,128)(2,1)S(1)}, bf16[512,512]{1,0:T(8,128)(2,1)}, u32[]{:S(2)}) copy-start(bf16[512,512]{1,0:T(8,128)(2,1)} %w_mid_ref.1) | copy-start | bytes 1572868
  81.8 8.2 %copy-start.4 = (bf16[512,512]{1,0:T(8,128)(2,1)S(1)}, bf16[512,512]{1,0:T(8,128)(2,1)}, u32[]{:S(2)}) copy-start(bf16[512,512]{1,0:T(8,128)(2,1)} %w_top_ref.1) | copy-start | bytes 1572868
  81.8 8.2 %copy-start.5 = (bf16[512,432]{0,1:T(8,128)(2,1)S(1)}, bf16[512,432]{0,1:T(8,128)(2,1)}, u32[]{:S(2)}) copy-start(bf16[512,432]{0,1:T(8,128)(2,1)} %param.16) | copy-start | bytes 1327108
  81.8 8.2 %copy-start.6 = (bf16[360,512]{1,0:T(8,128)(2,1)S(1)}, bf16[360,512]{1,0:T(8,128)(2,1)}, u32[]{:S(2)}) copy-start(bf16[360,512]{1,0:T(8,128)(2,1)} %w_out_ref.1) | copy-start | bytes 1105924
  90.0 2.0 %copy-start.1 = (f32[6912,128]{1,0:T(8,128)S(1)}, f32[6912,128]{1,0:T(8,128)}, u32[]{:S(2)}) copy-start(f32[6912,128]{1,0:T(8,128)} %shard_map.151.fin_ref) | copy-start | bytes 10616836
  92.0 11.6 %copy-start.7 = (s32[1,1,2048,1]{2,3,1,0:T(1,128)S(1)}, s32[1,1,2048,1]{2,3,1,0:T(1,128)}, u32[]{:S(2)}) copy-start(s32[1,1,2048,1]{2,3,1,0:T(1,128)} %param.24) | copy-start | bytes 24580

commit v10 on v9

--- a/solution.py
+++ b/solution.py
@@ -71,6 +71,38 @@
     return out
 
 
+def raw_stiff_x(slabs, sx, sy, fhi, flo, smat, right_edges, left_edges):
+    rows, width = slabs[0].shape
+    stacked = jnp.concatenate(slabs, axis=0)
+    hi = stacked.astype(jnp.bfloat16)
+    lo = (stacked - hi.astype(jnp.float32)).astype(jnp.bfloat16)
+    along_x = (
+        jnp.dot(hi, fhi, preferred_element_type=jnp.float32)
+        + jnp.dot(hi, flo, preferred_element_type=jnp.float32)
+        + jnp.dot(lo, fhi, preferred_element_type=jnp.float32)
+    )
+    averaged = jnp.dot(hi, smat, preferred_element_type=jnp.float32) + jnp.dot(
+        lo, smat, preferred_element_type=jnp.float32
+    )
+    lane = lanes((rows, width))
+    out = []
+    for y in range(len(slabs)):
+        base = (y // NP) * NP
+        j = y % NP
+        part = lambda k: averaged[k * rows : (k + 1) * rows]
+        along_y = float(TABLE[j, 0]) * part(base)
+        for i in range(1, NP):
+            along_y = along_y + float(TABLE[j, i]) * part(base + i)
+        dx = along_x[y * rows : (y + 1) * rows]
+        halo = jnp.where(
+            lane == width - 1,
+            roll(right_edges, width - 1 - 2 * y),
+            jnp.where(lane == 0, roll(left_edges, width - 1 - 2 * y), 0.0),
+        )
+        out.append(-(sx * dx + sy * along_y) + 0.5 * halo)
+    return out
+
+
 def pack_edges(tend):
     rows, width = tend[0].shape
     lane = lanes((rows, width))
@@ -105,8 +137,9 @@
     sx_ref, sy_ref, ahi_ref, alo_ref = refs[:4]
     refs = refs[4:]
     if not first:
-        exr_ref, exl_ref, dr_ref, dl_ref, top_ref, bottom_ref = refs[:6]
-        refs = refs[6:]
+        fhi_ref, flo_ref, smat_ref = refs[:3]
+        exr_ref, exl_ref, dr_ref, dl_ref, top_ref, bottom_ref = refs[3:9]
+        refs = refs[9:]
     rows = CHUNK
     height = 16
     sx = sx_ref[...]
@@ -114,8 +147,8 @@
     ahi = ahi_ref[...]
     alo = alo_ref[...]
     slabs = [sp_ref[pl.ds(y, rows, stride=height), :] for y in range(height)]
-    tend = raw_slabs(slabs, sx, sy, ahi, alo)
     if first:
+        tend = raw_slabs(slabs, sx, sy, ahi, alo)
         ex_ref, ey_ref = refs
         ex_ref[...] = pack_edges(tend)
         ey_ref[0] = tend[0]
@@ -125,7 +158,7 @@
     exl = unpack_edges(exl_ref[...])
     dr = unpack_edges(dr_ref[...])
     dl = unpack_edges(dl_ref[...])
-    tx = [stiff_x(t, exr, exl, y) for y, t in enumerate(tend)]
+    tx = raw_stiff_x(slabs, sx, sy, fhi_ref[...], flo_ref[...], smat_ref[...], exr, exl)
     down = stiff_x(top_ref[...], dr, dl, 0)
     up = stiff_x(bottom_ref[...], dr, dl, height - 1)
     ext = [up] + tx + [down]
@@ -168,6 +201,9 @@
     small_y = pl.BlockSpec((CHUNK, width), lambda i: (i + steps, 0))
     const = pl.BlockSpec((width, width), lambda i: (0, 0))
     const_lo = pl.BlockSpec((width, width), lambda i: (1, 0))
+    const_fhi = pl.BlockSpec((width, width), lambda i: (2, 0))
+    const_flo = pl.BlockSpec((width, width), lambda i: (3, 0))
+    const_s = pl.BlockSpec((width, width), lambda i: (4, 0))
     edge = pl.BlockSpec((FOLD, width), lambda i: (i, 0))
     rowsb = pl.BlockSpec((2, CHUNK, width), lambda i: (0, i, 0))
     args, specs = [], []
@@ -176,6 +212,9 @@
         specs.append(big)
     args += [field_rows, speeds, speeds, mats, mats]
     specs += [big, small, small_y, const, const_lo]
+    if not first:
+        args += [mats, mats, mats]
+        specs += [const_fhi, const_flo, const_s]
     if not first:
         exr, exl, partner = halos
         blocks = field_rows.shape[0] // (CHUNK * 16)
@@ -298,7 +337,24 @@
     across = np.kron(np.eye(breadth // NP, dtype=np.float32), TABLE.T)
     ahi_np = across.astype(jnp.bfloat16)
     alo_np = (across - ahi_np.astype(np.float32)).astype(jnp.bfloat16)
-    mats = jnp.asarray(np.concatenate([ahi_np, alo_np], axis=0))
+    smat = np.zeros((breadth, breadth), np.float64)
+    for lane in range(breadth):
+        if lane % NP == NP - 1:
+            smat[lane, lane] = 0.5
+            if lane + 1 < breadth:
+                smat[lane + 1, lane] = 0.5
+        elif lane % NP == 0:
+            smat[lane, lane] = 0.5
+            if lane > 0:
+                smat[lane - 1, lane] = 0.5
+        else:
+            smat[lane, lane] = 1.0
+    fused = (across.astype(np.float64) @ smat).astype(np.float32)
+    fhi_np = fused.astype(jnp.bfloat16)
+    flo_np = (fused - fhi_np.astype(np.float32)).astype(jnp.bfloat16)
+    mats = jnp.asarray(
+        np.concatenate([ahi_np, alo_np, fhi_np, flo_np, smat.astype(jnp.bfloat16)], axis=0)
+    )
     speeds = jnp.broadcast_to(jnp.concatenate([speed_x, speed_y])[:, None], (2 * feats, breadth))
     v0 = state.reshape(feats * height, breadth)
     ex, ey = run_section(v0, None, speeds, mats, None, first=True, combo=None, edges=True)

time: 120 us -> 121 us (level)
  no operation moved by 1% of the time
where the time goes in v10:
time: 121 us
  Pallas kernels  49.9 us (41%)
  waiting for transfers between devices  30.3 us (25%)
  starting transfers between devices  17.5 us (14%)
  blocking collectives  12.8 us (11%)
  local copies, waits for them, and re-layouts  5.53 us (5%)
  between operations  2.51 us (2%)
  other arithmetic  2.35 us (2%)
    pallas_call x4, Pallas kernels, run_section(): pl.pallas_call(kernel, grid=(steps,), in_specs=specs, out_specs=out_specs...  38.4 us
    ppermute x3, waiting for transfers between devices, exchange(): exl = lax.ppermute(ex, 'elem', from_left)  18.2 us
    all_to_all x1, blocking collectives, local(): lax.all_to_all(partial_sums.reshape(devices, 1), ('face', 'elem'), 0, 1,...  12.8 us
    pallas_call x1, Pallas kernels, run_mlp(): pl.pallas_call(mlp_kernel, out_shape=[jax.ShapeDtypeStruct((outs * height...  11.5 us
    ppermute x3, starting transfers between devices, exchange(): exr = lax.ppermute(ex, 'elem', from_right)  9.43 us
    ppermute x3, waiting for transfers between devices, exchange(): exr = lax.ppermute(ex, 'elem', from_right)  7.3 us
    ppermute x3, starting transfers between devices, exchange(): partner = lax.ppermute(bundle, 'face', [(0, 1), (1, 0)])  5.12 us
    unnamed x24, local copies, waits for them, and re-layouts  4.95 us
  transfers between devices with their start and end apart: 9, of which 9 were waited for; matrix products, arithmetic and copies ran while one was open for 0% of the time, Pallas kernels for 0%

profile of v10, /device:TPU:1, one launch (start us, length us, event | category | flops | bytes accessed | tf_op | source)
XLA Modules:
  0.0 120.9 jit_solution(4994999458234920262)
XLA Ops:
  1.6 2.0 %copy-done = f32[432,16,128]{2,1,0:T(8,128)S(1)} copy-done((f32[432,16,128]{2,1,0:T(8,128)S(1)}, f32[432,16,128]{2,1,0:T(8,128)}, u32[]{:S(2)}) %copy-start) | copy-done | bytes 3538968
  3.6 0.9 copy-done.1
  4.5 4.9 %shard_map.148 = (f32[216,128]{1,0:T(8,128)S(1)}, f32[2,432,128]{2,1,0:T(8,128)S(1)}) custom-call(f32[6912,128]{1,0:T(8,128)S(1)} %bitcast.11, f32[864,128]{1,0:T(8,128)S(1)} %broadcast_in_dim.2.refs_1_.refs_2_.refs_3_, f32[864,128]{1,0:T(8,128)S(1)} %broadcast_in_dim.2.refs_1_.refs_2_.refs_3_, bf16[640,128]{1,0:T(8,128)(2,1)S(1)} %copy-done.1, ...), custom_call_target="tpu_custom_call" | custom-call | tf_op jit(solution)/shard_map/pallas_call | solution.py:243
  9.4 9.3 %collective-permute-start = (f32[216,128]{1,0:T(8,128)S(1)}, f32[216,128]{1,0:T(8,128)S(1)}, u32[]{:S(2)}, u32[]{:S(2)}) collective-permute-start(f32[216,128]{1,0:T(8,128)S(1)} %get-tuple-element.13), channel_id=1, source_target_pairs={{0,63},{1,0},{2,1},{3,2},{4,3},{5,4},{6,5},{7,6},{8,7},{9,8},{10,9... | collective-permute-start | bytes 331784 | tf_op jit(solution)/shard_map/ppermute | solution.py:259
  18.7 1.8 %collective-permute-done.refs_8_ = f32[216,128]{1,0:T(8,128)S(1)} collective-permute-done((f32[216,128]{1,0:T(8,128)S(1)}, f32[216,128]{1,0:T(8,128)S(1)}, u32[]{:S(2)}, u32[]{:S(2)}) %collective-permute-start) | collective-permute-done | bytes 110624 | tf_op jit(solution)/shard_map/ppermute | solution.py:259
  20.5 7.3 %collective-permute-done.1.refs_9_ = f32[216,128]{1,0:T(8,128)S(1)} collective-permute-done((f32[216,128]{1,0:T(8,128)S(1)}, f32[216,128]{1,0:T(8,128)S(1)}, u32[]{:S(2)}, u32[]{:S(2)}) %collective-permute-start.1) | collective-permute-done | bytes 110624 | tf_op jit(solution)/shard_map/ppermute | solution.py:260
  27.8 2.2 %collective-permute-start.2 = (f32[1296,128]{1,0:T(8,128)S(1)}, f32[1296,128]{1,0:T(8,128)S(1)}, u32[]{:S(2)}, u32[]{:S(2)}) collective-permute-start(f32[1296,128]{1,0:T(8,128)S(1)} %pad_maximum_fusion), channel_id=1, source_target_pairs={{0,64},{64,0},{1,65},{65,1},{2,66},{66,2},{3,67},{67,3},{4,68},{68... | collective-permute-start | bytes 1990664 | tf_op jit(solution)/shard_map/ppermute | solution.py:263
  30.0 1.7 %collective-permute-done.2.refs_10_.refs_11_.refs_12_.refs_13_ = f32[1296,128]{1,0:T(8,128)S(1)} collective-permute-done((f32[1296,128]{1,0:T(8,128)S(1)}, f32[1296,128]{1,0:T(8,128)S(1)}, u32[]{:S(2)}, u32[]{:S(2)}) %collective-permute-start.2) | collective-permute-done | bytes 663584 | tf_op jit(solution)/shard_map/ppermute | solution.py:263
  31.7 12.2 %shard_map.149 = (f32[6912,128]{1,0:T(8,128)S(1)}, f32[216,128]{1,0:T(8,128)S(1)}, f32[2,432,128]{2,1,0:T(8,128)S(1)}) custom-call(f32[6912,128]{1,0:T(8,128)S(1)} %bitcast.12, f32[864,128]{1,0:T(8,128)S(1)} %broadcast_in_dim.2.refs_1_.refs_2_.refs_3_, f32[864,128]{1,0:T(8,128)S(1)} %broadcast_in_dim.2.refs_1_.refs_2_.refs_3_, ...), custom_call_target="tpu_custom_call" | custom-call | tf_op jit(solution)/shard_map/pallas_call | solution.py:243
  44.0 1.5 %collective-permute-start.4 = (f32[216,128]{1,0:T(8,128)S(1)}, f32[216,128]{1,0:T(8,128)S(1)}, u32[]{:S(2)}, u32[]{:S(2)}) collective-permute-start(f32[216,128]{1,0:T(8,128)S(1)} %get-tuple-element.16), channel_id=1, source_target_pairs={{0,1},{1,2},{2,3},{3,4},{4,5},{5,6},{6,7},{7,8},{8,9},{9,10},{10,1... | collective-permute-start | bytes 331784 | tf_op jit(solution)/shard_map/ppermute | solution.py:260
  45.5 2.8 %collective-permute-done.3.refs_9_ = f32[216,128]{1,0:T(8,128)S(1)} collective-permute-done((f32[216,128]{1,0:T(8,128)S(1)}, f32[216,128]{1,0:T(8,128)S(1)}, u32[]{:S(2)}, u32[]{:S(2)}) %collective-permute-start.3) | collective-permute-done | bytes 110624 | tf_op jit(solution)/shard_map/ppermute | solution.py:259
  48.2 5.5 %collective-permute-done.4.refs_10_ = f32[216,128]{1,0:T(8,128)S(1)} collective-permute-done((f32[216,128]{1,0:T(8,128)S(1)}, f32[216,128]{1,0:T(8,128)S(1)}, u32[]{:S(2)}, u32[]{:S(2)}) %collective-permute-start.4) | collective-permute-done | bytes 110624 | tf_op jit(solution)/shard_map/ppermute | solution.py:260
  53.8 1.3 %collective-permute-start.5 = (f32[1296,128]{1,0:T(8,128)S(1)}, f32[1296,128]{1,0:T(8,128)S(1)}, u32[]{:S(2)}, u32[]{:S(2)}) collective-permute-start(f32[1296,128]{1,0:T(8,128)S(1)} %pad_maximum_fusion.1), channel_id=1, source_target_pairs={{0,64},{64,0},{1,65},{65,1},{2,66},{66,2},{3,67},{67,3},{4,68},{68... | collective-permute-start | bytes 1990664 | tf_op jit(solution)/shard_map/ppermute | solution.py:263
  55.1 1.7 %collective-permute-done.5.refs_11_.refs_12_.refs_13_.refs_14_ = f32[1296,128]{1,0:T(8,128)S(1)} collective-permute-done((f32[1296,128]{1,0:T(8,128)S(1)}, f32[1296,128]{1,0:T(8,128)S(1)}, u32[]{:S(2)}, u32[]{:S(2)}) %collective-permute-start.5) | collective-permute-done | bytes 663584 | tf_op jit(solution)/shard_map/ppermute | solution.py:263
  56.9 13.2 %shard_map.150 = (f32[6912,128]{1,0:T(8,128)S(1)}, f32[216,128]{1,0:T(8,128)S(1)}, f32[2,432,128]{2,1,0:T(8,128)S(1)}) custom-call(f32[6912,128]{1,0:T(8,128)S(1)} %bitcast.13, f32[6912,128]{1,0:T(8,128)S(1)} %get-tuple-element.15.refs_1_, f32[864,128]{1,0:T(8,128)S(1)} %broadcast_in_dim.2.refs_1_.refs_2_.refs_3_, ...), custom_call_target="tpu_custom_call" | custom-call | tf_op jit(solution)/shard_map/pallas_call | solution.py:243
  70.2 1.5 %collective-permute-start.7 = (f32[216,128]{1,0:T(8,128)S(1)}, f32[216,128]{1,0:T(8,128)S(1)}, u32[]{:S(2)}, u32[]{:S(2)}) collective-permute-start(f32[216,128]{1,0:T(8,128)S(1)} %get-tuple-element.19), channel_id=1, source_target_pairs={{0,1},{1,2},{2,3},{3,4},{4,5},{5,6},{6,7},{7,8},{8,9},{9,10},{10,1... | collective-permute-start | bytes 331784 | tf_op jit(solution)/shard_map/ppermute | solution.py:260
  71.6 2.8 %collective-permute-done.6.refs_9_ = f32[216,128]{1,0:T(8,128)S(1)} collective-permute-done((f32[216,128]{1,0:T(8,128)S(1)}, f32[216,128]{1,0:T(8,128)S(1)}, u32[]{:S(2)}, u32[]{:S(2)}) %collective-permute-start.6) | collective-permute-done | bytes 110624 | tf_op jit(solution)/shard_map/ppermute | solution.py:259
  74.4 5.4 %collective-permute-done.7.refs_10_ = f32[216,128]{1,0:T(8,128)S(1)} collective-permute-done((f32[216,128]{1,0:T(8,128)S(1)}, f32[216,128]{1,0:T(8,128)S(1)}, u32[]{:S(2)}, u32[]{:S(2)}) %collective-permute-start.7) | collective-permute-done | bytes 110624 | tf_op jit(solution)/shard_map/ppermute | solution.py:260
  79.8 1.6 %collective-permute-start.8 = (f32[1296,128]{1,0:T(8,128)S(1)}, f32[1296,128]{1,0:T(8,128)S(1)}, u32[]{:S(2)}, u32[]{:S(2)}) collective-permute-start(f32[1296,128]{1,0:T(8,128)S(1)} %pad_maximum_fusion.2), channel_id=1, source_target_pairs={{0,64},{64,0},{1,65},{65,1},{2,66},{66,2},{3,67},{67,3},{4,68},{68... | collective-permute-start | bytes 1990664 | tf_op jit(solution)/shard_map/ppermute | solution.py:263
  81.8 1.4 %collective-permute-done.8.refs_11_.refs_12_.refs_13_.refs_14_ = f32[1296,128]{1,0:T(8,128)S(1)} collective-permute-done((f32[1296,128]{1,0:T(8,128)S(1)}, f32[1296,128]{1,0:T(8,128)S(1)}, u32[]{:S(2)}, u32[]{:S(2)}) %collective-permute-start.8) | collective-permute-done | bytes 663584 | tf_op jit(solution)/shard_map/ppermute | solution.py:263
  83.2 8.0 %shard_map.151.fin_ref = f32[6912,128]{1,0:T(8,128)} custom-call(f32[6912,128]{1,0:T(8,128)S(1)} %bitcast.14, f32[6912,128]{1,0:T(8,128)S(1)} %get-tuple-element.18.refs_1_, f32[864,128]{1,0:T(8,128)S(1)} %broadcast_in_dim.2.refs_1_.refs_2_.refs_3_, f32[864,128]{1,0:T(8,128)S(1)} %broadcast_in_dim.2.refs_1_.refs_2_.refs_3_, bf16[640,128]{1,0:T(8,128)(2,1)S(1)} %copy-done.1, ...), custom_call_target="tpu_custom_call" | custom-call | tf_op jit(solution)/shard_map/pallas_call | solution.py:243
  91.2 2.0 %copy-done.2 = f32[6912,128]{1,0:T(8,128)S(1)} copy-done((f32[6912,128]{1,0:T(8,128)S(1)}, f32[6912,128]{1,0:T(8,128)}, u32[]{:S(2)}) %copy-start.2) | copy-done | bytes 3538968
  93.2 11.5 %shard_map.152 = (bf16[5760,128]{1,0:T(8,128)(2,1)}, f32[16,128]{1,0:T(8,128)S(1)}) custom-call(f32[6912,128]{1,0:T(8,128)S(1)} %copy-done.2, bf16[432,512]{1,0:T(8,128)(2,1)S(1)} %bitcast.19, bf16[512,512]{1,0:T(8,128)(2,1)S(1)} %copy-done.3, bf16[512,512]{1,0:T(8,128)(2,1)S(1)} %copy-done.4, bf16[360,512]{1,0:T(8,128)(2,1)S(1)} %copy-done.6, ...), custom_call_target="tpu_custom_call" | custom-call | tf_op jit(solution)/shard_map/pallas_call | solution.py:324
  105.6 12.8 %all_to_all.13 = f32[128,1,1]{2,1,0:T(1,128)S(1)} all-to-all(f32[128,1,1]{2,1,0:T(1,128)S(1)} %copy.20), channel_id=1, replica_groups=mesh['face'=2,'elem'=64] {'face','elem'}, dimensions={0} | all-to-all | bytes 1024 | tf_op jit(solution)/shard_map/all_to_all | solution.py:381
  (34 shorter events, 3.1 us)
Async XLA Ops:
  1.6 2.0 %copy-start = (f32[432,16,128]{2,1,0:T(8,128)S(1)}, f32[432,16,128]{2,1,0:T(8,128)}, u32[]{:S(2)}) copy-start(f32[432,16,128]{2,1,0:T(8,128)} %param.13) | copy-start | bytes 10616836
  3.6 0.9 copy-start.1
  9.4 11.0 %collective-permute-start = (f32[216,128]{1,0:T(8,128)S(1)}, f32[216,128]{1,0:T(8,128)S(1)}, u32[]{:S(2)}, u32[]{:S(2)}) collective-permute-start(f32[216,128]{1,0:T(8,128)S(1)} %get-tuple-element.13), channel_id=1, source_target_pairs={{0,63},{1,0},{2,1},{3,2},{4,3},{5,4},{6,5},{7,6},{8,7},{9,8},{10,9... | collective-permute-start | bytes 331784 | tf_op jit(solution)/shard_map/ppermute | solution.py:259
  18.7 9.0 %collective-permute-start.1 = (f32[216,128]{1,0:T(8,128)S(1)}, f32[216,128]{1,0:T(8,128)S(1)}, u32[]{:S(2)}, u32[]{:S(2)}) collective-permute-start(f32[216,128]{1,0:T(8,128)S(1)} %get-tuple-element.13), channel_id=1, source_target_pairs={{0,1},{1,2},{2,3},{3,4},{4,5},{5,6},{6,7},{7,8},{8,9},{9,10},{10,1... | collective-permute-start | bytes 331784 | tf_op jit(solution)/shard_map/ppermute | solution.py:260
  27.8 3.9 %collective-permute-start.2 = (f32[1296,128]{1,0:T(8,128)S(1)}, f32[1296,128]{1,0:T(8,128)S(1)}, u32[]{:S(2)}, u32[]{:S(2)}) collective-permute-start(f32[1296,128]{1,0:T(8,128)S(1)} %pad_maximum_fusion), channel_id=1, source_target_pairs={{0,64},{64,0},{1,65},{65,1},{2,66},{66,2},{3,67},{67,3},{4,68},{68... | collective-permute-start | bytes 1990664 | tf_op jit(solution)/shard_map/ppermute | solution.py:263
  43.9 4.3 %collective-permute-start.3 = (f32[216,128]{1,0:T(8,128)S(1)}, f32[216,128]{1,0:T(8,128)S(1)}, u32[]{:S(2)}, u32[]{:S(2)}) collective-permute-start(f32[216,128]{1,0:T(8,128)S(1)} %get-tuple-element.16), channel_id=1, source_target_pairs={{0,63},{1,0},{2,1},{3,2},{4,3},{5,4},{6,5},{7,6},{8,7},{9,8},{10,9... | collective-permute-start | bytes 331784 | tf_op jit(solution)/shard_map/ppermute | solution.py:259
  44.0 9.7 %collective-permute-start.4 = (f32[216,128]{1,0:T(8,128)S(1)}, f32[216,128]{1,0:T(8,128)S(1)}, u32[]{:S(2)}, u32[]{:S(2)}) collective-permute-start(f32[216,128]{1,0:T(8,128)S(1)} %get-tuple-element.16), channel_id=1, source_target_pairs={{0,1},{1,2},{2,3},{3,4},{4,5},{5,6},{6,7},{7,8},{8,9},{9,10},{10,1... | collective-permute-start | bytes 331784 | tf_op jit(solution)/shard_map/ppermute | solution.py:260
  53.8 3.0 %collective-permute-start.5 = (f32[1296,128]{1,0:T(8,128)S(1)}, f32[1296,128]{1,0:T(8,128)S(1)}, u32[]{:S(2)}, u32[]{:S(2)}) collective-permute-start(f32[1296,128]{1,0:T(8,128)S(1)} %pad_maximum_fusion.1), channel_id=1, source_target_pairs={{0,64},{64,0},{1,65},{65,1},{2,66},{66,2},{3,67},{67,3},{4,68},{68... | collective-permute-start | bytes 1990664 | tf_op jit(solution)/shard_map/ppermute | solution.py:263
  56.8 24.6 %copy-start.8 = (f32[360]{0:T(512)S(1)}, f32[360]{0:T(512)}, u32[]{:S(2)}) copy-start(f32[360]{0:T(512)} %param.23) | copy-start | bytes 4324
  56.9 24.6 %copy-start.9 = (f32[512]{0:T(512)S(1)}, f32[512]{0:T(512)}, u32[]{:S(2)}) copy-start(f32[512]{0:T(512)} %param.21) | copy-start | bytes 6148
  56.9 24.6 %copy-start.10 = (f32[512]{0:T(512)S(1)}, f32[512]{0:T(512)}, u32[]{:S(2)}) copy-start(f32[512]{0:T(512)} %param.19) | copy-start | bytes 6148
  56.9 24.6 %copy-start.11 = (f32[512]{0:T(512)S(1)}, f32[512]{0:T(512)}, u32[]{:S(2)}) copy-start(f32[512]{0:T(512)} %param.17) | copy-start | bytes 6148
  70.1 4.3 %collective-permute-start.6 = (f32[216,128]{1,0:T(8,128)S(1)}, f32[216,128]{1,0:T(8,128)S(1)}, u32[]{:S(2)}, u32[]{:S(2)}) collective-permute-start(f32[216,128]{1,0:T(8,128)S(1)} %get-tuple-element.19), channel_id=1, source_target_pairs={{0,63},{1,0},{2,1},{3,2},{4,3},{5,4},{6,5},{7,6},{8,7},{9,8},{10,9... | collective-permute-start | bytes 331784 | tf_op jit(solution)/shard_map/ppermute | solution.py:259
  70.2 9.6 %collective-permute-start.7 = (f32[216,128]{1,0:T(8,128)S(1)}, f32[216,128]{1,0:T(8,128)S(1)}, u32[]{:S(2)}, u32[]{:S(2)}) collective-permute-start(f32[216,128]{1,0:T(8,128)S(1)} %get-tuple-element.19), channel_id=1, source_target_pairs={{0,1},{1,2},{2,3},{3,4},{4,5},{5,6},{6,7},{7,8},{8,9},{9,10},{10,1... | collective-permute-start | bytes 331784 | tf_op jit(solution)/shard_map/ppermute | solution.py:260
  79.8 3.4 %collective-permute-start.8 = (f32[1296,128]{1,0:T(8,128)S(1)}, f32[1296,128]{1,0:T(8,128)S(1)}, u32[]{:S(2)}, u32[]{:S(2)}) collective-permute-start(f32[1296,128]{1,0:T(8,128)S(1)} %pad_maximum_fusion.2), channel_id=1, source_target_pairs={{0,64},{64,0},{1,65},{65,1},{2,66},{66,2},{3,67},{67,3},{4,68},{68... | collective-permute-start | bytes 1990664 | tf_op jit(solution)/shard_map/ppermute | solution.py:263
  83.2 8.0 %copy-start.3 = (bf16[512,512]{1,0:T(8,128)(2,1)S(1)}, bf16[512,512]{1,0:T(8,128)(2,1)}, u32[]{:S(2)}) copy-start(bf16[512,512]{1,0:T(8,128)(2,1)} %w_mid_ref.1) | copy-start | bytes 1572868
  83.2 8.0 %copy-start.4 = (bf16[512,512]{1,0:T(8,128)(2,1)S(1)}, bf16[512,512]{1,0:T(8,128)(2,1)}, u32[]{:S(2)}) copy-start(bf16[512,512]{1,0:T(8,128)(2,1)} %w_top_ref.1) | copy-start | bytes 1572868
  83.2 8.0 %copy-start.5 = (bf16[512,432]{0,1:T(8,128)(2,1)S(1)}, bf16[512,432]{0,1:T(8,128)(2,1)}, u32[]{:S(2)}) copy-start(bf16[512,432]{0,1:T(8,128)(2,1)} %param.16) | copy-start | bytes 1327108
  83.2 8.0 %copy-start.6 = (bf16[360,512]{1,0:T(8,128)(2,1)S(1)}, bf16[360,512]{1,0:T(8,128)(2,1)}, u32[]{:S(2)}) copy-start(bf16[360,512]{1,0:T(8,128)(2,1)} %w_out_ref.1) | copy-start | bytes 1105924
  91.2 2.0 %copy-start.2 = (f32[6912,128]{1,0:T(8,128)S(1)}, f32[6912,128]{1,0:T(8,128)}, u32[]{:S(2)}) copy-start(f32[6912,128]{1,0:T(8,128)} %shard_map.151.fin_ref) | copy-start | bytes 10616836
  93.2 11.5 %copy-start.7 = (s32[1,1,2048,1]{2,3,1,0:T(1,128)S(1)}, s32[1,1,2048,1]{2,3,1,0:T(1,128)}, u32[]{:S(2)}) copy-start(s32[1,1,2048,1]{2,3,1,0:T(1,128)} %param.24) | copy-start | bytes 24580

commit v11 on v9

--- a/solution.py
+++ b/solution.py
@@ -98,7 +98,7 @@
     )
 
 
-def section_kernel(*refs, first, combo, edges):
+def section_kernel(*refs, first, combo, edges, mlp):
     refs = list(refs)
     v0_ref = None if combo is None or combo[0] is None else refs.pop(0)
     sp_ref = refs.pop(0)
@@ -107,6 +107,9 @@
     if not first:
         exr_ref, exl_ref, dr_ref, dl_ref, top_ref, bottom_ref = refs[:6]
         refs = refs[6:]
+    if mlp:
+        mlp_in = refs[:5]
+        refs = refs[5:]
     rows = CHUNK
     height = 16
     sx = sx_ref[...]
@@ -151,6 +154,16 @@
     out_ref = refs[0]
     for y in range(height):
         out_ref[pl.ds(y, rows, stride=height), :] = new[y]
+    if mlp:
+        tend_ref, heat_ref, held, scratch = refs[1:5]
+        step = pl.program_id(0)
+        start = pl.multiple_of(step * rows, rows)
+        for y in range(height):
+            held[y, pl.ds(start, rows), :] = new[y]
+
+        @pl.when(step == pl.num_programs(0) - 1)
+        def _():
+            mlp_body(lambda y: held[y], *mlp_in, tend_ref, heat_ref, scratch)
     if edges:
         ex_ref, ey_ref = refs[1:3]
         tend = raw_slabs(new, sx, sy, ahi, alo)
@@ -159,7 +172,7 @@
         ey_ref[1] = tend[height - 1]
 
 
-def run_section(field_rows, v0, speeds, mats, halos, *, first, combo, edges):
+def run_section(field_rows, v0, speeds, mats, halos, *, first, combo, edges, mlp=None):
     total, width = field_rows.shape
     feats = speeds.shape[0] // 2
     steps = feats // CHUNK
@@ -200,14 +213,33 @@
         if edges:
             out_shape += [ex_shape, ey_shape]
             out_specs += [edge, rowsb]
-    kernel = functools.partial(section_kernel, first=first, combo=combo, edges=edges)
+    scratch_shapes = []
+    limit = 16
+    if mlp is not None:
+        height = field_rows.shape[0] // feats
+        outs = mlp[3].shape[0]
+        whole = lambda a: pl.BlockSpec(a.shape, lambda i: (0,) * a.ndim)
+        args += list(mlp)
+        specs += [whole(a) for a in mlp]
+        out_shape += [
+            jax.ShapeDtypeStruct((outs * height, width), jnp.bfloat16),
+            jax.ShapeDtypeStruct((height, width), jnp.float32),
+        ]
+        out_specs += [whole(out_shape[-2]), whole(out_shape[-1])]
+        scratch_shapes = [
+            pltpu.VMEM((height, feats, width), jnp.float32),
+            pltpu.VMEM((outs * height, width), jnp.float32),
+        ]
+        limit = 32
+    kernel = functools.partial(section_kernel, first=first, combo=combo, edges=edges, mlp=mlp is not None)
     return pl.pallas_call(
         kernel,
         grid=(steps,),
         in_specs=specs,
         out_specs=out_specs,
         out_shape=out_shape,
-        compiler_params=pltpu.CompilerParams(vmem_limit_bytes=16 * 1024 * 1024),
+        scratch_shapes=scratch_shapes,
+        compiler_params=pltpu.CompilerParams(vmem_limit_bytes=limit * 1024 * 1024),
     )(*args)
 
 
@@ -242,6 +274,14 @@
 
 def mlp_kernel(fin_ref, w_in_ref, w_mid_ref, w_top_ref, w_out_ref, b_ref, tend_ref, heat_ref, scratch):
     feats = w_in_ref.shape[0]
+    height = heat_ref.shape[0]
+    mlp_body(
+        lambda y: fin_ref[pl.ds(y, feats, stride=height), :],
+        w_in_ref, w_mid_ref, w_top_ref, w_out_ref, b_ref, tend_ref, heat_ref, scratch,
+    )
+
+
+def mlp_body(slab, w_in_ref, w_mid_ref, w_top_ref, w_out_ref, b_ref, tend_ref, heat_ref, scratch):
     outs = w_out_ref.shape[0]
     height = heat_ref.shape[0]
     width = heat_ref.shape[1]
@@ -257,10 +297,7 @@
 
     for pair in range(height // 2):
         y = 2 * pair
-        x = jnp.concatenate(
-            [fin_ref[pl.ds(y, feats, stride=height), :], fin_ref[pl.ds(y + 1, feats, stride=height), :]],
-            axis=1,
-        ).astype(jnp.bfloat16)
+        x = jnp.concatenate([slab(y), slab(y + 1)], axis=1).astype(jnp.bfloat16)
         h = act(
             lax.dot_general(
                 w_in_ref[...], x, (((0,), (0,)), ((), ())), preferred_element_type=jnp.float32
@@ -306,19 +343,22 @@
     combos = [(None, None), (0.75, 0.25), ("third", None)]
     for k, combo in enumerate(combos):
         halos = exchange(ex, ey)
+        extra = None
+        if k == 2:
+            biases = jnp.concatenate([b_in, b_mid, b_top, b_out]).reshape(-1, 1)
+            extra = (w_in.T, w_mid, w_top, w_out, biases)
         outs = run_section(
-            field, v0, speeds, mats, halos, first=False, combo=combo, edges=k < 2
+            field, v0, speeds, mats, halos, first=False, combo=combo, edges=k < 2, mlp=extra
         )
         if k < 2:
             field, ex, ey = outs
         else:
-            (field,) = outs
+            field, tend_rows, heat_rows = outs
     final_state = field.reshape(feats, height, breadth)
     column_count = height * breadth
     target = span_of.reshape(column_count)
     devices = lax.axis_size("face") * lax.axis_size("elem")
     span_ids = jnp.arange(devices, dtype=jnp.int32)
-    tend_rows, heat_rows = run_mlp(field, height, w_in, b_in, w_mid, b_mid, w_top, b_top, w_out, b_out)
     heating = heat_rows.reshape(column_count)
     member = (target[:, None] == span_ids[None, :]).astype(jnp.float32)
     partial_sums = jnp.sum(member * heating[:, None], axis=0)

time: 120 us -> 115 us (0.958)
  waiting for transfers between devices: 30.3 us -> 13.1 us
  starting transfers between devices: 17.4 us -> 27.6 us
  blocking collectives: 12.8 us -> 17.9 us
  local copies, waits for them, and re-layouts: 5.46 us -> 3.48 us
    ppermute x3, starting transfers between devices: 9.41 us -> 21.3 us  [exchange(): exr = lax.ppermute(ex, 'elem', from_right)]
    pallas_call x1 -> x0, Pallas kernels: 11.6 us -> none  [run_mlp(): pl.pallas_call(mlp_kernel, out_shape=[jax.ShapeDtypeStruct((outs * height...]
    pallas_call x4, Pallas kernels: 37.2 us -> 48.3 us  [run_section(): pl.pallas_call(kernel, grid=(steps,), in_specs=specs, out_specs=out_specs...]
    ppermute x3, waiting for transfers between devices: 18.2 us -> 8.22 us  [exchange(): exl = lax.ppermute(ex, 'elem', from_left)]
    ppermute x3, waiting for transfers between devices: 7.29 us -> 0.01 us  [exchange(): exr = lax.ppermute(ex, 'elem', from_right)]
    all_to_all x1, blocking collectives: 12.8 us -> 17.9 us  [local(): lax.all_to_all(partial_sums.reshape(devices, 1), ('face', 'elem'), 0, 1,...]
    unnamed x24 -> x26, local copies, waits for them, and re-layouts: 4.87 us -> 2.9 us
  transfers between devices with their start and end apart: 9 -> 9, of which waited for: 9 -> 6; matrix products, arithmetic and copies ran while one was open for 0% -> 0% of each run, Pallas kernels for 0% -> 0%
where the time goes in v11:
time: 115 us
  Pallas kernels  48.3 us (42%)
  starting transfers between devices  27.6 us (24%)
  blocking collectives  17.9 us (16%)
  waiting for transfers between devices  13.1 us (11%)
  local copies, waits for them, and re-layouts  3.48 us (3%)
  between operations  2.57 us (2%)
  other arithmetic  2.35 us (2%)
    pallas_call x4, Pallas kernels, run_section(): pl.pallas_call(kernel, grid=(steps,), in_specs=specs, out_specs=out_specs...  48.3 us
    ppermute x3, starting transfers between devices, exchange(): exr = lax.ppermute(ex, 'elem', from_right)  21.3 us
    all_to_all x1, blocking collectives, local(): lax.all_to_all(partial_sums.reshape(devices, 1), ('face', 'elem'), 0, 1,...  17.9 us
    ppermute x3, waiting for transfers between devices, exchange(): exl = lax.ppermute(ex, 'elem', from_left)  8.22 us
    ppermute x3, waiting for transfers between devices, exchange(): partner = lax.ppermute(bundle, 'face', [(0, 1), (1, 0)])  4.87 us
    ppermute x3, starting transfers between devices, exchange(): partner = lax.ppermute(bundle, 'face', [(0, 1), (1, 0)])  3.99 us
    unnamed x26, local copies, waits for them, and re-layouts  2.9 us
  transfers between devices with their start and end apart: 9, of which 6 were waited for; matrix products, arithmetic and copies ran while one was open for 0% of the time, Pallas kernels for 0%

profile of v11, /device:TPU:1, one launch (start us, length us, event | category | flops | bytes accessed | tf_op | source)
XLA Modules:
  0.0 115.2 jit_solution(13938329905712218026)
XLA Ops:
  0.6 0.8 pad_maximum_fusion.4
  1.6 2.0 %copy-done = f32[432,16,128]{2,1,0:T(8,128)S(1)} copy-done((f32[432,16,128]{2,1,0:T(8,128)S(1)}, f32[432,16,128]{2,1,0:T(8,128)}, u32[]{:S(2)}) %copy-start) | copy-done | bytes 3538968
  3.6 0.8 copy-done.2
  4.4 4.9 %shard_map.148 = (f32[216,128]{1,0:T(8,128)S(1)}, f32[2,432,128]{2,1,0:T(8,128)S(1)}) custom-call(f32[6912,128]{1,0:T(8,128)S(1)} %bitcast.11, f32[864,128]{1,0:T(8,128)S(1)} %broadcast_in_dim.2.refs_1_.refs_2_.refs_3_, f32[864,128]{1,0:T(8,128)S(1)} %broadcast_in_dim.2.refs_1_.refs_2_.refs_3_, bf16[256,128]{1,0:T(8,128)(2,1)S(1)} %copy-done.2, ...), custom_call_target="tpu_custom_call" | custom-call | tf_op jit(solution)/shard_map/pallas_call | solution.py:235
  9.4 2.1 %collective-permute-start.1 = (f32[216,128]{1,0:T(8,128)S(1)}, f32[216,128]{1,0:T(8,128)S(1)}, u32[]{:S(2)}, u32[]{:S(2)}) collective-permute-start(f32[216,128]{1,0:T(8,128)S(1)} %get-tuple-element.14), channel_id=1, source_target_pairs={{0,1},{1,2},{2,3},{3,4},{4,5},{5,6},{6,7},{7,8},{8,9},{9,10},{10,1... | collective-permute-start | bytes 331784 | tf_op jit(solution)/shard_map/ppermute | solution.py:253
  11.4 7.3 %collective-permute-start = (f32[216,128]{1,0:T(8,128)S(1)}, f32[216,128]{1,0:T(8,128)S(1)}, u32[]{:S(2)}, u32[]{:S(2)}) collective-permute-start(f32[216,128]{1,0:T(8,128)S(1)} %get-tuple-element.14), channel_id=1, source_target_pairs={{0,63},{1,0},{2,1},{3,2},{4,3},{5,4},{6,5},{7,6},{8,7},{9,8},{10,9... | collective-permute-start | bytes 331784 | tf_op jit(solution)/shard_map/ppermute | solution.py:252
  18.7 2.7 %collective-permute-done.1.refs_6_ = f32[216,128]{1,0:T(8,128)S(1)} collective-permute-done((f32[216,128]{1,0:T(8,128)S(1)}, f32[216,128]{1,0:T(8,128)S(1)}, u32[]{:S(2)}, u32[]{:S(2)}) %collective-permute-start.1) | collective-permute-done | bytes 110624 | tf_op jit(solution)/shard_map/ppermute | solution.py:253
  21.4 1.3 %collective-permute-start.2 = (f32[1296,128]{1,0:T(8,128)S(1)}, f32[1296,128]{1,0:T(8,128)S(1)}, u32[]{:S(2)}, u32[]{:S(2)}) collective-permute-start(f32[1296,128]{1,0:T(8,128)S(1)} %pad_maximum_fusion), channel_id=1, source_target_pairs={{0,64},{64,0},{1,65},{65,1},{2,66},{66,2},{3,67},{67,3},{4,68},{68... | collective-permute-start | bytes 1990664 | tf_op jit(solution)/shard_map/ppermute | solution.py:256
  22.8 1.7 %collective-permute-done.2.refs_7_.refs_8_.refs_9_.refs_10_ = f32[1296,128]{1,0:T(8,128)S(1)} collective-permute-done((f32[1296,128]{1,0:T(8,128)S(1)}, f32[1296,128]{1,0:T(8,128)S(1)}, u32[]{:S(2)}, u32[]{:S(2)}) %collective-permute-start.2) | collective-permute-done | bytes 663584 | tf_op jit(solution)/shard_map/ppermute | solution.py:256
  24.5 11.8 %shard_map.149 = (f32[6912,128]{1,0:T(8,128)S(1)}, f32[216,128]{1,0:T(8,128)S(1)}, f32[2,432,128]{2,1,0:T(8,128)S(1)}) custom-call(f32[6912,128]{1,0:T(8,128)S(1)} %bitcast.12, f32[864,128]{1,0:T(8,128)S(1)} %broadcast_in_dim.2.refs_1_.refs_2_.refs_3_, f32[864,128]{1,0:T(8,128)S(1)} %broadcast_in_dim.2.refs_1_.refs_2_.refs_3_, ...), custom_call_target="tpu_custom_call" | custom-call | tf_op jit(solution)/shard_map/pallas_call | solution.py:235
  36.4 7.0 %collective-permute-start.3 = (f32[216,128]{1,0:T(8,128)S(1)}, f32[216,128]{1,0:T(8,128)S(1)}, u32[]{:S(2)}, u32[]{:S(2)}) collective-permute-start(f32[216,128]{1,0:T(8,128)S(1)} %get-tuple-element.17), channel_id=1, source_target_pairs={{0,63},{1,0},{2,1},{3,2},{4,3},{5,4},{6,5},{7,6},{8,7},{9,8},{10,9... | collective-permute-start | bytes 331784 | tf_op jit(solution)/shard_map/ppermute | solution.py:252
  43.5 2.8 %collective-permute-done.4.refs_7_ = f32[216,128]{1,0:T(8,128)S(1)} collective-permute-done((f32[216,128]{1,0:T(8,128)S(1)}, f32[216,128]{1,0:T(8,128)S(1)}, u32[]{:S(2)}, u32[]{:S(2)}) %collective-permute-start.4) | collective-permute-done | bytes 110624 | tf_op jit(solution)/shard_map/ppermute | solution.py:253
  46.3 1.2 %collective-permute-start.5 = (f32[1296,128]{1,0:T(8,128)S(1)}, f32[1296,128]{1,0:T(8,128)S(1)}, u32[]{:S(2)}, u32[]{:S(2)}) collective-permute-start(f32[1296,128]{1,0:T(8,128)S(1)} %pad_maximum_fusion.1), channel_id=1, source_target_pairs={{0,64},{64,0},{1,65},{65,1},{2,66},{66,2},{3,67},{67,3},{4,68},{68... | collective-permute-start | bytes 1990664 | tf_op jit(solution)/shard_map/ppermute | solution.py:256
  47.5 1.7 %collective-permute-done.5.refs_8_.refs_9_.refs_10_.refs_11_ = f32[1296,128]{1,0:T(8,128)S(1)} collective-permute-done((f32[1296,128]{1,0:T(8,128)S(1)}, f32[1296,128]{1,0:T(8,128)S(1)}, u32[]{:S(2)}, u32[]{:S(2)}) %collective-permute-start.5) | collective-permute-done | bytes 663584 | tf_op jit(solution)/shard_map/ppermute | solution.py:256
  49.3 12.3 %shard_map.150 = (f32[6912,128]{1,0:T(8,128)S(1)}, f32[216,128]{1,0:T(8,128)S(1)}, f32[2,432,128]{2,1,0:T(8,128)S(1)}) custom-call(f32[6912,128]{1,0:T(8,128)S(1)} %bitcast.13, f32[6912,128]{1,0:T(8,128)S(1)} %get-tuple-element.16.refs_1_, f32[864,128]{1,0:T(8,128)S(1)} %broadcast_in_dim.2.refs_1_.refs_2_.refs_3_, ...), custom_call_target="tpu_custom_call" | custom-call | tf_op jit(solution)/shard_map/pallas_call | solution.py:235
  61.7 7.0 %collective-permute-start.6 = (f32[216,128]{1,0:T(8,128)S(1)}, f32[216,128]{1,0:T(8,128)S(1)}, u32[]{:S(2)}, u32[]{:S(2)}) collective-permute-start(f32[216,128]{1,0:T(8,128)S(1)} %get-tuple-element.20), channel_id=1, source_target_pairs={{0,63},{1,0},{2,1},{3,2},{4,3},{5,4},{6,5},{7,6},{8,7},{9,8},{10,9... | collective-permute-start | bytes 331784 | tf_op jit(solution)/shard_map/ppermute | solution.py:252
  68.7 2.8 %collective-permute-done.7.refs_7_ = f32[216,128]{1,0:T(8,128)S(1)} collective-permute-done((f32[216,128]{1,0:T(8,128)S(1)}, f32[216,128]{1,0:T(8,128)S(1)}, u32[]{:S(2)}, u32[]{:S(2)}) %collective-permute-start.7) | collective-permute-done | bytes 110624 | tf_op jit(solution)/shard_map/ppermute | solution.py:253
  71.6 1.4 %collective-permute-start.8 = (f32[1296,128]{1,0:T(8,128)S(1)}, f32[1296,128]{1,0:T(8,128)S(1)}, u32[]{:S(2)}, u32[]{:S(2)}) collective-permute-start(f32[1296,128]{1,0:T(8,128)S(1)} %pad_maximum_fusion.2), channel_id=1, source_target_pairs={{0,64},{64,0},{1,65},{65,1},{2,66},{66,2},{3,67},{67,3},{4,68},{68... | collective-permute-start | bytes 1990664 | tf_op jit(solution)/shard_map/ppermute | solution.py:256
  73.0 0.3 reshape.47.refs_16_
  73.3 1.4 %collective-permute-done.8.refs_8_.refs_9_.refs_10_.refs_11_ = f32[1296,128]{1,0:T(8,128)S(1)} collective-permute-done((f32[1296,128]{1,0:T(8,128)S(1)}, f32[1296,128]{1,0:T(8,128)S(1)}, u32[]{:S(2)}, u32[]{:S(2)}) %collective-permute-start.8) | collective-permute-done | bytes 663584 | tf_op jit(solution)/shard_map/ppermute | solution.py:256
  74.8 19.2 %shard_map.151 = (f32[6912,128]{1,0:T(8,128)}, bf16[5760,128]{1,0:T(8,128)(2,1)}, f32[16,128]{1,0:T(8,128)S(1)}) custom-call(f32[6912,128]{1,0:T(8,128)S(1)} %bitcast.14, f32[6912,128]{1,0:T(8,128)S(1)} %get-tuple-element.19.refs_1_, f32[864,128]{1,0:T(8,128)S(1)} %broadcast_in_dim.2.refs_1_.refs_2_.refs_3_, ...), custom_call_target="tpu_custom_call" | custom-call | tf_op jit(solution)/shard_map/pallas_call | solution.py:235
  94.0 0.7 select_reduce_fusion
  94.8 17.9 %all_to_all.13 = f32[128,1,1]{2,1,0:T(1,128)S(1)} all-to-all(f32[128,1,1]{2,1,0:T(1,128)S(1)} %copy.20), channel_id=1, replica_groups=mesh['face'=2,'elem'=64] {'face','elem'}, dimensions={0} | all-to-all | bytes 1024 | tf_op jit(solution)/shard_map/all_to_all | solution.py:365
  112.7 0.7 reduce_sum.19
  (35 shorter events, 0.6 us)
Async XLA Ops:
  1.6 2.0 %copy-start = (f32[432,16,128]{2,1,0:T(8,128)S(1)}, f32[432,16,128]{2,1,0:T(8,128)}, u32[]{:S(2)}) copy-start(f32[432,16,128]{2,1,0:T(8,128)} %param.13) | copy-start | bytes 10616836
  3.6 0.8 copy-start.2
  9.4 12.0 %collective-permute-start.1 = (f32[216,128]{1,0:T(8,128)S(1)}, f32[216,128]{1,0:T(8,128)S(1)}, u32[]{:S(2)}, u32[]{:S(2)}) collective-permute-start(f32[216,128]{1,0:T(8,128)S(1)} %get-tuple-element.14), channel_id=1, source_target_pairs={{0,1},{1,2},{2,3},{3,4},{4,5},{5,6},{6,7},{7,8},{8,9},{9,10},{10,1... | collective-permute-start | bytes 331784 | tf_op jit(solution)/shard_map/ppermute | solution.py:253
  11.4 10.0 %collective-permute-start = (f32[216,128]{1,0:T(8,128)S(1)}, f32[216,128]{1,0:T(8,128)S(1)}, u32[]{:S(2)}, u32[]{:S(2)}) collective-permute-start(f32[216,128]{1,0:T(8,128)S(1)} %get-tuple-element.14), channel_id=1, source_target_pairs={{0,63},{1,0},{2,1},{3,2},{4,3},{5,4},{6,5},{7,6},{8,7},{9,8},{10,9... | collective-permute-start | bytes 331784 | tf_op jit(solution)/shard_map/ppermute | solution.py:252
  21.4 3.1 %collective-permute-start.2 = (f32[1296,128]{1,0:T(8,128)S(1)}, f32[1296,128]{1,0:T(8,128)S(1)}, u32[]{:S(2)}, u32[]{:S(2)}) collective-permute-start(f32[1296,128]{1,0:T(8,128)S(1)} %pad_maximum_fusion), channel_id=1, source_target_pairs={{0,64},{64,0},{1,65},{65,1},{2,66},{66,2},{3,67},{67,3},{4,68},{68... | collective-permute-start | bytes 1990664 | tf_op jit(solution)/shard_map/ppermute | solution.py:256
  36.4 9.9 %collective-permute-start.4 = (f32[216,128]{1,0:T(8,128)S(1)}, f32[216,128]{1,0:T(8,128)S(1)}, u32[]{:S(2)}, u32[]{:S(2)}) collective-permute-start(f32[216,128]{1,0:T(8,128)S(1)} %get-tuple-element.17), channel_id=1, source_target_pairs={{0,1},{1,2},{2,3},{3,4},{4,5},{5,6},{6,7},{7,8},{8,9},{9,10},{10,1... | collective-permute-start | bytes 331784 | tf_op jit(solution)/shard_map/ppermute | solution.py:253
  36.4 9.8 %collective-permute-start.3 = (f32[216,128]{1,0:T(8,128)S(1)}, f32[216,128]{1,0:T(8,128)S(1)}, u32[]{:S(2)}, u32[]{:S(2)}) collective-permute-start(f32[216,128]{1,0:T(8,128)S(1)} %get-tuple-element.17), channel_id=1, source_target_pairs={{0,63},{1,0},{2,1},{3,2},{4,3},{5,4},{6,5},{7,6},{8,7},{9,8},{10,9... | collective-permute-start | bytes 331784 | tf_op jit(solution)/shard_map/ppermute | solution.py:252
  46.3 3.0 %collective-permute-start.5 = (f32[1296,128]{1,0:T(8,128)S(1)}, f32[1296,128]{1,0:T(8,128)S(1)}, u32[]{:S(2)}, u32[]{:S(2)}) collective-permute-start(f32[1296,128]{1,0:T(8,128)S(1)} %pad_maximum_fusion.1), channel_id=1, source_target_pairs={{0,64},{64,0},{1,65},{65,1},{2,66},{66,2},{3,67},{67,3},{4,68},{68... | collective-permute-start | bytes 1990664 | tf_op jit(solution)/shard_map/ppermute | solution.py:256
  49.3 23.7 %copy-start.9 = (f32[360]{0:T(512)S(1)}, f32[360]{0:T(512)}, u32[]{:S(2)}) copy-start(f32[360]{0:T(512)} %param.23) | copy-start | bytes 4324
  49.3 23.7 %copy-start.10 = (f32[512]{0:T(512)S(1)}, f32[512]{0:T(512)}, u32[]{:S(2)}) copy-start(f32[512]{0:T(512)} %param.21) | copy-start | bytes 6148
  49.3 23.7 %copy-start.11 = (f32[512]{0:T(512)S(1)}, f32[512]{0:T(512)}, u32[]{:S(2)}) copy-start(f32[512]{0:T(512)} %param.19) | copy-start | bytes 6148
  49.3 23.7 %copy-start.12 = (f32[512]{0:T(512)S(1)}, f32[512]{0:T(512)}, u32[]{:S(2)}) copy-start(f32[512]{0:T(512)} %param.17) | copy-start | bytes 6148
  49.3 25.5 %copy-start.1 = (f32[432,16,128]{2,1,0:T(8,128)S(1)}, f32[432,16,128]{2,1,0:T(8,128)}, u32[]{:S(2)}) copy-start(f32[432,16,128]{2,1,0:T(8,128)} %param.13) | copy-start | bytes 10616836
  49.3 25.5 %copy-start.3 = (bf16[256,128]{1,0:T(8,128)(2,1)S(1)}, bf16[256,128]{1,0:T(8,128)(2,1)}, u32[]{:S(2)}) copy-start(bf16[256,128]{1,0:T(8,128)(2,1)} %constant.9.clone.refs_3_.refs_4_.refs_5_) | copy-start | bytes 196612
  49.3 25.4 %copy-start.4 = (bf16[512,512]{1,0:T(8,128)(2,1)S(1)}, bf16[512,512]{1,0:T(8,128)(2,1)}, u32[]{:S(2)}) copy-start(bf16[512,512]{1,0:T(8,128)(2,1)} %refs_13_.1) | copy-start | bytes 1572868
  49.3 25.4 %copy-start.5 = (bf16[512,512]{1,0:T(8,128)(2,1)S(1)}, bf16[512,512]{1,0:T(8,128)(2,1)}, u32[]{:S(2)}) copy-start(bf16[512,512]{1,0:T(8,128)(2,1)} %refs_14_.1) | copy-start | bytes 1572868
  49.3 25.4 %copy-start.6 = (bf16[512,432]{0,1:T(8,128)(2,1)S(1)}, bf16[512,432]{0,1:T(8,128)(2,1)}, u32[]{:S(2)}) copy-start(bf16[512,432]{0,1:T(8,128)(2,1)} %param.16) | copy-start | bytes 1327108
  49.3 25.4 %copy-start.7 = (bf16[360,512]{1,0:T(8,128)(2,1)S(1)}, bf16[360,512]{1,0:T(8,128)(2,1)}, u32[]{:S(2)}) copy-start(bf16[360,512]{1,0:T(8,128)(2,1)} %refs_15_.1) | copy-start | bytes 1105924
  61.6 9.9 %collective-permute-start.7 = (f32[216,128]{1,0:T(8,128)S(1)}, f32[216,128]{1,0:T(8,128)S(1)}, u32[]{:S(2)}, u32[]{:S(2)}) collective-permute-start(f32[216,128]{1,0:T(8,128)S(1)} %get-tuple-element.20), channel_id=1, source_target_pairs={{0,1},{1,2},{2,3},{3,4},{4,5},{5,6},{6,7},{7,8},{8,9},{9,10},{10,1... | collective-permute-start | bytes 331784 | tf_op jit(solution)/shard_map/ppermute | solution.py:253
  61.7 9.8 %collective-permute-start.6 = (f32[216,128]{1,0:T(8,128)S(1)}, f32[216,128]{1,0:T(8,128)S(1)}, u32[]{:S(2)}, u32[]{:S(2)}) collective-permute-start(f32[216,128]{1,0:T(8,128)S(1)} %get-tuple-element.20), channel_id=1, source_target_pairs={{0,63},{1,0},{2,1},{3,2},{4,3},{5,4},{6,5},{7,6},{8,7},{9,8},{10,9... | collective-permute-start | bytes 331784 | tf_op jit(solution)/shard_map/ppermute | solution.py:252
  71.6 3.2 %collective-permute-start.8 = (f32[1296,128]{1,0:T(8,128)S(1)}, f32[1296,128]{1,0:T(8,128)S(1)}, u32[]{:S(2)}, u32[]{:S(2)}) collective-permute-start(f32[1296,128]{1,0:T(8,128)S(1)} %pad_maximum_fusion.2), channel_id=1, source_target_pairs={{0,64},{64,0},{1,65},{65,1},{2,66},{66,2},{3,67},{67,3},{4,68},{68... | collective-permute-start | bytes 1990664 | tf_op jit(solution)/shard_map/ppermute | solution.py:256
  74.8 19.2 %copy-start.8 = (s32[1,1,2048,1]{2,3,1,0:T(1,128)S(1)}, s32[1,1,2048,1]{2,3,1,0:T(1,128)}, u32[]{:S(2)}) copy-start(s32[1,1,2048,1]{2,3,1,0:T(1,128)} %param.24) | copy-start | bytes 24580

commit v12 on v11

--- a/solution.py
+++ b/solution.py
@@ -190,14 +190,14 @@
     args += [field_rows, speeds, speeds, mats, mats]
     specs += [big, small, small_y, const, const_lo]
     if not first:
-        exr, exl, partner = halos
+        exr, exl, corners, rows = halos
         blocks = field_rows.shape[0] // (CHUNK * 16)
-        args += [exr, exl, partner, partner, partner, partner]
+        args += [exr, exl, corners, corners, rows, rows]
         specs += [
             edge,
             edge,
-            pl.BlockSpec((FOLD, width), lambda i: (4 * blocks + i, 0)),
-            pl.BlockSpec((FOLD, width), lambda i: (5 * blocks + i, 0)),
+            pl.BlockSpec((FOLD, width), lambda i: (i, 0)),
+            pl.BlockSpec((FOLD, width), lambda i: (blocks + i, 0)),
             pl.BlockSpec((CHUNK, width), lambda i: (i, 0)),
             pl.BlockSpec((CHUNK, width), lambda i: (blocks + i, 0)),
         ]
@@ -252,9 +252,10 @@
     exr = lax.ppermute(ex, "elem", from_right)
     exl = lax.ppermute(ex, "elem", from_left)
     feats = ey.shape[1]
-    bundle = jnp.concatenate([ey.reshape(2 * feats, ey.shape[2]), exr, exl], axis=0)
-    partner = lax.ppermute(bundle, "face", [(0, 1), (1, 0)])
-    return (exr, exl, partner)
+    swap = [(0, 1), (1, 0)]
+    rows = lax.ppermute(ey.reshape(2 * feats, ey.shape[2]), "face", swap)
+    corners = lax.ppermute(jnp.concatenate([exr, exl], axis=0), "face", swap)
+    return (exr, exl, corners, rows)
 
 
 def column_model(inputs, w_in, b_in, w_mid, b_mid, w_top, b_top, w_out, b_out):

time: 115 us -> 113 us (0.983)
  waiting for transfers between devices: 13.1 us -> 8.69 us
  starting transfers between devices: 27.6 us -> 30.1 us
    ppermute x3, waiting for transfers between devices: 8.22 us -> 5.71 us  [exchange(): exl = lax.ppermute(ex, 'elem', from_left)]
    ppermute x3 -> x6, starting transfers between devices: 3.99 us -> 6.5 us  [the longest x3 3.98 us: exchange(): corners = lax.ppermute(jnp.concatenate([exr, exl], axis=0), 'face', swap)]
    ppermute x3 -> x6, waiting for transfers between devices: 4.87 us -> 2.98 us  [the longest x3 2.97 us: exchange(): corners = lax.ppermute(jnp.concatenate([exr, exl], axis=0), 'face', swap)]
  transfers between devices with their start and end apart: 9 -> 12, of which waited for: 6 -> 6; matrix products, arithmetic and copies ran while one was open for 0% -> 0% of each run, Pallas kernels for 0% -> 0%
where the time goes in v12:
time: 113 us
  Pallas kernels  48.1 us (43%)
  starting transfers between devices  30.1 us (27%)
  blocking collectives  17.8 us (16%)
  waiting for transfers between devices  8.69 us (8%)
  local copies, waits for them, and re-layouts  3.49 us (3%)
  between operations  2.59 us (2%)
  other arithmetic  2.26 us (2%)
    pallas_call x4, Pallas kernels, run_section(): pl.pallas_call(kernel, grid=(steps,), in_specs=specs, out_specs=out_specs...  48.1 us
    ppermute x3, starting transfers between devices, exchange(): exr = lax.ppermute(ex, 'elem', from_right)  21.3 us
    all_to_all x1, blocking collectives, local(): lax.all_to_all(partial_sums.reshape(devices, 1), ('face', 'elem'), 0, 1,...  17.8 us
    ppermute x3, waiting for transfers between devices, exchange(): exl = lax.ppermute(ex, 'elem', from_left)  5.71 us
    ppermute x3, starting transfers between devices, exchange(): corners = lax.ppermute(jnp.concatenate([exr, exl], axis=0), 'face', swap)  3.98 us
    ppermute x3, waiting for transfers between devices, exchange(): corners = lax.ppermute(jnp.concatenate([exr, exl], axis=0), 'face', swap)  2.97 us
    unnamed x26, local copies, waits for them, and re-layouts  2.9 us
    ppermute x3, starting transfers between devices, exchange(): rows = lax.ppermute(ey.reshape(2 * feats, ey.shape[2]), 'face', swap)  2.52 us
  transfers between devices with their start and end apart: 12, of which 6 were waited for; matrix products, arithmetic and copies ran while one was open for 0% of the time, Pallas kernels for 0%

profile of v12, /device:TPU:1, one launch (start us, length us, event | category | flops | bytes accessed | tf_op | source)
XLA Modules:
  0.0 113.1 jit_solution(1638574400143383741)
XLA Ops:
  0.6 0.8 pad_maximum_fusion.4
  1.6 2.0 %copy-done = f32[432,16,128]{2,1,0:T(8,128)S(1)} copy-done((f32[432,16,128]{2,1,0:T(8,128)S(1)}, f32[432,16,128]{2,1,0:T(8,128)}, u32[]{:S(2)}) %copy-start) | copy-done | bytes 3538968
  3.6 0.8 copy-done.2
  4.4 4.9 %shard_map.148 = (f32[216,128]{1,0:T(8,128)S(1)}, f32[2,432,128]{2,1,0:T(8,128)S(1)}) custom-call(f32[6912,128]{1,0:T(8,128)S(1)} %bitcast.11, f32[864,128]{1,0:T(8,128)S(1)} %broadcast_in_dim.2.refs_1_.refs_2_.refs_3_, f32[864,128]{1,0:T(8,128)S(1)} %broadcast_in_dim.2.refs_1_.refs_2_.refs_3_, bf16[256,128]{1,0:T(8,128)(2,1)S(1)} %copy-done.2, ...), custom_call_target="tpu_custom_call" | custom-call | tf_op jit(solution)/shard_map/pallas_call | solution.py:235
  9.4 2.1 %collective-permute-start.1 = (f32[216,128]{1,0:T(8,128)S(1)}, f32[216,128]{1,0:T(8,128)S(1)}, u32[]{:S(2)}, u32[]{:S(2)}) collective-permute-start(f32[216,128]{1,0:T(8,128)S(1)} %get-tuple-element.14), channel_id=1, source_target_pairs={{0,1},{1,2},{2,3},{3,4},{4,5},{5,6},{6,7},{7,8},{8,9},{9,10},{10,1... | collective-permute-start | bytes 331784 | tf_op jit(solution)/shard_map/ppermute | solution.py:253
  11.4 7.3 %collective-permute-start = (f32[216,128]{1,0:T(8,128)S(1)}, f32[216,128]{1,0:T(8,128)S(1)}, u32[]{:S(2)}, u32[]{:S(2)}) collective-permute-start(f32[216,128]{1,0:T(8,128)S(1)} %get-tuple-element.14), channel_id=1, source_target_pairs={{0,63},{1,0},{2,1},{3,2},{4,3},{5,4},{6,5},{7,6},{8,7},{9,8},{10,9... | collective-permute-start | bytes 331784 | tf_op jit(solution)/shard_map/ppermute | solution.py:252
  18.7 1.0 collective-permute-start.3
  19.7 1.7 %collective-permute-done.1.refs_6_ = f32[216,128]{1,0:T(8,128)S(1)} collective-permute-done((f32[216,128]{1,0:T(8,128)S(1)}, f32[216,128]{1,0:T(8,128)S(1)}, u32[]{:S(2)}, u32[]{:S(2)}) %collective-permute-start.1) | collective-permute-done | bytes 110624 | tf_op jit(solution)/shard_map/ppermute | solution.py:253
  21.4 1.3 %collective-permute-start.2 = (f32[432,128]{1,0:T(8,128)S(1)}, f32[432,128]{1,0:T(8,128)S(1)}, u32[]{:S(2)}, u32[]{:S(2)}) collective-permute-start(f32[432,128]{1,0:T(8,128)S(1)} %pad_maximum_fusion), channel_id=1, source_target_pairs={{0,64},{64,0},{1,65},{65,1},{2,66},{66,2},{3,67},{67,3},{4,68},{68... | collective-permute-start | bytes 663560 | tf_op jit(solution)/shard_map/ppermute | solution.py:257
  22.8 1.1 collective-permute-done.2.refs_7_.refs_8_
  23.9 11.8 %shard_map.149 = (f32[6912,128]{1,0:T(8,128)S(1)}, f32[216,128]{1,0:T(8,128)S(1)}, f32[2,432,128]{2,1,0:T(8,128)S(1)}) custom-call(f32[6912,128]{1,0:T(8,128)S(1)} %bitcast.12, f32[864,128]{1,0:T(8,128)S(1)} %broadcast_in_dim.2.refs_1_.refs_2_.refs_3_, f32[864,128]{1,0:T(8,128)S(1)} %broadcast_in_dim.2.refs_1_.refs_2_.refs_3_, ...), custom_call_target="tpu_custom_call" | custom-call | tf_op jit(solution)/shard_map/pallas_call | solution.py:235
  35.7 7.0 %collective-permute-start.4 = (f32[216,128]{1,0:T(8,128)S(1)}, f32[216,128]{1,0:T(8,128)S(1)}, u32[]{:S(2)}, u32[]{:S(2)}) collective-permute-start(f32[216,128]{1,0:T(8,128)S(1)} %get-tuple-element.17), channel_id=1, source_target_pairs={{0,63},{1,0},{2,1},{3,2},{4,3},{5,4},{6,5},{7,6},{8,7},{9,8},{10,9... | collective-permute-start | bytes 331784 | tf_op jit(solution)/shard_map/ppermute | solution.py:252
  42.8 0.8 collective-permute-start.7
  43.5 2.0 %collective-permute-done.5.refs_7_ = f32[216,128]{1,0:T(8,128)S(1)} collective-permute-done((f32[216,128]{1,0:T(8,128)S(1)}, f32[216,128]{1,0:T(8,128)S(1)}, u32[]{:S(2)}, u32[]{:S(2)}) %collective-permute-start.5) | collective-permute-done | bytes 110624 | tf_op jit(solution)/shard_map/ppermute | solution.py:253
  45.6 1.2 %collective-permute-start.6 = (f32[432,128]{1,0:T(8,128)S(1)}, f32[432,128]{1,0:T(8,128)S(1)}, u32[]{:S(2)}, u32[]{:S(2)}) collective-permute-start(f32[432,128]{1,0:T(8,128)S(1)} %pad_maximum_fusion.1), channel_id=1, source_target_pairs={{0,64},{64,0},{1,65},{65,1},{2,66},{66,2},{3,67},{67,3},{4,68},{68... | collective-permute-start | bytes 663560 | tf_op jit(solution)/shard_map/ppermute | solution.py:257
  46.8 1.1 collective-permute-done.6.refs_8_.refs_9_
  48.0 12.2 %shard_map.150 = (f32[6912,128]{1,0:T(8,128)S(1)}, f32[216,128]{1,0:T(8,128)S(1)}, f32[2,432,128]{2,1,0:T(8,128)S(1)}) custom-call(f32[6912,128]{1,0:T(8,128)S(1)} %bitcast.13, f32[6912,128]{1,0:T(8,128)S(1)} %get-tuple-element.16.refs_1_, f32[864,128]{1,0:T(8,128)S(1)} %broadcast_in_dim.2.refs_1_.refs_2_.refs_3_, ...), custom_call_target="tpu_custom_call" | custom-call | tf_op jit(solution)/shard_map/pallas_call | solution.py:235
  60.3 7.0 %collective-permute-start.8 = (f32[216,128]{1,0:T(8,128)S(1)}, f32[216,128]{1,0:T(8,128)S(1)}, u32[]{:S(2)}, u32[]{:S(2)}) collective-permute-start(f32[216,128]{1,0:T(8,128)S(1)} %get-tuple-element.20), channel_id=1, source_target_pairs={{0,63},{1,0},{2,1},{3,2},{4,3},{5,4},{6,5},{7,6},{8,7},{9,8},{10,9... | collective-permute-start | bytes 331784 | tf_op jit(solution)/shard_map/ppermute | solution.py:252
  67.3 0.8 collective-permute-start.11
  68.1 2.0 %collective-permute-done.9.refs_7_ = f32[216,128]{1,0:T(8,128)S(1)} collective-permute-done((f32[216,128]{1,0:T(8,128)S(1)}, f32[216,128]{1,0:T(8,128)S(1)}, u32[]{:S(2)}, u32[]{:S(2)}) %collective-permute-start.9) | collective-permute-done | bytes 110624 | tf_op jit(solution)/shard_map/ppermute | solution.py:253
  70.1 1.4 %collective-permute-start.10 = (f32[432,128]{1,0:T(8,128)S(1)}, f32[432,128]{1,0:T(8,128)S(1)}, u32[]{:S(2)}, u32[]{:S(2)}) collective-permute-start(f32[432,128]{1,0:T(8,128)S(1)} %pad_maximum_fusion.2), channel_id=1, source_target_pairs={{0,64},{64,0},{1,65},{65,1},{2,66},{66,2},{3,67},{67,3},{4,68},{68... | collective-permute-start | bytes 663560 | tf_op jit(solution)/shard_map/ppermute | solution.py:257
  71.9 0.8 collective-permute-done.10.refs_8_.refs_9_
  72.7 19.2 %shard_map.151 = (f32[6912,128]{1,0:T(8,128)}, bf16[5760,128]{1,0:T(8,128)(2,1)}, f32[16,128]{1,0:T(8,128)S(1)}) custom-call(f32[6912,128]{1,0:T(8,128)S(1)} %bitcast.14, f32[6912,128]{1,0:T(8,128)S(1)} %get-tuple-element.19.refs_1_, f32[864,128]{1,0:T(8,128)S(1)} %broadcast_in_dim.2.refs_1_.refs_2_.refs_3_, ...), custom_call_target="tpu_custom_call" | custom-call | tf_op jit(solution)/shard_map/pallas_call | solution.py:235
  92.7 17.8 %all_to_all.13 = f32[128,1,1]{2,1,0:T(1,128)S(1)} all-to-all(f32[128,1,1]{2,1,0:T(1,128)S(1)} %copy.20), channel_id=1, replica_groups=mesh['face'=2,'elem'=64] {'face','elem'}, dimensions={0} | all-to-all | bytes 1024 | tf_op jit(solution)/shard_map/all_to_all | solution.py:366
  (41 shorter events, 2.3 us)
Async XLA Ops:
  1.6 2.0 %copy-start = (f32[432,16,128]{2,1,0:T(8,128)S(1)}, f32[432,16,128]{2,1,0:T(8,128)}, u32[]{:S(2)}) copy-start(f32[432,16,128]{2,1,0:T(8,128)} %param.13) | copy-start | bytes 10616836
  9.4 12.0 %collective-permute-start.1 = (f32[216,128]{1,0:T(8,128)S(1)}, f32[216,128]{1,0:T(8,128)S(1)}, u32[]{:S(2)}, u32[]{:S(2)}) collective-permute-start(f32[216,128]{1,0:T(8,128)S(1)} %get-tuple-element.14), channel_id=1, source_target_pairs={{0,1},{1,2},{2,3},{3,4},{4,5},{5,6},{6,7},{7,8},{8,9},{9,10},{10,1... | collective-permute-start | bytes 331784 | tf_op jit(solution)/shard_map/ppermute | solution.py:253
  11.4 10.0 %collective-permute-start = (f32[216,128]{1,0:T(8,128)S(1)}, f32[216,128]{1,0:T(8,128)S(1)}, u32[]{:S(2)}, u32[]{:S(2)}) collective-permute-start(f32[216,128]{1,0:T(8,128)S(1)} %get-tuple-element.14), channel_id=1, source_target_pairs={{0,63},{1,0},{2,1},{3,2},{4,3},{5,4},{6,5},{7,6},{8,7},{9,8},{10,9... | collective-permute-start | bytes 331784 | tf_op jit(solution)/shard_map/ppermute | solution.py:252
  18.7 5.1 %collective-permute-start.3 = (f32[864,128]{1,0:T(8,128)S(1)}, f32[864,128]{1,0:T(8,128)S(1)}, u32[]{:S(2)}, u32[]{:S(2)}) collective-permute-start(f32[864,128]{1,0:T(8,128)S(1)} %bitcast.19), channel_id=1, source_target_pairs={{0,64},{64,0},{1,65},{65,1},{2,66},{66,2},{3,67},{67,3},{4,68},{68... | collective-permute-start | bytes 1327112 | tf_op jit(solution)/shard_map/ppermute | solution.py:256
  21.4 2.4 %collective-permute-start.2 = (f32[432,128]{1,0:T(8,128)S(1)}, f32[432,128]{1,0:T(8,128)S(1)}, u32[]{:S(2)}, u32[]{:S(2)}) collective-permute-start(f32[432,128]{1,0:T(8,128)S(1)} %pad_maximum_fusion), channel_id=1, source_target_pairs={{0,64},{64,0},{1,65},{65,1},{2,66},{66,2},{3,67},{67,3},{4,68},{68... | collective-permute-start | bytes 663560 | tf_op jit(solution)/shard_map/ppermute | solution.py:257
  35.7 9.9 %collective-permute-start.5 = (f32[216,128]{1,0:T(8,128)S(1)}, f32[216,128]{1,0:T(8,128)S(1)}, u32[]{:S(2)}, u32[]{:S(2)}) collective-permute-start(f32[216,128]{1,0:T(8,128)S(1)} %get-tuple-element.17), channel_id=1, source_target_pairs={{0,1},{1,2},{2,3},{3,4},{4,5},{5,6},{6,7},{7,8},{8,9},{9,10},{10,1... | collective-permute-start | bytes 331784 | tf_op jit(solution)/shard_map/ppermute | solution.py:253
  35.7 9.8 %collective-permute-start.4 = (f32[216,128]{1,0:T(8,128)S(1)}, f32[216,128]{1,0:T(8,128)S(1)}, u32[]{:S(2)}, u32[]{:S(2)}) collective-permute-start(f32[216,128]{1,0:T(8,128)S(1)} %get-tuple-element.17), channel_id=1, source_target_pairs={{0,63},{1,0},{2,1},{3,2},{4,3},{5,4},{6,5},{7,6},{8,7},{9,8},{10,9... | collective-permute-start | bytes 331784 | tf_op jit(solution)/shard_map/ppermute | solution.py:252
  42.8 5.1 %collective-permute-start.7 = (f32[864,128]{1,0:T(8,128)S(1)}, f32[864,128]{1,0:T(8,128)S(1)}, u32[]{:S(2)}, u32[]{:S(2)}) collective-permute-start(f32[864,128]{1,0:T(8,128)S(1)} %bitcast.18), channel_id=1, source_target_pairs={{0,64},{64,0},{1,65},{65,1},{2,66},{66,2},{3,67},{67,3},{4,68},{68... | collective-permute-start | bytes 1327112 | tf_op jit(solution)/shard_map/ppermute | solution.py:256
  45.6 2.3 %collective-permute-start.6 = (f32[432,128]{1,0:T(8,128)S(1)}, f32[432,128]{1,0:T(8,128)S(1)}, u32[]{:S(2)}, u32[]{:S(2)}) collective-permute-start(f32[432,128]{1,0:T(8,128)S(1)} %pad_maximum_fusion.1), channel_id=1, source_target_pairs={{0,64},{64,0},{1,65},{65,1},{2,66},{66,2},{3,67},{67,3},{4,68},{68... | collective-permute-start | bytes 663560 | tf_op jit(solution)/shard_map/ppermute | solution.py:257
  47.9 23.6 %copy-start.9 = (f32[360]{0:T(512)S(1)}, f32[360]{0:T(512)}, u32[]{:S(2)}) copy-start(f32[360]{0:T(512)} %param.23) | copy-start | bytes 4324
  47.9 23.6 %copy-start.10 = (f32[512]{0:T(512)S(1)}, f32[512]{0:T(512)}, u32[]{:S(2)}) copy-start(f32[512]{0:T(512)} %param.21) | copy-start | bytes 6148
  47.9 23.6 %copy-start.11 = (f32[512]{0:T(512)S(1)}, f32[512]{0:T(512)}, u32[]{:S(2)}) copy-start(f32[512]{0:T(512)} %param.19) | copy-start | bytes 6148
  47.9 23.6 %copy-start.12 = (f32[512]{0:T(512)S(1)}, f32[512]{0:T(512)}, u32[]{:S(2)}) copy-start(f32[512]{0:T(512)} %param.17) | copy-start | bytes 6148
  47.9 24.7 %copy-start.1 = (f32[432,16,128]{2,1,0:T(8,128)S(1)}, f32[432,16,128]{2,1,0:T(8,128)}, u32[]{:S(2)}) copy-start(f32[432,16,128]{2,1,0:T(8,128)} %param.13) | copy-start | bytes 10616836
  47.9 24.7 %copy-start.3 = (bf16[256,128]{1,0:T(8,128)(2,1)S(1)}, bf16[256,128]{1,0:T(8,128)(2,1)}, u32[]{:S(2)}) copy-start(bf16[256,128]{1,0:T(8,128)(2,1)} %constant.9.clone.refs_3_.refs_4_.refs_5_) | copy-start | bytes 196612
  48.0 24.7 %copy-start.4 = (bf16[512,512]{1,0:T(8,128)(2,1)S(1)}, bf16[512,512]{1,0:T(8,128)(2,1)}, u32[]{:S(2)}) copy-start(bf16[512,512]{1,0:T(8,128)(2,1)} %refs_13_.1) | copy-start | bytes 1572868
  48.0 24.7 %copy-start.5 = (bf16[512,512]{1,0:T(8,128)(2,1)S(1)}, bf16[512,512]{1,0:T(8,128)(2,1)}, u32[]{:S(2)}) copy-start(bf16[512,512]{1,0:T(8,128)(2,1)} %refs_14_.1) | copy-start | bytes 1572868
  48.0 24.7 %copy-start.6 = (bf16[512,432]{0,1:T(8,128)(2,1)S(1)}, bf16[512,432]{0,1:T(8,128)(2,1)}, u32[]{:S(2)}) copy-start(bf16[512,432]{0,1:T(8,128)(2,1)} %param.16) | copy-start | bytes 1327108
  48.0 24.7 %copy-start.7 = (bf16[360,512]{1,0:T(8,128)(2,1)S(1)}, bf16[360,512]{1,0:T(8,128)(2,1)}, u32[]{:S(2)}) copy-start(bf16[360,512]{1,0:T(8,128)(2,1)} %refs_15_.1) | copy-start | bytes 1105924
  60.2 9.9 %collective-permute-start.9 = (f32[216,128]{1,0:T(8,128)S(1)}, f32[216,128]{1,0:T(8,128)S(1)}, u32[]{:S(2)}, u32[]{:S(2)}) collective-permute-start(f32[216,128]{1,0:T(8,128)S(1)} %get-tuple-element.20), channel_id=1, source_target_pairs={{0,1},{1,2},{2,3},{3,4},{4,5},{5,6},{6,7},{7,8},{8,9},{9,10},{10,1... | collective-permute-start | bytes 331784 | tf_op jit(solution)/shard_map/ppermute | solution.py:253
  60.3 9.8 %collective-permute-start.8 = (f32[216,128]{1,0:T(8,128)S(1)}, f32[216,128]{1,0:T(8,128)S(1)}, u32[]{:S(2)}, u32[]{:S(2)}) collective-permute-start(f32[216,128]{1,0:T(8,128)S(1)} %get-tuple-element.20), channel_id=1, source_target_pairs={{0,63},{1,0},{2,1},{3,2},{4,3},{5,4},{6,5},{7,6},{8,7},{9,8},{10,9... | collective-permute-start | bytes 331784 | tf_op jit(solution)/shard_map/ppermute | solution.py:252
  67.3 5.3 %collective-permute-start.11 = (f32[864,128]{1,0:T(8,128)S(1)}, f32[864,128]{1,0:T(8,128)S(1)}, u32[]{:S(2)}, u32[]{:S(2)}) collective-permute-start(f32[864,128]{1,0:T(8,128)S(1)} %bitcast.17), channel_id=1, source_target_pairs={{0,64},{64,0},{1,65},{65,1},{2,66},{66,2},{3,67},{67,3},{4,68},{68... | collective-permute-start | bytes 1327112 | tf_op jit(solution)/shard_map/ppermute | solution.py:256
  70.1 2.5 %collective-permute-start.10 = (f32[432,128]{1,0:T(8,128)S(1)}, f32[432,128]{1,0:T(8,128)S(1)}, u32[]{:S(2)}, u32[]{:S(2)}) collective-permute-start(f32[432,128]{1,0:T(8,128)S(1)} %pad_maximum_fusion.2), channel_id=1, source_target_pairs={{0,64},{64,0},{1,65},{65,1},{2,66},{66,2},{3,67},{67,3},{4,68},{68... | collective-permute-start | bytes 663560 | tf_op jit(solution)/shard_map/ppermute | solution.py:257
  72.7 19.2 %copy-start.8 = (s32[1,1,2048,1]{2,3,1,0:T(1,128)S(1)}, s32[1,1,2048,1]{2,3,1,0:T(1,128)}, u32[]{:S(2)}) copy-start(s32[1,1,2048,1]{2,3,1,0:T(1,128)} %param.24) | copy-start | bytes 24580
  (1 other events, 0.8 us)

commit v13 on v12

--- a/solution.py
+++ b/solution.py
@@ -190,14 +190,14 @@
     args += [field_rows, speeds, speeds, mats, mats]
     specs += [big, small, small_y, const, const_lo]
     if not first:
-        exr, exl, corners, rows = halos
+        exr, exl, corner_r, corner_l, rows = halos
         blocks = field_rows.shape[0] // (CHUNK * 16)
-        args += [exr, exl, corners, corners, rows, rows]
+        args += [exr, exl, corner_r, corner_l, rows, rows]
         specs += [
             edge,
             edge,
-            pl.BlockSpec((FOLD, width), lambda i: (i, 0)),
-            pl.BlockSpec((FOLD, width), lambda i: (blocks + i, 0)),
+            edge,
+            edge,
             pl.BlockSpec((CHUNK, width), lambda i: (i, 0)),
             pl.BlockSpec((CHUNK, width), lambda i: (blocks + i, 0)),
         ]
@@ -254,8 +254,9 @@
     feats = ey.shape[1]
     swap = [(0, 1), (1, 0)]
     rows = lax.ppermute(ey.reshape(2 * feats, ey.shape[2]), "face", swap)
-    corners = lax.ppermute(jnp.concatenate([exr, exl], axis=0), "face", swap)
-    return (exr, exl, corners, rows)
+    corner_r = lax.ppermute(exr, "face", swap)
+    corner_l = lax.ppermute(exl, "face", swap)
+    return (exr, exl, corner_r, corner_l, rows)
 
 
 def column_model(inputs, w_in, b_in, w_mid, b_mid, w_top, b_top, w_out, b_out):

time: 113 us -> 114 us (level)
  waiting for transfers between devices: 8.69 us -> 12.5 us
  starting transfers between devices: 30.1 us -> 27.3 us
    ppermute x3, waiting for transfers between devices: 5.71 us -> 8.93 us  [exchange(): exl = lax.ppermute(ex, 'elem', from_left)]
    ppermute x3 -> x6, starting transfers between devices: 3.98 us -> 3.1 us  [the longest x3 3.09 us: exchange(): corner_l = lax.ppermute(exl, 'face', swap)]
    ppermute x3 -> x6, waiting for transfers between devices: 2.97 us -> 3.58 us  [the longest x3 2.49 us: exchange(): corner_l = lax.ppermute(exl, 'face', swap)]
  transfers between devices with their start and end apart: 12 -> 15, of which waited for: 6 -> 9; matrix products, arithmetic and copies ran while one was open for 0% -> 0% of each run, Pallas kernels for 0% -> 0%
where the time goes in v13:
time: 114 us
  Pallas kernels  48 us (42%)
  starting transfers between devices  27.3 us (24%)
  blocking collectives  17.4 us (15%)
  waiting for transfers between devices  12.5 us (11%)
  local copies, waits for them, and re-layouts  3.49 us (3%)
  between operations  2.59 us (2%)
  other arithmetic  2.22 us (2%)
    pallas_call x4, Pallas kernels, run_section(): pl.pallas_call(kernel, grid=(steps,), in_specs=specs, out_specs=out_specs...  48 us
    ppermute x3, starting transfers between devices, exchange(): exr = lax.ppermute(ex, 'elem', from_right)  21 us
    all_to_all x1, blocking collectives, local(): lax.all_to_all(partial_sums.reshape(devices, 1), ('face', 'elem'), 0, 1,...  17.4 us
    ppermute x3, waiting for transfers between devices, exchange(): exl = lax.ppermute(ex, 'elem', from_left)  8.93 us
    ppermute x3, starting transfers between devices, exchange(): corner_l = lax.ppermute(exl, 'face', swap)  3.09 us
    unnamed x26, local copies, waits for them, and re-layouts  2.9 us
    ppermute x3, waiting for transfers between devices, exchange(): corner_l = lax.ppermute(exl, 'face', swap)  2.49 us
  transfers between devices with their start and end apart: 15, of which 9 were waited for; matrix products, arithmetic and copies ran while one was open for 0% of the time, Pallas kernels for 0%

profile of v13, /device:TPU:1, one launch (start us, length us, event | category | flops | bytes accessed | tf_op | source)
XLA Modules:
  0.0 113.6 jit_solution(16691299423801817920)
XLA Ops:
  0.6 0.8 pad_maximum_fusion.1
  1.6 2.0 %copy-done = f32[432,16,128]{2,1,0:T(8,128)S(1)} copy-done((f32[432,16,128]{2,1,0:T(8,128)S(1)}, f32[432,16,128]{2,1,0:T(8,128)}, u32[]{:S(2)}) %copy-start) | copy-done | bytes 3538968
  3.6 0.8 copy-done.2
  4.4 4.9 %shard_map.148 = (f32[216,128]{1,0:T(8,128)S(1)}, f32[2,432,128]{2,1,0:T(8,128)S(1)}) custom-call(f32[6912,128]{1,0:T(8,128)S(1)} %bitcast.11, f32[864,128]{1,0:T(8,128)S(1)} %broadcast_in_dim.2.refs_1_.refs_2_.refs_3_, f32[864,128]{1,0:T(8,128)S(1)} %broadcast_in_dim.2.refs_1_.refs_2_.refs_3_, bf16[256,128]{1,0:T(8,128)(2,1)S(1)} %copy-done.2, ...), custom_call_target="tpu_custom_call" | custom-call | tf_op jit(solution)/shard_map/pallas_call | solution.py:235
  9.4 1.4 %collective-permute-start.4 = (f32[864,128]{1,0:T(8,128)S(1)}, f32[864,128]{1,0:T(8,128)S(1)}, u32[]{:S(2)}, u32[]{:S(2)}) collective-permute-start(f32[864,128]{1,0:T(8,128)S(1)} %bitcast.19), channel_id=1, source_target_pairs={{0,64},{64,0},{1,65},{65,1},{2,66},{66,2},{3,67},{67,3},{4,68},{68... | collective-permute-start | bytes 1327112 | tf_op jit(solution)/shard_map/ppermute | solution.py:256
  10.8 1.3 %collective-permute-start.1 = (f32[216,128]{1,0:T(8,128)S(1)}, f32[216,128]{1,0:T(8,128)S(1)}, u32[]{:S(2)}, u32[]{:S(2)}) collective-permute-start(f32[216,128]{1,0:T(8,128)S(1)} %get-tuple-element.14), channel_id=1, source_target_pairs={{0,1},{1,2},{2,3},{3,4},{4,5},{5,6},{6,7},{7,8},{8,9},{9,10},{10,1... | collective-permute-start | bytes 331784 | tf_op jit(solution)/shard_map/ppermute | solution.py:253
  12.1 7.2 %collective-permute-start = (f32[216,128]{1,0:T(8,128)S(1)}, f32[216,128]{1,0:T(8,128)S(1)}, u32[]{:S(2)}, u32[]{:S(2)}) collective-permute-start(f32[216,128]{1,0:T(8,128)S(1)} %get-tuple-element.14), channel_id=1, source_target_pairs={{0,63},{1,0},{2,1},{3,2},{4,3},{5,4},{6,5},{7,6},{8,7},{9,8},{10,9... | collective-permute-start | bytes 331784 | tf_op jit(solution)/shard_map/ppermute | solution.py:252
  19.3 3.3 %collective-permute-done.1.refs_6_ = f32[216,128]{1,0:T(8,128)S(1)} collective-permute-done((f32[216,128]{1,0:T(8,128)S(1)}, f32[216,128]{1,0:T(8,128)S(1)}, u32[]{:S(2)}, u32[]{:S(2)}) %collective-permute-start.1) | collective-permute-done | bytes 110624 | tf_op jit(solution)/shard_map/ppermute | solution.py:253
  22.7 0.7 collective-permute-start.3
  23.3 1.0 collective-permute-done.3.refs_8_
  24.7 11.8 %shard_map.149 = (f32[6912,128]{1,0:T(8,128)S(1)}, f32[216,128]{1,0:T(8,128)S(1)}, f32[2,432,128]{2,1,0:T(8,128)S(1)}) custom-call(f32[6912,128]{1,0:T(8,128)S(1)} %bitcast.12, f32[864,128]{1,0:T(8,128)S(1)} %broadcast_in_dim.2.refs_1_.refs_2_.refs_3_, f32[864,128]{1,0:T(8,128)S(1)} %broadcast_in_dim.2.refs_1_.refs_2_.refs_3_, ...), custom_call_target="tpu_custom_call" | custom-call | tf_op jit(solution)/shard_map/pallas_call | solution.py:235
  36.7 6.9 %collective-permute-start.5 = (f32[216,128]{1,0:T(8,128)S(1)}, f32[216,128]{1,0:T(8,128)S(1)}, u32[]{:S(2)}, u32[]{:S(2)}) collective-permute-start(f32[216,128]{1,0:T(8,128)S(1)} %get-tuple-element.17), channel_id=1, source_target_pairs={{0,63},{1,0},{2,1},{3,2},{4,3},{5,4},{6,5},{7,6},{8,7},{9,8},{10,9... | collective-permute-start | bytes 331784 | tf_op jit(solution)/shard_map/ppermute | solution.py:252
  43.6 2.8 %collective-permute-done.6.refs_7_ = f32[216,128]{1,0:T(8,128)S(1)} collective-permute-done((f32[216,128]{1,0:T(8,128)S(1)}, f32[216,128]{1,0:T(8,128)S(1)}, u32[]{:S(2)}, u32[]{:S(2)}) %collective-permute-start.6) | collective-permute-done | bytes 110624 | tf_op jit(solution)/shard_map/ppermute | solution.py:253
  46.3 1.2 %collective-permute-start.8 = (f32[216,128]{1,0:T(8,128)S(1)}, f32[216,128]{1,0:T(8,128)S(1)}, u32[]{:S(2)}, u32[]{:S(2)}) collective-permute-start(f32[216,128]{1,0:T(8,128)S(1)} %collective-permute-done.6.refs_7_), channel_id=1, source_target_pairs={{0,64},{64,0},{1,65},{65,1},{2,66},{66,2},{3,67},{67,3},{4,68},{68... | collective-permute-start | bytes 331784 | tf_op jit(solution)/shard_map/ppermute | solution.py:258
  47.6 1.0 collective-permute-done.8.refs_9_
  49.0 12.2 %shard_map.150 = (f32[6912,128]{1,0:T(8,128)S(1)}, f32[216,128]{1,0:T(8,128)S(1)}, f32[2,432,128]{2,1,0:T(8,128)S(1)}) custom-call(f32[6912,128]{1,0:T(8,128)S(1)} %bitcast.13, f32[6912,128]{1,0:T(8,128)S(1)} %get-tuple-element.16.refs_1_, f32[864,128]{1,0:T(8,128)S(1)} %broadcast_in_dim.2.refs_1_.refs_2_.refs_3_, ...), custom_call_target="tpu_custom_call" | custom-call | tf_op jit(solution)/shard_map/pallas_call | solution.py:235
  61.5 6.9 %collective-permute-start.10 = (f32[216,128]{1,0:T(8,128)S(1)}, f32[216,128]{1,0:T(8,128)S(1)}, u32[]{:S(2)}, u32[]{:S(2)}) collective-permute-start(f32[216,128]{1,0:T(8,128)S(1)} %get-tuple-element.20), channel_id=1, source_target_pairs={{0,63},{1,0},{2,1},{3,2},{4,3},{5,4},{6,5},{7,6},{8,7},{9,8},{10,9... | collective-permute-start | bytes 331784 | tf_op jit(solution)/shard_map/ppermute | solution.py:252
  68.4 2.8 %collective-permute-done.11.refs_7_ = f32[216,128]{1,0:T(8,128)S(1)} collective-permute-done((f32[216,128]{1,0:T(8,128)S(1)}, f32[216,128]{1,0:T(8,128)S(1)}, u32[]{:S(2)}, u32[]{:S(2)}) %collective-permute-start.11) | collective-permute-done | bytes 110624 | tf_op jit(solution)/shard_map/ppermute | solution.py:253
  71.1 1.2 %collective-permute-start.13 = (f32[216,128]{1,0:T(8,128)S(1)}, f32[216,128]{1,0:T(8,128)S(1)}, u32[]{:S(2)}, u32[]{:S(2)}) collective-permute-start(f32[216,128]{1,0:T(8,128)S(1)} %collective-permute-done.11.refs_7_), channel_id=1, source_target_pairs={{0,64},{64,0},{1,65},{65,1},{2,66},{66,2},{3,67},{67,3},{4,68},{68... | collective-permute-start | bytes 331784 | tf_op jit(solution)/shard_map/ppermute | solution.py:258
  72.7 0.6 collective-permute-done.13.refs_9_
  73.7 19.1 %shard_map.151 = (f32[6912,128]{1,0:T(8,128)}, bf16[5760,128]{1,0:T(8,128)(2,1)}, f32[16,128]{1,0:T(8,128)S(1)}) custom-call(f32[6912,128]{1,0:T(8,128)S(1)} %bitcast.14, f32[6912,128]{1,0:T(8,128)S(1)} %get-tuple-element.19.refs_1_, f32[864,128]{1,0:T(8,128)S(1)} %broadcast_in_dim.2.refs_1_.refs_2_.refs_3_, ...), custom_call_target="tpu_custom_call" | custom-call | tf_op jit(solution)/shard_map/pallas_call | solution.py:235
  92.9 0.7 select_reduce_fusion
  93.7 17.4 %all_to_all.13 = f32[128,1,1]{2,1,0:T(1,128)S(1)} all-to-all(f32[128,1,1]{2,1,0:T(1,128)S(1)} %copy.20), channel_id=1, replica_groups=mesh['face'=2,'elem'=64] {'face','elem'}, dimensions={0} | all-to-all | bytes 1024 | tf_op jit(solution)/shard_map/all_to_all | solution.py:367
  111.1 0.7 reduce_sum.19
  (44 shorter events, 2.2 us)
Async XLA Ops:
  9.4 15.3 %collective-permute-start.4 = (f32[864,128]{1,0:T(8,128)S(1)}, f32[864,128]{1,0:T(8,128)S(1)}, u32[]{:S(2)}, u32[]{:S(2)}) collective-permute-start(f32[864,128]{1,0:T(8,128)S(1)} %bitcast.19), channel_id=1, source_target_pairs={{0,64},{64,0},{1,65},{65,1},{2,66},{66,2},{3,67},{67,3},{4,68},{68... | collective-permute-start | bytes 1327112 | tf_op jit(solution)/shard_map/ppermute | solution.py:256
  10.8 11.9 %collective-permute-start.1 = (f32[216,128]{1,0:T(8,128)S(1)}, f32[216,128]{1,0:T(8,128)S(1)}, u32[]{:S(2)}, u32[]{:S(2)}) collective-permute-start(f32[216,128]{1,0:T(8,128)S(1)} %get-tuple-element.14), channel_id=1, source_target_pairs={{0,1},{1,2},{2,3},{3,4},{4,5},{5,6},{6,7},{7,8},{8,9},{9,10},{10,1... | collective-permute-start | bytes 331784 | tf_op jit(solution)/shard_map/ppermute | solution.py:253
  12.1 11.2 %collective-permute-start = (f32[216,128]{1,0:T(8,128)S(1)}, f32[216,128]{1,0:T(8,128)S(1)}, u32[]{:S(2)}, u32[]{:S(2)}) collective-permute-start(f32[216,128]{1,0:T(8,128)S(1)} %get-tuple-element.14), channel_id=1, source_target_pairs={{0,63},{1,0},{2,1},{3,2},{4,3},{5,4},{6,5},{7,6},{8,7},{9,8},{10,9... | collective-permute-start | bytes 331784 | tf_op jit(solution)/shard_map/ppermute | solution.py:252
  22.7 1.6 %collective-permute-start.3 = (f32[216,128]{1,0:T(8,128)S(1)}, f32[216,128]{1,0:T(8,128)S(1)}, u32[]{:S(2)}, u32[]{:S(2)}) collective-permute-start(f32[216,128]{1,0:T(8,128)S(1)} %collective-permute-done.1.refs_6_), channel_id=1, source_target_pairs={{0,64},{64,0},{1,65},{65,1},{2,66},{66,2},{3,67},{67,3},{4,68},{68... | collective-permute-start | bytes 331784 | tf_op jit(solution)/shard_map/ppermute | solution.py:258
  23.3 1.3 %collective-permute-start.2 = (f32[216,128]{1,0:T(8,128)S(1)}, f32[216,128]{1,0:T(8,128)S(1)}, u32[]{:S(2)}, u32[]{:S(2)}) collective-permute-start(f32[216,128]{1,0:T(8,128)S(1)} %collective-permute-done.refs_5_), channel_id=1, source_target_pairs={{0,64},{64,0},{1,65},{65,1},{2,66},{66,2},{3,67},{67,3},{4,68},{68... | collective-permute-start | bytes 331784 | tf_op jit(solution)/shard_map/ppermute | solution.py:257
  36.4 12.5 %collective-permute-start.9 = (f32[864,128]{1,0:T(8,128)S(1)}, f32[864,128]{1,0:T(8,128)S(1)}, u32[]{:S(2)}, u32[]{:S(2)}) collective-permute-start(f32[864,128]{1,0:T(8,128)S(1)} %bitcast.18), channel_id=1, source_target_pairs={{0,64},{64,0},{1,65},{65,1},{2,66},{66,2},{3,67},{67,3},{4,68},{68... | collective-permute-start | bytes 1327112 | tf_op jit(solution)/shard_map/ppermute | solution.py:256
  36.7 9.7 %collective-permute-start.6 = (f32[216,128]{1,0:T(8,128)S(1)}, f32[216,128]{1,0:T(8,128)S(1)}, u32[]{:S(2)}, u32[]{:S(2)}) collective-permute-start(f32[216,128]{1,0:T(8,128)S(1)} %get-tuple-element.17), channel_id=1, source_target_pairs={{0,1},{1,2},{2,3},{3,4},{4,5},{5,6},{6,7},{7,8},{8,9},{9,10},{10,1... | collective-permute-start | bytes 331784 | tf_op jit(solution)/shard_map/ppermute | solution.py:253
  36.7 10.9 %collective-permute-start.5 = (f32[216,128]{1,0:T(8,128)S(1)}, f32[216,128]{1,0:T(8,128)S(1)}, u32[]{:S(2)}, u32[]{:S(2)}) collective-permute-start(f32[216,128]{1,0:T(8,128)S(1)} %get-tuple-element.17), channel_id=1, source_target_pairs={{0,63},{1,0},{2,1},{3,2},{4,3},{5,4},{6,5},{7,6},{8,7},{9,8},{10,9... | collective-permute-start | bytes 331784 | tf_op jit(solution)/shard_map/ppermute | solution.py:252
  46.3 2.2 %collective-permute-start.8 = (f32[216,128]{1,0:T(8,128)S(1)}, f32[216,128]{1,0:T(8,128)S(1)}, u32[]{:S(2)}, u32[]{:S(2)}) collective-permute-start(f32[216,128]{1,0:T(8,128)S(1)} %collective-permute-done.6.refs_7_), channel_id=1, source_target_pairs={{0,64},{64,0},{1,65},{65,1},{2,66},{66,2},{3,67},{67,3},{4,68},{68... | collective-permute-start | bytes 331784 | tf_op jit(solution)/shard_map/ppermute | solution.py:258
  47.6 1.3 %collective-permute-start.7 = (f32[216,128]{1,0:T(8,128)S(1)}, f32[216,128]{1,0:T(8,128)S(1)}, u32[]{:S(2)}, u32[]{:S(2)}) collective-permute-start(f32[216,128]{1,0:T(8,128)S(1)} %collective-permute-done.5.refs_6_), channel_id=1, source_target_pairs={{0,64},{64,0},{1,65},{65,1},{2,66},{66,2},{3,67},{67,3},{4,68},{68... | collective-permute-start | bytes 331784 | tf_op jit(solution)/shard_map/ppermute | solution.py:257
  48.9 23.5 %copy-start.10 = (f32[512]{0:T(512)S(1)}, f32[512]{0:T(512)}, u32[]{:S(2)}) copy-start(f32[512]{0:T(512)} %param.21) | copy-start | bytes 6148
  48.9 23.5 %copy-start.11 = (f32[512]{0:T(512)S(1)}, f32[512]{0:T(512)}, u32[]{:S(2)}) copy-start(f32[512]{0:T(512)} %param.19) | copy-start | bytes 6148
  48.9 23.5 %copy-start.12 = (f32[512]{0:T(512)S(1)}, f32[512]{0:T(512)}, u32[]{:S(2)}) copy-start(f32[512]{0:T(512)} %param.17) | copy-start | bytes 6148
  48.9 24.8 %copy-start.1 = (f32[432,16,128]{2,1,0:T(8,128)S(1)}, f32[432,16,128]{2,1,0:T(8,128)}, u32[]{:S(2)}) copy-start(f32[432,16,128]{2,1,0:T(8,128)} %param.13) | copy-start | bytes 10616836
  48.9 24.8 %copy-start.3 = (bf16[256,128]{1,0:T(8,128)(2,1)S(1)}, bf16[256,128]{1,0:T(8,128)(2,1)}, u32[]{:S(2)}) copy-start(bf16[256,128]{1,0:T(8,128)(2,1)} %constant.9.clone.refs_3_.refs_4_.refs_5_) | copy-start | bytes 196612
  48.9 24.8 %copy-start.4 = (bf16[512,512]{1,0:T(8,128)(2,1)S(1)}, bf16[512,512]{1,0:T(8,128)(2,1)}, u32[]{:S(2)}) copy-start(bf16[512,512]{1,0:T(8,128)(2,1)} %refs_13_.1) | copy-start | bytes 1572868
  48.9 24.8 %copy-start.5 = (bf16[512,512]{1,0:T(8,128)(2,1)S(1)}, bf16[512,512]{1,0:T(8,128)(2,1)}, u32[]{:S(2)}) copy-start(bf16[512,512]{1,0:T(8,128)(2,1)} %refs_14_.1) | copy-start | bytes 1572868
  49.0 24.8 %copy-start.6 = (bf16[512,432]{0,1:T(8,128)(2,1)S(1)}, bf16[512,432]{0,1:T(8,128)(2,1)}, u32[]{:S(2)}) copy-start(bf16[512,432]{0,1:T(8,128)(2,1)} %param.16) | copy-start | bytes 1327108
  49.0 24.8 %copy-start.7 = (bf16[360,512]{1,0:T(8,128)(2,1)S(1)}, bf16[360,512]{1,0:T(8,128)(2,1)}, u32[]{:S(2)}) copy-start(bf16[360,512]{1,0:T(8,128)(2,1)} %refs_15_.1) | copy-start | bytes 1105924
  61.2 12.5 %collective-permute-start.14 = (f32[864,128]{1,0:T(8,128)S(1)}, f32[864,128]{1,0:T(8,128)S(1)}, u32[]{:S(2)}, u32[]{:S(2)}) collective-permute-start(f32[864,128]{1,0:T(8,128)S(1)} %bitcast.17), channel_id=1, source_target_pairs={{0,64},{64,0},{1,65},{65,1},{2,66},{66,2},{3,67},{67,3},{4,68},{68... | collective-permute-start | bytes 1327112 | tf_op jit(solution)/shard_map/ppermute | solution.py:256
  61.5 9.7 %collective-permute-start.11 = (f32[216,128]{1,0:T(8,128)S(1)}, f32[216,128]{1,0:T(8,128)S(1)}, u32[]{:S(2)}, u32[]{:S(2)}) collective-permute-start(f32[216,128]{1,0:T(8,128)S(1)} %get-tuple-element.20), channel_id=1, source_target_pairs={{0,1},{1,2},{2,3},{3,4},{4,5},{5,6},{6,7},{7,8},{8,9},{9,10},{10,1... | collective-permute-start | bytes 331784 | tf_op jit(solution)/shard_map/ppermute | solution.py:253
  61.5 10.9 %collective-permute-start.10 = (f32[216,128]{1,0:T(8,128)S(1)}, f32[216,128]{1,0:T(8,128)S(1)}, u32[]{:S(2)}, u32[]{:S(2)}) collective-permute-start(f32[216,128]{1,0:T(8,128)S(1)} %get-tuple-element.20), channel_id=1, source_target_pairs={{0,63},{1,0},{2,1},{3,2},{4,3},{5,4},{6,5},{7,6},{8,7},{9,8},{10,9... | collective-permute-start | bytes 331784 | tf_op jit(solution)/shard_map/ppermute | solution.py:252
  71.1 2.2 %collective-permute-start.13 = (f32[216,128]{1,0:T(8,128)S(1)}, f32[216,128]{1,0:T(8,128)S(1)}, u32[]{:S(2)}, u32[]{:S(2)}) collective-permute-start(f32[216,128]{1,0:T(8,128)S(1)} %collective-permute-done.11.refs_7_), channel_id=1, source_target_pairs={{0,64},{64,0},{1,65},{65,1},{2,66},{66,2},{3,67},{67,3},{4,68},{68... | collective-permute-start | bytes 331784 | tf_op jit(solution)/shard_map/ppermute | solution.py:258
  72.4 1.3 %collective-permute-start.12 = (f32[216,128]{1,0:T(8,128)S(1)}, f32[216,128]{1,0:T(8,128)S(1)}, u32[]{:S(2)}, u32[]{:S(2)}) collective-permute-start(f32[216,128]{1,0:T(8,128)S(1)} %collective-permute-done.10.refs_6_), channel_id=1, source_target_pairs={{0,64},{64,0},{1,65},{65,1},{2,66},{66,2},{3,67},{67,3},{4,68},{68... | collective-permute-start | bytes 331784 | tf_op jit(solution)/shard_map/ppermute | solution.py:257
  (4 other events, 45.5 us)

commit v14 on v13

--- a/solution.py
+++ b/solution.py
@@ -98,7 +98,7 @@
     )
 
 
-def section_kernel(*refs, first, combo, edges, mlp):
+def section_kernel(*refs, first, combo, edges, mlp, given):
     refs = list(refs)
     v0_ref = None if combo is None or combo[0] is None else refs.pop(0)
     sp_ref = refs.pop(0)
@@ -107,6 +107,8 @@
     if not first:
         exr_ref, exl_ref, dr_ref, dl_ref, top_ref, bottom_ref = refs[:6]
         refs = refs[6:]
+    if given:
+        t_in_ref = refs.pop(0)
     if mlp:
         mlp_in = refs[:5]
         refs = refs[5:]
@@ -117,9 +119,14 @@
     ahi = ahi_ref[...]
     alo = alo_ref[...]
     slabs = [sp_ref[pl.ds(y, rows, stride=height), :] for y in range(height)]
-    tend = raw_slabs(slabs, sx, sy, ahi, alo)
+    if given:
+        tend = [t_in_ref[pl.ds(y, rows, stride=height), :] for y in range(height)]
+    else:
+        tend = raw_slabs(slabs, sx, sy, ahi, alo)
     if first:
-        ex_ref, ey_ref = refs
+        ex_ref, ey_ref, t_out_ref = refs
+        for y in range(height):
+            t_out_ref[pl.ds(y, rows, stride=height), :] = tend[y]
         ex_ref[...] = pack_edges(tend)
         ey_ref[0] = tend[0]
         ey_ref[1] = tend[height - 1]
@@ -172,7 +179,7 @@
         ey_ref[1] = tend[height - 1]
 
 
-def run_section(field_rows, v0, speeds, mats, halos, *, first, combo, edges, mlp=None):
+def run_section(field_rows, v0, speeds, mats, halos, *, first, combo, edges, mlp=None, given=None):
     total, width = field_rows.shape
     feats = speeds.shape[0] // 2
     steps = feats // CHUNK
@@ -201,12 +208,15 @@
             pl.BlockSpec((CHUNK, width), lambda i: (i, 0)),
             pl.BlockSpec((CHUNK, width), lambda i: (blocks + i, 0)),
         ]
+    if given is not None:
+        args.append(given)
+        specs.append(big)
     out_shape, out_specs = [], []
     ex_shape = jax.ShapeDtypeStruct((feats // 2, width), jnp.float32)
     ey_shape = jax.ShapeDtypeStruct((2, feats, width), jnp.float32)
     if first:
-        out_shape = [ex_shape, ey_shape]
-        out_specs = [edge, rowsb]
+        out_shape = [ex_shape, ey_shape, jax.ShapeDtypeStruct((total, width), jnp.float32)]
+        out_specs = [edge, rowsb, big]
     else:
         out_shape = [jax.ShapeDtypeStruct((total, width), jnp.float32)]
         out_specs = [big]
@@ -231,7 +241,8 @@
             pltpu.VMEM((outs * height, width), jnp.float32),
         ]
         limit = 32
-    kernel = functools.partial(section_kernel, first=first, combo=combo, edges=edges, mlp=mlp is not None)
+    kernel = functools.partial(section_kernel, first=first, combo=combo, edges=edges, mlp=mlp is not None,
+                               given=given is not None)
     return pl.pallas_call(
         kernel,
         grid=(steps,),
@@ -340,7 +351,7 @@
     mats = jnp.asarray(np.concatenate([ahi_np, alo_np], axis=0))
     speeds = jnp.broadcast_to(jnp.concatenate([speed_x, speed_y])[:, None], (2 * feats, breadth))
     v0 = state.reshape(feats * height, breadth)
-    ex, ey = run_section(v0, None, speeds, mats, None, first=True, combo=None, edges=True)
+    ex, ey, tend0 = run_section(v0, None, speeds, mats, None, first=True, combo=None, edges=True)
     field = v0
     combos = [(None, None), (0.75, 0.25), ("third", None)]
     for k, combo in enumerate(combos):
@@ -350,7 +361,8 @@
             biases = jnp.concatenate([b_in, b_mid, b_top, b_out]).reshape(-1, 1)
             extra = (w_in.T, w_mid, w_top, w_out, biases)
         outs = run_section(
-            field, v0, speeds, mats, halos, first=False, combo=combo, edges=k < 2, mlp=extra
+            field, v0, speeds, mats, halos, first=False, combo=combo, edges=k < 2, mlp=extra,
+            given=tend0 if k == 0 else None,
         )
         if k < 2:
             field, ex, ey = outs

time: 114 us -> 112 us (0.982)
  Pallas kernels: 48 us -> 46.7 us
    pallas_call x4, Pallas kernels: 48 us -> 46.7 us  [run_section(): pl.pallas_call(kernel, grid=(steps,), in_specs=specs, out_specs=out_specs...]
where the time goes in v14:
time: 112 us
  Pallas kernels  46.7 us (42%)
  starting transfers between devices  27.3 us (24%)
  blocking collectives  17.4 us (16%)
  waiting for transfers between devices  12.5 us (11%)
  local copies, waits for them, and re-layouts  3.49 us (3%)
  between operations  2.59 us (2%)
  other arithmetic  2.22 us (2%)
    pallas_call x4, Pallas kernels, run_section(): pl.pallas_call(kernel, grid=(steps,), in_specs=specs, out_specs=out_specs...  46.7 us
    ppermute x3, starting transfers between devices, exchange(): exr = lax.ppermute(ex, 'elem', from_right)  21 us
    all_to_all x1, blocking collectives, local(): lax.all_to_all(partial_sums.reshape(devices, 1), ('face', 'elem'), 0, 1,...  17.4 us
    ppermute x3, waiting for transfers between devices, exchange(): exl = lax.ppermute(ex, 'elem', from_left)  8.93 us
    ppermute x3, starting transfers between devices, exchange(): corner_l = lax.ppermute(exl, 'face', swap)  3.09 us
    unnamed x26, local copies, waits for them, and re-layouts  2.9 us
    ppermute x3, waiting for transfers between devices, exchange(): corner_l = lax.ppermute(exl, 'face', swap)  2.49 us
  transfers between devices with their start and end apart: 15, of which 9 were waited for; matrix products, arithmetic and copies ran while one was open for 0% of the time, Pallas kernels for 0%

profile of v14, /device:TPU:1, one launch (start us, length us, event | category | flops | bytes accessed | tf_op | source)
XLA Modules:
  0.0 112.2 jit_solution(12517439699657773911)
XLA Ops:
  0.6 0.8 pad_maximum_fusion.1
  1.6 2.0 %copy-done = f32[432,16,128]{2,1,0:T(8,128)S(1)} copy-done((f32[432,16,128]{2,1,0:T(8,128)S(1)}, f32[432,16,128]{2,1,0:T(8,128)}, u32[]{:S(2)}) %copy-start) | copy-done | bytes 3538968
  3.6 0.8 copy-done.2
  4.4 6.1 %shard_map.148 = (f32[216,128]{1,0:T(8,128)S(1)}, f32[2,432,128]{2,1,0:T(8,128)S(1)}, f32[6912,128]{1,0:T(8,128)S(1)}) custom-call(f32[6912,128]{1,0:T(8,128)S(1)} %bitcast.11, f32[864,128]{1,0:T(8,128)S(1)} %broadcast_in_dim.2.refs_1_.refs_2_.refs_3_, f32[864,128]{1,0:T(8,128)S(1)} %broadcast_in_dim.2.refs_1_.refs_2_.refs_3_, ...), custom_call_target="tpu_custom_call" | custom-call | tf_op jit(solution)/shard_map/pallas_call | solution.py:246
  10.5 1.5 %collective-permute-start.4 = (f32[864,128]{1,0:T(8,128)S(1)}, f32[864,128]{1,0:T(8,128)S(1)}, u32[]{:S(2)}, u32[]{:S(2)}) collective-permute-start(f32[864,128]{1,0:T(8,128)S(1)} %bitcast.19), channel_id=1, source_target_pairs={{0,64},{64,0},{1,65},{65,1},{2,66},{66,2},{3,67},{67,3},{4,68},{68... | collective-permute-start | bytes 1327112 | tf_op jit(solution)/shard_map/ppermute | solution.py:267
  11.9 1.3 %collective-permute-start.1 = (f32[216,128]{1,0:T(8,128)S(1)}, f32[216,128]{1,0:T(8,128)S(1)}, u32[]{:S(2)}, u32[]{:S(2)}) collective-permute-start(f32[216,128]{1,0:T(8,128)S(1)} %get-tuple-element.15), channel_id=1, source_target_pairs={{0,1},{1,2},{2,3},{3,4},{4,5},{5,6},{6,7},{7,8},{8,9},{9,10},{10,1... | collective-permute-start | bytes 331784 | tf_op jit(solution)/shard_map/ppermute | solution.py:264
  13.3 7.2 %collective-permute-start = (f32[216,128]{1,0:T(8,128)S(1)}, f32[216,128]{1,0:T(8,128)S(1)}, u32[]{:S(2)}, u32[]{:S(2)}) collective-permute-start(f32[216,128]{1,0:T(8,128)S(1)} %get-tuple-element.15), channel_id=1, source_target_pairs={{0,63},{1,0},{2,1},{3,2},{4,3},{5,4},{6,5},{7,6},{8,7},{9,8},{10,9... | collective-permute-start | bytes 331784 | tf_op jit(solution)/shard_map/ppermute | solution.py:263
  20.5 3.3 %collective-permute-done.1.refs_6_ = f32[216,128]{1,0:T(8,128)S(1)} collective-permute-done((f32[216,128]{1,0:T(8,128)S(1)}, f32[216,128]{1,0:T(8,128)S(1)}, u32[]{:S(2)}, u32[]{:S(2)}) %collective-permute-start.1) | collective-permute-done | bytes 110624 | tf_op jit(solution)/shard_map/ppermute | solution.py:264
  23.8 0.7 collective-permute-start.3
  24.5 1.0 collective-permute-done.3.refs_8_
  25.8 9.3 %shard_map.149 = (f32[6912,128]{1,0:T(8,128)S(1)}, f32[216,128]{1,0:T(8,128)S(1)}, f32[2,432,128]{2,1,0:T(8,128)S(1)}) custom-call(f32[6912,128]{1,0:T(8,128)S(1)} %bitcast.12, f32[864,128]{1,0:T(8,128)S(1)} %broadcast_in_dim.2.refs_1_.refs_2_.refs_3_, f32[864,128]{1,0:T(8,128)S(1)} %broadcast_in_dim.2.refs_1_.refs_2_.refs_3_, ...), custom_call_target="tpu_custom_call" | custom-call | tf_op jit(solution)/shard_map/pallas_call | solution.py:246
  35.4 6.9 %collective-permute-start.5 = (f32[216,128]{1,0:T(8,128)S(1)}, f32[216,128]{1,0:T(8,128)S(1)}, u32[]{:S(2)}, u32[]{:S(2)}) collective-permute-start(f32[216,128]{1,0:T(8,128)S(1)} %get-tuple-element.19), channel_id=1, source_target_pairs={{0,63},{1,0},{2,1},{3,2},{4,3},{5,4},{6,5},{7,6},{8,7},{9,8},{10,9... | collective-permute-start | bytes 331784 | tf_op jit(solution)/shard_map/ppermute | solution.py:263
  42.3 2.8 %collective-permute-done.6.refs_7_ = f32[216,128]{1,0:T(8,128)S(1)} collective-permute-done((f32[216,128]{1,0:T(8,128)S(1)}, f32[216,128]{1,0:T(8,128)S(1)}, u32[]{:S(2)}, u32[]{:S(2)}) %collective-permute-start.6) | collective-permute-done | bytes 110624 | tf_op jit(solution)/shard_map/ppermute | solution.py:264
  45.1 1.2 %collective-permute-start.8 = (f32[216,128]{1,0:T(8,128)S(1)}, f32[216,128]{1,0:T(8,128)S(1)}, u32[]{:S(2)}, u32[]{:S(2)}) collective-permute-start(f32[216,128]{1,0:T(8,128)S(1)} %collective-permute-done.6.refs_7_), channel_id=1, source_target_pairs={{0,64},{64,0},{1,65},{65,1},{2,66},{66,2},{3,67},{67,3},{4,68},{68... | collective-permute-start | bytes 331784 | tf_op jit(solution)/shard_map/ppermute | solution.py:269
  46.3 1.0 collective-permute-done.8.refs_9_
  47.7 12.2 %shard_map.150 = (f32[6912,128]{1,0:T(8,128)S(1)}, f32[216,128]{1,0:T(8,128)S(1)}, f32[2,432,128]{2,1,0:T(8,128)S(1)}) custom-call(f32[6912,128]{1,0:T(8,128)S(1)} %bitcast.13, f32[6912,128]{1,0:T(8,128)S(1)} %get-tuple-element.18.refs_1_, f32[864,128]{1,0:T(8,128)S(1)} %broadcast_in_dim.2.refs_1_.refs_2_.refs_3_, ...), custom_call_target="tpu_custom_call" | custom-call | tf_op jit(solution)/shard_map/pallas_call | solution.py:246
  60.2 6.9 %collective-permute-start.10 = (f32[216,128]{1,0:T(8,128)S(1)}, f32[216,128]{1,0:T(8,128)S(1)}, u32[]{:S(2)}, u32[]{:S(2)}) collective-permute-start(f32[216,128]{1,0:T(8,128)S(1)} %get-tuple-element.22), channel_id=1, source_target_pairs={{0,63},{1,0},{2,1},{3,2},{4,3},{5,4},{6,5},{7,6},{8,7},{9,8},{10,9... | collective-permute-start | bytes 331784 | tf_op jit(solution)/shard_map/ppermute | solution.py:263
  67.1 2.8 %collective-permute-done.11.refs_7_ = f32[216,128]{1,0:T(8,128)S(1)} collective-permute-done((f32[216,128]{1,0:T(8,128)S(1)}, f32[216,128]{1,0:T(8,128)S(1)}, u32[]{:S(2)}, u32[]{:S(2)}) %collective-permute-start.11) | collective-permute-done | bytes 110624 | tf_op jit(solution)/shard_map/ppermute | solution.py:264
  69.9 1.2 %collective-permute-start.13 = (f32[216,128]{1,0:T(8,128)S(1)}, f32[216,128]{1,0:T(8,128)S(1)}, u32[]{:S(2)}, u32[]{:S(2)}) collective-permute-start(f32[216,128]{1,0:T(8,128)S(1)} %collective-permute-done.11.refs_7_), channel_id=1, source_target_pairs={{0,64},{64,0},{1,65},{65,1},{2,66},{66,2},{3,67},{67,3},{4,68},{68... | collective-permute-start | bytes 331784 | tf_op jit(solution)/shard_map/ppermute | solution.py:269
  71.4 0.6 collective-permute-done.13.refs_9_
  72.5 19.1 %shard_map.151 = (f32[6912,128]{1,0:T(8,128)}, bf16[5760,128]{1,0:T(8,128)(2,1)}, f32[16,128]{1,0:T(8,128)S(1)}) custom-call(f32[6912,128]{1,0:T(8,128)S(1)} %bitcast.14, f32[6912,128]{1,0:T(8,128)S(1)} %get-tuple-element.21.refs_1_, f32[864,128]{1,0:T(8,128)S(1)} %broadcast_in_dim.2.refs_1_.refs_2_.refs_3_, ...), custom_call_target="tpu_custom_call" | custom-call | tf_op jit(solution)/shard_map/pallas_call | solution.py:246
  91.5 0.7 select_reduce_fusion
  92.3 17.4 %all_to_all.13 = f32[128,1,1]{2,1,0:T(1,128)S(1)} all-to-all(f32[128,1,1]{2,1,0:T(1,128)S(1)} %copy.20), channel_id=1, replica_groups=mesh['face'=2,'elem'=64] {'face','elem'}, dimensions={0} | all-to-all | bytes 1024 | tf_op jit(solution)/shard_map/all_to_all | solution.py:379
  109.7 0.7 reduce_sum.19
  (44 shorter events, 2.2 us)
Async XLA Ops:
  10.5 15.3 %collective-permute-start.4 = (f32[864,128]{1,0:T(8,128)S(1)}, f32[864,128]{1,0:T(8,128)S(1)}, u32[]{:S(2)}, u32[]{:S(2)}) collective-permute-start(f32[864,128]{1,0:T(8,128)S(1)} %bitcast.19), channel_id=1, source_target_pairs={{0,64},{64,0},{1,65},{65,1},{2,66},{66,2},{3,67},{67,3},{4,68},{68... | collective-permute-start | bytes 1327112 | tf_op jit(solution)/shard_map/ppermute | solution.py:267
  11.9 11.9 %collective-permute-start.1 = (f32[216,128]{1,0:T(8,128)S(1)}, f32[216,128]{1,0:T(8,128)S(1)}, u32[]{:S(2)}, u32[]{:S(2)}) collective-permute-start(f32[216,128]{1,0:T(8,128)S(1)} %get-tuple-element.15), channel_id=1, source_target_pairs={{0,1},{1,2},{2,3},{3,4},{4,5},{5,6},{6,7},{7,8},{8,9},{9,10},{10,1... | collective-permute-start | bytes 331784 | tf_op jit(solution)/shard_map/ppermute | solution.py:264
  13.3 11.2 %collective-permute-start = (f32[216,128]{1,0:T(8,128)S(1)}, f32[216,128]{1,0:T(8,128)S(1)}, u32[]{:S(2)}, u32[]{:S(2)}) collective-permute-start(f32[216,128]{1,0:T(8,128)S(1)} %get-tuple-element.15), channel_id=1, source_target_pairs={{0,63},{1,0},{2,1},{3,2},{4,3},{5,4},{6,5},{7,6},{8,7},{9,8},{10,9... | collective-permute-start | bytes 331784 | tf_op jit(solution)/shard_map/ppermute | solution.py:263
  23.8 1.6 %collective-permute-start.3 = (f32[216,128]{1,0:T(8,128)S(1)}, f32[216,128]{1,0:T(8,128)S(1)}, u32[]{:S(2)}, u32[]{:S(2)}) collective-permute-start(f32[216,128]{1,0:T(8,128)S(1)} %collective-permute-done.1.refs_6_), channel_id=1, source_target_pairs={{0,64},{64,0},{1,65},{65,1},{2,66},{66,2},{3,67},{67,3},{4,68},{68... | collective-permute-start | bytes 331784 | tf_op jit(solution)/shard_map/ppermute | solution.py:269
  24.5 1.3 %collective-permute-start.2 = (f32[216,128]{1,0:T(8,128)S(1)}, f32[216,128]{1,0:T(8,128)S(1)}, u32[]{:S(2)}, u32[]{:S(2)}) collective-permute-start(f32[216,128]{1,0:T(8,128)S(1)} %collective-permute-done.refs_5_), channel_id=1, source_target_pairs={{0,64},{64,0},{1,65},{65,1},{2,66},{66,2},{3,67},{67,3},{4,68},{68... | collective-permute-start | bytes 331784 | tf_op jit(solution)/shard_map/ppermute | solution.py:268
  35.1 12.5 %collective-permute-start.9 = (f32[864,128]{1,0:T(8,128)S(1)}, f32[864,128]{1,0:T(8,128)S(1)}, u32[]{:S(2)}, u32[]{:S(2)}) collective-permute-start(f32[864,128]{1,0:T(8,128)S(1)} %bitcast.18), channel_id=1, source_target_pairs={{0,64},{64,0},{1,65},{65,1},{2,66},{66,2},{3,67},{67,3},{4,68},{68... | collective-permute-start | bytes 1327112 | tf_op jit(solution)/shard_map/ppermute | solution.py:267
  35.4 9.7 %collective-permute-start.6 = (f32[216,128]{1,0:T(8,128)S(1)}, f32[216,128]{1,0:T(8,128)S(1)}, u32[]{:S(2)}, u32[]{:S(2)}) collective-permute-start(f32[216,128]{1,0:T(8,128)S(1)} %get-tuple-element.19), channel_id=1, source_target_pairs={{0,1},{1,2},{2,3},{3,4},{4,5},{5,6},{6,7},{7,8},{8,9},{9,10},{10,1... | collective-permute-start | bytes 331784 | tf_op jit(solution)/shard_map/ppermute | solution.py:264
  35.4 10.9 %collective-permute-start.5 = (f32[216,128]{1,0:T(8,128)S(1)}, f32[216,128]{1,0:T(8,128)S(1)}, u32[]{:S(2)}, u32[]{:S(2)}) collective-permute-start(f32[216,128]{1,0:T(8,128)S(1)} %get-tuple-element.19), channel_id=1, source_target_pairs={{0,63},{1,0},{2,1},{3,2},{4,3},{5,4},{6,5},{7,6},{8,7},{9,8},{10,9... | collective-permute-start | bytes 331784 | tf_op jit(solution)/shard_map/ppermute | solution.py:263
  45.1 2.2 %collective-permute-start.8 = (f32[216,128]{1,0:T(8,128)S(1)}, f32[216,128]{1,0:T(8,128)S(1)}, u32[]{:S(2)}, u32[]{:S(2)}) collective-permute-start(f32[216,128]{1,0:T(8,128)S(1)} %collective-permute-done.6.refs_7_), channel_id=1, source_target_pairs={{0,64},{64,0},{1,65},{65,1},{2,66},{66,2},{3,67},{67,3},{4,68},{68... | collective-permute-start | bytes 331784 | tf_op jit(solution)/shard_map/ppermute | solution.py:269
  46.3 1.3 %collective-permute-start.7 = (f32[216,128]{1,0:T(8,128)S(1)}, f32[216,128]{1,0:T(8,128)S(1)}, u32[]{:S(2)}, u32[]{:S(2)}) collective-permute-start(f32[216,128]{1,0:T(8,128)S(1)} %collective-permute-done.5.refs_6_), channel_id=1, source_target_pairs={{0,64},{64,0},{1,65},{65,1},{2,66},{66,2},{3,67},{67,3},{4,68},{68... | collective-permute-start | bytes 331784 | tf_op jit(solution)/shard_map/ppermute | solution.py:268
  47.6 23.5 %copy-start.10 = (f32[512]{0:T(512)S(1)}, f32[512]{0:T(512)}, u32[]{:S(2)}) copy-start(f32[512]{0:T(512)} %param.21) | copy-start | bytes 6148
  47.6 23.5 %copy-start.11 = (f32[512]{0:T(512)S(1)}, f32[512]{0:T(512)}, u32[]{:S(2)}) copy-start(f32[512]{0:T(512)} %param.19) | copy-start | bytes 6148
  47.6 23.5 %copy-start.12 = (f32[512]{0:T(512)S(1)}, f32[512]{0:T(512)}, u32[]{:S(2)}) copy-start(f32[512]{0:T(512)} %param.17) | copy-start | bytes 6148
  47.6 24.8 %copy-start.1 = (f32[432,16,128]{2,1,0:T(8,128)S(1)}, f32[432,16,128]{2,1,0:T(8,128)}, u32[]{:S(2)}) copy-start(f32[432,16,128]{2,1,0:T(8,128)} %param.13) | copy-start | bytes 10616836
  47.6 24.8 %copy-start.3 = (bf16[256,128]{1,0:T(8,128)(2,1)S(1)}, bf16[256,128]{1,0:T(8,128)(2,1)}, u32[]{:S(2)}) copy-start(bf16[256,128]{1,0:T(8,128)(2,1)} %constant.9.clone.refs_3_.refs_4_.refs_5_) | copy-start | bytes 196612
  47.7 24.8 %copy-start.4 = (bf16[512,512]{1,0:T(8,128)(2,1)S(1)}, bf16[512,512]{1,0:T(8,128)(2,1)}, u32[]{:S(2)}) copy-start(bf16[512,512]{1,0:T(8,128)(2,1)} %refs_13_.1) | copy-start | bytes 1572868
  47.7 24.8 %copy-start.5 = (bf16[512,512]{1,0:T(8,128)(2,1)S(1)}, bf16[512,512]{1,0:T(8,128)(2,1)}, u32[]{:S(2)}) copy-start(bf16[512,512]{1,0:T(8,128)(2,1)} %refs_14_.1) | copy-start | bytes 1572868
  47.7 24.8 %copy-start.6 = (bf16[512,432]{0,1:T(8,128)(2,1)S(1)}, bf16[512,432]{0,1:T(8,128)(2,1)}, u32[]{:S(2)}) copy-start(bf16[512,432]{0,1:T(8,128)(2,1)} %param.16) | copy-start | bytes 1327108
  47.7 24.8 %copy-start.7 = (bf16[360,512]{1,0:T(8,128)(2,1)S(1)}, bf16[360,512]{1,0:T(8,128)(2,1)}, u32[]{:S(2)}) copy-start(bf16[360,512]{1,0:T(8,128)(2,1)} %refs_15_.1) | copy-start | bytes 1105924
  59.9 12.5 %collective-permute-start.14 = (f32[864,128]{1,0:T(8,128)S(1)}, f32[864,128]{1,0:T(8,128)S(1)}, u32[]{:S(2)}, u32[]{:S(2)}) collective-permute-start(f32[864,128]{1,0:T(8,128)S(1)} %bitcast.17), channel_id=1, source_target_pairs={{0,64},{64,0},{1,65},{65,1},{2,66},{66,2},{3,67},{67,3},{4,68},{68... | collective-permute-start | bytes 1327112 | tf_op jit(solution)/shard_map/ppermute | solution.py:267
  60.2 9.7 %collective-permute-start.11 = (f32[216,128]{1,0:T(8,128)S(1)}, f32[216,128]{1,0:T(8,128)S(1)}, u32[]{:S(2)}, u32[]{:S(2)}) collective-permute-start(f32[216,128]{1,0:T(8,128)S(1)} %get-tuple-element.22), channel_id=1, source_target_pairs={{0,1},{1,2},{2,3},{3,4},{4,5},{5,6},{6,7},{7,8},{8,9},{9,10},{10,1... | collective-permute-start | bytes 331784 | tf_op jit(solution)/shard_map/ppermute | solution.py:264
  60.2 10.9 %collective-permute-start.10 = (f32[216,128]{1,0:T(8,128)S(1)}, f32[216,128]{1,0:T(8,128)S(1)}, u32[]{:S(2)}, u32[]{:S(2)}) collective-permute-start(f32[216,128]{1,0:T(8,128)S(1)} %get-tuple-element.22), channel_id=1, source_target_pairs={{0,63},{1,0},{2,1},{3,2},{4,3},{5,4},{6,5},{7,6},{8,7},{9,8},{10,9... | collective-permute-start | bytes 331784 | tf_op jit(solution)/shard_map/ppermute | solution.py:263
  69.9 2.2 %collective-permute-start.13 = (f32[216,128]{1,0:T(8,128)S(1)}, f32[216,128]{1,0:T(8,128)S(1)}, u32[]{:S(2)}, u32[]{:S(2)}) collective-permute-start(f32[216,128]{1,0:T(8,128)S(1)} %collective-permute-done.11.refs_7_), channel_id=1, source_target_pairs={{0,64},{64,0},{1,65},{65,1},{2,66},{66,2},{3,67},{67,3},{4,68},{68... | collective-permute-start | bytes 331784 | tf_op jit(solution)/shard_map/ppermute | solution.py:269
  71.1 1.3 %collective-permute-start.12 = (f32[216,128]{1,0:T(8,128)S(1)}, f32[216,128]{1,0:T(8,128)S(1)}, u32[]{:S(2)}, u32[]{:S(2)}) collective-permute-start(f32[216,128]{1,0:T(8,128)S(1)} %collective-permute-done.10.refs_6_), channel_id=1, source_target_pairs={{0,64},{64,0},{1,65},{65,1},{2,66},{66,2},{3,67},{67,3},{4,68},{68... | collective-permute-start | bytes 331784 | tf_op jit(solution)/shard_map/ppermute | solution.py:268
  (4 other events, 45.4 us)
